TPU v7x, 256 devices: a whole 4x4x8 slice. The times are simulated.
256 devices in a mesh: seq: 32 (over z, y), tp: 8 (over x, core).
Axes of the slice: x: 4, y: 4, z: 8, core: 2. Of those that a mesh axis runs over, the one named last changes fastest.
Arguments:
- tokens: bfloat16 [4096, 2048], P('seq'), may hold values from -6 to 6
- norm_gain: float32 [2048], replicated, may hold values from 0.5 to 1.5
- w_x: bfloat16 [2048, 2048], P(None, 'tp'), may hold values from -0.125 to 0.125
- w_z: bfloat16 [2048, 2048], P(None, 'tp'), may hold values from -0.125 to 0.125
- conv_w: float32 [4, 2048], P(None, 'tp'), may hold values from -3 to 3
- conv_b: float32 [2048], P('tp'), may hold values from -0.5 to 0.5
- w_xproj: bfloat16 [2048, 160], P('tp'), may hold values from -0.125 to 0.125
- w_dt: bfloat16 [128, 2048], P(None, 'tp'), may hold values from -0.5 to 0.5
- dt_bias: float32 [2048], P('tp'), may hold values from -4.6 to -3.4
- a_log: float32 [16, 2048], P(None, 'tp'), may hold values from -3.9 to -0.7
- d_skip: float32 [2048], P('tp'), may hold values from 0.5 to 1.5
- w_out: bfloat16 [2048, 2048], P('tp'), may hold values from -0.125 to 0.125
- mlp_gain: float32 [2048], replicated, may hold values from 0.5 to 1.5
- w_gate: bfloat16 [2048, 4096], P(None, 'tp'), may hold values from -0.125 to 0.125
- w_up: bfloat16 [2048, 4096], P(None, 'tp'), may hold values from -0.125 to 0.125
- w_down: bfloat16 [4096, 2048], P('tp'), may hold values from -0.09375 to 0.09375
- prompt_lengths: int32 [16], replicated, may hold values from 1 to 2048, as said below
- request_prompt: int32 [128], P('seq'), may hold values from 0 to 15, as said below
Outputs:
- mixed_out: bfloat16 [4096, 2048], P(('seq', 'tp'))
- req_states: float32 [128, 16, 2048], P('seq', None, 'tp')
- req_edges: bfloat16 [128, 3, 2048], P('seq', None, 'tp')
Inputs may be any that keep to these rules, and one draw needn't show every extreme that they name: `prompt_lengths`: the prompts are packed in order from slot 0 and sum to 4032 tokens; the remaining slots are padding; the last prompt is exactly 2048 long. `request_prompt`: every prompt is continued by at least one request.
All inputs are finite; a program needn't handle non-finite values.
Results may differ from a plain program's by a relative error of at most 0.025.
Values may be sent and summed in bfloat16 or wider, within the bound.
No kernel may reach another device: no remote copies, remote signals or barrier semaphores. Data moves between devices by JAX's collectives and lax.ppermute only.
A program may use at most 64 MiB of HBM per device.

v0:
```python
import jax
import jax.numpy as jnp
from jax import lax
from jax.sharding import PartitionSpec as P

EPSILON = 1e-05


def from_behind(x, axis, by):
    devices = lax.axis_size(axis)
    pairs = [(i, i + by) for i in range(devices) if 0 <= i + by < devices]
    return lax.ppermute(x, axis, pairs)


def entering(x, axis, join, neutral):
    place = lax.axis_index(axis)
    gathered = jax.tree.map(
        lambda a, kind: lax.all_gather(a.astype(kind), axis), x, (jnp.bfloat16, jnp.bfloat16)
    )
    state = jax.tree.map(lambda a, e: jnp.zeros_like(a) + jnp.asarray(e, a.dtype), x, neutral)

    def one(step, state):
        return join(
            state,
            jax.tree.map(
                lambda a, own: lax.dynamic_index_in_dim(a, step, 0, False).astype(own.dtype),
                gathered,
                x,
            ),
        )

    return lax.fori_loop(0, place, one, state)


def rms_norm(values, gain):
    scale = lax.rsqrt(jnp.mean(values * values, axis=-1, keepdims=True) + EPSILON)
    return values * scale * gain


def link(earlier, later):
    return (earlier[0] * later[0], later[0] * earlier[1] + later[1])


def local(
    tokens,
    norm_gain,
    w_x,
    w_z,
    conv_w,
    conv_b,
    w_xproj,
    w_dt,
    dt_bias,
    a_log,
    d_skip,
    w_out,
    mlp_gain,
    w_gate,
    w_up,
    w_down,
    prompt_lengths,
    request_prompt,
):
    block_len = tokens.shape[0]
    tp_count = lax.axis_size("tp")
    row_count = block_len // tp_count
    seq_pos = lax.axis_index("seq")
    tp_pos = lax.axis_index("tp")
    first_row = seq_pos * block_len
    prompts = prompt_lengths.shape[0]
    kernel_len = conv_w.shape[0]
    edge_len = kernel_len - 1
    low_dim = w_dt.shape[0]
    state_dim = a_log.shape[0]
    chans = w_x.shape[1]
    places = first_row + jnp.arange(block_len, dtype=jnp.int32)
    prompt_end = jnp.cumsum(prompt_lengths)
    prompt_start = prompt_end - prompt_lengths
    prompt_ids = jnp.arange(prompts, dtype=jnp.int32)
    prompt_of = jnp.sum((places[:, None] >= prompt_end[None, :]).astype(jnp.int32), axis=1)
    start_of = jnp.sum(
        jnp.where(prompt_of[:, None] == prompt_ids[None, :], prompt_start[None, :], 0), axis=1
    )
    offset = places - start_of
    starts_here = jnp.any(places[:, None] == prompt_start[None, :], axis=1)
    is_live = prompt_of < prompts
    normed = rms_norm(tokens.astype(jnp.float32), norm_gain).astype(jnp.bfloat16)
    x_branch = jnp.dot(normed, w_x, preferred_element_type=jnp.float32).astype(jnp.bfloat16)
    z_branch = jnp.dot(normed, w_z, preferred_element_type=jnp.float32).astype(jnp.bfloat16)
    carried = from_behind(x_branch[block_len - edge_len :], "seq", 1)
    extended = jnp.concatenate([carried, x_branch], axis=0)
    conv_sum = jnp.zeros((block_len, chans), jnp.float32) + conv_b[None, :]
    for lag_steps in range(kernel_len):
        window = extended[edge_len - lag_steps : edge_len - lag_steps + block_len].astype(
            jnp.float32
        )
        reach_mask = (offset >= lag_steps).astype(jnp.float32)[:, None]
        conv_sum = conv_sum + conv_w[edge_len - lag_steps][None, :] * window * reach_mask
    conv_out = jax.nn.silu(conv_sum).astype(jnp.bfloat16)
    conv_float = conv_out.astype(jnp.float32)
    projected = lax.psum(
        jnp.dot(conv_out, w_xproj, preferred_element_type=jnp.float32).astype(jnp.bfloat16), "tp"
    ).astype(jnp.float32)
    low_rank = projected[:, :low_dim].astype(jnp.bfloat16)
    in_map = projected[:, low_dim : low_dim + state_dim]
    out_map = projected[:, low_dim + state_dim :]
    step_size = jax.nn.softplus(
        jnp.dot(low_rank, w_dt, preferred_element_type=jnp.float32) + dt_bias[None, :]
    )
    decay_rates = -jnp.exp(a_log)
    carry_on = 1.0 - starts_here.astype(jnp.float32)
    decay = jnp.exp(step_size[:, None, :] * decay_rates[None, :, :]) * carry_on[:, None, None]
    drive = (step_size * conv_float)[:, None, :] * in_map[:, :, None]
    acc_decay, acc_state = lax.associative_scan(link, (decay, drive), axis=0)
    last_decay = acc_decay[block_len - 1]
    last_state = acc_state[block_len - 1]
    identity = (jnp.ones_like(last_decay), jnp.zeros_like(last_state))
    incoming = entering((last_decay, last_state), "seq", link, identity)
    state_in = incoming[1]
    states = acc_state + acc_decay * state_in[None]
    mixer_y = jnp.einsum("tn,tne->te", out_map, states, precision=lax.Precision.HIGHEST)
    mixer_y = mixer_y + d_skip[None, :] * conv_float
    gated = (mixer_y * jax.nn.silu(z_branch.astype(jnp.float32))).astype(jnp.bfloat16)
    end_pick = (places[None, :] == prompt_end[:, None] - 1).astype(jnp.float32)
    final_part = jnp.einsum("pt,tne->pne", end_pick, states, precision=lax.Precision.HIGHEST)
    ends_local = (prompt_end - 1 >= first_row) & (prompt_end - 1 < first_row + block_len)
    lag_ids = jnp.arange(edge_len, dtype=jnp.int32)
    ext_rows = jnp.arange(block_len + edge_len, dtype=jnp.int32)
    target_row = prompt_end[:, None] + lag_ids[None, :] - first_row
    inside = (
        prompt_end[:, None] - edge_len + lag_ids[None, :] >= prompt_start[:, None]
    ) & ends_local[:, None]
    edge_pick = ((ext_rows[None, None, :] == target_row[:, :, None]) & inside[:, :, None]).astype(
        jnp.bfloat16
    )
    edge_part = jnp.einsum("pji,ie->pje", edge_pick, extended, preferred_element_type=jnp.float32)
    final_all, edge_all = (
        lax.psum(final_part.astype(jnp.bfloat16), "seq").astype(jnp.float32),
        lax.psum(edge_part.astype(jnp.bfloat16), "seq").astype(jnp.float32),
    )
    chooser = (request_prompt[:, None] == prompt_ids[None, :]).astype(jnp.float32)
    req_states = jnp.einsum("rp,pne->rne", chooser, final_all, precision=lax.Precision.HIGHEST)
    req_edges = jnp.einsum(
        "rp,pje->rje", chooser, edge_all, precision=lax.Precision.HIGHEST
    ).astype(jnp.bfloat16)
    mixed_sum = lax.psum(
        jnp.dot(gated, w_out, preferred_element_type=jnp.float32).astype(jnp.bfloat16), "tp"
    ).astype(jnp.float32)
    residual = tokens.astype(jnp.float32) + mixed_sum
    normed_two = rms_norm(residual, mlp_gain).astype(jnp.bfloat16)
    residual_rows = lax.dynamic_slice_in_dim(residual, tp_pos * row_count, row_count, 0)
    gate_val = jnp.dot(normed_two, w_gate, preferred_element_type=jnp.float32)
    up_val = jnp.dot(normed_two, w_up, preferred_element_type=jnp.float32)
    hidden = (jax.nn.silu(gate_val) * up_val).astype(jnp.bfloat16)
    mlp_share = lax.psum_scatter(
        jnp.dot(hidden, w_down, preferred_element_type=jnp.float32).astype(jnp.bfloat16),
        "tp",
        scatter_dimension=0,
        tiled=True,
    ).astype(jnp.float32)
    live_rows = lax.dynamic_slice_in_dim(is_live, tp_pos * row_count, row_count, 0).astype(
        jnp.float32
    )
    mixed_out = ((residual_rows + mlp_share) * live_rows[:, None]).astype(jnp.bfloat16)
    return (mixed_out, req_states, req_edges)


def solution(mesh):
    placed = (
        P("seq", None),
        P(),
        P(None, "tp"),
        P(None, "tp"),
        P(None, "tp"),
        P("tp"),
        P("tp", None),
        P(None, "tp"),
        P("tp"),
        P(None, "tp"),
        P("tp"),
        P("tp", None),
        P(),
        P(None, "tp"),
        P(None, "tp"),
        P("tp", None),
        P(),
        P("seq"),
    )
    return jax.shard_map(
        local,
        mesh=mesh,
        in_specs=placed,
        out_specs=(P(("seq", "tp"), None), P("seq", None, "tp"), P("seq", None, "tp")),
        check_vma=False,
    )
```

profile of v0, /device:TPU:40, one launch (start us, length us, event | category | flops | bytes accessed | tf_op | source)
XLA Modules:
  0.0 676.3 jit_solution(7324895840370239036)
XLA Ops:
  8.7 1.8 convolution_convert_fusion.3
  10.5 3.5 collective-permute-start
  17.2 25.7 %psum.28 = bf16[128,160]{0,1:T(8,128)(2,1)S(1)} all-reduce(bf16[128,160]{0,1:T(8,128)(2,1)S(1)} %convolution_convert_fusion.4), channel_id=1, replica_groups=mesh['seq'=32,'tp'=8] {'tp'}, use_global_device_ids=true, to_apply=%region_4.5 | all-reduce | flops 20480 | bytes 81920 | tf_op jit(solution)/shard_map/psum | solution.py:101
  54.5 1.9 pad.88
  56.4 2.0 pad.89
  58.4 1.9 pad.103
  61.7 2.0 pad.102
  72.4 3.3 pad.90
  75.7 3.3 pad.91
  79.0 3.3 pad.105
  83.8 1.7 fusion.28
  85.6 1.7 add.335
  88.6 2.9 pad.106
  93.1 4.8 pad.92
  97.9 4.8 pad.93
  102.7 3.1 pad.107
  105.8 1.8 add.347
  107.6 2.3 fusion.17
  111.3 8.7 %pad.108 = f32[32,16,256]{2,1,0:T(8,128)} pad(f32[16,16,256]{2,1,0:T(8,128)} %pad_maximum_fusion.5, f32[]{:T(128)} %constant.27.clone.1), padding=0_1_1x0_0_0x0_0_0 | pad | bytes 786436 | tf_op jit(solution)/shard_map/pad | solution.py:114
  120.0 1.7 pad_maximum_fusion.4
  121.7 8.7 %pad.94 = f32[32,16,256]{2,1,0:T(8,128)} pad(f32[16,16,256]{2,1,0:T(8,128)} %pad_maximum_fusion.4, f32[]{:T(128)} %constant.27.clone.1), padding=0_1_1x0_0_0x0_0_0 | pad | bytes 786436 | tf_op jit(solution)/shard_map/pad | solution.py:114
  130.4 8.7 %pad.95 = f32[32,16,256]{2,1,0:T(8,128)} pad(f32[16,16,256]{2,1,0:T(8,128)} %add.337, f32[]{:T(128)} %constant.27.clone.1), padding=1_0_1x0_0_0x0_0_0 | pad | bytes 786436 | tf_op jit(solution)/shard_map/pad | solution.py:114
  139.1 5.7 pad.109
  144.8 2.1 add.348
  146.8 2.9 fusion.11
  151.5 11.6 %pad.110 = f32[64,16,256]{2,1,0:T(8,128)S(1)} pad(f32[32,16,256]{2,1,0:T(8,128)} %pad_maximum_fusion.3, f32[]{:T(128)} %constant.27.clone.1), padding=0_1_1x0_0_0x0_0_0 | pad | bytes 1572868 | tf_op jit(solution)/shard_map/pad | solution.py:114
  163.1 1.9 pad_maximum_fusion.2
  164.9 15.6 %pad.96 = f32[64,16,256]{2,1,0:T(8,128)} pad(f32[32,16,256]{2,1,0:T(8,128)} %pad_maximum_fusion.2, f32[]{:T(128)} %constant.27.clone.1), padding=0_1_1x0_0_0x0_0_0 | pad | bytes 1572868 | tf_op jit(solution)/shard_map/pad | solution.py:114
  180.6 15.6 %pad.97 = f32[64,16,256]{2,1,0:T(8,128)} pad(f32[32,16,256]{2,1,0:T(8,128)} %add.339, f32[]{:T(128)} %constant.27.clone.1), padding=1_0_1x0_0_0x0_0_0 | pad | bytes 1572868 | tf_op jit(solution)/shard_map/pad | solution.py:114
  196.2 15.7 %pad.111 = f32[64,16,256]{2,1,0:T(8,128)} pad(f32[32,16,256]{2,1,0:T(8,128)} %add.348, f32[]{:T(128)} %constant.27.clone.1), padding=1_0_1x0_0_0x0_0_0 | pad | bytes 1572868 | tf_op jit(solution)/shard_map/pad | solution.py:114
  211.9 2.6 add.349
  214.4 3.6 fusion.10
  220.7 20.6 %pad.112 = f32[128,16,256]{2,1,0:T(8,128)} pad(f32[64,16,256]{2,1,0:T(8,128)S(1)} %pad_maximum_fusion.1, f32[]{:T(128)} %constant.27.clone.1), padding=0_1_1x0_0_0x0_0_0 | pad | bytes 3145732 | tf_op jit(solution)/shard_map/pad | solution.py:114
  242.6 20.5 %pad.98 = f32[128,16,256]{2,1,0:T(8,128)} pad(f32[64,16,256]{2,1,0:T(8,128)S(1)} %pad_maximum_fusion, f32[]{:T(128)} %constant.27.clone.1), padding=0_1_1x0_0_0x0_0_0 | pad | bytes 3145732 | tf_op jit(solution)/shard_map/pad | solution.py:114
  263.2 30.3 %pad.99 = f32[128,16,256]{2,1,0:T(8,128)} pad(f32[64,16,256]{2,1,0:T(8,128)} %add.341, f32[]{:T(128)} %constant.27.clone.1), padding=1_0_1x0_0_0x0_0_0 | pad | bytes 3145732 | tf_op jit(solution)/shard_map/pad | solution.py:114
  294.2 50.1 %all_gather.9 = bf16[32,16,256]{2,1,0:T(8,128)(2,1)S(1)} all-gather(bf16[1,16,256]{2,1,0:T(8,128)(2,1)S(1)} %add_convert_fusion), channel_id=1, replica_groups=mesh['seq'=32,'tp'=8] {'seq'}, dimensions={0}, use_global_device_ids=true | all-gather | bytes 270336 | tf_op jit(solution)/shard_map/all_gather | solution.py:18
  344.3 20.6 %pad.113 = f32[128,16,256]{2,1,0:T(8,128)} pad(f32[64,16,256]{2,1,0:T(8,128)S(1)} %copy-done.11, f32[]{:T(128)} %constant.27.clone.1), padding=1_0_1x0_0_0x0_0_0 | pad | bytes 3145732 | tf_op jit(solution)/shard_map/pad | solution.py:114
  365.7 48.2 %all_gather.8 = bf16[32,16,256]{2,1,0:T(8,128)(2,1)S(1)} all-gather(bf16[1,16,256]{2,1,0:T(8,128)(2,1)S(1)} %add_convert_fusion.1), channel_id=1, replica_groups=mesh['seq'=32,'tp'=8] {'seq'}, dimensions={0}, use_global_device_ids=true | all-gather | bytes 270336 | tf_op jit(solution)/shard_map/all_gather | solution.py:18
  414.1 4.5 multiply_add_fusion
  421.0 3.2 convolution_convert_fusion.1
  424.5 4.1 fusion.3
  428.7 59.6 %all-reduce.31.cloned.1.call-done = bf16[128,2048]{1,0:T(8,128)(2,1)} async-done(((bf16[128,2048]{1,0:T(8,128)(2,1)}), bf16[128,2048]{1,0:T(8,128)(2,1)}) %all-reduce.31.cloned.1.call-update) | async-done | bytes 524304 | tf_op jit(solution)/shard_map/psum | solution.py:146
  488.3 2.3 convert_add_fusion.1
  492.4 3.3 convolution_convert_fusion
  496.1 132.0 %psum.31 = bf16[16,3,256]{2,0,1:T(8,128)(2,1)S(1)} all-reduce(bf16[16,3,256]{2,0,1:T(8,128)(2,1)S(1)} %convolution_convert_fusion.5), channel_id=1, replica_groups=mesh['seq'=32,'tp'=8] {'seq'}, use_global_device_ids=true, to_apply=%region_12.13 | all-reduce | flops 12288 | bytes 49152 | tf_op jit(solution)/shard_map/psum | solution.py:139
  628.9 4.4 all-reduce.33.cloned.1.call-done
  635.0 33.2 %reduce-scatter.2.cloned.1.call-done = bf16[16,2048]{1,0:T(8,128)(2,1)} async-done(((bf16[128,2048]{1,0:T(8,128)(2,1)}), bf16[16,2048]{1,0:T(8,128)(2,1)}) %reduce-scatter.2.cloned.1.call-update) | async-done | bytes 65552 | tf_op jit(solution)/shard_map/reduce_scatter | solution.py:155
  668.2 1.6 multiply_convert_fusion.1
  (199 shorter events, 46.6 us)
Async XLA Ops:
  7.2 485.1 %copy-start = (bf16[512,2048]{1,0:T(8,128)(2,1)S(1)}, bf16[512,2048]{1,0:T(8,128)(2,1)}, u32[]{:S(2)}) copy-start(bf16[512,2048]{1,0:T(8,128)(2,1)} %param.35) | copy-start | bytes 6291460
  7.2 6.8 %copy-start.38 = (f32[4,256]{1,0:T(4,128)S(1)}, f32[4,256]{1,0:T(4,128)}, u32[]{:S(2)}) copy-start(f32[4,256]{1,0:T(4,128)} %param.24) | copy-start | bytes 12292
  7.2 6.8 %copy-start.41 = (s32[16]{0:T(128)S(1)}, s32[16]{0:T(128)}, u32[]{:S(2)}) copy-start(s32[16]{0:T(128)} %param.36) | copy-start | bytes 196
  7.2 8.4 %copy-start.34 = (f32[16,256]{1,0:T(8,128)S(1)}, f32[16,256]{1,0:T(8,128)}, u32[]{:S(2)}) copy-start(f32[16,256]{1,0:T(8,128)} %param.29) | copy-start | bytes 49156
  7.2 9.6 %copy-start.43 = (f32[256]{0:T(256)S(1)}, f32[256]{0:T(256)}, u32[]{:S(2)}) copy-start(f32[256]{0:T(256)} %param.25) | copy-start | bytes 3076
  7.2 9.8 %copy-start.24 = (bf16[256,160]{0,1:T(8,128)(2,1)S(1)}, bf16[256,160]{0,1:T(8,128)(2,1)}, u32[]{:S(2)}) copy-start(bf16[256,160]{0,1:T(8,128)(2,1)} %param.26) | copy-start | bytes 245764
  7.2 36.4 %copy-start.44 = (f32[256]{0:T(256)S(1)}, f32[256]{0:T(256)}, u32[]{:S(2)}) copy-start(f32[256]{0:T(256)} %param.28) | copy-start | bytes 3076
  7.2 36.4 %copy-start.32 = (bf16[128,256]{1,0:T(8,128)(2,1)S(1)}, bf16[128,256]{1,0:T(8,128)(2,1)}, u32[]{:S(2)}) copy-start(bf16[128,256]{1,0:T(8,128)(2,1)} %param.27) | copy-start | bytes 196612
  7.3 481.1 %all-reduce.31.cloned.1.call-start = ((), (), s32[]{:S(2)}) async-start(), calls=%async_computation.1 | async-start | bytes 1048576 | tf_op jit(solution)/shard_map/psum | solution.py:146
  8.7 5.3 copy-start.53
  10.4 34.0 %copy-start.25 = (bf16[128,256]{1,0:T(8,128)(2,1)}, bf16[128,256]{1,0:T(8,128)(2,1)S(1)}, u32[]{:S(2)}) copy-start(bf16[128,256]{1,0:T(8,128)(2,1)S(1)} %convolution_convert_fusion.3) | copy-start | bytes 196612
  10.5 5.8 collective-permute-start
  14.0 1.6 copy-start.47
  17.0 27.5 %copy-start.21 = (bf16[128,256]{1,0:T(8,128)(2,1)}, bf16[128,256]{1,0:T(8,128)(2,1)S(1)}, u32[]{:S(2)}) copy-start(bf16[128,256]{1,0:T(8,128)(2,1)S(1)} %multiply_convert_fusion.2) | copy-start | bytes 196612
  44.5 1.3 copy-start.2
  44.5 2.0 copy-start.3
  46.5 2.9 copy-start.7
  48.0 1.4 copy-start.12
  48.0 2.1 copy-start.13
  85.6 17.1 %copy-start.23 = (f32[8,16,256]{2,1,0:T(8,128)S(1)}, f32[8,16,256]{2,1,0:T(8,128)}, u32[]{:S(2)}) copy-start(f32[8,16,256]{2,1,0:T(8,128)} %add.346) | copy-start | bytes 393220
  105.8 4.0 copy-start.14
  105.8 4.0 copy-start.15
  105.8 4.8 copy-start.31
  107.6 12.4 %copy-start.30 = (f32[1,16,256]{2,1,0:T(8,128)S(1)}, f32[1,16,256]{2,1,0:T(8,128)}, u32[]{:S(2)}) copy-start(f32[1,16,256]{2,1,0:T(8,128)} %slice.335) | copy-start | bytes 49156
  109.9 29.2 %copy-start.19 = (f32[16,16,256]{2,1,0:T(8,128)S(1)}, f32[16,16,256]{2,1,0:T(8,128)}, u32[]{:S(2)}) copy-start(f32[16,16,256]{2,1,0:T(8,128)} %add.347) | copy-start | bytes 786436
  146.8 2.9 copy-start.9
  146.8 2.9 copy-start.10
  146.8 3.8 copy-start.29
  149.8 13.3 %copy-start.28 = (f32[1,16,256]{2,1,0:T(8,128)S(1)}, f32[1,16,256]{2,1,0:T(8,128)}, u32[]{:S(2)}) copy-start(f32[1,16,256]{2,1,0:T(8,128)} %slice.334) | copy-start | bytes 49156
  211.9 2.6 copy-start.4
  211.9 2.6 copy-start.5
  211.9 2.6 copy-start.6
  218.1 1.4 copy-start.27
  263.1 81.2 %copy-start.11 = (f32[64,16,256]{2,1,0:T(8,128)S(1)}, f32[64,16,256]{2,1,0:T(8,128)}, u32[]{:S(2)}) copy-start(f32[64,16,256]{2,1,0:T(8,128)} %add.349) | copy-start | bytes 3145732
  418.6 1.3 copy-start.1
  421.0 3.4 copy-start.42
  421.0 3.4 copy-start.48
  424.2 209.0 %all-reduce.33.cloned.1.call-start = ((), (), s32[]{:S(2)}) async-start(), calls=%async_computation.3 | async-start | bytes 262144 | tf_op jit(solution)/shard_map/psum | solution.py:138
  424.5 66.2 %copy-start.35 = (f32[2048]{0:T(1024)S(1)}, f32[2048]{0:T(1024)}, u32[]{:S(2)}) copy-start(f32[2048]{0:T(1024)} %param.32) | copy-start | bytes 24580
  428.6 239.5 %reduce-scatter.2.cloned.1.call-start = ((), (), s32[]{:S(2)}) async-start(), calls=%async_computation.2 | async-start | bytes 589824 | tf_op jit(solution)/shard_map/reduce_scatter | solution.py:155
  488.3 2.4 copy-start.16
  490.7 1.6 copy-start.17
  492.3 3.4 copy-start.52
  492.3 3.5 copy-start.37
  492.3 3.5 copy-start.26
  492.3 3.5 copy-start.40
  492.3 3.5 copy-start.46
  492.4 135.7 %copy-start.45 = (s32[4]{0:T(128)S(1)}, s32[4]{0:T(128)}, u32[]{:S(2)}) copy-start(s32[4]{0:T(128)} %param.37) | copy-start | bytes 52
  (11 other events, 11.5 us)
Sparse Core Ops, SparseCore 0:
  424.3 63.9 all-reduce.30
  491.8 141.4 all-reduce.32
  635.8 32.3 reduce-scatter.1
where the time goes:
time: 689 us; the launch traced here: 676 us
  blocking collectives  256 us (37%)
  local copies, waits for them, and re-layouts  227 us (33%)
  waiting for transfers between devices  97.2 us (14%)
  other arithmetic  60 us (9%)
  matrix products  17.4 us (3%)
  between operations  14.4 us (2%)
    pad x24, local copies, waits for them, and re-layouts, local(): acc_decay, acc_state = lax.associative_scan(link, (decay, drive), axis=0)  217 us
    psum x1, blocking collectives, local(): lax.psum(edge_part.astype(jnp.bfloat16), 'seq').astype(jnp.float32)  132 us
    all_gather x2, blocking collectives, entering(): lax.all_gather(a.astype(kind), axis)  98.3 us
    psum x1, waiting for transfers between devices, local(): lax.psum(jnp.dot(gated, w_out, preferred_element_type=jnp.float32).astype...  59.6 us
    reduce_scatter x1, waiting for transfers between devices, local(): lax.psum_scatter(jnp.dot(hidden, w_down, preferred_element_type=jnp.float...  33.2 us
    psum x1, blocking collectives, local(): lax.psum(jnp.dot(conv_out, w_xproj, preferred_element_type=jnp.float32).a...  25.7 us
    add x12, other arithmetic, local(): acc_decay, acc_state = lax.associative_scan(link, (decay, drive), axis=0)  16.7 us
    concatenate x12, other arithmetic, local(): acc_decay, acc_state = lax.associative_scan(link, (decay, drive), axis=0)  15.3 us
  transfers between devices with their start and end apart: 4, of which 3 were waited for; matrix products, arithmetic and copies ran while one was open for 2% of the time, Pallas kernels for 0%

commit v1 on v0

--- a/solution.py
+++ b/solution.py
@@ -1,9 +1,14 @@
+import functools
+
 import jax
 import jax.numpy as jnp
 from jax import lax
+from jax.experimental import pallas as pl
+from jax.experimental.pallas import tpu as pltpu
 from jax.sharding import PartitionSpec as P
 
 EPSILON = 1e-05
+INTERPRET = False
 
 
 def from_behind(x, axis, by):
@@ -12,24 +17,58 @@
     return lax.ppermute(x, axis, pairs)
 
 
-def entering(x, axis, join, neutral):
-    place = lax.axis_index(axis)
-    gathered = jax.tree.map(
-        lambda a, kind: lax.all_gather(a.astype(kind), axis), x, (jnp.bfloat16, jnp.bfloat16)
-    )
-    state = jax.tree.map(lambda a, e: jnp.zeros_like(a) + jnp.asarray(e, a.dtype), x, neutral)
-
-    def one(step, state):
-        return join(
-            state,
-            jax.tree.map(
-                lambda a, own: lax.dynamic_index_in_dim(a, step, 0, False).astype(own.dtype),
-                gathered,
-                x,
-            ),
-        )
-
-    return lax.fori_loop(0, place, one, state)
+def swap(x, axis, bit):
+    devices = lax.axis_size(axis)
+    return lax.ppermute(x, axis, [(i, i ^ bit) for i in range(devices)])
+
+
+def bits_of(devices):
+    out = []
+    bit = 1
+    while bit < devices:
+        out.append(bit)
+        bit *= 2
+    assert bit == devices
+    return out
+
+
+def butterfly_sum(x, axis, send_dtype):
+    for bit in bits_of(lax.axis_size(axis)):
+        x = x + swap(x.astype(send_dtype), axis, bit).astype(x.dtype)
+    return x
+
+
+def scatter_rows(x, axis, first_dtype):
+    devices = lax.axis_size(axis)
+    bits = bits_of(devices)
+    me = lax.axis_index(axis)
+    depth = len(bits)
+    rows = x.shape[0] // devices
+    buf = x.reshape((2,) * depth + (rows, x.shape[1]))
+    send_dtype = first_dtype
+    for level, bit in enumerate(bits):
+        at = depth - 1 - level
+        mine = ((me // bit) % 2).astype(jnp.int32)
+        keep = lax.dynamic_index_in_dim(buf, mine, at, False)
+        give = lax.dynamic_index_in_dim(buf, 1 - mine, at, False)
+        got = swap(give.astype(send_dtype), axis, bit)
+        buf = keep.astype(jnp.float32) + got.astype(jnp.float32)
+        send_dtype = jnp.float32
+    return buf
+
+
+def gather_rows(x, axis):
+    devices = lax.axis_size(axis)
+    bits = bits_of(devices)
+    me = lax.axis_index(axis)
+    buf = x
+    for level, bit in enumerate(reversed(bits)):
+        got = swap(buf, axis, bit)
+        upper = ((me // bit) % 2) == 1
+        low = jnp.where(upper, got, buf)
+        high = jnp.where(upper, buf, got)
+        buf = jnp.stack([low, high], axis=level)
+    return buf.reshape((devices * x.shape[0], x.shape[1]))
 
 
 def rms_norm(values, gain):
@@ -37,8 +76,101 @@
     return values * scale * gain
 
 
-def link(earlier, later):
-    return (earlier[0] * later[0], later[0] * earlier[1] + later[1])
+def block_summary_kernel(da_ref, dr_ref, send_ref, atot_ref):
+    steps = da_ref.shape[0]
+
+    def chunk(c, carry):
+        state, acum = carry
+        base = c * 8
+        for i in range(8):
+            da = da_ref[base + i]
+            state = da * state + dr_ref[base + i]
+            acum = da * acum
+        return state, acum
+
+    zero = jnp.zeros(send_ref.shape, jnp.float32)
+    one = jnp.ones(atot_ref.shape, jnp.float32)
+    state, acum = lax.fori_loop(0, steps // 8, chunk, (zero, one))
+    send_ref[...] = state
+    atot_ref[...] = acum
+
+
+def block_output_kernel(da_ref, dr_ref, om_ref, sin_ref, endf_ref, pid_ref, y_ref, fin_ref):
+    steps = da_ref.shape[0]
+    width = y_ref.shape[1]
+    fin_ref[...] = jnp.zeros(fin_ref.shape, jnp.float32)
+    row_ids = lax.broadcasted_iota(jnp.int32, (8, width), 0)
+
+    def chunk(c, state):
+        base = pl.multiple_of(c * 8, 8)
+        rows = jnp.zeros((8, width), jnp.float32)
+        for i in range(8):
+            t = base + i
+            state = da_ref[t] * state + dr_ref[t]
+            here = jnp.sum(om_ref[t] * state, axis=0, keepdims=True)
+            rows = jnp.where(row_ids == i, here, rows)
+
+            @pl.when(endf_ref[t] != 0)
+            def _():
+                fin_ref[pid_ref[t]] = state
+
+        y_ref[pl.ds(base, 8), :] = rows
+        return state
+
+    lax.fori_loop(0, steps // 8, chunk, sin_ref[...])
+
+
+def block_summary(da, dr):
+    _, n, e = da.shape
+    vmem = pl.BlockSpec(memory_space=pltpu.VMEM)
+    return pl.pallas_call(
+        block_summary_kernel,
+        out_shape=(
+            jax.ShapeDtypeStruct((n, e), jnp.float32),
+            jax.ShapeDtypeStruct((n, e), jnp.float32),
+        ),
+        in_specs=[vmem, vmem],
+        out_specs=(vmem, vmem),
+        interpret=INTERPRET,
+    )(da, dr)
+
+
+def block_output(da, dr, om, sin, endf, pid, prompts):
+    t, n, e = da.shape
+    vmem = pl.BlockSpec(memory_space=pltpu.VMEM)
+    smem = pl.BlockSpec(memory_space=pltpu.SMEM)
+    return pl.pallas_call(
+        block_output_kernel,
+        out_shape=(
+            jax.ShapeDtypeStruct((t, e), jnp.float32),
+            jax.ShapeDtypeStruct((prompts, n, e), jnp.float32),
+        ),
+        in_specs=[vmem, vmem, vmem, vmem, smem, smem],
+        out_specs=(vmem, vmem),
+        interpret=INTERPRET,
+    )(da, dr, om, sin, endf, pid)
+
+
+def entering_state(a_blk, s_blk, axis):
+    me = lax.axis_index(axis)
+    devices = lax.axis_size(axis)
+    inc_a, inc_s = a_blk, s_blk
+    exc_a, exc_s = jnp.ones_like(a_blk), jnp.zeros_like(s_blk)
+    shift = 1
+    while shift < devices:
+        got = from_behind(jnp.stack([inc_a, inc_s]), axis, shift)
+        got_a, got_s = got[0], got[1]
+        has = me >= shift
+        new_exc_a = got_a * exc_a
+        new_exc_s = exc_a * got_s + exc_s
+        new_inc_a = got_a * inc_a
+        new_inc_s = inc_a * got_s + inc_s
+        exc_a = jnp.where(has, new_exc_a, exc_a)
+        exc_s = jnp.where(has, new_exc_s, exc_s)
+        inc_a = jnp.where(has, new_inc_a, inc_a)
+        inc_s = jnp.where(has, new_inc_s, inc_s)
+        shift *= 2
+    return exc_s
 
 
 def local(
@@ -83,6 +215,7 @@
     )
     offset = places - start_of
     starts_here = jnp.any(places[:, None] == prompt_start[None, :], axis=1)
+    ends_here = jnp.any(places[:, None] == prompt_end[None, :] - 1, axis=1)
     is_live = prompt_of < prompts
     normed = rms_norm(tokens.astype(jnp.float32), norm_gain).astype(jnp.bfloat16)
     x_branch = jnp.dot(normed, w_x, preferred_element_type=jnp.float32).astype(jnp.bfloat16)
@@ -98,9 +231,9 @@
         conv_sum = conv_sum + conv_w[edge_len - lag_steps][None, :] * window * reach_mask
     conv_out = jax.nn.silu(conv_sum).astype(jnp.bfloat16)
     conv_float = conv_out.astype(jnp.float32)
-    projected = lax.psum(
-        jnp.dot(conv_out, w_xproj, preferred_element_type=jnp.float32).astype(jnp.bfloat16), "tp"
-    ).astype(jnp.float32)
+    projected = butterfly_sum(
+        jnp.dot(conv_out, w_xproj, preferred_element_type=jnp.float32), "tp", jnp.float32
+    )
     low_rank = projected[:, :low_dim].astype(jnp.bfloat16)
     in_map = projected[:, low_dim : low_dim + state_dim]
     out_map = projected[:, low_dim + state_dim :]
@@ -111,18 +244,14 @@
     carry_on = 1.0 - starts_here.astype(jnp.float32)
     decay = jnp.exp(step_size[:, None, :] * decay_rates[None, :, :]) * carry_on[:, None, None]
     drive = (step_size * conv_float)[:, None, :] * in_map[:, :, None]
-    acc_decay, acc_state = lax.associative_scan(link, (decay, drive), axis=0)
-    last_decay = acc_decay[block_len - 1]
-    last_state = acc_state[block_len - 1]
-    identity = (jnp.ones_like(last_decay), jnp.zeros_like(last_state))
-    incoming = entering((last_decay, last_state), "seq", link, identity)
-    state_in = incoming[1]
-    states = acc_state + acc_decay * state_in[None]
-    mixer_y = jnp.einsum("tn,tne->te", out_map, states, precision=lax.Precision.HIGHEST)
+    out_wide = jnp.broadcast_to(out_map[:, :, None], decay.shape)
+    s_blk, a_blk = block_summary(decay, drive)
+    state_in = entering_state(a_blk, s_blk, "seq")
+    end_flag = ends_here.astype(jnp.int32)
+    slot_of = jnp.minimum(prompt_of, prompts - 1).astype(jnp.int32)
+    mixer_y, final_part = block_output(decay, drive, out_wide, state_in, end_flag, slot_of, prompts)
     mixer_y = mixer_y + d_skip[None, :] * conv_float
     gated = (mixer_y * jax.nn.silu(z_branch.astype(jnp.float32))).astype(jnp.bfloat16)
-    end_pick = (places[None, :] == prompt_end[:, None] - 1).astype(jnp.float32)
-    final_part = jnp.einsum("pt,tne->pne", end_pick, states, precision=lax.Precision.HIGHEST)
     ends_local = (prompt_end - 1 >= first_row) & (prompt_end - 1 < first_row + block_len)
     lag_ids = jnp.arange(edge_len, dtype=jnp.int32)
     ext_rows = jnp.arange(block_len + edge_len, dtype=jnp.int32)
@@ -134,30 +263,34 @@
         jnp.bfloat16
     )
     edge_part = jnp.einsum("pji,ie->pje", edge_pick, extended, preferred_element_type=jnp.float32)
-    final_all, edge_all = (
-        lax.psum(final_part.astype(jnp.bfloat16), "seq").astype(jnp.float32),
-        lax.psum(edge_part.astype(jnp.bfloat16), "seq").astype(jnp.float32),
-    )
+    handed = jnp.concatenate(
+        [final_part.astype(jnp.bfloat16), edge_part.astype(jnp.bfloat16)], axis=1
+    )
+    handed = butterfly_sum(handed, "seq", jnp.bfloat16).astype(jnp.float32)
+    final_all = handed[:, :state_dim]
+    edge_all = handed[:, state_dim:]
     chooser = (request_prompt[:, None] == prompt_ids[None, :]).astype(jnp.float32)
     req_states = jnp.einsum("rp,pne->rne", chooser, final_all, precision=lax.Precision.HIGHEST)
     req_edges = jnp.einsum(
         "rp,pje->rje", chooser, edge_all, precision=lax.Precision.HIGHEST
     ).astype(jnp.bfloat16)
-    mixed_sum = lax.psum(
-        jnp.dot(gated, w_out, preferred_element_type=jnp.float32).astype(jnp.bfloat16), "tp"
-    ).astype(jnp.float32)
-    residual = tokens.astype(jnp.float32) + mixed_sum
-    normed_two = rms_norm(residual, mlp_gain).astype(jnp.bfloat16)
-    residual_rows = lax.dynamic_slice_in_dim(residual, tp_pos * row_count, row_count, 0)
+    mixed_rows = scatter_rows(
+        jnp.dot(gated, w_out, preferred_element_type=jnp.float32).astype(jnp.bfloat16),
+        "tp",
+        jnp.bfloat16,
+    )
+    token_rows = lax.dynamic_slice_in_dim(tokens, tp_pos * row_count, row_count, 0)
+    residual_rows = token_rows.astype(jnp.float32) + mixed_rows
+    normed_rows = rms_norm(residual_rows, mlp_gain).astype(jnp.bfloat16)
+    normed_two = gather_rows(normed_rows, "tp")
     gate_val = jnp.dot(normed_two, w_gate, preferred_element_type=jnp.float32)
     up_val = jnp.dot(normed_two, w_up, preferred_element_type=jnp.float32)
     hidden = (jax.nn.silu(gate_val) * up_val).astype(jnp.bfloat16)
-    mlp_share = lax.psum_scatter(
+    mlp_share = scatter_rows(
         jnp.dot(hidden, w_down, preferred_element_type=jnp.float32).astype(jnp.bfloat16),
         "tp",
-        scatter_dimension=0,
-        tiled=True,
-    ).astype(jnp.float32)
+        jnp.bfloat16,
+    )
     live_rows = lax.dynamic_slice_in_dim(is_live, tp_pos * row_count, row_count, 0).astype(
         jnp.float32
     )

time: 689 us -> 169 us (0.25)
  the two profiles are of different devices: /device:TPU:40 before, /device:TPU:4 now
where the time goes in v1:
time: 169 us
  waiting for transfers between devices  72.8 us (43%)
  starting transfers between devices  58.1 us (34%)
  other arithmetic  14.7 us (9%)
  matrix products  9.54 us (6%)
  Pallas kernels  8.56 us (5%)
  local copies, waits for them, and re-layouts  3.54 us (2%)
    ppermute x17, waiting for transfers between devices, swap(): return lax.ppermute(x, axis, [(i, i ^ bit) for i in range(devices)])  65.8 us
    ppermute x6, starting transfers between devices, from_behind(): return lax.ppermute(x, axis, pairs)  43.7 us
    ppermute x17, starting transfers between devices, swap(): return lax.ppermute(x, axis, [(i, i ^ bit) for i in range(devices)])  14.4 us
    ppermute x6, waiting for transfers between devices, from_behind(): return lax.ppermute(x, axis, pairs)  7.05 us
    pallas_call x1, Pallas kernels, block_output(): pl.pallas_call(block_output_kernel, out_shape=(jax.ShapeDtypeStruct((t, e...  5.42 us
  transfers between devices with their start and end apart: 23, of which 20 were waited for; matrix products, arithmetic and copies ran while one was open for 7% of the time, Pallas kernels for 0%

profile of v1, /device:TPU:4, one launch (start us, length us, event | category | flops | bytes accessed | tf_op | source)
XLA Modules:
  0.0 168.7 jit_solution(14658811411326226739)
XLA Ops:
  0.7 1.4 fusion.2
  2.1 1.8 %convolution_convert_fusion.3 = bf16[128,256]{1,0:T(8,128)(2,1)S(1)} fusion(bf16[2048,256]{1,0:T(8,128)(2,1)} %param.20, bf16[128,2048]{1,0:T(8,128)(2,1)} %param.18, f32[2048]{0:T(1024)} %param.19, f32[128]{0:T(128)S(1)} %add_rsqrt_fusion.1), kind=kOutput, calls=%fused_computation.10 | convolution fusion | flops 135299072 | bytes 1647104 | tf_op jit(solution)/shard_map/dot_general | solution.py:221
  3.9 3.5 %collective-permute-start = (bf16[3,256]{1,0:T(4,128)(2,1)S(1)}, bf16[3,256]{1,0:T(4,128)(2,1)S(1)}, u32[]{:S(2)}, u32[]{:S(2)}) collective-permute-start(bf16[3,256]{1,0:T(4,128)(2,1)S(1)} %slice.89), channel_id=1, source_target_pairs={{0,8},{8,16},{16,24},{24,32},{32,40},{40,48},{48,56},{56,64},{64,7... | collective-permute-start | bytes 4616 | tf_op jit(solution)/shard_map/ppermute | solution.py:17
  9.1 1.2 collective-permute-done.1
  10.4 1.3 collective-permute-start.2
  11.8 3.2 %collective-permute-done.2 = f32[128,160]{0,1:T(8,128)S(1)} collective-permute-done((f32[128,160]{0,1:T(8,128)S(1)}, f32[128,160]{0,1:T(8,128)S(1)}, u32[]{:S(2)}, u32[]{:S(2)}) %collective-permute-start.2) | collective-permute-done | bytes 81952 | tf_op jit(solution)/shard_map/ppermute | solution.py:22
  15.6 5.4 %collective-permute-done.3 = f32[128,160]{0,1:T(8,128)S(1)} collective-permute-done((f32[128,160]{0,1:T(8,128)S(1)}, f32[128,160]{0,1:T(8,128)S(1)}, u32[]{:S(2)}, u32[]{:S(2)}) %collective-permute-start.3) | collective-permute-done | bytes 81952 | tf_op jit(solution)/shard_map/ppermute | solution.py:22
  21.5 2.4 %exponential_multiply_fusion = (f32[128,16,256]{2,1,0:T(8,128)}, f32[128,16,256]{2,1,0:T(8,128)}) fusion(f32[128]{0:T(128)S(1)} %convert_subtract_fusion, f32[16,256]{1,0:T(8,128)S(1)} %exponential_negate_fusion, f32[128,256]{1,0:T(8,128)S(1)} %get-tuple-element.56, f32[128,16]{1,0:T(8,128)S(1)} %copy.47, f32[128,256]{1,0:T(8,128)S(1)} %get-tuple-element.55), kind=kLoop, calls=%fused_computation.2 | loop fusion | flops 1572864 | bytes 4481536 | tf_op jit(solution)/shard_map/mul | solution.py:245
  23.8 3.1 %shard_map.193 = (f32[16,256]{1,0:T(8,128)}, f32[16,256]{1,0:T(8,128)}) custom-call(f32[128,16,256]{2,1,0:T(8,128)} %get-tuple-element.57.da_ref, f32[128,16,256]{2,1,0:T(8,128)} %get-tuple-element.58.dr_ref), custom_call_target="tpu_custom_call" | custom-call | tf_op jit(solution)/shard_map/pallas_call | solution.py:126
  27.0 0.7 pad_maximum_fusion.5
  27.7 4.2 %collective-permute-start.4 = (f32[2,16,256]{2,1,0:T(8,128)S(1)}, f32[2,16,256]{2,1,0:T(8,128)S(1)}, u32[]{:S(2)}, u32[]{:S(2)}) collective-permute-start(f32[2,16,256]{2,1,0:T(8,128)S(1)} %pad_maximum_fusion.5), channel_id=1, source_target_pairs={{0,8},{8,16},{16,24},{24,32},{32,40},{40,48},{48,56},{56,64},{64,7... | collective-permute-start | bytes 98312 | tf_op jit(solution)/shard_map/ppermute | solution.py:17
  31.9 1.6 collective-permute-done.4
  33.5 0.7 multiply_select_fusion.6
  34.2 5.8 %collective-permute-start.5 = (f32[2,16,256]{2,1,0:T(8,128)S(1)}, f32[2,16,256]{2,1,0:T(8,128)S(1)}, u32[]{:S(2)}, u32[]{:S(2)}) collective-permute-start(f32[2,16,256]{2,1,0:T(8,128)S(1)} %pad_maximum_fusion.6), channel_id=1, source_target_pairs={{0,16},{8,24},{16,32},{24,40},{32,48},{40,56},{48,64},{56,72},{64,... | collective-permute-start | bytes 98312 | tf_op jit(solution)/shard_map/ppermute | solution.py:17
  40.1 1.6 collective-permute-done.5
  41.7 9.6 %collective-permute-start.6 = (f32[2,16,256]{2,1,0:T(8,128)S(1)}, f32[2,16,256]{2,1,0:T(8,128)S(1)}, u32[]{:S(2)}, u32[]{:S(2)}) collective-permute-start(f32[2,16,256]{2,1,0:T(8,128)S(1)} %pad_maximum_fusion.7), channel_id=1, source_target_pairs={{0,32},{8,40},{16,48},{24,56},{32,64},{40,72},{48,80},{56,88},{64,... | collective-permute-start | bytes 98312 | tf_op jit(solution)/shard_map/ppermute | solution.py:17
  51.2 1.6 collective-permute-done.6
  52.8 5.6 %collective-permute-start.7 = (f32[2,16,256]{2,1,0:T(8,128)S(1)}, f32[2,16,256]{2,1,0:T(8,128)S(1)}, u32[]{:S(2)}, u32[]{:S(2)}) collective-permute-start(f32[2,16,256]{2,1,0:T(8,128)S(1)} %pad_maximum_fusion.8), channel_id=1, source_target_pairs={{0,64},{8,72},{16,80},{24,88},{32,96},{40,104},{48,112},{56,120},{... | collective-permute-start | bytes 98312 | tf_op jit(solution)/shard_map/ppermute | solution.py:17
  58.4 1.6 collective-permute-done.7
  60.0 15.1 %collective-permute-start.8 = (f32[2,16,256]{2,1,0:T(8,128)S(1)}, f32[2,16,256]{2,1,0:T(8,128)S(1)}, u32[]{:S(2)}, u32[]{:S(2)}) collective-permute-start(f32[2,16,256]{2,1,0:T(8,128)S(1)} %pad_maximum_fusion.9), channel_id=1, source_target_pairs={{0,128},{8,136},{16,144},{24,152},{32,160},{40,168},{48,176},{56,1... | collective-permute-start | bytes 98312 | tf_op jit(solution)/shard_map/ppermute | solution.py:17
  76.7 0.6 add_select_fusion.sin_ref
  77.3 1.7 %broadcast_in_dim.20.om_ref = f32[128,16,256]{2,1,0:T(8,128)} broadcast(f32[128,16]{1,0:T(8,128)S(1)} %copy.48), dimensions={0,1} | broadcast | bytes 2105344 | tf_op jit(solution)/shard_map/broadcast_in_dim | solution.py:247
  79.0 5.4 %shard_map.194 = (f32[128,256]{1,0:T(8,128)}, f32[16,16,256]{2,1,0:T(8,128)}) custom-call(f32[128,16,256]{2,1,0:T(8,128)} %get-tuple-element.57.da_ref, f32[128,16,256]{2,1,0:T(8,128)} %get-tuple-element.58.dr_ref, f32[128,16,256]{2,1,0:T(8,128)} %broadcast_in_dim.20.om_ref, f32[16,256]{1,0:T(8,128)} %add_select_fusion.sin_ref, ...), custom_call_target="tpu_custom_call" | custom-call | tf_op jit(solution)/shard_map/pallas_call | solution.py:142
  84.5 2.5 %convolution_convert_fusion.1 = bf16[128,2048]{1,0:T(8,128)(2,1)S(1)} fusion(bf16[256,2048]{1,0:T(8,128)(2,1)} %param.29, f32[128,256]{1,0:T(8,128)} %get-tuple-element.9, bf16[128,256]{1,0:T(8,128)(2,1)S(1)} %multiply_convert_fusion.1, bf16[2048,256]{1,0:T(8,128)(2,1)} %param.21, bf16[128,2048]{1,0:T(8,128)(2,1)S(1)} %copy-done.2, f32[2048]{0:T(1024)S(1)} %copy-done.15, ...), kind=kOutput, calls=%fused_computation.1 | convolution fusion | flops 270106624 | bytes 3352064 | tf_op jit(solution)/shard_map/dot_general | solution.py:278
  87.7 1.0 collective-permute-done.9
  88.8 1.1 convert_add_fusion.1
  89.9 1.3 collective-permute-start.10
  91.7 6.7 %collective-permute-done.10 = f32[2,16,2048]{2,1,0:T(8,128)} collective-permute-done((f32[2,16,2048]{2,1,0:T(8,128)S(1)}, f32[2,16,2048]{2,1,0:T(8,128)}, u32[]{:S(2)}, u32[]{:S(2)}) %collective-permute-start.10) | collective-permute-done | bytes 262176 | tf_op jit(solution)/shard_map/ppermute | solution.py:22
  98.4 1.0 bitcast_add_fusion.1
  100.1 6.0 %collective-permute-done.11 = f32[16,2048]{1,0:T(8,128)S(1)} collective-permute-done((f32[16,2048]{1,0:T(8,128)S(1)}, f32[16,2048]{1,0:T(8,128)S(1)}, u32[]{:S(2)}, u32[]{:S(2)}) %collective-permute-start.11) | collective-permute-done | bytes 131104 | tf_op jit(solution)/shard_map/ppermute | solution.py:22
  107.5 4.9 %collective-permute-done.12 = bf16[16,2048]{1,0:T(8,128)(2,1)S(1)} collective-permute-done((bf16[16,2048]{1,0:T(8,128)(2,1)S(1)}, bf16[16,2048]{1,0:T(8,128)(2,1)S(1)}, u32[]{:S(2)}, u32[]{:S(2)}) %collective-permute-start.12) | collective-permute-done | bytes 65568 | tf_op jit(solution)/shard_map/ppermute | solution.py:22
  112.5 1.3 collective-permute-start.13
  113.8 1.1 convolution_convert_fusion.4
  115.1 2.5 %collective-permute-done.13 = bf16[2,16,2048]{2,1,0:T(8,128)(2,1)S(1)} collective-permute-done((bf16[2,16,2048]{2,1,0:T(8,128)(2,1)S(1)}, bf16[2,16,2048]{2,1,0:T(8,128)(2,1)S(1)}, u32[]{:S(2)}, u32[]{:S(2)}) %collective-permute-start.13) | collective-permute-done | bytes 131104 | tf_op jit(solution)/shard_map/ppermute | solution.py:22
  117.7 5.0 %collective-permute-done.18 = bf16[16,19,256]{2,1,0:T(8,128)(2,1)S(1)} collective-permute-done((bf16[16,19,256]{2,1,0:T(8,128)(2,1)S(1)}, bf16[16,19,256]{2,1,0:T(8,128)(2,1)S(1)}, u32[]{:S(2)}, u32[]{:S(2)}) %collective-permute-start.18) | collective-permute-done | bytes 155680 | tf_op jit(solution)/shard_map/ppermute | solution.py:22
  122.9 7.1 %collective-permute-done.19 = bf16[16,19,256]{2,1,0:T(8,128)(2,1)S(1)} collective-permute-done((bf16[16,19,256]{2,1,0:T(8,128)(2,1)S(1)}, bf16[16,19,256]{2,1,0:T(8,128)(2,1)S(1)}, u32[]{:S(2)}, u32[]{:S(2)}) %collective-permute-start.19) | collective-permute-done | bytes 155680 | tf_op jit(solution)/shard_map/ppermute | solution.py:22
  130.0 0.7 add.317
  131.3 2.4 %convolution_convert_fusion = bf16[128,2048]{1,0:T(8,128)(2,1)S(1)} fusion(bf16[512,2048]{1,0:T(8,128)(2,1)S(1)} %copy-done, bf16[128,2048]{1,0:T(8,128)(2,1)S(1)} %bitcast.142, bf16[2048,512]{1,0:T(8,128)(2,1)} %param.32, f32[128,512]{1,0:T(8,128)S(1)} %fusion.58), kind=kOutput, calls=%fused_computation | convolution fusion | flops 537526272 | bytes 5505024 | tf_op jit(solution)/shard_map/dot_general | solution.py:290
  134.1 2.6 %collective-permute-done.20 = bf16[16,19,256]{2,1,0:T(8,128)(2,1)} collective-permute-done((bf16[16,19,256]{2,1,0:T(8,128)(2,1)}, bf16[16,19,256]{2,1,0:T(8,128)(2,1)}, u32[]{:S(2)}, u32[]{:S(2)}) %collective-permute-start.20) | collective-permute-done | bytes 155680 | tf_op jit(solution)/shard_map/ppermute | solution.py:22
  136.7 1.1 add.318
  137.9 9.7 %collective-permute-done.21 = bf16[16,19,256]{2,1,0:T(8,128)(2,1)S(1)} collective-permute-done((bf16[16,19,256]{2,1,0:T(8,128)(2,1)S(1)}, bf16[16,19,256]{2,1,0:T(8,128)(2,1)S(1)}, u32[]{:S(2)}, u32[]{:S(2)}) %collective-permute-start.21) | collective-permute-done | bytes 155680 | tf_op jit(solution)/shard_map/ppermute | solution.py:22
  147.7 6.4 %collective-permute-start.22 = (bf16[16,19,256]{2,1,0:T(8,128)(2,1)S(1)}, bf16[16,19,256]{2,1,0:T(8,128)(2,1)S(1)}, u32[]{:S(2)}, u32[]{:S(2)}) collective-permute-start(bf16[16,19,256]{2,1,0:T(8,128)(2,1)S(1)} %add.319), channel_id=1, source_target_pairs={{0,128},{8,136},{16,144},{24,152},{32,160},{40,168},{48,176},{56,1... | collective-permute-start | bytes 466952 | tf_op jit(solution)/shard_map/ppermute | solution.py:22
  154.2 0.9 collective-permute-start.16
  155.2 5.2 %collective-permute-done.22 = bf16[16,19,256]{2,1,0:T(8,128)(2,1)S(1)} collective-permute-done((bf16[16,19,256]{2,1,0:T(8,128)(2,1)S(1)}, bf16[16,19,256]{2,1,0:T(8,128)(2,1)S(1)}, u32[]{:S(2)}, u32[]{:S(2)}) %collective-permute-start.22) | collective-permute-done | bytes 155680 | tf_op jit(solution)/shard_map/ppermute | solution.py:22
  160.7 0.6 copy.54
  162.0 0.8 convolution_convert_fusion.5
  162.8 5.2 %collective-permute-done.17 = f32[16,2048]{1,0:T(8,128)S(1)} collective-permute-done((f32[16,2048]{1,0:T(8,128)S(1)}, f32[16,2048]{1,0:T(8,128)S(1)}, u32[]{:S(2)}, u32[]{:S(2)}) %collective-permute-start.17) | collective-permute-done | bytes 131104 | tf_op jit(solution)/shard_map/ppermute | solution.py:22
  167.9 0.7 fusion.17
  (120 shorter events, 10.5 us)
Async XLA Ops:
  0.6 130.7 %copy-start = (bf16[512,2048]{1,0:T(8,128)(2,1)S(1)}, bf16[512,2048]{1,0:T(8,128)(2,1)}, u32[]{:S(2)}) copy-start(bf16[512,2048]{1,0:T(8,128)(2,1)} %param.33) | copy-start | bytes 6291460
  0.6 6.8 %copy-start.10 = (f32[4,256]{1,0:T(4,128)S(1)}, f32[4,256]{1,0:T(4,128)}, u32[]{:S(2)}) copy-start(f32[4,256]{1,0:T(4,128)} %param.22) | copy-start | bytes 12292
  0.7 6.8 %copy-start.11 = (s32[16]{0:T(128)S(1)}, s32[16]{0:T(128)}, u32[]{:S(2)}) copy-start(s32[16]{0:T(128)} %param.34) | copy-start | bytes 196
  0.7 8.0 %copy-start.12 = (f32[256]{0:T(256)S(1)}, f32[256]{0:T(256)}, u32[]{:S(2)}) copy-start(f32[256]{0:T(256)} %param.23) | copy-start | bytes 3076
  0.7 8.2 %copy-start.5 = (bf16[256,160]{0,1:T(8,128)(2,1)S(1)}, bf16[256,160]{0,1:T(8,128)(2,1)}, u32[]{:S(2)}) copy-start(bf16[256,160]{0,1:T(8,128)(2,1)} %param.24) | copy-start | bytes 245764
  0.7 8.4 %copy-start.9 = (f32[16,256]{1,0:T(8,128)S(1)}, f32[16,256]{1,0:T(8,128)}, u32[]{:S(2)}) copy-start(f32[16,256]{1,0:T(8,128)} %param.27) | copy-start | bytes 49156
  0.7 20.5 %copy-start.13 = (f32[256]{0:T(256)S(1)}, f32[256]{0:T(256)}, u32[]{:S(2)}) copy-start(f32[256]{0:T(256)} %param.26) | copy-start | bytes 3076
  0.7 20.5 %copy-start.7 = (bf16[128,256]{1,0:T(8,128)(2,1)S(1)}, bf16[128,256]{1,0:T(8,128)(2,1)}, u32[]{:S(2)}) copy-start(bf16[128,256]{1,0:T(8,128)(2,1)} %param.25) | copy-start | bytes 196612
  3.9 17.2 %copy-start.6 = (bf16[128,256]{1,0:T(8,128)(2,1)}, bf16[128,256]{1,0:T(8,128)(2,1)S(1)}, u32[]{:S(2)}) copy-start(bf16[128,256]{1,0:T(8,128)(2,1)S(1)} %convolution_convert_fusion.3) | copy-start | bytes 196612
  3.9 4.8 %collective-permute-start = (bf16[3,256]{1,0:T(4,128)(2,1)S(1)}, bf16[3,256]{1,0:T(4,128)(2,1)S(1)}, u32[]{:S(2)}, u32[]{:S(2)}) collective-permute-start(bf16[3,256]{1,0:T(4,128)(2,1)S(1)} %slice.89), channel_id=1, source_target_pairs={{0,8},{8,16},{16,24},{24,32},{32,40},{40,48},{48,56},{56,64},{64,7... | collective-permute-start | bytes 4616 | tf_op jit(solution)/shard_map/ppermute | solution.py:17
  8.3 66.8 %copy-start.17 = (s32[128]{0:T(128)}, s32[128]{0:T(128)S(1)}, u32[]{:S(2)}) copy-start(s32[128]{0:T(128)S(1)} %convert_reduce_fusion) | copy-start | bytes 1540
  9.0 1.4 collective-permute-start.1
  10.4 4.6 %collective-permute-start.2 = (f32[128,160]{0,1:T(8,128)S(1)}, f32[128,160]{0,1:T(8,128)S(1)}, u32[]{:S(2)}, u32[]{:S(2)}) collective-permute-start(f32[128,160]{0,1:T(8,128)S(1)} %add.274), channel_id=1, source_target_pairs={{0,2},{1,3},{2,0},{3,1},{4,6},{5,7},{6,4},{7,5},{8,10},{9,11},{10,... | collective-permute-start | bytes 245768 | tf_op jit(solution)/shard_map/ppermute | solution.py:22
  15.0 6.0 %collective-permute-start.3 = (f32[128,160]{0,1:T(8,128)S(1)}, f32[128,160]{0,1:T(8,128)S(1)}, u32[]{:S(2)}, u32[]{:S(2)}) collective-permute-start(f32[128,160]{0,1:T(8,128)S(1)} %add.275), channel_id=1, source_target_pairs={{0,4},{1,5},{2,6},{3,7},{4,0},{5,1},{6,2},{7,3},{8,12},{9,13},{10,... | collective-permute-start | bytes 245768 | tf_op jit(solution)/shard_map/ppermute | solution.py:22
  27.7 5.8 %collective-permute-start.4 = (f32[2,16,256]{2,1,0:T(8,128)S(1)}, f32[2,16,256]{2,1,0:T(8,128)S(1)}, u32[]{:S(2)}, u32[]{:S(2)}) collective-permute-start(f32[2,16,256]{2,1,0:T(8,128)S(1)} %pad_maximum_fusion.5), channel_id=1, source_target_pairs={{0,8},{8,16},{16,24},{24,32},{32,40},{40,48},{48,56},{56,64},{64,7... | collective-permute-start | bytes 98312 | tf_op jit(solution)/shard_map/ppermute | solution.py:17
  34.2 7.4 %collective-permute-start.5 = (f32[2,16,256]{2,1,0:T(8,128)S(1)}, f32[2,16,256]{2,1,0:T(8,128)S(1)}, u32[]{:S(2)}, u32[]{:S(2)}) collective-permute-start(f32[2,16,256]{2,1,0:T(8,128)S(1)} %pad_maximum_fusion.6), channel_id=1, source_target_pairs={{0,16},{8,24},{16,32},{24,40},{32,48},{40,56},{48,64},{56,72},{64,... | collective-permute-start | bytes 98312 | tf_op jit(solution)/shard_map/ppermute | solution.py:17
  41.7 11.2 %collective-permute-start.6 = (f32[2,16,256]{2,1,0:T(8,128)S(1)}, f32[2,16,256]{2,1,0:T(8,128)S(1)}, u32[]{:S(2)}, u32[]{:S(2)}) collective-permute-start(f32[2,16,256]{2,1,0:T(8,128)S(1)} %pad_maximum_fusion.7), channel_id=1, source_target_pairs={{0,32},{8,40},{16,48},{24,56},{32,64},{40,72},{48,80},{56,88},{64,... | collective-permute-start | bytes 98312 | tf_op jit(solution)/shard_map/ppermute | solution.py:17
  52.8 7.2 %collective-permute-start.7 = (f32[2,16,256]{2,1,0:T(8,128)S(1)}, f32[2,16,256]{2,1,0:T(8,128)S(1)}, u32[]{:S(2)}, u32[]{:S(2)}) collective-permute-start(f32[2,16,256]{2,1,0:T(8,128)S(1)} %pad_maximum_fusion.8), channel_id=1, source_target_pairs={{0,64},{8,72},{16,80},{24,88},{32,96},{40,104},{48,112},{56,120},{... | collective-permute-start | bytes 98312 | tf_op jit(solution)/shard_map/ppermute | solution.py:17
  60.0 16.7 %collective-permute-start.8 = (f32[2,16,256]{2,1,0:T(8,128)S(1)}, f32[2,16,256]{2,1,0:T(8,128)S(1)}, u32[]{:S(2)}, u32[]{:S(2)}) collective-permute-start(f32[2,16,256]{2,1,0:T(8,128)S(1)} %pad_maximum_fusion.9), channel_id=1, source_target_pairs={{0,128},{8,136},{16,144},{24,152},{32,160},{40,168},{48,176},{56,1... | collective-permute-start | bytes 98312 | tf_op jit(solution)/shard_map/ppermute | solution.py:17
  79.0 5.4 %copy-start.2 = (bf16[128,2048]{1,0:T(8,128)(2,1)S(1)}, bf16[128,2048]{1,0:T(8,128)(2,1)}, u32[]{:S(2)}) copy-start(bf16[128,2048]{1,0:T(8,128)(2,1)} %param.18) | copy-start | bytes 1572868
  79.0 5.4 %copy-start.15 = (f32[2048]{0:T(1024)S(1)}, f32[2048]{0:T(1024)}, u32[]{:S(2)}) copy-start(f32[2048]{0:T(1024)} %param.19) | copy-start | bytes 24580
  79.0 5.4 %copy-start.16 = (f32[256]{0:T(256)S(1)}, f32[256]{0:T(256)}, u32[]{:S(2)}) copy-start(f32[256]{0:T(256)} %param.28) | copy-start | bytes 3076
  86.9 0.8 copy-start.3
  87.0 19.2 %copy-start.8 = (f32[2048]{0:T(1024)S(1)}, f32[2048]{0:T(1024)}, u32[]{:S(2)}) copy-start(f32[2048]{0:T(1024)} %param.30) | copy-start | bytes 24580
  87.0 1.8 %collective-permute-start.9 = (bf16[2,2,16,2048]{3,2,1,0:T(8,128)(2,1)S(1)}, bf16[2,2,16,2048]{3,2,1,0:T(8,128)(2,1)}, u32[]{:S(2)}, u32[]{:S(2)}) collective-permute-start(bf16[2,2,16,2048]{3,2,1,0:T(8,128)(2,1)S(1)} %dynamic-slice_bitcast_fusion.3), channel_id=1, source_target_pairs={{0,1},{1,0},{2,3},{3,2},{4,5},{5,4},{6,7},{7,6},{8,9},{9,8},{10,11... | collective-permute-start | bytes 786440 | tf_op jit(solution)/shard_map/ppermute | solution.py:22
  89.9 8.5 %collective-permute-start.10 = (f32[2,16,2048]{2,1,0:T(8,128)S(1)}, f32[2,16,2048]{2,1,0:T(8,128)}, u32[]{:S(2)}, u32[]{:S(2)}) collective-permute-start(f32[2,16,2048]{2,1,0:T(8,128)S(1)} %dynamic-slice_bitcast_fusion.2), channel_id=1, source_target_pairs={{0,2},{1,3},{2,0},{3,1},{4,6},{5,7},{6,4},{7,5},{8,10},{9,11},{10,... | collective-permute-start | bytes 786440 | tf_op jit(solution)/shard_map/ppermute | solution.py:22
  98.4 16.5 %copy-start.4 = (f32[16,16,256]{2,1,0:T(8,128)S(1)}, f32[16,16,256]{2,1,0:T(8,128)}, u32[]{:S(2)}) copy-start(f32[16,16,256]{2,1,0:T(8,128)} %get-tuple-element.10) | copy-start | bytes 786436
  99.5 6.6 %collective-permute-start.11 = (f32[16,2048]{1,0:T(8,128)S(1)}, f32[16,2048]{1,0:T(8,128)S(1)}, u32[]{:S(2)}, u32[]{:S(2)}) collective-permute-start(f32[16,2048]{1,0:T(8,128)S(1)} %dynamic-slice_bitcast_fusion.5), channel_id=1, source_target_pairs={{0,4},{1,5},{2,6},{3,7},{4,0},{5,1},{6,2},{7,3},{8,12},{9,13},{10,... | collective-permute-start | bytes 393224 | tf_op jit(solution)/shard_map/ppermute | solution.py:22
  106.3 6.1 %collective-permute-start.12 = (bf16[16,2048]{1,0:T(8,128)(2,1)S(1)}, bf16[16,2048]{1,0:T(8,128)(2,1)S(1)}, u32[]{:S(2)}, u32[]{:S(2)}) collective-permute-start(bf16[16,2048]{1,0:T(8,128)(2,1)S(1)} %multiply_convert_fusion), channel_id=1, source_target_pairs={{0,4},{1,5},{2,6},{3,7},{4,0},{5,1},{6,2},{7,3},{8,12},{9,13},{10,... | collective-permute-start | bytes 196616 | tf_op jit(solution)/shard_map/ppermute | solution.py:22
  112.5 5.1 %collective-permute-start.13 = (bf16[2,16,2048]{2,1,0:T(8,128)(2,1)S(1)}, bf16[2,16,2048]{2,1,0:T(8,128)(2,1)S(1)}, u32[]{:S(2)}, u32[]{:S(2)}) collective-permute-start(bf16[2,16,2048]{2,1,0:T(8,128)(2,1)S(1)} %pad_maximum_fusion.4), channel_id=1, source_target_pairs={{0,2},{1,3},{2,0},{3,1},{4,6},{5,7},{6,4},{7,5},{8,10},{9,11},{10,... | collective-permute-start | bytes 393224 | tf_op jit(solution)/shard_map/ppermute | solution.py:22
  115.0 7.7 %collective-permute-start.18 = (bf16[16,19,256]{2,1,0:T(8,128)(2,1)S(1)}, bf16[16,19,256]{2,1,0:T(8,128)(2,1)S(1)}, u32[]{:S(2)}, u32[]{:S(2)}) collective-permute-start(bf16[16,19,256]{2,1,0:T(8,128)(2,1)S(1)} %pad_maximum_fusion.2), channel_id=1, source_target_pairs={{0,8},{8,0},{16,24},{24,16},{32,40},{40,32},{48,56},{56,48},{64,72... | collective-permute-start | bytes 466952 | tf_op jit(solution)/shard_map/ppermute | solution.py:22
  117.6 13.1 %collective-permute-start.14 = (bf16[2,2,16,2048]{3,2,1,0:T(8,128)(2,1)S(1)}, bf16[2,2,16,2048]{3,2,1,0:T(8,128)(2,1)S(1)}, u32[]{:S(2)}, u32[]{:S(2)}) collective-permute-start(bf16[2,2,16,2048]{3,2,1,0:T(8,128)(2,1)S(1)} %pad_maximum_fusion.1), channel_id=1, source_target_pairs={{0,1},{1,0},{2,3},{3,2},{4,5},{5,4},{6,7},{7,6},{8,9},{9,8},{10,11... | collective-permute-start | bytes 786440 | tf_op jit(solution)/shard_map/ppermute | solution.py:22
  122.8 7.3 %collective-permute-start.19 = (bf16[16,19,256]{2,1,0:T(8,128)(2,1)S(1)}, bf16[16,19,256]{2,1,0:T(8,128)(2,1)S(1)}, u32[]{:S(2)}, u32[]{:S(2)}) collective-permute-start(bf16[16,19,256]{2,1,0:T(8,128)(2,1)S(1)} %fusion.52), channel_id=1, source_target_pairs={{0,16},{8,24},{16,0},{24,8},{32,48},{40,56},{48,32},{56,40},{64,80... | collective-permute-start | bytes 466952 | tf_op jit(solution)/shard_map/ppermute | solution.py:22
  122.9 8.0 %copy-start.1 = (bf16[2048,512]{1,0:T(8,128)(2,1)S(1)}, bf16[2048,512]{1,0:T(8,128)(2,1)}, u32[]{:S(2)}) copy-start(bf16[2048,512]{1,0:T(8,128)(2,1)} %param.31) | copy-start | bytes 6291460
  130.8 6.0 %collective-permute-start.20 = (bf16[16,19,256]{2,1,0:T(8,128)(2,1)}, bf16[16,19,256]{2,1,0:T(8,128)(2,1)}, u32[]{:S(2)}, u32[]{:S(2)}) collective-permute-start(bf16[16,19,256]{2,1,0:T(8,128)(2,1)} %add.317), channel_id=1, source_target_pairs={{0,32},{8,40},{16,48},{24,56},{32,0},{40,8},{48,16},{56,24},{64,96... | collective-permute-start | bytes 466952 | tf_op jit(solution)/shard_map/ppermute | solution.py:22
  131.3 6.6 %copy-start.18 = (s32[128]{0:T(128)S(1)}, s32[128]{0:T(128)}, u32[]{:S(2)}) copy-start(s32[128]{0:T(128)} %copy-done.17) | copy-start | bytes 1540
  133.8 26.7 %copy-start.14 = (s32[4]{0:T(128)S(1)}, s32[4]{0:T(128)}, u32[]{:S(2)}) copy-start(s32[4]{0:T(128)} %param.35) | copy-start | bytes 52
  133.8 20.3 %collective-permute-start.15 = (bf16[2,2,16,2048]{3,2,1,0:T(8,128)(2,1)S(1)}, bf16[2,2,16,2048]{3,2,1,0:T(8,128)(2,1)S(1)}, u32[]{:S(2)}, u32[]{:S(2)}) collective-permute-start(bf16[2,2,16,2048]{3,2,1,0:T(8,128)(2,1)S(1)} %dynamic-slice_bitcast_fusion.1), channel_id=1, source_target_pairs={{0,1},{1,0},{2,3},{3,2},{4,5},{5,4},{6,7},{7,6},{8,9},{9,8},{10,11... | collective-permute-start | bytes 786440 | tf_op jit(solution)/shard_map/ppermute | solution.py:22
  137.8 9.9 %collective-permute-start.21 = (bf16[16,19,256]{2,1,0:T(8,128)(2,1)S(1)}, bf16[16,19,256]{2,1,0:T(8,128)(2,1)S(1)}, u32[]{:S(2)}, u32[]{:S(2)}) collective-permute-start(bf16[16,19,256]{2,1,0:T(8,128)(2,1)S(1)} %add.318), channel_id=1, source_target_pairs={{0,64},{8,72},{16,80},{24,88},{32,96},{40,104},{48,112},{56,120},{... | collective-permute-start | bytes 466952 | tf_op jit(solution)/shard_map/ppermute | solution.py:22
  147.7 12.6 %collective-permute-start.22 = (bf16[16,19,256]{2,1,0:T(8,128)(2,1)S(1)}, bf16[16,19,256]{2,1,0:T(8,128)(2,1)S(1)}, u32[]{:S(2)}, u32[]{:S(2)}) collective-permute-start(bf16[16,19,256]{2,1,0:T(8,128)(2,1)S(1)} %add.319), channel_id=1, source_target_pairs={{0,128},{8,136},{16,144},{24,152},{32,160},{40,168},{48,176},{56,1... | collective-permute-start | bytes 466952 | tf_op jit(solution)/shard_map/ppermute | solution.py:22
  154.2 7.1 %collective-permute-start.16 = (f32[2,16,2048]{2,1,0:T(8,128)S(1)}, f32[2,16,2048]{2,1,0:T(8,128)S(1)}, u32[]{:S(2)}, u32[]{:S(2)}) collective-permute-start(f32[2,16,2048]{2,1,0:T(8,128)S(1)} %dynamic-slice_bitcast_fusion), channel_id=1, source_target_pairs={{0,2},{1,3},{2,0},{3,1},{4,6},{5,7},{6,4},{7,5},{8,10},{9,11},{10,... | collective-permute-start | bytes 786440 | tf_op jit(solution)/shard_map/ppermute | solution.py:22
  161.4 6.6 %collective-permute-start.17 = (f32[16,2048]{1,0:T(8,128)S(1)}, f32[16,2048]{1,0:T(8,128)S(1)}, u32[]{:S(2)}, u32[]{:S(2)}) collective-permute-start(f32[16,2048]{1,0:T(8,128)S(1)} %dynamic-slice_bitcast_fusion.4), channel_id=1, source_target_pairs={{0,4},{1,5},{2,6},{3,7},{4,0},{5,1},{6,2},{7,3},{8,12},{9,13},{10,... | collective-permute-start | bytes 393224 | tf_op jit(solution)/shard_map/ppermute | solution.py:22

commit v2 on v1

--- a/solution.py
+++ b/solution.py
@@ -156,20 +156,19 @@
     devices = lax.axis_size(axis)
     inc_a, inc_s = a_blk, s_blk
     exc_a, exc_s = jnp.ones_like(a_blk), jnp.zeros_like(s_blk)
-    shift = 1
-    while shift < devices:
-        got = from_behind(jnp.stack([inc_a, inc_s]), axis, shift)
-        got_a, got_s = got[0], got[1]
-        has = me >= shift
-        new_exc_a = got_a * exc_a
-        new_exc_s = exc_a * got_s + exc_s
-        new_inc_a = got_a * inc_a
-        new_inc_s = inc_a * got_s + inc_s
-        exc_a = jnp.where(has, new_exc_a, exc_a)
-        exc_s = jnp.where(has, new_exc_s, exc_s)
-        inc_a = jnp.where(has, new_inc_a, inc_a)
-        inc_s = jnp.where(has, new_inc_s, inc_s)
-        shift *= 2
+    span = 1
+    while span < devices:
+        radix = min(8, devices // span)
+        pack = jnp.stack([inc_a, inc_s])
+        got = [from_behind(pack, axis, span * j) for j in range(radix - 1, 0, -1)]
+        acc_a, acc_s = jnp.ones_like(a_blk), jnp.zeros_like(s_blk)
+        for j, one in zip(range(radix - 1, 0, -1), got):
+            has = me >= span * j
+            acc_s = jnp.where(has, one[0] * acc_s + one[1], acc_s)
+            acc_a = jnp.where(has, one[0] * acc_a, acc_a)
+        exc_a, exc_s = acc_a * exc_a, exc_a * acc_s + exc_s
+        inc_a, inc_s = acc_a * inc_a, inc_a * acc_s + inc_s
+        span *= radix
     return exc_s
 
 
@@ -266,14 +265,6 @@
     handed = jnp.concatenate(
         [final_part.astype(jnp.bfloat16), edge_part.astype(jnp.bfloat16)], axis=1
     )
-    handed = butterfly_sum(handed, "seq", jnp.bfloat16).astype(jnp.float32)
-    final_all = handed[:, :state_dim]
-    edge_all = handed[:, state_dim:]
-    chooser = (request_prompt[:, None] == prompt_ids[None, :]).astype(jnp.float32)
-    req_states = jnp.einsum("rp,pne->rne", chooser, final_all, precision=lax.Precision.HIGHEST)
-    req_edges = jnp.einsum(
-        "rp,pje->rje", chooser, edge_all, precision=lax.Precision.HIGHEST
-    ).astype(jnp.bfloat16)
     mixed_rows = scatter_rows(
         jnp.dot(gated, w_out, preferred_element_type=jnp.float32).astype(jnp.bfloat16),
         "tp",
@@ -291,6 +282,15 @@
         "tp",
         jnp.bfloat16,
     )
+    handed, mlp_share = lax.optimization_barrier((handed, mlp_share))
+    handed = butterfly_sum(handed, "seq", jnp.bfloat16).astype(jnp.float32)
+    final_all = handed[:, :state_dim]
+    edge_all = handed[:, state_dim:]
+    chooser = (request_prompt[:, None] == prompt_ids[None, :]).astype(jnp.float32)
+    req_states = jnp.einsum("rp,pne->rne", chooser, final_all, precision=lax.Precision.HIGHEST)
+    req_edges = jnp.einsum(
+        "rp,pje->rje", chooser, edge_all, precision=lax.Precision.HIGHEST
+    ).astype(jnp.bfloat16)
     live_rows = lax.dynamic_slice_in_dim(is_live, tp_pos * row_count, row_count, 0).astype(
         jnp.float32
     )

time: 169 us -> 183 us (1.083)
  the two profiles are of different devices: /device:TPU:4 before, /device:TPU:6 now
where the time goes in v2:
time: 183 us; the launch traced here: 182 us
  waiting for transfers between devices  85.3 us (47%)
  starting transfers between devices  61.9 us (34%)
  other arithmetic  12.7 us (7%)
  matrix products  8.7 us (5%)
  Pallas kernels  8.58 us (5%)
  local copies, waits for them, and re-layouts  3.53 us (2%)
    ppermute x17, waiting for transfers between devices, swap(): return lax.ppermute(x, axis, [(i, i ^ bit) for i in range(devices)])  83.1 us
    ppermute x11, starting transfers between devices, from_behind(): return lax.ppermute(x, axis, pairs)  42.9 us
    ppermute x17, starting transfers between devices, swap(): return lax.ppermute(x, axis, [(i, i ^ bit) for i in range(devices)])  19 us
    pallas_call x1, Pallas kernels, block_output(): pl.pallas_call(block_output_kernel, out_shape=(jax.ShapeDtypeStruct((t, e...  5.43 us
  transfers between devices with their start and end apart: 28, of which 20 were waited for; matrix products, arithmetic and copies ran while one was open for 2% of the time, Pallas kernels for 0%

profile of v2, /device:TPU:6, one launch (start us, length us, event | category | flops | bytes accessed | tf_op | source)
XLA Modules:
  0.0 182.2 jit_solution(15203080402268509190)
XLA Ops:
  0.7 1.4 fusion.2
  2.1 1.8 convolution_convert_fusion.3
  3.9 3.5 %collective-permute-start = (bf16[3,256]{1,0:T(4,128)(2,1)S(1)}, bf16[3,256]{1,0:T(4,128)(2,1)S(1)}, u32[]{:S(2)}, u32[]{:S(2)}) collective-permute-start(bf16[3,256]{1,0:T(4,128)(2,1)S(1)} %slice.140), channel_id=1, source_target_pairs={{0,8},{8,16},{16,24},{24,32},{32,40},{40,48},{48,56},{56,64},{64,7... | collective-permute-start | bytes 4616 | tf_op jit(solution)/shard_map/ppermute | solution.py:17
  9.1 1.2 collective-permute-done.1
  10.4 0.9 collective-permute-start.2
  11.4 3.6 %collective-permute-done.2 = f32[128,160]{0,1:T(8,128)S(1)} collective-permute-done((f32[128,160]{0,1:T(8,128)S(1)}, f32[128,160]{0,1:T(8,128)S(1)}, u32[]{:S(2)}, u32[]{:S(2)}) %collective-permute-start.2) | collective-permute-done | bytes 81952 | tf_op jit(solution)/shard_map/ppermute | solution.py:22
  15.0 1.5 collective-permute-start.3
  16.5 4.5 %collective-permute-done.3 = f32[128,160]{0,1:T(8,128)S(1)} collective-permute-done((f32[128,160]{0,1:T(8,128)S(1)}, f32[128,160]{0,1:T(8,128)S(1)}, u32[]{:S(2)}, u32[]{:S(2)}) %collective-permute-start.3) | collective-permute-done | bytes 81952 | tf_op jit(solution)/shard_map/ppermute | solution.py:22
  21.5 2.4 %exponential_multiply_fusion = (f32[128,16,256]{2,1,0:T(8,128)}, f32[128,16,256]{2,1,0:T(8,128)}) fusion(f32[128]{0:T(128)S(1)} %convert_subtract_fusion, f32[16,256]{1,0:T(8,128)S(1)} %exponential_negate_fusion, f32[128,256]{1,0:T(8,128)S(1)} %get-tuple-element.56, f32[128,16]{1,0:T(8,128)S(1)} %copy.47, f32[128,256]{1,0:T(8,128)S(1)} %get-tuple-element.55), kind=kLoop, calls=%fused_computation.2 | loop fusion | flops 1572864 | bytes 4481536 | tf_op jit(solution)/shard_map/mul | solution.py:244
  23.9 3.1 %shard_map.193 = (f32[16,256]{1,0:T(8,128)}, f32[16,256]{1,0:T(8,128)}) custom-call(f32[128,16,256]{2,1,0:T(8,128)} %get-tuple-element.57.da_ref, f32[128,16,256]{2,1,0:T(8,128)} %get-tuple-element.58.dr_ref), custom_call_target="tpu_custom_call" | custom-call | tf_op jit(solution)/shard_map/pallas_call | solution.py:126
  27.7 7.0 %collective-permute-start.10 = (f32[2,16,256]{2,1,0:T(8,128)S(1)}, f32[2,16,256]{2,1,0:T(8,128)S(1)}, u32[]{:S(2)}, u32[]{:S(2)}) collective-permute-start(f32[2,16,256]{2,1,0:T(8,128)S(1)} %pad_maximum_fusion.5), channel_id=1, source_target_pairs={{0,56},{8,64},{16,72},{24,80},{32,88},{40,96},{48,104},{56,112},{6... | collective-permute-start | bytes 98312 | tf_op jit(solution)/shard_map/ppermute | solution.py:17
  34.7 5.2 %collective-permute-start.9 = (f32[2,16,256]{2,1,0:T(8,128)S(1)}, f32[2,16,256]{2,1,0:T(8,128)S(1)}, u32[]{:S(2)}, u32[]{:S(2)}) collective-permute-start(f32[2,16,256]{2,1,0:T(8,128)S(1)} %pad_maximum_fusion.5), channel_id=1, source_target_pairs={{0,48},{8,56},{16,64},{24,72},{32,80},{40,88},{48,96},{56,104},{64... | collective-permute-start | bytes 98312 | tf_op jit(solution)/shard_map/ppermute | solution.py:17
  40.0 5.4 %collective-permute-start.8 = (f32[2,16,256]{2,1,0:T(8,128)S(1)}, f32[2,16,256]{2,1,0:T(8,128)S(1)}, u32[]{:S(2)}, u32[]{:S(2)}) collective-permute-start(f32[2,16,256]{2,1,0:T(8,128)S(1)} %pad_maximum_fusion.5), channel_id=1, source_target_pairs={{0,40},{8,48},{16,56},{24,64},{32,72},{40,80},{48,88},{56,96},{64,... | collective-permute-start | bytes 98312 | tf_op jit(solution)/shard_map/ppermute | solution.py:17
  45.4 3.2 %collective-permute-start.7 = (f32[2,16,256]{2,1,0:T(8,128)S(1)}, f32[2,16,256]{2,1,0:T(8,128)S(1)}, u32[]{:S(2)}, u32[]{:S(2)}) collective-permute-start(f32[2,16,256]{2,1,0:T(8,128)S(1)} %pad_maximum_fusion.5), channel_id=1, source_target_pairs={{0,32},{8,40},{16,48},{24,56},{32,64},{40,72},{48,80},{56,88},{64,... | collective-permute-start | bytes 98312 | tf_op jit(solution)/shard_map/ppermute | solution.py:17
  48.6 4.3 %collective-permute-start.6 = (f32[2,16,256]{2,1,0:T(8,128)S(1)}, f32[2,16,256]{2,1,0:T(8,128)S(1)}, u32[]{:S(2)}, u32[]{:S(2)}) collective-permute-start(f32[2,16,256]{2,1,0:T(8,128)S(1)} %pad_maximum_fusion.5), channel_id=1, source_target_pairs={{0,24},{8,32},{16,40},{24,48},{32,56},{40,64},{48,72},{56,80},{64,... | collective-permute-start | bytes 98312 | tf_op jit(solution)/shard_map/ppermute | solution.py:17
  53.0 3.6 %collective-permute-start.5 = (f32[2,16,256]{2,1,0:T(8,128)S(1)}, f32[2,16,256]{2,1,0:T(8,128)S(1)}, u32[]{:S(2)}, u32[]{:S(2)}) collective-permute-start(f32[2,16,256]{2,1,0:T(8,128)S(1)} %pad_maximum_fusion.5), channel_id=1, source_target_pairs={{0,16},{8,24},{16,32},{24,40},{32,48},{40,56},{48,64},{56,72},{64,... | collective-permute-start | bytes 98312 | tf_op jit(solution)/shard_map/ppermute | solution.py:17
  56.6 3.5 %collective-permute-start.4 = (f32[2,16,256]{2,1,0:T(8,128)S(1)}, f32[2,16,256]{2,1,0:T(8,128)S(1)}, u32[]{:S(2)}, u32[]{:S(2)}) collective-permute-start(f32[2,16,256]{2,1,0:T(8,128)S(1)} %pad_maximum_fusion.5), channel_id=1, source_target_pairs={{0,8},{8,16},{16,24},{24,32},{32,40},{40,48},{48,56},{56,64},{64,7... | collective-permute-start | bytes 98312 | tf_op jit(solution)/shard_map/ppermute | solution.py:17
  60.2 1.5 collective-permute-done.4
  63.2 1.3 collective-permute-start.13
  64.5 3.8 %collective-permute-start.12 = (f32[2,16,256]{2,1,0:T(8,128)S(1)}, f32[2,16,256]{2,1,0:T(8,128)S(1)}, u32[]{:S(2)}, u32[]{:S(2)}) collective-permute-start(f32[2,16,256]{2,1,0:T(8,128)S(1)} %pad_maximum_fusion.6), channel_id=1, source_target_pairs={{0,128},{8,136},{16,144},{24,152},{32,160},{40,168},{48,176},{56,1... | collective-permute-start | bytes 98312 | tf_op jit(solution)/shard_map/ppermute | solution.py:17
  68.3 2.1 %collective-permute-start.11 = (f32[2,16,256]{2,1,0:T(8,128)S(1)}, f32[2,16,256]{2,1,0:T(8,128)S(1)}, u32[]{:S(2)}, u32[]{:S(2)}) collective-permute-start(f32[2,16,256]{2,1,0:T(8,128)S(1)} %pad_maximum_fusion.6), channel_id=1, source_target_pairs={{0,64},{8,72},{16,80},{24,88},{32,96},{40,104},{48,112},{56,120},{... | collective-permute-start | bytes 98312 | tf_op jit(solution)/shard_map/ppermute | solution.py:17
  72.6 1.7 broadcast_in_dim.18.om_ref
  74.3 5.4 %shard_map.194 = (f32[128,256]{1,0:T(8,128)}, f32[16,16,256]{2,1,0:T(8,128)}) custom-call(f32[128,16,256]{2,1,0:T(8,128)} %get-tuple-element.57.da_ref, f32[128,16,256]{2,1,0:T(8,128)} %get-tuple-element.58.dr_ref, f32[128,16,256]{2,1,0:T(8,128)} %broadcast_in_dim.18.om_ref, f32[16,256]{1,0:T(8,128)} %fusion.39.sin_ref, s32[128]{0:T(128)} %convert_element_type.145.endf_ref, ...), custom_call_target="tpu_custom_call" | custom-call | tf_op jit(solution)/shard_map/pallas_call | solution.py:142
  79.8 2.5 %convolution_convert_fusion.1 = bf16[128,2048]{1,0:T(8,128)(2,1)S(1)} fusion(bf16[256,2048]{1,0:T(8,128)(2,1)} %param.29, f32[128,256]{1,0:T(8,128)} %get-tuple-element.11, bf16[128,256]{1,0:T(8,128)(2,1)S(1)} %multiply_convert_fusion.2, bf16[2048,256]{1,0:T(8,128)(2,1)} %param.21, bf16[128,2048]{1,0:T(8,128)(2,1)S(1)} %copy-done.2, ...), kind=kOutput, calls=%fused_computation.1 | convolution fusion | flops 270106624 | bytes 3352064 | tf_op jit(solution)/shard_map/dot_general | solution.py:269
  83.0 1.0 collective-permute-done.14
  84.1 1.1 convert_add_fusion.1
  85.2 0.9 collective-permute-start.15
  86.1 7.6 %collective-permute-done.15 = f32[2,16,2048]{2,1,0:T(8,128)} collective-permute-done((f32[2,16,2048]{2,1,0:T(8,128)S(1)}, f32[2,16,2048]{2,1,0:T(8,128)}, u32[]{:S(2)}, u32[]{:S(2)}) %collective-permute-start.15) | collective-permute-done | bytes 262176 | tf_op jit(solution)/shard_map/ppermute | solution.py:22
  93.7 1.0 bitcast_add_fusion.1
  94.7 1.5 collective-permute-start.16
  96.2 5.1 %collective-permute-done.16 = f32[16,2048]{1,0:T(8,128)S(1)} collective-permute-done((f32[16,2048]{1,0:T(8,128)S(1)}, f32[16,2048]{1,0:T(8,128)S(1)}, u32[]{:S(2)}, u32[]{:S(2)}) %collective-permute-start.16) | collective-permute-done | bytes 131104 | tf_op jit(solution)/shard_map/ppermute | solution.py:22
  101.5 1.5 collective-permute-start.17
  103.0 4.7 %collective-permute-done.17 = bf16[16,2048]{1,0:T(8,128)(2,1)S(1)} collective-permute-done((bf16[16,2048]{1,0:T(8,128)(2,1)S(1)}, bf16[16,2048]{1,0:T(8,128)(2,1)S(1)}, u32[]{:S(2)}, u32[]{:S(2)}) %collective-permute-start.17) | collective-permute-done | bytes 65568 | tf_op jit(solution)/shard_map/ppermute | solution.py:22
  108.7 4.2 %collective-permute-done.18 = bf16[2,16,2048]{2,1,0:T(8,128)(2,1)S(1)} collective-permute-done((bf16[2,16,2048]{2,1,0:T(8,128)(2,1)S(1)}, bf16[2,16,2048]{2,1,0:T(8,128)(2,1)S(1)}, u32[]{:S(2)}, u32[]{:S(2)}) %collective-permute-start.18) | collective-permute-done | bytes 131104 | tf_op jit(solution)/shard_map/ppermute | solution.py:22
  113.0 1.5 collective-permute-done.19
  115.1 2.4 %convolution_convert_fusion = bf16[128,2048]{1,0:T(8,128)(2,1)S(1)} fusion(bf16[512,2048]{1,0:T(8,128)(2,1)S(1)} %copy-done, bf16[128,2048]{1,0:T(8,128)(2,1)S(1)} %bitcast.224, bf16[2048,512]{1,0:T(8,128)(2,1)} %param.32, f32[128,512]{1,0:T(8,128)S(1)} %fusion.76), kind=kOutput, calls=%fused_computation | convolution fusion | flops 537526272 | bytes 5505024 | tf_op jit(solution)/shard_map/dot_general | solution.py:281
  118.2 1.2 collective-permute-done.20
  119.4 0.9 collective-permute-start.21
  120.3 7.8 %collective-permute-done.21 = f32[2,16,2048]{2,1,0:T(8,128)S(1)} collective-permute-done((f32[2,16,2048]{2,1,0:T(8,128)S(1)}, f32[2,16,2048]{2,1,0:T(8,128)S(1)}, u32[]{:S(2)}, u32[]{:S(2)}) %collective-permute-start.21) | collective-permute-done | bytes 262176 | tf_op jit(solution)/shard_map/ppermute | solution.py:22
  128.1 1.4 collective-permute-start.22
  129.8 5.0 %collective-permute-done.22 = f32[16,2048]{1,0:T(8,128)S(1)} collective-permute-done((f32[16,2048]{1,0:T(8,128)S(1)}, f32[16,2048]{1,0:T(8,128)S(1)}, u32[]{:S(2)}, u32[]{:S(2)}) %collective-permute-start.22) | collective-permute-done | bytes 131104 | tf_op jit(solution)/shard_map/ppermute | solution.py:22
  135.0 7.2 %collective-permute-done.23 = bf16[16,19,256]{2,1,0:T(8,128)(2,1)S(1)} collective-permute-done((bf16[16,19,256]{2,1,0:T(8,128)(2,1)S(1)}, bf16[16,19,256]{2,1,0:T(8,128)(2,1)S(1)}, u32[]{:S(2)}, u32[]{:S(2)}) %collective-permute-start.23) | collective-permute-done | bytes 155680 | tf_op jit(solution)/shard_map/ppermute | solution.py:22
  142.3 7.2 %collective-permute-done.24 = bf16[16,19,256]{2,1,0:T(8,128)(2,1)S(1)} collective-permute-done((bf16[16,19,256]{2,1,0:T(8,128)(2,1)S(1)}, bf16[16,19,256]{2,1,0:T(8,128)(2,1)S(1)}, u32[]{:S(2)}, u32[]{:S(2)}) %collective-permute-start.24) | collective-permute-done | bytes 155680 | tf_op jit(solution)/shard_map/ppermute | solution.py:22
  150.2 5.2 %collective-permute-done.25 = bf16[16,19,256]{2,1,0:T(8,128)(2,1)S(1)} collective-permute-done((bf16[16,19,256]{2,1,0:T(8,128)(2,1)S(1)}, bf16[16,19,256]{2,1,0:T(8,128)(2,1)S(1)}, u32[]{:S(2)}, u32[]{:S(2)}) %collective-permute-start.25) | collective-permute-done | bytes 155680 | tf_op jit(solution)/shard_map/ppermute | solution.py:22
  155.4 3.2 %collective-permute-start.26 = (bf16[16,19,256]{2,1,0:T(8,128)(2,1)S(1)}, bf16[16,19,256]{2,1,0:T(8,128)(2,1)S(1)}, u32[]{:S(2)}, u32[]{:S(2)}) collective-permute-start(bf16[16,19,256]{2,1,0:T(8,128)(2,1)S(1)} %add.336), channel_id=1, source_target_pairs={{0,64},{8,72},{16,80},{24,88},{32,96},{40,104},{48,112},{56,120},{... | collective-permute-start | bytes 466952 | tf_op jit(solution)/shard_map/ppermute | solution.py:22
  158.7 9.9 %collective-permute-done.26 = bf16[16,19,256]{2,1,0:T(8,128)(2,1)S(1)} collective-permute-done((bf16[16,19,256]{2,1,0:T(8,128)(2,1)S(1)}, bf16[16,19,256]{2,1,0:T(8,128)(2,1)S(1)}, u32[]{:S(2)}, u32[]{:S(2)}) %collective-permute-start.26) | collective-permute-done | bytes 155680 | tf_op jit(solution)/shard_map/ppermute | solution.py:22
  168.7 4.7 %collective-permute-start.27 = (bf16[16,19,256]{2,1,0:T(8,128)(2,1)S(1)}, bf16[16,19,256]{2,1,0:T(8,128)(2,1)S(1)}, u32[]{:S(2)}, u32[]{:S(2)}) collective-permute-start(bf16[16,19,256]{2,1,0:T(8,128)(2,1)S(1)} %add.337), channel_id=1, source_target_pairs={{0,128},{8,136},{16,144},{24,152},{32,160},{40,168},{48,176},{56,1... | collective-permute-start | bytes 466952 | tf_op jit(solution)/shard_map/ppermute | solution.py:22
  174.1 6.3 %collective-permute-done.27 = bf16[16,19,256]{2,1,0:T(8,128)(2,1)S(1)} collective-permute-done((bf16[16,19,256]{2,1,0:T(8,128)(2,1)S(1)}, bf16[16,19,256]{2,1,0:T(8,128)(2,1)S(1)}, u32[]{:S(2)}, u32[]{:S(2)}) %collective-permute-start.27) | collective-permute-done | bytes 155680 | tf_op jit(solution)/shard_map/ppermute | solution.py:22
  (134 shorter events, 13.9 us)
Async XLA Ops:
  0.6 114.5 %copy-start = (bf16[512,2048]{1,0:T(8,128)(2,1)S(1)}, bf16[512,2048]{1,0:T(8,128)(2,1)}, u32[]{:S(2)}) copy-start(bf16[512,2048]{1,0:T(8,128)(2,1)} %param.33) | copy-start | bytes 6291460
  0.6 6.8 %copy-start.11 = (f32[4,256]{1,0:T(4,128)S(1)}, f32[4,256]{1,0:T(4,128)}, u32[]{:S(2)}) copy-start(f32[4,256]{1,0:T(4,128)} %param.22) | copy-start | bytes 12292
  0.7 6.8 %copy-start.14 = (s32[16]{0:T(128)S(1)}, s32[16]{0:T(128)}, u32[]{:S(2)}) copy-start(s32[16]{0:T(128)} %param.34) | copy-start | bytes 196
  0.7 8.0 %copy-start.16 = (f32[256]{0:T(256)S(1)}, f32[256]{0:T(256)}, u32[]{:S(2)}) copy-start(f32[256]{0:T(256)} %param.23) | copy-start | bytes 3076
  0.7 8.2 %copy-start.5 = (bf16[256,160]{0,1:T(8,128)(2,1)S(1)}, bf16[256,160]{0,1:T(8,128)(2,1)}, u32[]{:S(2)}) copy-start(bf16[256,160]{0,1:T(8,128)(2,1)} %param.24) | copy-start | bytes 245764
  0.7 8.4 %copy-start.10 = (f32[16,256]{1,0:T(8,128)S(1)}, f32[16,256]{1,0:T(8,128)}, u32[]{:S(2)}) copy-start(f32[16,256]{1,0:T(8,128)} %param.27) | copy-start | bytes 49156
  0.7 20.5 %copy-start.17 = (f32[256]{0:T(256)S(1)}, f32[256]{0:T(256)}, u32[]{:S(2)}) copy-start(f32[256]{0:T(256)} %param.26) | copy-start | bytes 3076
  0.7 20.5 %copy-start.8 = (bf16[128,256]{1,0:T(8,128)(2,1)S(1)}, bf16[128,256]{1,0:T(8,128)(2,1)}, u32[]{:S(2)}) copy-start(bf16[128,256]{1,0:T(8,128)(2,1)} %param.25) | copy-start | bytes 196612
  3.9 17.2 %copy-start.6 = (bf16[128,256]{1,0:T(8,128)(2,1)}, bf16[128,256]{1,0:T(8,128)(2,1)S(1)}, u32[]{:S(2)}) copy-start(bf16[128,256]{1,0:T(8,128)(2,1)S(1)} %convolution_convert_fusion.3) | copy-start | bytes 196612
  3.9 4.8 %collective-permute-start = (bf16[3,256]{1,0:T(4,128)(2,1)S(1)}, bf16[3,256]{1,0:T(4,128)(2,1)S(1)}, u32[]{:S(2)}, u32[]{:S(2)}) collective-permute-start(bf16[3,256]{1,0:T(4,128)(2,1)S(1)} %slice.140), channel_id=1, source_target_pairs={{0,8},{8,16},{16,24},{24,32},{32,40},{40,48},{48,56},{56,64},{64,7... | collective-permute-start | bytes 4616 | tf_op jit(solution)/shard_map/ppermute | solution.py:17
  8.3 62.1 %copy-start.21 = (s32[128]{0:T(128)}, s32[128]{0:T(128)S(1)}, u32[]{:S(2)}) copy-start(s32[128]{0:T(128)S(1)} %convert_reduce_fusion) | copy-start | bytes 1540
  8.7 12.4 %copy-start.12 = (bf16[3,256]{1,0:T(4,128)(2,1)}, bf16[3,256]{1,0:T(4,128)(2,1)S(1)}, u32[]{:S(2)}) copy-start(bf16[3,256]{1,0:T(4,128)(2,1)S(1)} %collective-permute-done) | copy-start | bytes 4612
  9.0 1.4 collective-permute-start.1
  10.4 4.6 %collective-permute-start.2 = (f32[128,160]{0,1:T(8,128)S(1)}, f32[128,160]{0,1:T(8,128)S(1)}, u32[]{:S(2)}, u32[]{:S(2)}) collective-permute-start(f32[128,160]{0,1:T(8,128)S(1)} %add.288), channel_id=1, source_target_pairs={{0,2},{1,3},{2,0},{3,1},{4,6},{5,7},{6,4},{7,5},{8,10},{9,11},{10,... | collective-permute-start | bytes 245768 | tf_op jit(solution)/shard_map/ppermute | solution.py:22
  15.0 6.0 %collective-permute-start.3 = (f32[128,160]{0,1:T(8,128)S(1)}, f32[128,160]{0,1:T(8,128)S(1)}, u32[]{:S(2)}, u32[]{:S(2)}) collective-permute-start(f32[128,160]{0,1:T(8,128)S(1)} %add.289), channel_id=1, source_target_pairs={{0,4},{1,5},{2,6},{3,7},{4,0},{5,1},{6,2},{7,3},{8,12},{9,13},{10,... | collective-permute-start | bytes 245768 | tf_op jit(solution)/shard_map/ppermute | solution.py:22
  27.7 25.2 %collective-permute-start.10 = (f32[2,16,256]{2,1,0:T(8,128)S(1)}, f32[2,16,256]{2,1,0:T(8,128)S(1)}, u32[]{:S(2)}, u32[]{:S(2)}) collective-permute-start(f32[2,16,256]{2,1,0:T(8,128)S(1)} %pad_maximum_fusion.5), channel_id=1, source_target_pairs={{0,56},{8,64},{16,72},{24,80},{32,88},{40,96},{48,104},{56,112},{6... | collective-permute-start | bytes 98312 | tf_op jit(solution)/shard_map/ppermute | solution.py:17
  34.7 21.9 %collective-permute-start.9 = (f32[2,16,256]{2,1,0:T(8,128)S(1)}, f32[2,16,256]{2,1,0:T(8,128)S(1)}, u32[]{:S(2)}, u32[]{:S(2)}) collective-permute-start(f32[2,16,256]{2,1,0:T(8,128)S(1)} %pad_maximum_fusion.5), channel_id=1, source_target_pairs={{0,48},{8,56},{16,64},{24,72},{32,80},{40,88},{48,96},{56,104},{64... | collective-permute-start | bytes 98312 | tf_op jit(solution)/shard_map/ppermute | solution.py:17
  40.0 20.2 %collective-permute-start.8 = (f32[2,16,256]{2,1,0:T(8,128)S(1)}, f32[2,16,256]{2,1,0:T(8,128)S(1)}, u32[]{:S(2)}, u32[]{:S(2)}) collective-permute-start(f32[2,16,256]{2,1,0:T(8,128)S(1)} %pad_maximum_fusion.5), channel_id=1, source_target_pairs={{0,40},{8,48},{16,56},{24,64},{32,72},{40,80},{48,88},{56,96},{64,... | collective-permute-start | bytes 98312 | tf_op jit(solution)/shard_map/ppermute | solution.py:17
  45.4 14.7 %collective-permute-start.7 = (f32[2,16,256]{2,1,0:T(8,128)S(1)}, f32[2,16,256]{2,1,0:T(8,128)S(1)}, u32[]{:S(2)}, u32[]{:S(2)}) collective-permute-start(f32[2,16,256]{2,1,0:T(8,128)S(1)} %pad_maximum_fusion.5), channel_id=1, source_target_pairs={{0,32},{8,40},{16,48},{24,56},{32,64},{40,72},{48,80},{56,88},{64,... | collective-permute-start | bytes 98312 | tf_op jit(solution)/shard_map/ppermute | solution.py:17
  48.6 11.5 %collective-permute-start.6 = (f32[2,16,256]{2,1,0:T(8,128)S(1)}, f32[2,16,256]{2,1,0:T(8,128)S(1)}, u32[]{:S(2)}, u32[]{:S(2)}) collective-permute-start(f32[2,16,256]{2,1,0:T(8,128)S(1)} %pad_maximum_fusion.5), channel_id=1, source_target_pairs={{0,24},{8,32},{16,40},{24,48},{32,56},{40,64},{48,72},{56,80},{64,... | collective-permute-start | bytes 98312 | tf_op jit(solution)/shard_map/ppermute | solution.py:17
  53.0 7.2 %collective-permute-start.5 = (f32[2,16,256]{2,1,0:T(8,128)S(1)}, f32[2,16,256]{2,1,0:T(8,128)S(1)}, u32[]{:S(2)}, u32[]{:S(2)}) collective-permute-start(f32[2,16,256]{2,1,0:T(8,128)S(1)} %pad_maximum_fusion.5), channel_id=1, source_target_pairs={{0,16},{8,24},{16,32},{24,40},{32,48},{40,56},{48,64},{56,72},{64,... | collective-permute-start | bytes 98312 | tf_op jit(solution)/shard_map/ppermute | solution.py:17
  56.6 5.1 %collective-permute-start.4 = (f32[2,16,256]{2,1,0:T(8,128)S(1)}, f32[2,16,256]{2,1,0:T(8,128)S(1)}, u32[]{:S(2)}, u32[]{:S(2)}) collective-permute-start(f32[2,16,256]{2,1,0:T(8,128)S(1)} %pad_maximum_fusion.5), channel_id=1, source_target_pairs={{0,8},{8,16},{16,24},{24,32},{32,40},{40,48},{48,56},{56,64},{64,7... | collective-permute-start | bytes 98312 | tf_op jit(solution)/shard_map/ppermute | solution.py:17
  63.2 8.4 %collective-permute-start.13 = (f32[2,16,256]{2,1,0:T(8,128)S(1)}, f32[2,16,256]{2,1,0:T(8,128)S(1)}, u32[]{:S(2)}, u32[]{:S(2)}) collective-permute-start(f32[2,16,256]{2,1,0:T(8,128)S(1)} %pad_maximum_fusion.6), channel_id=1, source_target_pairs={{0,192},{8,200},{16,208},{24,216},{32,224},{40,232},{48,240},{56,2... | collective-permute-start | bytes 98312 | tf_op jit(solution)/shard_map/ppermute | solution.py:17
  64.5 7.1 %collective-permute-start.12 = (f32[2,16,256]{2,1,0:T(8,128)S(1)}, f32[2,16,256]{2,1,0:T(8,128)S(1)}, u32[]{:S(2)}, u32[]{:S(2)}) collective-permute-start(f32[2,16,256]{2,1,0:T(8,128)S(1)} %pad_maximum_fusion.6), channel_id=1, source_target_pairs={{0,128},{8,136},{16,144},{24,152},{32,160},{40,168},{48,176},{56,1... | collective-permute-start | bytes 98312 | tf_op jit(solution)/shard_map/ppermute | solution.py:17
  68.3 3.7 %collective-permute-start.11 = (f32[2,16,256]{2,1,0:T(8,128)S(1)}, f32[2,16,256]{2,1,0:T(8,128)S(1)}, u32[]{:S(2)}, u32[]{:S(2)}) collective-permute-start(f32[2,16,256]{2,1,0:T(8,128)S(1)} %pad_maximum_fusion.6), channel_id=1, source_target_pairs={{0,64},{8,72},{16,80},{24,88},{32,96},{40,104},{48,112},{56,120},{... | collective-permute-start | bytes 98312 | tf_op jit(solution)/shard_map/ppermute | solution.py:17
  74.3 5.4 %copy-start.2 = (bf16[128,2048]{1,0:T(8,128)(2,1)S(1)}, bf16[128,2048]{1,0:T(8,128)(2,1)}, u32[]{:S(2)}) copy-start(bf16[128,2048]{1,0:T(8,128)(2,1)} %param.18) | copy-start | bytes 1572868
  74.3 5.4 %copy-start.19 = (f32[2048]{0:T(1024)S(1)}, f32[2048]{0:T(1024)}, u32[]{:S(2)}) copy-start(f32[2048]{0:T(1024)} %param.19) | copy-start | bytes 24580
  74.3 5.4 %copy-start.20 = (f32[256]{0:T(256)S(1)}, f32[256]{0:T(256)}, u32[]{:S(2)}) copy-start(f32[256]{0:T(256)} %param.28) | copy-start | bytes 3076
  82.2 19.2 %copy-start.9 = (f32[2048]{0:T(1024)S(1)}, f32[2048]{0:T(1024)}, u32[]{:S(2)}) copy-start(f32[2048]{0:T(1024)} %param.30) | copy-start | bytes 24580
  82.3 1.8 collective-permute-start.14
  85.2 8.5 %collective-permute-start.15 = (f32[2,16,2048]{2,1,0:T(8,128)S(1)}, f32[2,16,2048]{2,1,0:T(8,128)}, u32[]{:S(2)}, u32[]{:S(2)}) collective-permute-start(f32[2,16,2048]{2,1,0:T(8,128)S(1)} %dynamic-slice_bitcast_fusion.2), channel_id=1, source_target_pairs={{0,2},{1,3},{2,0},{3,1},{4,6},{5,7},{6,4},{7,5},{8,10},{9,11},{10,... | collective-permute-start | bytes 786440 | tf_op jit(solution)/shard_map/ppermute | solution.py:22
  94.7 6.6 %collective-permute-start.16 = (f32[16,2048]{1,0:T(8,128)S(1)}, f32[16,2048]{1,0:T(8,128)S(1)}, u32[]{:S(2)}, u32[]{:S(2)}) collective-permute-start(f32[16,2048]{1,0:T(8,128)S(1)} %dynamic-slice_bitcast_fusion.5), channel_id=1, source_target_pairs={{0,4},{1,5},{2,6},{3,7},{4,0},{5,1},{6,2},{7,3},{8,12},{9,13},{10,... | collective-permute-start | bytes 393224 | tf_op jit(solution)/shard_map/ppermute | solution.py:22
  101.5 6.2 %collective-permute-start.17 = (bf16[16,2048]{1,0:T(8,128)(2,1)S(1)}, bf16[16,2048]{1,0:T(8,128)(2,1)S(1)}, u32[]{:S(2)}, u32[]{:S(2)}) collective-permute-start(bf16[16,2048]{1,0:T(8,128)(2,1)S(1)} %multiply_convert_fusion.1), channel_id=1, source_target_pairs={{0,4},{1,5},{2,6},{3,7},{4,0},{5,1},{6,2},{7,3},{8,12},{9,13},{10,... | collective-permute-start | bytes 196616 | tf_op jit(solution)/shard_map/ppermute | solution.py:22
  107.8 5.1 %collective-permute-start.18 = (bf16[2,16,2048]{2,1,0:T(8,128)(2,1)S(1)}, bf16[2,16,2048]{2,1,0:T(8,128)(2,1)S(1)}, u32[]{:S(2)}, u32[]{:S(2)}) collective-permute-start(bf16[2,16,2048]{2,1,0:T(8,128)(2,1)S(1)} %pad_maximum_fusion.4), channel_id=1, source_target_pairs={{0,2},{1,3},{2,0},{3,1},{4,6},{5,7},{6,4},{7,5},{8,10},{9,11},{10,... | collective-permute-start | bytes 393224 | tf_op jit(solution)/shard_map/ppermute | solution.py:22
  112.9 1.6 collective-permute-start.19
  117.6 12.0 %copy-start.13 = (bf16[3,256]{1,0:T(4,128)(2,1)S(1)}, bf16[3,256]{1,0:T(4,128)(2,1)}, u32[]{:S(2)}) copy-start(bf16[3,256]{1,0:T(4,128)(2,1)} %copy-done.12) | copy-start | bytes 4612
  117.6 12.2 %copy-start.4 = (f32[16,16,256]{2,1,0:T(8,128)S(1)}, f32[16,16,256]{2,1,0:T(8,128)}, u32[]{:S(2)}) copy-start(f32[16,16,256]{2,1,0:T(8,128)} %get-tuple-element.12) | copy-start | bytes 786436
  117.6 1.7 collective-permute-start.20
  118.1 11.4 %copy-start.7 = (bf16[128,256]{1,0:T(8,128)(2,1)S(1)}, bf16[128,256]{1,0:T(8,128)(2,1)}, u32[]{:S(2)}) copy-start(bf16[128,256]{1,0:T(8,128)(2,1)} %copy-done.6) | copy-start | bytes 196612
  119.4 8.7 %collective-permute-start.21 = (f32[2,16,2048]{2,1,0:T(8,128)S(1)}, f32[2,16,2048]{2,1,0:T(8,128)S(1)}, u32[]{:S(2)}, u32[]{:S(2)}) collective-permute-start(f32[2,16,2048]{2,1,0:T(8,128)S(1)} %dynamic-slice_bitcast_fusion), channel_id=1, source_target_pairs={{0,2},{1,3},{2,0},{3,1},{4,6},{5,7},{6,4},{7,5},{8,10},{9,11},{10,... | collective-permute-start | bytes 786440 | tf_op jit(solution)/shard_map/ppermute | solution.py:22
  120.3 38.3 %copy-start.22 = (s32[128]{0:T(128)S(1)}, s32[128]{0:T(128)}, u32[]{:S(2)}) copy-start(s32[128]{0:T(128)} %copy-done.21) | copy-start | bytes 1540
  128.1 6.7 %collective-permute-start.22 = (f32[16,2048]{1,0:T(8,128)S(1)}, f32[16,2048]{1,0:T(8,128)S(1)}, u32[]{:S(2)}, u32[]{:S(2)}) collective-permute-start(f32[16,2048]{1,0:T(8,128)S(1)} %dynamic-slice_bitcast_fusion.4), channel_id=1, source_target_pairs={{0,4},{1,5},{2,6},{3,7},{4,0},{5,1},{6,2},{7,3},{8,12},{9,13},{10,... | collective-permute-start | bytes 393224 | tf_op jit(solution)/shard_map/ppermute | solution.py:22
  129.8 50.7 %copy-start.18 = (s32[4]{0:T(128)S(1)}, s32[4]{0:T(128)}, u32[]{:S(2)}) copy-start(s32[4]{0:T(128)} %param.35) | copy-start | bytes 52
  134.9 7.3 %collective-permute-start.23 = (bf16[16,19,256]{2,1,0:T(8,128)(2,1)S(1)}, bf16[16,19,256]{2,1,0:T(8,128)(2,1)S(1)}, u32[]{:S(2)}, u32[]{:S(2)}) collective-permute-start(bf16[16,19,256]{2,1,0:T(8,128)(2,1)S(1)} %pad_maximum_fusion.2), channel_id=1, source_target_pairs={{0,8},{8,0},{16,24},{24,16},{32,40},{40,32},{48,56},{56,48},{64,72... | collective-permute-start | bytes 466952 | tf_op jit(solution)/shard_map/ppermute | solution.py:22
  142.2 7.3 %collective-permute-start.24 = (bf16[16,19,256]{2,1,0:T(8,128)(2,1)S(1)}, bf16[16,19,256]{2,1,0:T(8,128)(2,1)S(1)}, u32[]{:S(2)}, u32[]{:S(2)}) collective-permute-start(bf16[16,19,256]{2,1,0:T(8,128)(2,1)S(1)} %add.334), channel_id=1, source_target_pairs={{0,16},{8,24},{16,0},{24,8},{32,48},{40,56},{48,32},{56,40},{64,80... | collective-permute-start | bytes 466952 | tf_op jit(solution)/shard_map/ppermute | solution.py:22
  149.5 5.9 %collective-permute-start.25 = (bf16[16,19,256]{2,1,0:T(8,128)(2,1)S(1)}, bf16[16,19,256]{2,1,0:T(8,128)(2,1)S(1)}, u32[]{:S(2)}, u32[]{:S(2)}) collective-permute-start(bf16[16,19,256]{2,1,0:T(8,128)(2,1)S(1)} %add.335), channel_id=1, source_target_pairs={{0,32},{8,40},{16,48},{24,56},{32,0},{40,8},{48,16},{56,24},{64,96... | collective-permute-start | bytes 466952 | tf_op jit(solution)/shard_map/ppermute | solution.py:22
  155.4 13.2 %collective-permute-start.26 = (bf16[16,19,256]{2,1,0:T(8,128)(2,1)S(1)}, bf16[16,19,256]{2,1,0:T(8,128)(2,1)S(1)}, u32[]{:S(2)}, u32[]{:S(2)}) collective-permute-start(bf16[16,19,256]{2,1,0:T(8,128)(2,1)S(1)} %add.336), channel_id=1, source_target_pairs={{0,64},{8,72},{16,80},{24,88},{32,96},{40,104},{48,112},{56,120},{... | collective-permute-start | bytes 466952 | tf_op jit(solution)/shard_map/ppermute | solution.py:22
  168.7 11.8 %collective-permute-start.27 = (bf16[16,19,256]{2,1,0:T(8,128)(2,1)S(1)}, bf16[16,19,256]{2,1,0:T(8,128)(2,1)S(1)}, u32[]{:S(2)}, u32[]{:S(2)}) collective-permute-start(bf16[16,19,256]{2,1,0:T(8,128)(2,1)S(1)} %add.337), channel_id=1, source_target_pairs={{0,128},{8,136},{16,144},{24,152},{32,160},{40,168},{48,176},{56,1... | collective-permute-start | bytes 466952 | tf_op jit(solution)/shard_map/ppermute | solution.py:22
  (3 other events, 5.1 us)

commit v3 on v1

--- a/solution.py
+++ b/solution.py
@@ -53,7 +53,6 @@
         give = lax.dynamic_index_in_dim(buf, 1 - mine, at, False)
         got = swap(give.astype(send_dtype), axis, bit)
         buf = keep.astype(jnp.float32) + got.astype(jnp.float32)
-        send_dtype = jnp.float32
     return buf
 
 
@@ -217,11 +216,13 @@
     starts_here = jnp.any(places[:, None] == prompt_start[None, :], axis=1)
     ends_here = jnp.any(places[:, None] == prompt_end[None, :] - 1, axis=1)
     is_live = prompt_of < prompts
+    behind = from_behind(tokens[block_len - edge_len :], "seq", 1)
     normed = rms_norm(tokens.astype(jnp.float32), norm_gain).astype(jnp.bfloat16)
+    normed_behind = rms_norm(behind.astype(jnp.float32), norm_gain).astype(jnp.bfloat16)
     x_branch = jnp.dot(normed, w_x, preferred_element_type=jnp.float32).astype(jnp.bfloat16)
     z_branch = jnp.dot(normed, w_z, preferred_element_type=jnp.float32).astype(jnp.bfloat16)
-    carried = from_behind(x_branch[block_len - edge_len :], "seq", 1)
-    extended = jnp.concatenate([carried, x_branch], axis=0)
+    x_behind = jnp.dot(normed_behind, w_x, preferred_element_type=jnp.float32).astype(jnp.bfloat16)
+    extended = jnp.concatenate([x_behind, x_branch], axis=0)
     conv_sum = jnp.zeros((block_len, chans), jnp.float32) + conv_b[None, :]
     for lag_steps in range(kernel_len):
         window = extended[edge_len - lag_steps : edge_len - lag_steps + block_len].astype(

time: 169 us -> 158 us (0.935)
  the two profiles are of different devices: /device:TPU:4 before, /device:TPU:6 now
where the time goes in v3:
time: 158 us; the launch traced here: 157 us
  starting transfers between devices  62.7 us (40%)
  waiting for transfers between devices  57.5 us (36%)
  other arithmetic  12.6 us (8%)
  matrix products  8.99 us (6%)
  Pallas kernels  8.56 us (5%)
  local copies, waits for them, and re-layouts  5.37 us (3%)
    ppermute x17, waiting for transfers between devices, swap(): return lax.ppermute(x, axis, [(i, i ^ bit) for i in range(devices)])  50.8 us
    ppermute x6, starting transfers between devices, from_behind(): return lax.ppermute(x, axis, pairs)  39.9 us
    ppermute x17, starting transfers between devices, swap(): return lax.ppermute(x, axis, [(i, i ^ bit) for i in range(devices)])  22.8 us
    ppermute x6, waiting for transfers between devices, from_behind(): return lax.ppermute(x, axis, pairs)  6.71 us
    pallas_call x1, Pallas kernels, block_output(): pl.pallas_call(block_output_kernel, out_shape=(jax.ShapeDtypeStruct((t, e...  5.41 us
  transfers between devices with their start and end apart: 23, of which 20 were waited for; matrix products, arithmetic and copies ran while one was open for 10% of the time, Pallas kernels for 0%

profile of v3, /device:TPU:6, one launch (start us, length us, event | category | flops | bytes accessed | tf_op | source)
XLA Modules:
  0.0 157.1 jit_solution(13228495562305238388)
XLA Ops:
  0.7 0.9 slice.69
  1.6 3.6 %collective-permute-start = (bf16[3,2048]{1,0:T(4,128)(2,1)S(1)}, bf16[3,2048]{1,0:T(4,128)(2,1)S(1)}, u32[]{:S(2)}, u32[]{:S(2)}) collective-permute-start(bf16[3,2048]{1,0:T(4,128)(2,1)S(1)} %slice.69), channel_id=1, source_target_pairs={{0,8},{8,16},{16,24},{24,32},{32,40},{40,48},{48,56},{56,64},{64,7... | collective-permute-start | bytes 36872 | tf_op jit(solution)/shard_map/ppermute | solution.py:17
  5.2 1.2 fusion.2
  6.5 0.8 fusion.66
  7.3 0.7 copy.58
  9.1 1.8 %convolution_convert_fusion.3 = bf16[128,256]{1,0:T(8,128)(2,1)S(1)} fusion(bf16[2048,256]{1,0:T(8,128)(2,1)} %param.20, bf16[128,2048]{1,0:T(8,128)(2,1)} %param.18, f32[2048]{0:T(1024)} %param.19, f32[128]{0:T(128)S(1)} %add_rsqrt_fusion.2), kind=kOutput, calls=%fused_computation.10 | convolution fusion | flops 135299072 | bytes 1647104 | tf_op jit(solution)/shard_map/dot_general | solution.py:222
  11.8 1.2 collective-permute-done.1
  13.1 0.9 collective-permute-start.2
  14.1 3.6 %collective-permute-done.2 = f32[128,160]{0,1:T(8,128)S(1)} collective-permute-done((f32[128,160]{0,1:T(8,128)S(1)}, f32[128,160]{0,1:T(8,128)S(1)}, u32[]{:S(2)}, u32[]{:S(2)}) %collective-permute-start.2) | collective-permute-done | bytes 81952 | tf_op jit(solution)/shard_map/ppermute | solution.py:22
  17.7 1.5 collective-permute-start.3
  19.2 4.5 %collective-permute-done.3 = f32[128,160]{0,1:T(8,128)S(1)} collective-permute-done((f32[128,160]{0,1:T(8,128)S(1)}, f32[128,160]{0,1:T(8,128)S(1)}, u32[]{:S(2)}, u32[]{:S(2)}) %collective-permute-start.3) | collective-permute-done | bytes 81952 | tf_op jit(solution)/shard_map/ppermute | solution.py:22
  24.1 2.4 %exponential_multiply_fusion = (f32[128,16,256]{2,1,0:T(8,128)}, f32[128,16,256]{2,1,0:T(8,128)}) fusion(f32[128]{0:T(128)S(1)} %convert_subtract_fusion, f32[16,256]{1,0:T(8,128)S(1)} %exponential_negate_fusion, f32[128,256]{1,0:T(8,128)S(1)} %get-tuple-element.60, f32[128,16]{1,0:T(8,128)S(1)} %copy.59, f32[128,256]{1,0:T(8,128)S(1)} %get-tuple-element.59), kind=kLoop, calls=%fused_computation.2 | loop fusion | flops 1572864 | bytes 4481536 | tf_op jit(solution)/shard_map/mul | solution.py:246
  26.5 3.1 %shard_map.193 = (f32[16,256]{1,0:T(8,128)}, f32[16,256]{1,0:T(8,128)}) custom-call(f32[128,16,256]{2,1,0:T(8,128)} %get-tuple-element.61.da_ref, f32[128,16,256]{2,1,0:T(8,128)} %get-tuple-element.62.dr_ref), custom_call_target="tpu_custom_call" | custom-call | tf_op jit(solution)/shard_map/pallas_call | solution.py:125
  29.6 0.7 pad_maximum_fusion.5
  30.4 3.5 %collective-permute-start.4 = (f32[2,16,256]{2,1,0:T(8,128)S(1)}, f32[2,16,256]{2,1,0:T(8,128)S(1)}, u32[]{:S(2)}, u32[]{:S(2)}) collective-permute-start(f32[2,16,256]{2,1,0:T(8,128)S(1)} %pad_maximum_fusion.5), channel_id=1, source_target_pairs={{0,8},{8,16},{16,24},{24,32},{32,40},{40,48},{48,56},{56,64},{64,7... | collective-permute-start | bytes 98312 | tf_op jit(solution)/shard_map/ppermute | solution.py:17
  33.9 1.6 %collective-permute-done.4 = f32[2,16,256]{2,1,0:T(8,128)S(1)} collective-permute-done((f32[2,16,256]{2,1,0:T(8,128)S(1)}, f32[2,16,256]{2,1,0:T(8,128)S(1)}, u32[]{:S(2)}, u32[]{:S(2)}) %collective-permute-start.4) | collective-permute-done | bytes 32800 | tf_op jit(solution)/shard_map/ppermute | solution.py:17
  35.4 0.7 multiply_select_fusion.6
  36.2 5.5 %collective-permute-start.5 = (f32[2,16,256]{2,1,0:T(8,128)S(1)}, f32[2,16,256]{2,1,0:T(8,128)S(1)}, u32[]{:S(2)}, u32[]{:S(2)}) collective-permute-start(f32[2,16,256]{2,1,0:T(8,128)S(1)} %pad_maximum_fusion.6), channel_id=1, source_target_pairs={{0,16},{8,24},{16,32},{24,40},{32,48},{40,56},{48,64},{56,72},{64,... | collective-permute-start | bytes 98312 | tf_op jit(solution)/shard_map/ppermute | solution.py:17
  41.8 1.6 %collective-permute-done.5 = f32[2,16,256]{2,1,0:T(8,128)S(1)} collective-permute-done((f32[2,16,256]{2,1,0:T(8,128)S(1)}, f32[2,16,256]{2,1,0:T(8,128)S(1)}, u32[]{:S(2)}, u32[]{:S(2)}) %collective-permute-start.5) | collective-permute-done | bytes 32800 | tf_op jit(solution)/shard_map/ppermute | solution.py:17
  43.3 7.8 %collective-permute-start.6 = (f32[2,16,256]{2,1,0:T(8,128)S(1)}, f32[2,16,256]{2,1,0:T(8,128)S(1)}, u32[]{:S(2)}, u32[]{:S(2)}) collective-permute-start(f32[2,16,256]{2,1,0:T(8,128)S(1)} %pad_maximum_fusion.7), channel_id=1, source_target_pairs={{0,32},{8,40},{16,48},{24,56},{32,64},{40,72},{48,80},{56,88},{64,... | collective-permute-start | bytes 98312 | tf_op jit(solution)/shard_map/ppermute | solution.py:17
  51.1 1.6 %collective-permute-done.6 = f32[2,16,256]{2,1,0:T(8,128)S(1)} collective-permute-done((f32[2,16,256]{2,1,0:T(8,128)S(1)}, f32[2,16,256]{2,1,0:T(8,128)S(1)}, u32[]{:S(2)}, u32[]{:S(2)}) %collective-permute-start.6) | collective-permute-done | bytes 32800 | tf_op jit(solution)/shard_map/ppermute | solution.py:17
  52.7 5.6 %collective-permute-start.7 = (f32[2,16,256]{2,1,0:T(8,128)S(1)}, f32[2,16,256]{2,1,0:T(8,128)S(1)}, u32[]{:S(2)}, u32[]{:S(2)}) collective-permute-start(f32[2,16,256]{2,1,0:T(8,128)S(1)} %pad_maximum_fusion.8), channel_id=1, source_target_pairs={{0,64},{8,72},{16,80},{24,88},{32,96},{40,104},{48,112},{56,120},{... | collective-permute-start | bytes 98312 | tf_op jit(solution)/shard_map/ppermute | solution.py:17
  58.8 1.1 collective-permute-done.7
  59.9 13.9 %collective-permute-start.8 = (f32[2,16,256]{2,1,0:T(8,128)S(1)}, f32[2,16,256]{2,1,0:T(8,128)S(1)}, u32[]{:S(2)}, u32[]{:S(2)}) collective-permute-start(f32[2,16,256]{2,1,0:T(8,128)S(1)} %pad_maximum_fusion.9), channel_id=1, source_target_pairs={{0,128},{8,136},{16,144},{24,152},{32,160},{40,168},{48,176},{56,1... | collective-permute-start | bytes 98312 | tf_op jit(solution)/shard_map/ppermute | solution.py:17
  74.4 0.9 collective-permute-done.8
  76.0 1.7 %broadcast_in_dim.20.om_ref = f32[128,16,256]{2,1,0:T(8,128)} broadcast(f32[128,16]{1,0:T(8,128)S(1)} %copy.60), dimensions={0,1} | broadcast | bytes 2105344 | tf_op jit(solution)/shard_map/broadcast_in_dim | solution.py:248
  77.7 5.4 %shard_map.194 = (f32[128,256]{1,0:T(8,128)}, f32[16,16,256]{2,1,0:T(8,128)}) custom-call(f32[128,16,256]{2,1,0:T(8,128)} %get-tuple-element.61.da_ref, f32[128,16,256]{2,1,0:T(8,128)} %get-tuple-element.62.dr_ref, f32[128,16,256]{2,1,0:T(8,128)} %broadcast_in_dim.20.om_ref, f32[16,256]{1,0:T(8,128)} %add_select_fusion.sin_ref, ...), custom_call_target="tpu_custom_call" | custom-call | tf_op jit(solution)/shard_map/pallas_call | solution.py:141
  83.1 2.5 %convolution_convert_fusion.1 = bf16[128,2048]{1,0:T(8,128)(2,1)S(1)} fusion(bf16[256,2048]{1,0:T(8,128)(2,1)} %param.29, f32[128,256]{1,0:T(8,128)} %get-tuple-element.9, bf16[128,256]{1,0:T(8,128)(2,1)S(1)} %multiply_convert_fusion.1, bf16[2048,256]{1,0:T(8,128)(2,1)} %param.21, bf16[128,2048]{1,0:T(8,128)(2,1)S(1)} %copy-done.3, f32[2048]{0:T(1024)S(1)} %copy-done.8, ...), kind=kOutput, calls=%fused_computation.1 | convolution fusion | flops 270106624 | bytes 3352064 | tf_op jit(solution)/shard_map/dot_general | solution.py:279
  85.9 1.4 collective-permute-done.9
  87.4 0.9 collective-permute-start.10
  88.5 1.0 convert_element_type.221
  89.5 3.5 %collective-permute-done.10 = bf16[2,16,2048]{2,1,0:T(8,128)(2,1)S(1)} collective-permute-done((bf16[2,16,2048]{2,1,0:T(8,128)(2,1)S(1)}, bf16[2,16,2048]{2,1,0:T(8,128)(2,1)S(1)}, u32[]{:S(2)}, u32[]{:S(2)}) %collective-permute-start.10) | collective-permute-done | bytes 131104 | tf_op jit(solution)/shard_map/ppermute | solution.py:22
  93.0 1.5 collective-permute-start.11
  94.7 4.2 %collective-permute-done.11 = bf16[16,2048]{1,0:T(8,128)(2,1)S(1)} collective-permute-done((bf16[16,2048]{1,0:T(8,128)(2,1)S(1)}, bf16[16,2048]{1,0:T(8,128)(2,1)S(1)}, u32[]{:S(2)}, u32[]{:S(2)}) %collective-permute-start.11) | collective-permute-done | bytes 65568 | tf_op jit(solution)/shard_map/ppermute | solution.py:22
  99.2 1.5 collective-permute-start.12
  100.9 4.4 %collective-permute-done.12 = bf16[16,2048]{1,0:T(8,128)(2,1)S(1)} collective-permute-done((bf16[16,2048]{1,0:T(8,128)(2,1)S(1)}, bf16[16,2048]{1,0:T(8,128)(2,1)S(1)}, u32[]{:S(2)}, u32[]{:S(2)}) %collective-permute-start.12) | collective-permute-done | bytes 65568 | tf_op jit(solution)/shard_map/ppermute | solution.py:22
  105.4 0.9 collective-permute-start.13
  106.3 1.8 %collective-permute-done.19 = bf16[16,19,256]{2,1,0:T(8,128)(2,1)S(1)} collective-permute-done((bf16[16,19,256]{2,1,0:T(8,128)(2,1)S(1)}, bf16[16,19,256]{2,1,0:T(8,128)(2,1)S(1)}, u32[]{:S(2)}, u32[]{:S(2)}) %collective-permute-start.19) | collective-permute-done | bytes 155680 | tf_op jit(solution)/shard_map/ppermute | solution.py:22
  108.2 2.3 %collective-permute-done.13 = bf16[2,16,2048]{2,1,0:T(8,128)(2,1)S(1)} collective-permute-done((bf16[2,16,2048]{2,1,0:T(8,128)(2,1)S(1)}, bf16[2,16,2048]{2,1,0:T(8,128)(2,1)S(1)}, u32[]{:S(2)}, u32[]{:S(2)}) %collective-permute-start.13) | collective-permute-done | bytes 131104 | tf_op jit(solution)/shard_map/ppermute | solution.py:22
  110.6 3.2 %collective-permute-done.20 = bf16[16,19,256]{2,1,0:T(8,128)(2,1)S(1)} collective-permute-done((bf16[16,19,256]{2,1,0:T(8,128)(2,1)S(1)}, bf16[16,19,256]{2,1,0:T(8,128)(2,1)S(1)}, u32[]{:S(2)}, u32[]{:S(2)}) %collective-permute-start.20) | collective-permute-done | bytes 155680 | tf_op jit(solution)/shard_map/ppermute | solution.py:22
  114.0 8.3 %collective-permute-done.21 = bf16[16,19,256]{2,1,0:T(8,128)(2,1)S(1)} collective-permute-done((bf16[16,19,256]{2,1,0:T(8,128)(2,1)S(1)}, bf16[16,19,256]{2,1,0:T(8,128)(2,1)S(1)}, u32[]{:S(2)}, u32[]{:S(2)}) %collective-permute-start.21) | collective-permute-done | bytes 155680 | tf_op jit(solution)/shard_map/ppermute | solution.py:22
  123.1 14.7 %collective-permute-start.22 = (bf16[16,19,256]{2,1,0:T(8,128)(2,1)}, bf16[16,19,256]{2,1,0:T(8,128)(2,1)}, u32[]{:S(2)}, u32[]{:S(2)}) collective-permute-start(bf16[16,19,256]{2,1,0:T(8,128)(2,1)} %add.328), channel_id=1, source_target_pairs={{0,128},{8,136},{16,144},{24,152},{32,160},{40,168},{48,176},{56,1... | collective-permute-start | bytes 466952 | tf_op jit(solution)/shard_map/ppermute | solution.py:22
  138.4 2.4 %convolution_convert_fusion = bf16[128,2048]{1,0:T(8,128)(2,1)S(1)} fusion(bf16[512,2048]{1,0:T(8,128)(2,1)S(1)} %copy-done, bf16[128,2048]{1,0:T(8,128)(2,1)S(1)} %bitcast.149, bf16[2048,512]{1,0:T(8,128)(2,1)} %param.32, f32[128,512]{1,0:T(8,128)S(1)} %fusion.68), kind=kOutput, calls=%fused_computation | convolution fusion | flops 537526272 | bytes 5505024 | tf_op jit(solution)/shard_map/dot_general | solution.py:291
  141.2 2.8 %collective-permute-done.22 = bf16[16,19,256]{2,1,0:T(8,128)(2,1)} collective-permute-done((bf16[16,19,256]{2,1,0:T(8,128)(2,1)}, bf16[16,19,256]{2,1,0:T(8,128)(2,1)}, u32[]{:S(2)}, u32[]{:S(2)}) %collective-permute-start.22) | collective-permute-done | bytes 155680 | tf_op jit(solution)/shard_map/ppermute | solution.py:22
  143.9 1.1 add.329
  145.5 5.0 %collective-permute-done.16 = bf16[2,16,2048]{2,1,0:T(8,128)(2,1)S(1)} collective-permute-done((bf16[2,16,2048]{2,1,0:T(8,128)(2,1)S(1)}, bf16[2,16,2048]{2,1,0:T(8,128)(2,1)S(1)}, u32[]{:S(2)}, u32[]{:S(2)}) %collective-permute-start.16) | collective-permute-done | bytes 131104 | tf_op jit(solution)/shard_map/ppermute | solution.py:22
  150.7 0.8 convolution_convert_fusion.5
  152.1 4.3 %collective-permute-done.17 = bf16[16,2048]{1,0:T(8,128)(2,1)S(1)} collective-permute-done((bf16[16,2048]{1,0:T(8,128)(2,1)S(1)}, bf16[16,2048]{1,0:T(8,128)(2,1)S(1)}, u32[]{:S(2)}, u32[]{:S(2)}) %collective-permute-start.17) | collective-permute-done | bytes 65568 | tf_op jit(solution)/shard_map/ppermute | solution.py:22
  (113 shorter events, 9.3 us)
Async XLA Ops:
  0.6 137.8 %copy-start = (bf16[512,2048]{1,0:T(8,128)(2,1)S(1)}, bf16[512,2048]{1,0:T(8,128)(2,1)}, u32[]{:S(2)}) copy-start(bf16[512,2048]{1,0:T(8,128)(2,1)} %param.33) | copy-start | bytes 6291460
  0.6 10.4 %copy-start.8 = (f32[2048]{0:T(1024)S(1)}, f32[2048]{0:T(1024)}, u32[]{:S(2)}) copy-start(f32[2048]{0:T(1024)} %param.19) | copy-start | bytes 24580
  0.7 10.4 %copy-start.2 = (bf16[2048,256]{1,0:T(8,128)(2,1)S(1)}, bf16[2048,256]{1,0:T(8,128)(2,1)}, u32[]{:S(2)}) copy-start(bf16[2048,256]{1,0:T(8,128)(2,1)} %param.20) | copy-start | bytes 3145732
  0.7 10.7 %copy-start.9 = (f32[256]{0:T(256)S(1)}, f32[256]{0:T(256)}, u32[]{:S(2)}) copy-start(f32[256]{0:T(256)} %param.23) | copy-start | bytes 3076
  0.7 10.8 %copy-start.4 = (bf16[256,160]{0,1:T(8,128)(2,1)S(1)}, bf16[256,160]{0,1:T(8,128)(2,1)}, u32[]{:S(2)}) copy-start(bf16[256,160]{0,1:T(8,128)(2,1)} %param.24) | copy-start | bytes 245764
  0.7 11.1 %copy-start.7 = (f32[16,256]{1,0:T(8,128)S(1)}, f32[16,256]{1,0:T(8,128)}, u32[]{:S(2)}) copy-start(f32[16,256]{1,0:T(8,128)} %param.27) | copy-start | bytes 49156
  1.6 9.3 %collective-permute-start = (bf16[3,2048]{1,0:T(4,128)(2,1)S(1)}, bf16[3,2048]{1,0:T(4,128)(2,1)S(1)}, u32[]{:S(2)}, u32[]{:S(2)}) collective-permute-start(bf16[3,2048]{1,0:T(4,128)(2,1)S(1)} %slice.69), channel_id=1, source_target_pairs={{0,8},{8,16},{16,24},{24,32},{32,40},{40,48},{48,56},{56,64},{64,7... | collective-permute-start | bytes 36872 | tf_op jit(solution)/shard_map/ppermute | solution.py:17
  9.1 14.8 %copy-start.5 = (bf16[128,256]{1,0:T(8,128)(2,1)S(1)}, bf16[128,256]{1,0:T(8,128)(2,1)}, u32[]{:S(2)}) copy-start(bf16[128,256]{1,0:T(8,128)(2,1)} %param.25) | copy-start | bytes 196612
  9.1 14.8 %copy-start.10 = (f32[256]{0:T(256)S(1)}, f32[256]{0:T(256)}, u32[]{:S(2)}) copy-start(f32[256]{0:T(256)} %param.26) | copy-start | bytes 3076
  11.7 1.4 collective-permute-start.1
  13.1 4.6 %collective-permute-start.2 = (f32[128,160]{0,1:T(8,128)S(1)}, f32[128,160]{0,1:T(8,128)S(1)}, u32[]{:S(2)}, u32[]{:S(2)}) collective-permute-start(f32[128,160]{0,1:T(8,128)S(1)} %add.283), channel_id=1, source_target_pairs={{0,2},{1,3},{2,0},{3,1},{4,6},{5,7},{6,4},{7,5},{8,10},{9,11},{10,... | collective-permute-start | bytes 245768 | tf_op jit(solution)/shard_map/ppermute | solution.py:22
  17.7 6.0 %collective-permute-start.3 = (f32[128,160]{0,1:T(8,128)S(1)}, f32[128,160]{0,1:T(8,128)S(1)}, u32[]{:S(2)}, u32[]{:S(2)}) collective-permute-start(f32[128,160]{0,1:T(8,128)S(1)} %add.284), channel_id=1, source_target_pairs={{0,4},{1,5},{2,6},{3,7},{4,0},{5,1},{6,2},{7,3},{8,12},{9,13},{10,... | collective-permute-start | bytes 245768 | tf_op jit(solution)/shard_map/ppermute | solution.py:22
  30.4 5.1 %collective-permute-start.4 = (f32[2,16,256]{2,1,0:T(8,128)S(1)}, f32[2,16,256]{2,1,0:T(8,128)S(1)}, u32[]{:S(2)}, u32[]{:S(2)}) collective-permute-start(f32[2,16,256]{2,1,0:T(8,128)S(1)} %pad_maximum_fusion.5), channel_id=1, source_target_pairs={{0,8},{8,16},{16,24},{24,32},{32,40},{40,48},{48,56},{56,64},{64,7... | collective-permute-start | bytes 98312 | tf_op jit(solution)/shard_map/ppermute | solution.py:17
  36.2 7.1 %collective-permute-start.5 = (f32[2,16,256]{2,1,0:T(8,128)S(1)}, f32[2,16,256]{2,1,0:T(8,128)S(1)}, u32[]{:S(2)}, u32[]{:S(2)}) collective-permute-start(f32[2,16,256]{2,1,0:T(8,128)S(1)} %pad_maximum_fusion.6), channel_id=1, source_target_pairs={{0,16},{8,24},{16,32},{24,40},{32,48},{40,56},{48,64},{56,72},{64,... | collective-permute-start | bytes 98312 | tf_op jit(solution)/shard_map/ppermute | solution.py:17
  43.3 9.3 %collective-permute-start.6 = (f32[2,16,256]{2,1,0:T(8,128)S(1)}, f32[2,16,256]{2,1,0:T(8,128)S(1)}, u32[]{:S(2)}, u32[]{:S(2)}) collective-permute-start(f32[2,16,256]{2,1,0:T(8,128)S(1)} %pad_maximum_fusion.7), channel_id=1, source_target_pairs={{0,32},{8,40},{16,48},{24,56},{32,64},{40,72},{48,80},{56,88},{64,... | collective-permute-start | bytes 98312 | tf_op jit(solution)/shard_map/ppermute | solution.py:17
  52.7 7.2 %collective-permute-start.7 = (f32[2,16,256]{2,1,0:T(8,128)S(1)}, f32[2,16,256]{2,1,0:T(8,128)S(1)}, u32[]{:S(2)}, u32[]{:S(2)}) collective-permute-start(f32[2,16,256]{2,1,0:T(8,128)S(1)} %pad_maximum_fusion.8), channel_id=1, source_target_pairs={{0,64},{8,72},{16,80},{24,88},{32,96},{40,104},{48,112},{56,120},{... | collective-permute-start | bytes 98312 | tf_op jit(solution)/shard_map/ppermute | solution.py:17
  59.9 15.5 %collective-permute-start.8 = (f32[2,16,256]{2,1,0:T(8,128)S(1)}, f32[2,16,256]{2,1,0:T(8,128)S(1)}, u32[]{:S(2)}, u32[]{:S(2)}) collective-permute-start(f32[2,16,256]{2,1,0:T(8,128)S(1)} %pad_maximum_fusion.9), channel_id=1, source_target_pairs={{0,128},{8,136},{16,144},{24,152},{32,160},{40,168},{48,176},{56,1... | collective-permute-start | bytes 98312 | tf_op jit(solution)/shard_map/ppermute | solution.py:17
  77.7 5.4 %copy-start.3 = (bf16[128,2048]{1,0:T(8,128)(2,1)S(1)}, bf16[128,2048]{1,0:T(8,128)(2,1)}, u32[]{:S(2)}) copy-start(bf16[128,2048]{1,0:T(8,128)(2,1)} %param.18) | copy-start | bytes 1572868
  77.7 5.4 %copy-start.12 = (f32[256]{0:T(256)S(1)}, f32[256]{0:T(256)}, u32[]{:S(2)}) copy-start(f32[256]{0:T(256)} %param.28) | copy-start | bytes 3076
  85.6 13.4 %copy-start.6 = (f32[2048]{0:T(1024)S(1)}, f32[2048]{0:T(1024)}, u32[]{:S(2)}) copy-start(f32[2048]{0:T(1024)} %param.30) | copy-start | bytes 24580
  85.7 1.6 %collective-permute-start.9 = (bf16[2,2,16,2048]{3,2,0,1:T(8,128)(2,1)S(1)}, bf16[2,2,16,2048]{3,2,0,1:T(8,128)(2,1)S(1)}, u32[]{:S(2)}, u32[]{:S(2)}) collective-permute-start(bf16[2,2,16,2048]{3,2,0,1:T(8,128)(2,1)S(1)} %bitcast.152), channel_id=1, source_target_pairs={{0,1},{1,0},{2,3},{3,2},{4,5},{5,4},{6,7},{7,6},{8,9},{9,8},{10,11... | collective-permute-start | bytes 786440 | tf_op jit(solution)/shard_map/ppermute | solution.py:22
  87.4 5.6 %collective-permute-start.10 = (bf16[2,16,2048]{2,1,0:T(8,128)(2,1)S(1)}, bf16[2,16,2048]{2,1,0:T(8,128)(2,1)S(1)}, u32[]{:S(2)}, u32[]{:S(2)}) collective-permute-start(bf16[2,16,2048]{2,1,0:T(8,128)(2,1)S(1)} %fusion.15), channel_id=1, source_target_pairs={{0,2},{1,3},{2,0},{3,1},{4,6},{5,7},{6,4},{7,5},{8,10},{9,11},{10,... | collective-permute-start | bytes 393224 | tf_op jit(solution)/shard_map/ppermute | solution.py:22
  93.0 5.9 %collective-permute-start.11 = (bf16[16,2048]{1,0:T(8,128)(2,1)S(1)}, bf16[16,2048]{1,0:T(8,128)(2,1)S(1)}, u32[]{:S(2)}, u32[]{:S(2)}) collective-permute-start(bf16[16,2048]{1,0:T(8,128)(2,1)S(1)} %fusion.30), channel_id=1, source_target_pairs={{0,4},{1,5},{2,6},{3,7},{4,0},{5,1},{6,2},{7,3},{8,12},{9,13},{10,... | collective-permute-start | bytes 196616 | tf_op jit(solution)/shard_map/ppermute | solution.py:22
  94.6 6.2 %collective-permute-start.18 = (bf16[16,19,256]{2,1,0:T(8,128)(2,1)S(1)}, bf16[16,19,256]{2,1,0:T(8,128)(2,1)S(1)}, u32[]{:S(2)}, u32[]{:S(2)}) collective-permute-start(bf16[16,19,256]{2,1,0:T(8,128)(2,1)S(1)} %pad_maximum_fusion.2), channel_id=1, source_target_pairs={{0,8},{8,0},{16,24},{24,16},{32,40},{40,32},{48,56},{56,48},{64,72... | collective-permute-start | bytes 466952 | tf_op jit(solution)/shard_map/ppermute | solution.py:22
  99.2 6.2 %collective-permute-start.12 = (bf16[16,2048]{1,0:T(8,128)(2,1)S(1)}, bf16[16,2048]{1,0:T(8,128)(2,1)S(1)}, u32[]{:S(2)}, u32[]{:S(2)}) collective-permute-start(bf16[16,2048]{1,0:T(8,128)(2,1)S(1)} %multiply_convert_fusion), channel_id=1, source_target_pairs={{0,4},{1,5},{2,6},{3,7},{4,0},{5,1},{6,2},{7,3},{8,12},{9,13},{10,... | collective-permute-start | bytes 196616 | tf_op jit(solution)/shard_map/ppermute | solution.py:22
  100.8 7.3 %collective-permute-start.19 = (bf16[16,19,256]{2,1,0:T(8,128)(2,1)S(1)}, bf16[16,19,256]{2,1,0:T(8,128)(2,1)S(1)}, u32[]{:S(2)}, u32[]{:S(2)}) collective-permute-start(bf16[16,19,256]{2,1,0:T(8,128)(2,1)S(1)} %fusion.62), channel_id=1, source_target_pairs={{0,16},{8,24},{16,0},{24,8},{32,48},{40,56},{48,32},{56,40},{64,80... | collective-permute-start | bytes 466952 | tf_op jit(solution)/shard_map/ppermute | solution.py:22
  105.4 5.1 %collective-permute-start.13 = (bf16[2,16,2048]{2,1,0:T(8,128)(2,1)S(1)}, bf16[2,16,2048]{2,1,0:T(8,128)(2,1)S(1)}, u32[]{:S(2)}, u32[]{:S(2)}) collective-permute-start(bf16[2,16,2048]{2,1,0:T(8,128)(2,1)S(1)} %pad_maximum_fusion.4), channel_id=1, source_target_pairs={{0,2},{1,3},{2,0},{3,1},{4,6},{5,7},{6,4},{7,5},{8,10},{9,11},{10,... | collective-permute-start | bytes 393224 | tf_op jit(solution)/shard_map/ppermute | solution.py:22
  108.1 5.8 %collective-permute-start.20 = (bf16[16,19,256]{2,1,0:T(8,128)(2,1)S(1)}, bf16[16,19,256]{2,1,0:T(8,128)(2,1)S(1)}, u32[]{:S(2)}, u32[]{:S(2)}) collective-permute-start(bf16[16,19,256]{2,1,0:T(8,128)(2,1)S(1)} %add.326), channel_id=1, source_target_pairs={{0,32},{8,40},{16,48},{24,56},{32,0},{40,8},{48,16},{56,24},{64,96... | collective-permute-start | bytes 466952 | tf_op jit(solution)/shard_map/ppermute | solution.py:22
  110.5 27.3 %collective-permute-start.14 = (bf16[2,2,16,2048]{3,2,1,0:T(8,128)(2,1)S(1)}, bf16[2,2,16,2048]{3,2,1,0:T(8,128)(2,1)S(1)}, u32[]{:S(2)}, u32[]{:S(2)}) collective-permute-start(bf16[2,2,16,2048]{3,2,1,0:T(8,128)(2,1)S(1)} %pad_maximum_fusion.1), channel_id=1, source_target_pairs={{0,1},{1,0},{2,3},{3,2},{4,5},{5,4},{6,7},{7,6},{8,9},{9,8},{10,11... | collective-permute-start | bytes 786440 | tf_op jit(solution)/shard_map/ppermute | solution.py:22
  113.9 8.5 %collective-permute-start.21 = (bf16[16,19,256]{2,1,0:T(8,128)(2,1)S(1)}, bf16[16,19,256]{2,1,0:T(8,128)(2,1)S(1)}, u32[]{:S(2)}, u32[]{:S(2)}) collective-permute-start(bf16[16,19,256]{2,1,0:T(8,128)(2,1)S(1)} %add.327), channel_id=1, source_target_pairs={{0,64},{8,72},{16,80},{24,88},{32,96},{40,104},{48,112},{56,120},{... | collective-permute-start | bytes 466952 | tf_op jit(solution)/shard_map/ppermute | solution.py:22
  114.0 23.9 %copy-start.1 = (bf16[2048,512]{1,0:T(8,128)(2,1)S(1)}, bf16[2048,512]{1,0:T(8,128)(2,1)}, u32[]{:S(2)}) copy-start(bf16[2048,512]{1,0:T(8,128)(2,1)} %param.31) | copy-start | bytes 6291460
  123.1 20.8 %collective-permute-start.22 = (bf16[16,19,256]{2,1,0:T(8,128)(2,1)}, bf16[16,19,256]{2,1,0:T(8,128)(2,1)}, u32[]{:S(2)}, u32[]{:S(2)}) collective-permute-start(bf16[16,19,256]{2,1,0:T(8,128)(2,1)} %add.328), channel_id=1, source_target_pairs={{0,128},{8,136},{16,144},{24,152},{32,160},{40,168},{48,176},{56,1... | collective-permute-start | bytes 466952 | tf_op jit(solution)/shard_map/ppermute | solution.py:22
  140.9 4.4 %copy-start.11 = (s32[4]{0:T(128)S(1)}, s32[4]{0:T(128)}, u32[]{:S(2)}) copy-start(s32[4]{0:T(128)} %param.35) | copy-start | bytes 52
  141.0 4.1 %collective-permute-start.15 = (bf16[2,2,16,2048]{3,2,0,1:T(8,128)(2,1)S(1)}, bf16[2,2,16,2048]{3,2,0,1:T(8,128)(2,1)S(1)}, u32[]{:S(2)}, u32[]{:S(2)}) collective-permute-start(bf16[2,2,16,2048]{3,2,0,1:T(8,128)(2,1)S(1)} %bitcast.153), channel_id=1, source_target_pairs={{0,1},{1,0},{2,3},{3,2},{4,5},{5,4},{6,7},{7,6},{8,9},{9,8},{10,11... | collective-permute-start | bytes 786440 | tf_op jit(solution)/shard_map/ppermute | solution.py:22
  145.1 5.4 %collective-permute-start.16 = (bf16[2,16,2048]{2,1,0:T(8,128)(2,1)S(1)}, bf16[2,16,2048]{2,1,0:T(8,128)(2,1)S(1)}, u32[]{:S(2)}, u32[]{:S(2)}) collective-permute-start(bf16[2,16,2048]{2,1,0:T(8,128)(2,1)S(1)} %fusion.16), channel_id=1, source_target_pairs={{0,2},{1,3},{2,0},{3,1},{4,6},{5,7},{6,4},{7,5},{8,10},{9,11},{10,... | collective-permute-start | bytes 393224 | tf_op jit(solution)/shard_map/ppermute | solution.py:22
  150.6 5.9 %collective-permute-start.17 = (bf16[16,2048]{1,0:T(8,128)(2,1)S(1)}, bf16[16,2048]{1,0:T(8,128)(2,1)S(1)}, u32[]{:S(2)}, u32[]{:S(2)}) collective-permute-start(bf16[16,2048]{1,0:T(8,128)(2,1)S(1)} %fusion.31), channel_id=1, source_target_pairs={{0,4},{1,5},{2,6},{3,7},{4,0},{5,1},{6,2},{7,3},{8,12},{9,13},{10,... | collective-permute-start | bytes 196616 | tf_op jit(solution)/shard_map/ppermute | solution.py:22

commit v4 on v3

--- a/solution.py
+++ b/solution.py
@@ -94,29 +94,38 @@
     atot_ref[...] = acum
 
 
-def block_output_kernel(da_ref, dr_ref, om_ref, sin_ref, endf_ref, pid_ref, y_ref, fin_ref):
+def block_local_kernel(da_ref, dr_ref, om_ref, endf_ref, pid_ref, y_ref, g_ref, fs_ref, fd_ref):
     steps = da_ref.shape[0]
     width = y_ref.shape[1]
-    fin_ref[...] = jnp.zeros(fin_ref.shape, jnp.float32)
+    fs_ref[...] = jnp.zeros(fs_ref.shape, jnp.float32)
+    fd_ref[...] = jnp.zeros(fd_ref.shape, jnp.float32)
     row_ids = lax.broadcasted_iota(jnp.int32, (8, width), 0)
 
-    def chunk(c, state):
+    def chunk(c, carry):
+        state, acum = carry
         base = pl.multiple_of(c * 8, 8)
         rows = jnp.zeros((8, width), jnp.float32)
         for i in range(8):
             t = base + i
-            state = da_ref[t] * state + dr_ref[t]
-            here = jnp.sum(om_ref[t] * state, axis=0, keepdims=True)
+            da = da_ref[t]
+            state = da * state + dr_ref[t]
+            acum = da * acum
+            om = om_ref[t]
+            here = jnp.sum(om * state, axis=0, keepdims=True)
             rows = jnp.where(row_ids == i, here, rows)
+            g_ref[t] = om * acum
 
             @pl.when(endf_ref[t] != 0)
             def _():
-                fin_ref[pid_ref[t]] = state
+                fs_ref[pid_ref[t]] = state
+                fd_ref[pid_ref[t]] = acum
 
         y_ref[pl.ds(base, 8), :] = rows
-        return state
-
-    lax.fori_loop(0, steps // 8, chunk, sin_ref[...])
+        return state, acum
+
+    zero = jnp.zeros(fs_ref.shape[1:], jnp.float32)
+    one = jnp.ones(fd_ref.shape[1:], jnp.float32)
+    lax.fori_loop(0, steps // 8, chunk, (zero, one))
 
 
 def block_summary(da, dr):
@@ -134,20 +143,22 @@
     )(da, dr)
 
 
-def block_output(da, dr, om, sin, endf, pid, prompts):
+def block_local(da, dr, om, endf, pid, prompts):
     t, n, e = da.shape
     vmem = pl.BlockSpec(memory_space=pltpu.VMEM)
     smem = pl.BlockSpec(memory_space=pltpu.SMEM)
     return pl.pallas_call(
-        block_output_kernel,
+        block_local_kernel,
         out_shape=(
             jax.ShapeDtypeStruct((t, e), jnp.float32),
+            jax.ShapeDtypeStruct((t, n, e), jnp.float32),
+            jax.ShapeDtypeStruct((prompts, n, e), jnp.float32),
             jax.ShapeDtypeStruct((prompts, n, e), jnp.float32),
         ),
-        in_specs=[vmem, vmem, vmem, vmem, smem, smem],
-        out_specs=(vmem, vmem),
+        in_specs=[vmem, vmem, vmem, smem, smem],
+        out_specs=(vmem, vmem, vmem, vmem),
         interpret=INTERPRET,
-    )(da, dr, om, sin, endf, pid)
+    )(da, dr, om, endf, pid)
 
 
 def entering_state(a_blk, s_blk, axis):
@@ -247,10 +258,14 @@
     drive = (step_size * conv_float)[:, None, :] * in_map[:, :, None]
     out_wide = jnp.broadcast_to(out_map[:, :, None], decay.shape)
     s_blk, a_blk = block_summary(decay, drive)
-    state_in = entering_state(a_blk, s_blk, "seq")
     end_flag = ends_here.astype(jnp.int32)
     slot_of = jnp.minimum(prompt_of, prompts - 1).astype(jnp.int32)
-    mixer_y, final_part = block_output(decay, drive, out_wide, state_in, end_flag, slot_of, prompts)
+    y_zero, g_share, end_state, end_decay = block_local(
+        decay, drive, out_wide, end_flag, slot_of, prompts
+    )
+    state_in = entering_state(a_blk, s_blk, "seq")
+    mixer_y = y_zero + jnp.sum(g_share * state_in[None], axis=1)
+    final_part = end_state + end_decay * state_in[None]
     mixer_y = mixer_y + d_skip[None, :] * conv_float
     gated = (mixer_y * jax.nn.silu(z_branch.astype(jnp.float32))).astype(jnp.bfloat16)
     ends_local = (prompt_end - 1 >= first_row) & (prompt_end - 1 < first_row + block_len)

time: 158 us -> 158 us (level)
  starting transfers between devices: 62.7 us -> 49.3 us
  waiting for transfers between devices: 57.5 us -> 64.1 us
  other arithmetic: 12.6 us -> 17.7 us
    ppermute x17, starting transfers between devices: 22.8 us -> 9.45 us  [swap(): return lax.ppermute(x, axis, [(i, i ^ bit) for i in range(devices)])]
    ppermute x17, waiting for transfers between devices: 50.8 us -> 59 us  [swap(): return lax.ppermute(x, axis, [(i, i ^ bit) for i in range(devices)])]
    reduce_sum x0 -> x1, other arithmetic: none -> 2.16 us  [local(): mixer_y = y_zero + jnp.sum(g_share * state_in[None], axis=1)]
  transfers between devices with their start and end apart: 23 -> 23, of which waited for: 20 -> 19; matrix products, arithmetic and copies ran while one was open for 10% -> 13% of each run, Pallas kernels for 0% -> 4%
where the time goes in v4:
time: 158 us
  waiting for transfers between devices  64.1 us (41%)
  starting transfers between devices  49.3 us (31%)
  other arithmetic  17.7 us (11%)
  matrix products  10.4 us (7%)
  Pallas kernels  9.37 us (6%)
  local copies, waits for them, and re-layouts  5.41 us (3%)
    ppermute x17, waiting for transfers between devices, swap(): return lax.ppermute(x, axis, [(i, i ^ bit) for i in range(devices)])  59 us
    ppermute x6, starting transfers between devices, from_behind(): return lax.ppermute(x, axis, pairs)  39.8 us
    ppermute x17, starting transfers between devices, swap(): return lax.ppermute(x, axis, [(i, i ^ bit) for i in range(devices)])  9.45 us
    pallas_call x1, Pallas kernels, block_local(): pl.pallas_call(block_local_kernel, out_shape=(jax.ShapeDtypeStruct((t, e)...  6.22 us
    ppermute x6, waiting for transfers between devices, from_behind(): return lax.ppermute(x, axis, pairs)  5.17 us
  transfers between devices with their start and end apart: 23, of which 19 were waited for; matrix products, arithmetic and copies ran while one was open for 13% of the time, Pallas kernels for 4%

profile of v4, /device:TPU:6, one launch (start us, length us, event | category | flops | bytes accessed | tf_op | source)
XLA Modules:
  0.0 157.6 jit_solution(11424179185109472638)
XLA Ops:
  0.7 0.9 slice.69
  1.6 3.6 %collective-permute-start = (bf16[3,2048]{1,0:T(4,128)(2,1)S(1)}, bf16[3,2048]{1,0:T(4,128)(2,1)S(1)}, u32[]{:S(2)}, u32[]{:S(2)}) collective-permute-start(bf16[3,2048]{1,0:T(4,128)(2,1)S(1)} %slice.69), channel_id=1, source_target_pairs={{0,8},{8,16},{16,24},{24,32},{32,40},{40,48},{48,56},{56,64},{64,7... | collective-permute-start | bytes 36872 | tf_op jit(solution)/shard_map/ppermute | solution.py:17
  5.2 1.2 fusion.2
  7.4 1.2 broadcast_add_fusion
  8.8 0.8 fusion.68
  9.6 1.8 %convolution_convert_fusion.3 = bf16[128,256]{1,0:T(8,128)(2,1)S(1)} fusion(bf16[2048,256]{1,0:T(8,128)(2,1)} %param.20, bf16[128,2048]{1,0:T(8,128)(2,1)} %param.18, f32[2048]{0:T(1024)} %param.19, f32[128]{0:T(128)S(1)} %add_rsqrt_fusion.2), kind=kOutput, calls=%fused_computation.11 | convolution fusion | flops 135299072 | bytes 1647104 | tf_op jit(solution)/shard_map/dot_general | solution.py:233
  12.3 1.2 collective-permute-done.1
  13.6 0.9 collective-permute-start.2
  14.6 3.6 %collective-permute-done.2 = f32[128,160]{0,1:T(8,128)S(1)} collective-permute-done((f32[128,160]{0,1:T(8,128)S(1)}, f32[128,160]{0,1:T(8,128)S(1)}, u32[]{:S(2)}, u32[]{:S(2)}) %collective-permute-start.2) | collective-permute-done | bytes 81952 | tf_op jit(solution)/shard_map/ppermute | solution.py:22
  18.2 1.5 collective-permute-start.3
  19.7 4.5 %collective-permute-done.3 = f32[128,160]{0,1:T(8,128)S(1)} collective-permute-done((f32[128,160]{0,1:T(8,128)S(1)}, f32[128,160]{0,1:T(8,128)S(1)}, u32[]{:S(2)}, u32[]{:S(2)}) %collective-permute-start.3) | collective-permute-done | bytes 81952 | tf_op jit(solution)/shard_map/ppermute | solution.py:22
  24.7 2.4 %exponential_multiply_fusion = (f32[128,16,256]{2,1,0:T(8,128)}, f32[128,16,256]{2,1,0:T(8,128)}) fusion(f32[128]{0:T(128)S(1)} %convert_subtract_fusion, f32[16,256]{1,0:T(8,128)S(1)} %exponential_negate_fusion, f32[128,256]{1,0:T(8,128)S(1)} %get-tuple-element.64, f32[128,16]{1,0:T(8,128)S(1)} %copy.59, f32[128,256]{1,0:T(8,128)S(1)} %get-tuple-element.63), kind=kLoop, calls=%fused_computation.3 | loop fusion | flops 1572864 | bytes 4481536 | tf_op jit(solution)/shard_map/mul | solution.py:257
  27.0 3.1 %shard_map.194 = (f32[16,256]{1,0:T(8,128)}, f32[16,256]{1,0:T(8,128)}) custom-call(f32[128,16,256]{2,1,0:T(8,128)} %get-tuple-element.65.da_ref, f32[128,16,256]{2,1,0:T(8,128)} %get-tuple-element.66.dr_ref), custom_call_target="tpu_custom_call" | custom-call | tf_op jit(solution)/shard_map/pallas_call | solution.py:134
  30.9 3.5 %collective-permute-start.4 = (f32[2,16,256]{2,1,0:T(8,128)S(1)}, f32[2,16,256]{2,1,0:T(8,128)S(1)}, u32[]{:S(2)}, u32[]{:S(2)}) collective-permute-start(f32[2,16,256]{2,1,0:T(8,128)S(1)} %pad_maximum_fusion.5), channel_id=1, source_target_pairs={{0,8},{8,16},{16,24},{24,32},{32,40},{40,48},{48,56},{56,64},{64,7... | collective-permute-start | bytes 98312 | tf_op jit(solution)/shard_map/ppermute | solution.py:17
  34.4 1.6 collective-permute-done.4
  36.7 5.5 %collective-permute-start.5 = (f32[2,16,256]{2,1,0:T(8,128)S(1)}, f32[2,16,256]{2,1,0:T(8,128)S(1)}, u32[]{:S(2)}, u32[]{:S(2)}) collective-permute-start(f32[2,16,256]{2,1,0:T(8,128)S(1)} %pad_maximum_fusion.6), channel_id=1, source_target_pairs={{0,16},{8,24},{16,32},{24,40},{32,48},{40,56},{48,64},{56,72},{64,... | collective-permute-start | bytes 98312 | tf_op jit(solution)/shard_map/ppermute | solution.py:17
  42.3 1.6 collective-permute-done.5
  43.9 7.8 %collective-permute-start.6 = (f32[2,16,256]{2,1,0:T(8,128)S(1)}, f32[2,16,256]{2,1,0:T(8,128)S(1)}, u32[]{:S(2)}, u32[]{:S(2)}) collective-permute-start(f32[2,16,256]{2,1,0:T(8,128)S(1)} %pad_maximum_fusion.7), channel_id=1, source_target_pairs={{0,32},{8,40},{16,48},{24,56},{32,64},{40,72},{48,80},{56,88},{64,... | collective-permute-start | bytes 98312 | tf_op jit(solution)/shard_map/ppermute | solution.py:17
  52.2 1.0 collective-permute-done.6
  53.2 5.6 %collective-permute-start.7 = (f32[2,16,256]{2,1,0:T(8,128)S(1)}, f32[2,16,256]{2,1,0:T(8,128)S(1)}, u32[]{:S(2)}, u32[]{:S(2)}) collective-permute-start(f32[2,16,256]{2,1,0:T(8,128)S(1)} %pad_maximum_fusion.8), channel_id=1, source_target_pairs={{0,64},{8,72},{16,80},{24,88},{32,96},{40,104},{48,112},{56,120},{... | collective-permute-start | bytes 98312 | tf_op jit(solution)/shard_map/ppermute | solution.py:17
  59.4 1.0 collective-permute-done.7
  60.4 13.9 %collective-permute-start.8 = (f32[2,16,256]{2,1,0:T(8,128)S(1)}, f32[2,16,256]{2,1,0:T(8,128)S(1)}, u32[]{:S(2)}, u32[]{:S(2)}) collective-permute-start(f32[2,16,256]{2,1,0:T(8,128)S(1)} %pad_maximum_fusion.9), channel_id=1, source_target_pairs={{0,128},{8,136},{16,144},{24,152},{32,160},{40,168},{48,176},{56,1... | collective-permute-start | bytes 98312 | tf_op jit(solution)/shard_map/ppermute | solution.py:17
  75.5 1.7 %broadcast_in_dim.20.om_ref = f32[128,16,256]{2,1,0:T(8,128)} broadcast(f32[128,16]{1,0:T(8,128)S(1)} %copy.60), dimensions={0,1} | broadcast | bytes 2105344 | tf_op jit(solution)/shard_map/broadcast_in_dim | solution.py:259
  77.2 6.2 %shard_map.193 = (f32[128,256]{1,0:T(8,128)}, f32[128,16,256]{2,1,0:T(8,128)}, f32[16,16,256]{2,1,0:T(8,128)}, f32[16,16,256]{2,1,0:T(8,128)}) custom-call(f32[128,16,256]{2,1,0:T(8,128)} %get-tuple-element.65.da_ref, f32[128,16,256]{2,1,0:T(8,128)} %get-tuple-element.66.dr_ref, f32[128,16,256]{2,1,0:T(8,128)} %broadcast_in_dim.20.om_ref, ...), custom_call_target="tpu_custom_call" | custom-call | tf_op jit(solution)/shard_map/pallas_call | solution.py:150
  83.5 2.2 %multiply_reduce_fusion = f32[128,256]{1,0:T(8,128)S(1)} fusion(f32[128,16,256]{2,1,0:T(8,128)} %get-tuple-element.10, f32[16,256]{1,0:T(8,128)S(1)} %fusion.50), kind=kLoop, calls=%fused_computation.2 | loop fusion | flops 1015808 | bytes 2244608 | tf_op jit(solution)/shard_map/reduce_sum | solution.py:267
  85.6 2.4 %convolution_convert_fusion.1 = bf16[128,2048]{1,0:T(8,128)(2,1)S(1)} fusion(bf16[256,2048]{1,0:T(8,128)(2,1)} %param.29, bf16[128,256]{1,0:T(8,128)(2,1)S(1)} %multiply_convert_fusion.1, bf16[2048,256]{1,0:T(8,128)(2,1)} %param.21, bf16[128,2048]{1,0:T(8,128)(2,1)S(1)} %copy-done.1, f32[2048]{0:T(1024)} %param.19, f32[128]{0:T(128)} %copy-done.17, ...), kind=kOutput, calls=%fused_computation.1 | convolution fusion | flops 270139392 | bytes 3483136 | tf_op jit(solution)/shard_map/dot_general | solution.py:294
  89.0 0.9 convolution_convert_fusion.4
  89.9 1.0 convert_add_fusion.1
  91.0 0.9 collective-permute-start.10
  91.9 1.0 add_convert_fusion
  92.9 4.0 %collective-permute-done.10 = bf16[2,16,2048]{2,1,0:T(8,128)(2,1)S(1)} collective-permute-done((bf16[2,16,2048]{2,1,0:T(8,128)(2,1)S(1)}, bf16[2,16,2048]{2,1,0:T(8,128)(2,1)S(1)}, u32[]{:S(2)}, u32[]{:S(2)}) %collective-permute-start.10) | collective-permute-done | bytes 131104 | tf_op jit(solution)/shard_map/ppermute | solution.py:22
  97.0 1.5 collective-permute-start.11
  98.6 4.2 %collective-permute-done.11 = bf16[16,2048]{1,0:T(8,128)(2,1)S(1)} collective-permute-done((bf16[16,2048]{1,0:T(8,128)(2,1)S(1)}, bf16[16,2048]{1,0:T(8,128)(2,1)S(1)}, u32[]{:S(2)}, u32[]{:S(2)}) %collective-permute-start.11) | collective-permute-done | bytes 65568 | tf_op jit(solution)/shard_map/ppermute | solution.py:22
  103.1 1.5 collective-permute-start.12
  104.9 4.1 %collective-permute-done.12 = bf16[16,2048]{1,0:T(8,128)(2,1)S(1)} collective-permute-done((bf16[16,2048]{1,0:T(8,128)(2,1)S(1)}, bf16[16,2048]{1,0:T(8,128)(2,1)S(1)}, u32[]{:S(2)}, u32[]{:S(2)}) %collective-permute-start.12) | collective-permute-done | bytes 65568 | tf_op jit(solution)/shard_map/ppermute | solution.py:22
  109.1 0.9 collective-permute-start.13
  110.0 2.0 %collective-permute-done.19 = bf16[16,19,256]{2,1,0:T(8,128)(2,1)S(1)} collective-permute-done((bf16[16,19,256]{2,1,0:T(8,128)(2,1)S(1)}, bf16[16,19,256]{2,1,0:T(8,128)(2,1)S(1)}, u32[]{:S(2)}, u32[]{:S(2)}) %collective-permute-start.19) | collective-permute-done | bytes 155680 | tf_op jit(solution)/shard_map/ppermute | solution.py:22
  112.2 1.9 %collective-permute-done.13 = bf16[2,16,2048]{2,1,0:T(8,128)(2,1)S(1)} collective-permute-done((bf16[2,16,2048]{2,1,0:T(8,128)(2,1)S(1)}, bf16[2,16,2048]{2,1,0:T(8,128)(2,1)S(1)}, u32[]{:S(2)}, u32[]{:S(2)}) %collective-permute-start.13) | collective-permute-done | bytes 131104 | tf_op jit(solution)/shard_map/ppermute | solution.py:22
  114.3 3.6 %collective-permute-done.20 = bf16[16,19,256]{2,1,0:T(8,128)(2,1)S(1)} collective-permute-done((bf16[16,19,256]{2,1,0:T(8,128)(2,1)S(1)}, bf16[16,19,256]{2,1,0:T(8,128)(2,1)S(1)}, u32[]{:S(2)}, u32[]{:S(2)}) %collective-permute-start.20) | collective-permute-done | bytes 155680 | tf_op jit(solution)/shard_map/ppermute | solution.py:22
  118.2 16.8 %collective-permute-done.21 = bf16[16,19,256]{2,1,0:T(8,128)(2,1)S(1)} collective-permute-done((bf16[16,19,256]{2,1,0:T(8,128)(2,1)S(1)}, bf16[16,19,256]{2,1,0:T(8,128)(2,1)S(1)}, u32[]{:S(2)}, u32[]{:S(2)}) %collective-permute-start.21) | collective-permute-done | bytes 155680 | tf_op jit(solution)/shard_map/ppermute | solution.py:22
  135.1 1.0 select_bitcast_fusion.1
  136.2 1.1 fusion.70
  137.3 2.4 %convolution_convert_fusion = bf16[128,2048]{1,0:T(8,128)(2,1)S(1)} fusion(bf16[512,2048]{1,0:T(8,128)(2,1)S(1)} %copy-done, bf16[128,2048]{1,0:T(8,128)(2,1)S(1)} %bitcast.123, bf16[2048,512]{1,0:T(8,128)(2,1)} %param.32, f32[128,512]{1,0:T(8,128)} %fusion.70), kind=kOutput, calls=%fused_computation | convolution fusion | flops 537526272 | bytes 5505024 | tf_op jit(solution)/shard_map/dot_general | solution.py:306
  140.1 4.7 %collective-permute-done.22 = bf16[16,19,256]{2,1,0:T(8,128)(2,1)} collective-permute-done((bf16[16,19,256]{2,1,0:T(8,128)(2,1)S(1)}, bf16[16,19,256]{2,1,0:T(8,128)(2,1)}, u32[]{:S(2)}, u32[]{:S(2)}) %collective-permute-start.22) | collective-permute-done | bytes 155680 | tf_op jit(solution)/shard_map/ppermute | solution.py:22
  144.8 1.0 add.341
  146.2 4.7 %collective-permute-done.16 = bf16[2,16,2048]{2,1,0:T(8,128)(2,1)S(1)} collective-permute-done((bf16[2,16,2048]{2,1,0:T(8,128)(2,1)S(1)}, bf16[2,16,2048]{2,1,0:T(8,128)(2,1)S(1)}, u32[]{:S(2)}, u32[]{:S(2)}) %collective-permute-start.16) | collective-permute-done | bytes 131104 | tf_op jit(solution)/shard_map/ppermute | solution.py:22
  151.0 1.1 collective-permute-start.17
  153.6 3.3 %collective-permute-done.17 = bf16[16,2048]{1,0:T(8,128)(2,1)S(1)} collective-permute-done((bf16[16,2048]{1,0:T(8,128)(2,1)S(1)}, bf16[16,2048]{1,0:T(8,128)(2,1)S(1)}, u32[]{:S(2)}, u32[]{:S(2)}) %collective-permute-start.17) | collective-permute-done | bytes 65568 | tf_op jit(solution)/shard_map/ppermute | solution.py:22
  (128 shorter events, 11.7 us)
Async XLA Ops:
  0.6 136.7 %copy-start = (bf16[512,2048]{1,0:T(8,128)(2,1)S(1)}, bf16[512,2048]{1,0:T(8,128)(2,1)}, u32[]{:S(2)}) copy-start(bf16[512,2048]{1,0:T(8,128)(2,1)} %param.33) | copy-start | bytes 6291460
  0.6 10.9 %copy-start.3 = (bf16[2048,256]{1,0:T(8,128)(2,1)S(1)}, bf16[2048,256]{1,0:T(8,128)(2,1)}, u32[]{:S(2)}) copy-start(bf16[2048,256]{1,0:T(8,128)(2,1)} %param.20) | copy-start | bytes 3145732
  0.7 10.9 %copy-start.8 = (f32[2048]{0:T(1024)S(1)}, f32[2048]{0:T(1024)}, u32[]{:S(2)}) copy-start(f32[2048]{0:T(1024)} %param.19) | copy-start | bytes 24580
  0.7 11.2 %copy-start.14 = (f32[256]{0:T(256)S(1)}, f32[256]{0:T(256)}, u32[]{:S(2)}) copy-start(f32[256]{0:T(256)} %param.23) | copy-start | bytes 3076
  0.7 11.4 %copy-start.6 = (bf16[256,160]{0,1:T(8,128)(2,1)S(1)}, bf16[256,160]{0,1:T(8,128)(2,1)}, u32[]{:S(2)}) copy-start(bf16[256,160]{0,1:T(8,128)(2,1)} %param.24) | copy-start | bytes 245764
  0.7 11.6 %copy-start.11 = (f32[16,256]{1,0:T(8,128)S(1)}, f32[16,256]{1,0:T(8,128)}, u32[]{:S(2)}) copy-start(f32[16,256]{1,0:T(8,128)} %param.27) | copy-start | bytes 49156
  1.6 9.8 %collective-permute-start = (bf16[3,2048]{1,0:T(4,128)(2,1)S(1)}, bf16[3,2048]{1,0:T(4,128)(2,1)S(1)}, u32[]{:S(2)}, u32[]{:S(2)}) collective-permute-start(bf16[3,2048]{1,0:T(4,128)(2,1)S(1)} %slice.69), channel_id=1, source_target_pairs={{0,8},{8,16},{16,24},{24,32},{32,40},{40,48},{48,56},{56,64},{64,7... | collective-permute-start | bytes 36872 | tf_op jit(solution)/shard_map/ppermute | solution.py:17
  6.5 4.9 %copy-start.17 = (f32[128]{0:T(128)}, f32[128]{0:T(128)S(1)}, u32[]{:S(2)}) copy-start(f32[128]{0:T(128)S(1)} %add_rsqrt_fusion.2) | copy-start | bytes 1540
  8.6 15.8 %copy-start.13 = (s32[16]{0:T(128)}, s32[16]{0:T(128)S(1)}, u32[]{:S(2)}) copy-start(s32[16]{0:T(128)S(1)} %get-tuple-element.59) | copy-start | bytes 196
  8.7 50.2 %copy-start.18 = (s32[128]{0:T(128)}, s32[128]{0:T(128)S(1)}, u32[]{:S(2)}) copy-start(s32[128]{0:T(128)S(1)} %convert_reduce_fusion) | copy-start | bytes 1540
  9.6 14.8 %copy-start.7 = (bf16[128,256]{1,0:T(8,128)(2,1)S(1)}, bf16[128,256]{1,0:T(8,128)(2,1)}, u32[]{:S(2)}) copy-start(bf16[128,256]{1,0:T(8,128)(2,1)} %param.25) | copy-start | bytes 196612
  9.6 14.8 %copy-start.15 = (f32[256]{0:T(256)S(1)}, f32[256]{0:T(256)}, u32[]{:S(2)}) copy-start(f32[256]{0:T(256)} %param.26) | copy-start | bytes 3076
  11.9 15.2 %copy-start.12 = (bf16[3,256]{1,0:T(4,128)(2,1)}, bf16[3,256]{1,0:T(4,128)(2,1)S(1)}, u32[]{:S(2)}) copy-start(bf16[3,256]{1,0:T(4,128)(2,1)S(1)} %convolution_convert_fusion.6) | copy-start | bytes 4612
  12.2 1.4 collective-permute-start.1
  13.6 4.6 %collective-permute-start.2 = (f32[128,160]{0,1:T(8,128)S(1)}, f32[128,160]{0,1:T(8,128)S(1)}, u32[]{:S(2)}, u32[]{:S(2)}) collective-permute-start(f32[128,160]{0,1:T(8,128)S(1)} %add.293), channel_id=1, source_target_pairs={{0,2},{1,3},{2,0},{3,1},{4,6},{5,7},{6,4},{7,5},{8,10},{9,11},{10,... | collective-permute-start | bytes 245768 | tf_op jit(solution)/shard_map/ppermute | solution.py:22
  18.2 6.0 %collective-permute-start.3 = (f32[128,160]{0,1:T(8,128)S(1)}, f32[128,160]{0,1:T(8,128)S(1)}, u32[]{:S(2)}, u32[]{:S(2)}) collective-permute-start(f32[128,160]{0,1:T(8,128)S(1)} %add.294), channel_id=1, source_target_pairs={{0,4},{1,5},{2,6},{3,7},{4,0},{5,1},{6,2},{7,3},{8,12},{9,13},{10,... | collective-permute-start | bytes 245768 | tf_op jit(solution)/shard_map/ppermute | solution.py:22
  30.9 5.1 %collective-permute-start.4 = (f32[2,16,256]{2,1,0:T(8,128)S(1)}, f32[2,16,256]{2,1,0:T(8,128)S(1)}, u32[]{:S(2)}, u32[]{:S(2)}) collective-permute-start(f32[2,16,256]{2,1,0:T(8,128)S(1)} %pad_maximum_fusion.5), channel_id=1, source_target_pairs={{0,8},{8,16},{16,24},{24,32},{32,40},{40,48},{48,56},{56,64},{64,7... | collective-permute-start | bytes 98312 | tf_op jit(solution)/shard_map/ppermute | solution.py:17
  36.7 7.1 %collective-permute-start.5 = (f32[2,16,256]{2,1,0:T(8,128)S(1)}, f32[2,16,256]{2,1,0:T(8,128)S(1)}, u32[]{:S(2)}, u32[]{:S(2)}) collective-permute-start(f32[2,16,256]{2,1,0:T(8,128)S(1)} %pad_maximum_fusion.6), channel_id=1, source_target_pairs={{0,16},{8,24},{16,32},{24,40},{32,48},{40,56},{48,64},{56,72},{64,... | collective-permute-start | bytes 98312 | tf_op jit(solution)/shard_map/ppermute | solution.py:17
  43.9 9.3 %collective-permute-start.6 = (f32[2,16,256]{2,1,0:T(8,128)S(1)}, f32[2,16,256]{2,1,0:T(8,128)S(1)}, u32[]{:S(2)}, u32[]{:S(2)}) collective-permute-start(f32[2,16,256]{2,1,0:T(8,128)S(1)} %pad_maximum_fusion.7), channel_id=1, source_target_pairs={{0,32},{8,40},{16,48},{24,56},{32,64},{40,72},{48,80},{56,88},{64,... | collective-permute-start | bytes 98312 | tf_op jit(solution)/shard_map/ppermute | solution.py:17
  53.2 7.2 %collective-permute-start.7 = (f32[2,16,256]{2,1,0:T(8,128)S(1)}, f32[2,16,256]{2,1,0:T(8,128)S(1)}, u32[]{:S(2)}, u32[]{:S(2)}) collective-permute-start(f32[2,16,256]{2,1,0:T(8,128)S(1)} %pad_maximum_fusion.8), channel_id=1, source_target_pairs={{0,64},{8,72},{16,80},{24,88},{32,96},{40,104},{48,112},{56,120},{... | collective-permute-start | bytes 98312 | tf_op jit(solution)/shard_map/ppermute | solution.py:17
  60.4 23.0 %collective-permute-start.8 = (f32[2,16,256]{2,1,0:T(8,128)S(1)}, f32[2,16,256]{2,1,0:T(8,128)S(1)}, u32[]{:S(2)}, u32[]{:S(2)}) collective-permute-start(f32[2,16,256]{2,1,0:T(8,128)S(1)} %pad_maximum_fusion.9), channel_id=1, source_target_pairs={{0,128},{8,136},{16,144},{24,152},{32,160},{40,168},{48,176},{56,1... | collective-permute-start | bytes 98312 | tf_op jit(solution)/shard_map/ppermute | solution.py:17
  83.4 2.2 %copy-start.1 = (bf16[128,2048]{1,0:T(8,128)(2,1)S(1)}, bf16[128,2048]{1,0:T(8,128)(2,1)}, u32[]{:S(2)}) copy-start(bf16[128,2048]{1,0:T(8,128)(2,1)} %param.18) | copy-start | bytes 1572868
  83.4 2.2 %copy-start.5 = (f32[128,256]{1,0:T(8,128)S(1)}, f32[128,256]{1,0:T(8,128)}, u32[]{:S(2)}) copy-start(f32[128,256]{1,0:T(8,128)} %get-tuple-element.9) | copy-start | bytes 393220
  88.1 3.8 %copy-start.4 = (f32[16,16,256]{2,1,0:T(8,128)S(1)}, f32[16,16,256]{2,1,0:T(8,128)}, u32[]{:S(2)}) copy-start(f32[16,16,256]{2,1,0:T(8,128)} %get-tuple-element.13) | copy-start | bytes 786436
  88.1 14.9 %copy-start.9 = (f32[2048]{0:T(1024)S(1)}, f32[2048]{0:T(1024)}, u32[]{:S(2)}) copy-start(f32[2048]{0:T(1024)} %param.30) | copy-start | bytes 24580
  88.2 1.8 %collective-permute-start.9 = (bf16[2,2,16,2048]{3,2,0,1:T(8,128)(2,1)S(1)}, bf16[2,2,16,2048]{3,2,0,1:T(8,128)(2,1)}, u32[]{:S(2)}, u32[]{:S(2)}) collective-permute-start(bf16[2,2,16,2048]{3,2,0,1:T(8,128)(2,1)S(1)} %bitcast.126), channel_id=1, source_target_pairs={{0,1},{1,0},{2,3},{3,2},{4,5},{5,4},{6,7},{7,6},{8,9},{9,8},{10,11... | collective-permute-start | bytes 786440 | tf_op jit(solution)/shard_map/ppermute | solution.py:22
  89.9 19.0 %copy-start.10 = (f32[2048]{0:T(1024)S(1)}, f32[2048]{0:T(1024)}, u32[]{:S(2)}) copy-start(f32[2048]{0:T(1024)} %param.30) | copy-start | bytes 24580
  91.0 5.9 %collective-permute-start.10 = (bf16[2,16,2048]{2,1,0:T(8,128)(2,1)S(1)}, bf16[2,16,2048]{2,1,0:T(8,128)(2,1)S(1)}, u32[]{:S(2)}, u32[]{:S(2)}) collective-permute-start(bf16[2,16,2048]{2,1,0:T(8,128)(2,1)S(1)} %fusion.15), channel_id=1, source_target_pairs={{0,2},{1,3},{2,0},{3,1},{4,6},{5,7},{6,4},{7,5},{8,10},{9,11},{10,... | collective-permute-start | bytes 393224 | tf_op jit(solution)/shard_map/ppermute | solution.py:22
  97.0 5.9 %collective-permute-start.11 = (bf16[16,2048]{1,0:T(8,128)(2,1)S(1)}, bf16[16,2048]{1,0:T(8,128)(2,1)S(1)}, u32[]{:S(2)}, u32[]{:S(2)}) collective-permute-start(bf16[16,2048]{1,0:T(8,128)(2,1)S(1)} %fusion.31), channel_id=1, source_target_pairs={{0,4},{1,5},{2,6},{3,7},{4,0},{5,1},{6,2},{7,3},{8,12},{9,13},{10,... | collective-permute-start | bytes 196616 | tf_op jit(solution)/shard_map/ppermute | solution.py:22
  98.5 6.2 %collective-permute-start.18 = (bf16[16,19,256]{2,1,0:T(8,128)(2,1)S(1)}, bf16[16,19,256]{2,1,0:T(8,128)(2,1)S(1)}, u32[]{:S(2)}, u32[]{:S(2)}) collective-permute-start(bf16[16,19,256]{2,1,0:T(8,128)(2,1)S(1)} %pad_maximum_fusion.2), channel_id=1, source_target_pairs={{0,8},{8,0},{16,24},{24,16},{32,40},{40,32},{48,56},{56,48},{64,72... | collective-permute-start | bytes 466952 | tf_op jit(solution)/shard_map/ppermute | solution.py:22
  103.1 5.9 %collective-permute-start.12 = (bf16[16,2048]{1,0:T(8,128)(2,1)S(1)}, bf16[16,2048]{1,0:T(8,128)(2,1)S(1)}, u32[]{:S(2)}, u32[]{:S(2)}) collective-permute-start(bf16[16,2048]{1,0:T(8,128)(2,1)S(1)} %multiply_convert_fusion), channel_id=1, source_target_pairs={{0,4},{1,5},{2,6},{3,7},{4,0},{5,1},{6,2},{7,3},{8,12},{9,13},{10,... | collective-permute-start | bytes 196616 | tf_op jit(solution)/shard_map/ppermute | solution.py:22
  104.8 7.3 %collective-permute-start.19 = (bf16[16,19,256]{2,1,0:T(8,128)(2,1)S(1)}, bf16[16,19,256]{2,1,0:T(8,128)(2,1)S(1)}, u32[]{:S(2)}, u32[]{:S(2)}) collective-permute-start(bf16[16,19,256]{2,1,0:T(8,128)(2,1)S(1)} %fusion.64), channel_id=1, source_target_pairs={{0,16},{8,24},{16,0},{24,8},{32,48},{40,56},{48,32},{56,40},{64,80... | collective-permute-start | bytes 466952 | tf_op jit(solution)/shard_map/ppermute | solution.py:22
  109.1 5.1 %collective-permute-start.13 = (bf16[2,16,2048]{2,1,0:T(8,128)(2,1)S(1)}, bf16[2,16,2048]{2,1,0:T(8,128)(2,1)S(1)}, u32[]{:S(2)}, u32[]{:S(2)}) collective-permute-start(bf16[2,16,2048]{2,1,0:T(8,128)(2,1)S(1)} %pad_maximum_fusion.4), channel_id=1, source_target_pairs={{0,2},{1,3},{2,0},{3,1},{4,6},{5,7},{6,4},{7,5},{8,10},{9,11},{10,... | collective-permute-start | bytes 393224 | tf_op jit(solution)/shard_map/ppermute | solution.py:22
  112.1 5.8 %collective-permute-start.20 = (bf16[16,19,256]{2,1,0:T(8,128)(2,1)S(1)}, bf16[16,19,256]{2,1,0:T(8,128)(2,1)S(1)}, u32[]{:S(2)}, u32[]{:S(2)}) collective-permute-start(bf16[16,19,256]{2,1,0:T(8,128)(2,1)S(1)} %add.338), channel_id=1, source_target_pairs={{0,32},{8,40},{16,48},{24,56},{32,0},{40,8},{48,16},{56,24},{64,96... | collective-permute-start | bytes 466952 | tf_op jit(solution)/shard_map/ppermute | solution.py:22
  114.2 20.9 %collective-permute-start.14 = (bf16[2,2,16,2048]{3,2,1,0:T(8,128)(2,1)S(1)}, bf16[2,2,16,2048]{3,2,1,0:T(8,128)(2,1)}, u32[]{:S(2)}, u32[]{:S(2)}) collective-permute-start(bf16[2,2,16,2048]{3,2,1,0:T(8,128)(2,1)S(1)} %pad_maximum_fusion.1), channel_id=1, source_target_pairs={{0,1},{1,0},{2,3},{3,2},{4,5},{5,4},{6,7},{7,6},{8,9},{9,8},{10,11... | collective-permute-start | bytes 786440 | tf_op jit(solution)/shard_map/ppermute | solution.py:22
  117.9 17.1 %collective-permute-start.21 = (bf16[16,19,256]{2,1,0:T(8,128)(2,1)S(1)}, bf16[16,19,256]{2,1,0:T(8,128)(2,1)S(1)}, u32[]{:S(2)}, u32[]{:S(2)}) collective-permute-start(bf16[16,19,256]{2,1,0:T(8,128)(2,1)S(1)} %add.339), channel_id=1, source_target_pairs={{0,64},{8,72},{16,80},{24,88},{32,96},{40,104},{48,112},{56,120},{... | collective-permute-start | bytes 466952 | tf_op jit(solution)/shard_map/ppermute | solution.py:22
  118.2 18.0 %copy-start.2 = (bf16[2048,512]{1,0:T(8,128)(2,1)S(1)}, bf16[2048,512]{1,0:T(8,128)(2,1)}, u32[]{:S(2)}) copy-start(bf16[2048,512]{1,0:T(8,128)(2,1)} %param.31) | copy-start | bytes 6291460
  135.0 9.8 %collective-permute-start.22 = (bf16[16,19,256]{2,1,0:T(8,128)(2,1)S(1)}, bf16[16,19,256]{2,1,0:T(8,128)(2,1)}, u32[]{:S(2)}, u32[]{:S(2)}) collective-permute-start(bf16[16,19,256]{2,1,0:T(8,128)(2,1)S(1)} %add.340), channel_id=1, source_target_pairs={{0,128},{8,136},{16,144},{24,152},{32,160},{40,168},{48,176},{56,1... | collective-permute-start | bytes 466952 | tf_op jit(solution)/shard_map/ppermute | solution.py:22
  137.3 2.6 %copy-start.19 = (s32[128]{0:T(128)S(1)}, s32[128]{0:T(128)}, u32[]{:S(2)}) copy-start(s32[128]{0:T(128)} %copy-done.18) | copy-start | bytes 1540
  139.8 6.2 %copy-start.16 = (s32[4]{0:T(128)S(1)}, s32[4]{0:T(128)}, u32[]{:S(2)}) copy-start(s32[4]{0:T(128)} %param.35) | copy-start | bytes 52
  139.9 5.9 %collective-permute-start.15 = (bf16[2,2,16,2048]{3,2,0,1:T(8,128)(2,1)S(1)}, bf16[2,2,16,2048]{3,2,0,1:T(8,128)(2,1)S(1)}, u32[]{:S(2)}, u32[]{:S(2)}) collective-permute-start(bf16[2,2,16,2048]{3,2,0,1:T(8,128)(2,1)S(1)} %bitcast.127), channel_id=1, source_target_pairs={{0,1},{1,0},{2,3},{3,2},{4,5},{5,4},{6,7},{7,6},{8,9},{9,8},{10,11... | collective-permute-start | bytes 786440 | tf_op jit(solution)/shard_map/ppermute | solution.py:22
  145.9 5.1 %collective-permute-start.16 = (bf16[2,16,2048]{2,1,0:T(8,128)(2,1)S(1)}, bf16[2,16,2048]{2,1,0:T(8,128)(2,1)S(1)}, u32[]{:S(2)}, u32[]{:S(2)}) collective-permute-start(bf16[2,16,2048]{2,1,0:T(8,128)(2,1)S(1)} %fusion.16), channel_id=1, source_target_pairs={{0,2},{1,3},{2,0},{3,1},{4,6},{5,7},{6,4},{7,5},{8,10},{9,11},{10,... | collective-permute-start | bytes 393224 | tf_op jit(solution)/shard_map/ppermute | solution.py:22
  151.0 5.9 %collective-permute-start.17 = (bf16[16,2048]{1,0:T(8,128)(2,1)S(1)}, bf16[16,2048]{1,0:T(8,128)(2,1)S(1)}, u32[]{:S(2)}, u32[]{:S(2)}) collective-permute-start(bf16[16,2048]{1,0:T(8,128)(2,1)S(1)} %fusion.32), channel_id=1, source_target_pairs={{0,4},{1,5},{2,6},{3,7},{4,0},{5,1},{6,2},{7,3},{8,12},{9,13},{10,... | collective-permute-start | bytes 196616 | tf_op jit(solution)/shard_map/ppermute | solution.py:22

commit v5 on v3

--- a/solution.py
+++ b/solution.py
@@ -152,23 +152,21 @@
 
 def entering_state(a_blk, s_blk, axis):
     me = lax.axis_index(axis)
-    devices = lax.axis_size(axis)
-    inc_a, inc_s = a_blk, s_blk
+    tot_a, tot_s = a_blk, s_blk
     exc_a, exc_s = jnp.ones_like(a_blk), jnp.zeros_like(s_blk)
-    shift = 1
-    while shift < devices:
-        got = from_behind(jnp.stack([inc_a, inc_s]), axis, shift)
+    for bit in bits_of(lax.axis_size(axis)):
+        got = swap(jnp.stack([tot_a, tot_s]), axis, bit)
         got_a, got_s = got[0], got[1]
-        has = me >= shift
-        new_exc_a = got_a * exc_a
-        new_exc_s = exc_a * got_s + exc_s
-        new_inc_a = got_a * inc_a
-        new_inc_s = inc_a * got_s + inc_s
-        exc_a = jnp.where(has, new_exc_a, exc_a)
-        exc_s = jnp.where(has, new_exc_s, exc_s)
-        inc_a = jnp.where(has, new_inc_a, inc_a)
-        inc_s = jnp.where(has, new_inc_s, inc_s)
-        shift *= 2
+        upper = ((me // bit) % 2) == 1
+        low_a = jnp.where(upper, got_a, tot_a)
+        low_s = jnp.where(upper, got_s, tot_s)
+        high_a = jnp.where(upper, tot_a, got_a)
+        high_s = jnp.where(upper, tot_s, got_s)
+        exc_a, exc_s = (
+            jnp.where(upper, got_a * exc_a, exc_a),
+            jnp.where(upper, exc_a * got_s + exc_s, exc_s),
+        )
+        tot_a, tot_s = low_a * high_a, high_a * low_s + high_s
     return exc_s
 
 
@@ -216,7 +214,12 @@
     starts_here = jnp.any(places[:, None] == prompt_start[None, :], axis=1)
     ends_here = jnp.any(places[:, None] == prompt_end[None, :] - 1, axis=1)
     is_live = prompt_of < prompts
-    behind = from_behind(tokens[block_len - edge_len :], "seq", 1)
+    seq_count = lax.axis_size("seq")
+    behind = lax.ppermute(
+        tokens[block_len - edge_len :],
+        "seq",
+        [(i, (i + 1) % seq_count) for i in range(seq_count)],
+    )
     normed = rms_norm(tokens.astype(jnp.float32), norm_gain).astype(jnp.bfloat16)
     normed_behind = rms_norm(behind.astype(jnp.float32), norm_gain).astype(jnp.bfloat16)
     x_branch = jnp.dot(normed, w_x, preferred_element_type=jnp.float32).astype(jnp.bfloat16)

time: 158 us -> 135 us (0.85)
  the two profiles are of different devices: /device:TPU:6 before, /device:TPU:16 now
where the time goes in v5:
time: 135 us
  starting transfers between devices  54.4 us (40%)
  waiting for transfers between devices  43.5 us (32%)
  other arithmetic  12.6 us (9%)
  matrix products  8.99 us (7%)
  Pallas kernels  8.56 us (6%)
  local copies, waits for them, and re-layouts  5.37 us (4%)
    ppermute x22, starting transfers between devices, swap(): return lax.ppermute(x, axis, [(i, i ^ bit) for i in range(devices)])  53.1 us
    ppermute x22, waiting for transfers between devices, swap(): return lax.ppermute(x, axis, [(i, i ^ bit) for i in range(devices)])  43.5 us
    pallas_call x1, Pallas kernels, block_output(): pl.pallas_call(block_output_kernel, out_shape=(jax.ShapeDtypeStruct((t, e...  5.41 us
    pallas_call x1, Pallas kernels, block_summary(): pl.pallas_call(block_summary_kernel, out_shape=(jax.ShapeDtypeStruct((n,...  3.14 us
  transfers between devices with their start and end apart: 23, of which 17 were waited for; matrix products, arithmetic and copies ran while one was open for 11% of the time, Pallas kernels for 0%

profile of v5, /device:TPU:16, one launch (start us, length us, event | category | flops | bytes accessed | tf_op | source)
XLA Modules:
  0.0 134.8 jit_solution(6235272935736984089)
XLA Ops:
  0.7 0.9 slice.69
  1.6 1.4 %collective-permute-start = (bf16[3,2048]{1,0:T(4,128)(2,1)S(1)}, bf16[3,2048]{1,0:T(4,128)(2,1)S(1)}, u32[]{:S(2)}, u32[]{:S(2)}) collective-permute-start(bf16[3,2048]{1,0:T(4,128)(2,1)S(1)} %slice.69), channel_id=1, source_target_pairs={{0,8},{8,16},{16,24},{24,32},{32,40},{40,48},{48,56},{56,64},{64,7... | collective-permute-start | bytes 36872 | tf_op jit(solution)/shard_map/ppermute | solution.py:218
  3.0 1.2 fusion.2
  4.2 0.8 fusion.68
  6.8 1.8 %convolution_convert_fusion.3 = bf16[128,256]{1,0:T(8,128)(2,1)S(1)} fusion(bf16[2048,256]{1,0:T(8,128)(2,1)} %param.20, bf16[128,2048]{1,0:T(8,128)(2,1)} %param.18, f32[2048]{0:T(1024)} %param.19, f32[128]{0:T(128)S(1)} %add_rsqrt_fusion.2), kind=kOutput, calls=%fused_computation.10 | convolution fusion | flops 135299072 | bytes 1647104 | tf_op jit(solution)/shard_map/dot_general | solution.py:225
  9.6 1.2 collective-permute-done.1
  10.8 1.6 %collective-permute-start.2 = (f32[128,160]{0,1:T(8,128)S(1)}, f32[128,160]{0,1:T(8,128)S(1)}, u32[]{:S(2)}, u32[]{:S(2)}) collective-permute-start(f32[128,160]{0,1:T(8,128)S(1)} %add.303), channel_id=1, source_target_pairs={{0,2},{1,3},{2,0},{3,1},{4,6},{5,7},{6,4},{7,5},{8,10},{9,11},{10,... | collective-permute-start | bytes 245768 | tf_op jit(solution)/shard_map/ppermute | solution.py:22
  12.5 2.9 %collective-permute-done.2 = f32[128,160]{0,1:T(8,128)S(1)} collective-permute-done((f32[128,160]{0,1:T(8,128)S(1)}, f32[128,160]{0,1:T(8,128)S(1)}, u32[]{:S(2)}, u32[]{:S(2)}) %collective-permute-start.2) | collective-permute-done | bytes 81952 | tf_op jit(solution)/shard_map/ppermute | solution.py:22
  15.4 3.1 %collective-permute-start.3 = (f32[128,160]{0,1:T(8,128)S(1)}, f32[128,160]{0,1:T(8,128)S(1)}, u32[]{:S(2)}, u32[]{:S(2)}) collective-permute-start(f32[128,160]{0,1:T(8,128)S(1)} %add.304), channel_id=1, source_target_pairs={{0,4},{1,5},{2,6},{3,7},{4,0},{5,1},{6,2},{7,3},{8,12},{9,13},{10,... | collective-permute-start | bytes 245768 | tf_op jit(solution)/shard_map/ppermute | solution.py:22
  18.5 2.9 %collective-permute-done.3 = f32[128,160]{0,1:T(8,128)S(1)} collective-permute-done((f32[128,160]{0,1:T(8,128)S(1)}, f32[128,160]{0,1:T(8,128)S(1)}, u32[]{:S(2)}, u32[]{:S(2)}) %collective-permute-start.3) | collective-permute-done | bytes 81952 | tf_op jit(solution)/shard_map/ppermute | solution.py:22
  21.9 2.4 %exponential_multiply_fusion = (f32[128,16,256]{2,1,0:T(8,128)}, f32[128,16,256]{2,1,0:T(8,128)}) fusion(f32[128]{0:T(128)S(1)} %convert_subtract_fusion, f32[16,256]{1,0:T(8,128)S(1)} %exponential_negate_fusion, f32[128,256]{1,0:T(8,128)S(1)} %get-tuple-element.60, f32[128,16]{1,0:T(8,128)S(1)} %copy.59, f32[128,256]{1,0:T(8,128)S(1)} %get-tuple-element.59), kind=kLoop, calls=%fused_computation.2 | loop fusion | flops 1572864 | bytes 4481536 | tf_op jit(solution)/shard_map/mul | solution.py:249
  24.2 3.1 %shard_map.193 = (f32[16,256]{1,0:T(8,128)}, f32[16,256]{1,0:T(8,128)}) custom-call(f32[128,16,256]{2,1,0:T(8,128)} %get-tuple-element.61.da_ref, f32[128,16,256]{2,1,0:T(8,128)} %get-tuple-element.62.dr_ref), custom_call_target="tpu_custom_call" | custom-call | tf_op jit(solution)/shard_map/pallas_call | solution.py:125
  27.4 0.7 pad_maximum_fusion.5
  28.1 1.6 %collective-permute-start.4 = (f32[2,16,256]{2,1,0:T(8,128)S(1)}, f32[2,16,256]{2,1,0:T(8,128)S(1)}, u32[]{:S(2)}, u32[]{:S(2)}) collective-permute-start(f32[2,16,256]{2,1,0:T(8,128)S(1)} %pad_maximum_fusion.5), channel_id=1, source_target_pairs={{0,8},{8,0},{16,24},{24,16},{32,40},{40,32},{48,56},{56,48},{64,72... | collective-permute-start | bytes 98312 | tf_op jit(solution)/shard_map/ppermute | solution.py:22
  29.7 2.3 %collective-permute-done.4 = f32[2,16,256]{2,1,0:T(8,128)S(1)} collective-permute-done((f32[2,16,256]{2,1,0:T(8,128)S(1)}, f32[2,16,256]{2,1,0:T(8,128)S(1)}, u32[]{:S(2)}, u32[]{:S(2)}) %collective-permute-start.4) | collective-permute-done | bytes 32800 | tf_op jit(solution)/shard_map/ppermute | solution.py:22
  32.0 0.7 select_multiply_fusion.2
  32.8 3.7 %collective-permute-start.5 = (f32[2,16,256]{2,1,0:T(8,128)S(1)}, f32[2,16,256]{2,1,0:T(8,128)S(1)}, u32[]{:S(2)}, u32[]{:S(2)}) collective-permute-start(f32[2,16,256]{2,1,0:T(8,128)S(1)} %pad_maximum_fusion.6), channel_id=1, source_target_pairs={{0,16},{8,24},{16,0},{24,8},{32,48},{40,56},{48,32},{56,40},{64,80... | collective-permute-start | bytes 98312 | tf_op jit(solution)/shard_map/ppermute | solution.py:22
  36.5 1.9 %collective-permute-done.5 = f32[2,16,256]{2,1,0:T(8,128)S(1)} collective-permute-done((f32[2,16,256]{2,1,0:T(8,128)S(1)}, f32[2,16,256]{2,1,0:T(8,128)S(1)}, u32[]{:S(2)}, u32[]{:S(2)}) %collective-permute-start.5) | collective-permute-done | bytes 32800 | tf_op jit(solution)/shard_map/ppermute | solution.py:22
  38.4 1.9 %collective-permute-start.6 = (f32[2,16,256]{2,1,0:T(8,128)S(1)}, f32[2,16,256]{2,1,0:T(8,128)S(1)}, u32[]{:S(2)}, u32[]{:S(2)}) collective-permute-start(f32[2,16,256]{2,1,0:T(8,128)S(1)} %pad_maximum_fusion.7), channel_id=1, source_target_pairs={{0,32},{8,40},{16,48},{24,56},{32,0},{40,8},{48,16},{56,24},{64,96... | collective-permute-start | bytes 98312 | tf_op jit(solution)/shard_map/ppermute | solution.py:22
  40.3 2.1 %collective-permute-done.6 = f32[2,16,256]{2,1,0:T(8,128)S(1)} collective-permute-done((f32[2,16,256]{2,1,0:T(8,128)S(1)}, f32[2,16,256]{2,1,0:T(8,128)S(1)}, u32[]{:S(2)}, u32[]{:S(2)}) %collective-permute-start.6) | collective-permute-done | bytes 32800 | tf_op jit(solution)/shard_map/ppermute | solution.py:22
  42.4 3.9 %collective-permute-start.7 = (f32[2,16,256]{2,1,0:T(8,128)S(1)}, f32[2,16,256]{2,1,0:T(8,128)S(1)}, u32[]{:S(2)}, u32[]{:S(2)}) collective-permute-start(f32[2,16,256]{2,1,0:T(8,128)S(1)} %pad_maximum_fusion.8), channel_id=1, source_target_pairs={{0,64},{8,72},{16,80},{24,88},{32,96},{40,104},{48,112},{56,120},{... | collective-permute-start | bytes 98312 | tf_op jit(solution)/shard_map/ppermute | solution.py:22
  46.9 1.4 %collective-permute-done.7 = f32[2,16,256]{2,1,0:T(8,128)S(1)} collective-permute-done((f32[2,16,256]{2,1,0:T(8,128)S(1)}, f32[2,16,256]{2,1,0:T(8,128)S(1)}, u32[]{:S(2)}, u32[]{:S(2)}) %collective-permute-start.7) | collective-permute-done | bytes 32800 | tf_op jit(solution)/shard_map/ppermute | solution.py:22
  48.3 6.3 %collective-permute-start.8 = (f32[2,16,256]{2,1,0:T(8,128)S(1)}, f32[2,16,256]{2,1,0:T(8,128)S(1)}, u32[]{:S(2)}, u32[]{:S(2)}) collective-permute-start(f32[2,16,256]{2,1,0:T(8,128)S(1)} %pad_maximum_fusion.9), channel_id=1, source_target_pairs={{0,128},{8,136},{16,144},{24,152},{32,160},{40,168},{48,176},{56,1... | collective-permute-start | bytes 98312 | tf_op jit(solution)/shard_map/ppermute | solution.py:22
  55.2 1.3 collective-permute-done.8
  57.1 1.7 %broadcast_in_dim.20.om_ref = f32[128,16,256]{2,1,0:T(8,128)} broadcast(f32[128,16]{1,0:T(8,128)S(1)} %copy.60), dimensions={0,1} | broadcast | bytes 2105344 | tf_op jit(solution)/shard_map/broadcast_in_dim | solution.py:251
  58.8 5.4 %shard_map.194 = (f32[128,256]{1,0:T(8,128)}, f32[16,16,256]{2,1,0:T(8,128)}) custom-call(f32[128,16,256]{2,1,0:T(8,128)} %get-tuple-element.61.da_ref, f32[128,16,256]{2,1,0:T(8,128)} %get-tuple-element.62.dr_ref, f32[128,16,256]{2,1,0:T(8,128)} %broadcast_in_dim.20.om_ref, f32[16,256]{1,0:T(8,128)} %add_select_fusion.sin_ref, ...), custom_call_target="tpu_custom_call" | custom-call | tf_op jit(solution)/shard_map/pallas_call | solution.py:141
  64.2 2.5 %convolution_convert_fusion.1 = bf16[128,2048]{1,0:T(8,128)(2,1)S(1)} fusion(bf16[256,2048]{1,0:T(8,128)(2,1)} %param.29, f32[128,256]{1,0:T(8,128)} %get-tuple-element.9, bf16[128,256]{1,0:T(8,128)(2,1)S(1)} %multiply_convert_fusion.1, bf16[2048,256]{1,0:T(8,128)(2,1)} %param.21, bf16[128,2048]{1,0:T(8,128)(2,1)S(1)} %copy-done.3, f32[2048]{0:T(1024)S(1)} %copy-done.8, ...), kind=kOutput, calls=%fused_computation.1 | convolution fusion | flops 270106624 | bytes 3352064 | tf_op jit(solution)/shard_map/dot_general | solution.py:282
  66.9 1.4 %collective-permute-done.9 = bf16[2,2,16,2048]{3,2,0,1:T(8,128)(2,1)S(1)} collective-permute-done((bf16[2,2,16,2048]{3,2,0,1:T(8,128)(2,1)S(1)}, bf16[2,2,16,2048]{3,2,0,1:T(8,128)(2,1)S(1)}, u32[]{:S(2)}, u32[]{:S(2)}) %collective-permute-start.9) | collective-permute-done | bytes 262176 | tf_op jit(solution)/shard_map/ppermute | solution.py:22
  68.5 1.6 %collective-permute-start.10 = (bf16[2,16,2048]{2,1,0:T(8,128)(2,1)S(1)}, bf16[2,16,2048]{2,1,0:T(8,128)(2,1)S(1)}, u32[]{:S(2)}, u32[]{:S(2)}) collective-permute-start(bf16[2,16,2048]{2,1,0:T(8,128)(2,1)S(1)} %fusion.15), channel_id=1, source_target_pairs={{0,2},{1,3},{2,0},{3,1},{4,6},{5,7},{6,4},{7,5},{8,10},{9,11},{10,... | collective-permute-start | bytes 393224 | tf_op jit(solution)/shard_map/ppermute | solution.py:22
  70.3 1.0 convert_element_type.221
  71.2 2.8 %collective-permute-done.10 = bf16[2,16,2048]{2,1,0:T(8,128)(2,1)S(1)} collective-permute-done((bf16[2,16,2048]{2,1,0:T(8,128)(2,1)S(1)}, bf16[2,16,2048]{2,1,0:T(8,128)(2,1)S(1)}, u32[]{:S(2)}, u32[]{:S(2)}) %collective-permute-start.10) | collective-permute-done | bytes 131104 | tf_op jit(solution)/shard_map/ppermute | solution.py:22
  74.1 3.1 %collective-permute-start.11 = (bf16[16,2048]{1,0:T(8,128)(2,1)S(1)}, bf16[16,2048]{1,0:T(8,128)(2,1)S(1)}, u32[]{:S(2)}, u32[]{:S(2)}) collective-permute-start(bf16[16,2048]{1,0:T(8,128)(2,1)S(1)} %fusion.30), channel_id=1, source_target_pairs={{0,4},{1,5},{2,6},{3,7},{4,0},{5,1},{6,2},{7,3},{8,12},{9,13},{10,... | collective-permute-start | bytes 196616 | tf_op jit(solution)/shard_map/ppermute | solution.py:22
  77.3 1.9 %collective-permute-start.18 = (bf16[16,19,256]{2,1,0:T(8,128)(2,1)S(1)}, bf16[16,19,256]{2,1,0:T(8,128)(2,1)S(1)}, u32[]{:S(2)}, u32[]{:S(2)}) collective-permute-start(bf16[16,19,256]{2,1,0:T(8,128)(2,1)S(1)} %pad_maximum_fusion.2), channel_id=1, source_target_pairs={{0,8},{8,0},{16,24},{24,16},{32,40},{40,32},{48,56},{56,48},{64,72... | collective-permute-start | bytes 466952 | tf_op jit(solution)/shard_map/ppermute | solution.py:22
  79.1 0.9 collective-permute-done.11
  80.2 3.1 %collective-permute-start.12 = (bf16[16,2048]{1,0:T(8,128)(2,1)S(1)}, bf16[16,2048]{1,0:T(8,128)(2,1)S(1)}, u32[]{:S(2)}, u32[]{:S(2)}) collective-permute-start(bf16[16,2048]{1,0:T(8,128)(2,1)S(1)} %multiply_convert_fusion), channel_id=1, source_target_pairs={{0,4},{1,5},{2,6},{3,7},{4,0},{5,1},{6,2},{7,3},{8,12},{9,13},{10,... | collective-permute-start | bytes 196616 | tf_op jit(solution)/shard_map/ppermute | solution.py:22
  83.4 2.7 %collective-permute-start.19 = (bf16[16,19,256]{2,1,0:T(8,128)(2,1)S(1)}, bf16[16,19,256]{2,1,0:T(8,128)(2,1)S(1)}, u32[]{:S(2)}, u32[]{:S(2)}) collective-permute-start(bf16[16,19,256]{2,1,0:T(8,128)(2,1)S(1)} %fusion.64), channel_id=1, source_target_pairs={{0,16},{8,24},{16,0},{24,8},{32,48},{40,56},{48,32},{56,40},{64,80... | collective-permute-start | bytes 466952 | tf_op jit(solution)/shard_map/ppermute | solution.py:22
  86.3 1.5 %collective-permute-start.13 = (bf16[2,16,2048]{2,1,0:T(8,128)(2,1)S(1)}, bf16[2,16,2048]{2,1,0:T(8,128)(2,1)S(1)}, u32[]{:S(2)}, u32[]{:S(2)}) collective-permute-start(bf16[2,16,2048]{2,1,0:T(8,128)(2,1)S(1)} %pad_maximum_fusion.4), channel_id=1, source_target_pairs={{0,2},{1,3},{2,0},{3,1},{4,6},{5,7},{6,4},{7,5},{8,10},{9,11},{10,... | collective-permute-start | bytes 393224 | tf_op jit(solution)/shard_map/ppermute | solution.py:22
  87.8 3.1 %collective-permute-done.19 = bf16[16,19,256]{2,1,0:T(8,128)(2,1)S(1)} collective-permute-done((bf16[16,19,256]{2,1,0:T(8,128)(2,1)S(1)}, bf16[16,19,256]{2,1,0:T(8,128)(2,1)S(1)}, u32[]{:S(2)}, u32[]{:S(2)}) %collective-permute-start.19) | collective-permute-done | bytes 155680 | tf_op jit(solution)/shard_map/ppermute | solution.py:22
  90.9 2.1 %collective-permute-start.20 = (bf16[16,19,256]{2,1,0:T(8,128)(2,1)S(1)}, bf16[16,19,256]{2,1,0:T(8,128)(2,1)S(1)}, u32[]{:S(2)}, u32[]{:S(2)}) collective-permute-start(bf16[16,19,256]{2,1,0:T(8,128)(2,1)S(1)} %add.351), channel_id=1, source_target_pairs={{0,32},{8,40},{16,48},{24,56},{32,0},{40,8},{48,16},{56,24},{64,96... | collective-permute-start | bytes 466952 | tf_op jit(solution)/shard_map/ppermute | solution.py:22
  93.2 3.5 %collective-permute-done.20 = bf16[16,19,256]{2,1,0:T(8,128)(2,1)S(1)} collective-permute-done((bf16[16,19,256]{2,1,0:T(8,128)(2,1)S(1)}, bf16[16,19,256]{2,1,0:T(8,128)(2,1)S(1)}, u32[]{:S(2)}, u32[]{:S(2)}) %collective-permute-start.20) | collective-permute-done | bytes 155680 | tf_op jit(solution)/shard_map/ppermute | solution.py:22
  96.7 4.3 %collective-permute-start.21 = (bf16[16,19,256]{2,1,0:T(8,128)(2,1)S(1)}, bf16[16,19,256]{2,1,0:T(8,128)(2,1)S(1)}, u32[]{:S(2)}, u32[]{:S(2)}) collective-permute-start(bf16[16,19,256]{2,1,0:T(8,128)(2,1)S(1)} %add.352), channel_id=1, source_target_pairs={{0,64},{8,72},{16,80},{24,88},{32,96},{40,104},{48,112},{56,120},{... | collective-permute-start | bytes 466952 | tf_op jit(solution)/shard_map/ppermute | solution.py:22
  101.1 5.8 %collective-permute-done.21 = bf16[16,19,256]{2,1,0:T(8,128)(2,1)S(1)} collective-permute-done((bf16[16,19,256]{2,1,0:T(8,128)(2,1)S(1)}, bf16[16,19,256]{2,1,0:T(8,128)(2,1)S(1)}, u32[]{:S(2)}, u32[]{:S(2)}) %collective-permute-start.21) | collective-permute-done | bytes 155680 | tf_op jit(solution)/shard_map/ppermute | solution.py:22
  107.6 10.1 %collective-permute-start.22 = (bf16[16,19,256]{2,1,0:T(8,128)(2,1)}, bf16[16,19,256]{2,1,0:T(8,128)(2,1)}, u32[]{:S(2)}, u32[]{:S(2)}) collective-permute-start(bf16[16,19,256]{2,1,0:T(8,128)(2,1)} %add.353), channel_id=1, source_target_pairs={{0,128},{8,136},{16,144},{24,152},{32,160},{40,168},{48,176},{56,1... | collective-permute-start | bytes 466952 | tf_op jit(solution)/shard_map/ppermute | solution.py:22
  118.2 2.4 %convolution_convert_fusion = bf16[128,2048]{1,0:T(8,128)(2,1)S(1)} fusion(bf16[512,2048]{1,0:T(8,128)(2,1)S(1)} %copy-done, bf16[128,2048]{1,0:T(8,128)(2,1)S(1)} %bitcast.173, bf16[2048,512]{1,0:T(8,128)(2,1)} %param.32, f32[128,512]{1,0:T(8,128)S(1)} %fusion.70), kind=kOutput, calls=%fused_computation | convolution fusion | flops 537526272 | bytes 5505024 | tf_op jit(solution)/shard_map/dot_general | solution.py:294
  121.6 1.1 add.354
  123.1 5.0 %collective-permute-done.16 = bf16[2,16,2048]{2,1,0:T(8,128)(2,1)S(1)} collective-permute-done((bf16[2,16,2048]{2,1,0:T(8,128)(2,1)S(1)}, bf16[2,16,2048]{2,1,0:T(8,128)(2,1)S(1)}, u32[]{:S(2)}, u32[]{:S(2)}) %collective-permute-start.16) | collective-permute-done | bytes 131104 | tf_op jit(solution)/shard_map/ppermute | solution.py:22
  128.3 0.8 convolution_convert_fusion.5
  129.7 4.3 %collective-permute-done.17 = bf16[16,2048]{1,0:T(8,128)(2,1)S(1)} collective-permute-done((bf16[16,2048]{1,0:T(8,128)(2,1)S(1)}, bf16[16,2048]{1,0:T(8,128)(2,1)S(1)}, u32[]{:S(2)}, u32[]{:S(2)}) %collective-permute-start.17) | collective-permute-done | bytes 65568 | tf_op jit(solution)/shard_map/ppermute | solution.py:22
  (113 shorter events, 10.2 us)
Async XLA Ops:
  0.6 117.6 %copy-start = (bf16[512,2048]{1,0:T(8,128)(2,1)S(1)}, bf16[512,2048]{1,0:T(8,128)(2,1)}, u32[]{:S(2)}) copy-start(bf16[512,2048]{1,0:T(8,128)(2,1)} %param.33) | copy-start | bytes 6291460
  0.6 8.1 %copy-start.8 = (f32[2048]{0:T(1024)S(1)}, f32[2048]{0:T(1024)}, u32[]{:S(2)}) copy-start(f32[2048]{0:T(1024)} %param.19) | copy-start | bytes 24580
  0.7 8.1 %copy-start.2 = (bf16[2048,256]{1,0:T(8,128)(2,1)S(1)}, bf16[2048,256]{1,0:T(8,128)(2,1)}, u32[]{:S(2)}) copy-start(bf16[2048,256]{1,0:T(8,128)(2,1)} %param.20) | copy-start | bytes 3145732
  0.7 8.4 %copy-start.9 = (f32[256]{0:T(256)S(1)}, f32[256]{0:T(256)}, u32[]{:S(2)}) copy-start(f32[256]{0:T(256)} %param.23) | copy-start | bytes 3076
  0.7 8.6 %copy-start.4 = (bf16[256,160]{0,1:T(8,128)(2,1)S(1)}, bf16[256,160]{0,1:T(8,128)(2,1)}, u32[]{:S(2)}) copy-start(bf16[256,160]{0,1:T(8,128)(2,1)} %param.24) | copy-start | bytes 245764
  0.7 8.8 %copy-start.7 = (f32[16,256]{1,0:T(8,128)S(1)}, f32[16,256]{1,0:T(8,128)}, u32[]{:S(2)}) copy-start(f32[16,256]{1,0:T(8,128)} %param.27) | copy-start | bytes 49156
  1.6 7.0 %collective-permute-start = (bf16[3,2048]{1,0:T(4,128)(2,1)S(1)}, bf16[3,2048]{1,0:T(4,128)(2,1)S(1)}, u32[]{:S(2)}, u32[]{:S(2)}) collective-permute-start(bf16[3,2048]{1,0:T(4,128)(2,1)S(1)} %slice.69), channel_id=1, source_target_pairs={{0,8},{8,16},{16,24},{24,32},{32,40},{40,48},{48,56},{56,64},{64,7... | collective-permute-start | bytes 36872 | tf_op jit(solution)/shard_map/ppermute | solution.py:218
  6.8 14.8 %copy-start.5 = (bf16[128,256]{1,0:T(8,128)(2,1)S(1)}, bf16[128,256]{1,0:T(8,128)(2,1)}, u32[]{:S(2)}) copy-start(bf16[128,256]{1,0:T(8,128)(2,1)} %param.25) | copy-start | bytes 196612
  6.8 14.8 %copy-start.10 = (f32[256]{0:T(256)S(1)}, f32[256]{0:T(256)}, u32[]{:S(2)}) copy-start(f32[256]{0:T(256)} %param.26) | copy-start | bytes 3076
  9.4 1.4 %collective-permute-start.1 = (f32[128,160]{0,1:T(8,128)S(1)}, f32[128,160]{0,1:T(8,128)S(1)}, u32[]{:S(2)}, u32[]{:S(2)}) collective-permute-start(f32[128,160]{0,1:T(8,128)S(1)} %fusion.69), channel_id=1, source_target_pairs={{0,1},{1,0},{2,3},{3,2},{4,5},{5,4},{6,7},{7,6},{8,9},{9,8},{10,11... | collective-permute-start | bytes 245768 | tf_op jit(solution)/shard_map/ppermute | solution.py:22
  10.8 4.6 %collective-permute-start.2 = (f32[128,160]{0,1:T(8,128)S(1)}, f32[128,160]{0,1:T(8,128)S(1)}, u32[]{:S(2)}, u32[]{:S(2)}) collective-permute-start(f32[128,160]{0,1:T(8,128)S(1)} %add.303), channel_id=1, source_target_pairs={{0,2},{1,3},{2,0},{3,1},{4,6},{5,7},{6,4},{7,5},{8,10},{9,11},{10,... | collective-permute-start | bytes 245768 | tf_op jit(solution)/shard_map/ppermute | solution.py:22
  15.4 6.0 %collective-permute-start.3 = (f32[128,160]{0,1:T(8,128)S(1)}, f32[128,160]{0,1:T(8,128)S(1)}, u32[]{:S(2)}, u32[]{:S(2)}) collective-permute-start(f32[128,160]{0,1:T(8,128)S(1)} %add.304), channel_id=1, source_target_pairs={{0,4},{1,5},{2,6},{3,7},{4,0},{5,1},{6,2},{7,3},{8,12},{9,13},{10,... | collective-permute-start | bytes 245768 | tf_op jit(solution)/shard_map/ppermute | solution.py:22
  28.1 3.9 %collective-permute-start.4 = (f32[2,16,256]{2,1,0:T(8,128)S(1)}, f32[2,16,256]{2,1,0:T(8,128)S(1)}, u32[]{:S(2)}, u32[]{:S(2)}) collective-permute-start(f32[2,16,256]{2,1,0:T(8,128)S(1)} %pad_maximum_fusion.5), channel_id=1, source_target_pairs={{0,8},{8,0},{16,24},{24,16},{32,40},{40,32},{48,56},{56,48},{64,72... | collective-permute-start | bytes 98312 | tf_op jit(solution)/shard_map/ppermute | solution.py:22
  32.8 5.6 %collective-permute-start.5 = (f32[2,16,256]{2,1,0:T(8,128)S(1)}, f32[2,16,256]{2,1,0:T(8,128)S(1)}, u32[]{:S(2)}, u32[]{:S(2)}) collective-permute-start(f32[2,16,256]{2,1,0:T(8,128)S(1)} %pad_maximum_fusion.6), channel_id=1, source_target_pairs={{0,16},{8,24},{16,0},{24,8},{32,48},{40,56},{48,32},{56,40},{64,80... | collective-permute-start | bytes 98312 | tf_op jit(solution)/shard_map/ppermute | solution.py:22
  38.4 4.0 %collective-permute-start.6 = (f32[2,16,256]{2,1,0:T(8,128)S(1)}, f32[2,16,256]{2,1,0:T(8,128)S(1)}, u32[]{:S(2)}, u32[]{:S(2)}) collective-permute-start(f32[2,16,256]{2,1,0:T(8,128)S(1)} %pad_maximum_fusion.7), channel_id=1, source_target_pairs={{0,32},{8,40},{16,48},{24,56},{32,0},{40,8},{48,16},{56,24},{64,96... | collective-permute-start | bytes 98312 | tf_op jit(solution)/shard_map/ppermute | solution.py:22
  42.4 5.8 %collective-permute-start.7 = (f32[2,16,256]{2,1,0:T(8,128)S(1)}, f32[2,16,256]{2,1,0:T(8,128)S(1)}, u32[]{:S(2)}, u32[]{:S(2)}) collective-permute-start(f32[2,16,256]{2,1,0:T(8,128)S(1)} %pad_maximum_fusion.8), channel_id=1, source_target_pairs={{0,64},{8,72},{16,80},{24,88},{32,96},{40,104},{48,112},{56,120},{... | collective-permute-start | bytes 98312 | tf_op jit(solution)/shard_map/ppermute | solution.py:22
  48.3 8.2 %collective-permute-start.8 = (f32[2,16,256]{2,1,0:T(8,128)S(1)}, f32[2,16,256]{2,1,0:T(8,128)S(1)}, u32[]{:S(2)}, u32[]{:S(2)}) collective-permute-start(f32[2,16,256]{2,1,0:T(8,128)S(1)} %pad_maximum_fusion.9), channel_id=1, source_target_pairs={{0,128},{8,136},{16,144},{24,152},{32,160},{40,168},{48,176},{56,1... | collective-permute-start | bytes 98312 | tf_op jit(solution)/shard_map/ppermute | solution.py:22
  58.8 5.4 %copy-start.3 = (bf16[128,2048]{1,0:T(8,128)(2,1)S(1)}, bf16[128,2048]{1,0:T(8,128)(2,1)}, u32[]{:S(2)}) copy-start(bf16[128,2048]{1,0:T(8,128)(2,1)} %param.18) | copy-start | bytes 1572868
  58.8 5.4 %copy-start.12 = (f32[256]{0:T(256)S(1)}, f32[256]{0:T(256)}, u32[]{:S(2)}) copy-start(f32[256]{0:T(256)} %param.28) | copy-start | bytes 3076
  66.7 13.4 %copy-start.6 = (f32[2048]{0:T(1024)S(1)}, f32[2048]{0:T(1024)}, u32[]{:S(2)}) copy-start(f32[2048]{0:T(1024)} %param.30) | copy-start | bytes 24580
  66.7 1.6 %collective-permute-start.9 = (bf16[2,2,16,2048]{3,2,0,1:T(8,128)(2,1)S(1)}, bf16[2,2,16,2048]{3,2,0,1:T(8,128)(2,1)S(1)}, u32[]{:S(2)}, u32[]{:S(2)}) collective-permute-start(bf16[2,2,16,2048]{3,2,0,1:T(8,128)(2,1)S(1)} %bitcast.176), channel_id=1, source_target_pairs={{0,1},{1,0},{2,3},{3,2},{4,5},{5,4},{6,7},{7,6},{8,9},{9,8},{10,11... | collective-permute-start | bytes 786440 | tf_op jit(solution)/shard_map/ppermute | solution.py:22
  68.5 5.6 %collective-permute-start.10 = (bf16[2,16,2048]{2,1,0:T(8,128)(2,1)S(1)}, bf16[2,16,2048]{2,1,0:T(8,128)(2,1)S(1)}, u32[]{:S(2)}, u32[]{:S(2)}) collective-permute-start(bf16[2,16,2048]{2,1,0:T(8,128)(2,1)S(1)} %fusion.15), channel_id=1, source_target_pairs={{0,2},{1,3},{2,0},{3,1},{4,6},{5,7},{6,4},{7,5},{8,10},{9,11},{10,... | collective-permute-start | bytes 393224 | tf_op jit(solution)/shard_map/ppermute | solution.py:22
  74.1 5.9 %collective-permute-start.11 = (bf16[16,2048]{1,0:T(8,128)(2,1)S(1)}, bf16[16,2048]{1,0:T(8,128)(2,1)S(1)}, u32[]{:S(2)}, u32[]{:S(2)}) collective-permute-start(bf16[16,2048]{1,0:T(8,128)(2,1)S(1)} %fusion.30), channel_id=1, source_target_pairs={{0,4},{1,5},{2,6},{3,7},{4,0},{5,1},{6,2},{7,3},{8,12},{9,13},{10,... | collective-permute-start | bytes 196616 | tf_op jit(solution)/shard_map/ppermute | solution.py:22
  77.3 6.1 %collective-permute-start.18 = (bf16[16,19,256]{2,1,0:T(8,128)(2,1)S(1)}, bf16[16,19,256]{2,1,0:T(8,128)(2,1)S(1)}, u32[]{:S(2)}, u32[]{:S(2)}) collective-permute-start(bf16[16,19,256]{2,1,0:T(8,128)(2,1)S(1)} %pad_maximum_fusion.2), channel_id=1, source_target_pairs={{0,8},{8,0},{16,24},{24,16},{32,40},{40,32},{48,56},{56,48},{64,72... | collective-permute-start | bytes 466952 | tf_op jit(solution)/shard_map/ppermute | solution.py:22
  80.2 5.9 %collective-permute-start.12 = (bf16[16,2048]{1,0:T(8,128)(2,1)S(1)}, bf16[16,2048]{1,0:T(8,128)(2,1)S(1)}, u32[]{:S(2)}, u32[]{:S(2)}) collective-permute-start(bf16[16,2048]{1,0:T(8,128)(2,1)S(1)} %multiply_convert_fusion), channel_id=1, source_target_pairs={{0,4},{1,5},{2,6},{3,7},{4,0},{5,1},{6,2},{7,3},{8,12},{9,13},{10,... | collective-permute-start | bytes 196616 | tf_op jit(solution)/shard_map/ppermute | solution.py:22
  83.4 7.4 %collective-permute-start.19 = (bf16[16,19,256]{2,1,0:T(8,128)(2,1)S(1)}, bf16[16,19,256]{2,1,0:T(8,128)(2,1)S(1)}, u32[]{:S(2)}, u32[]{:S(2)}) collective-permute-start(bf16[16,19,256]{2,1,0:T(8,128)(2,1)S(1)} %fusion.64), channel_id=1, source_target_pairs={{0,16},{8,24},{16,0},{24,8},{32,48},{40,56},{48,32},{56,40},{64,80... | collective-permute-start | bytes 466952 | tf_op jit(solution)/shard_map/ppermute | solution.py:22
  86.3 6.7 %collective-permute-start.13 = (bf16[2,16,2048]{2,1,0:T(8,128)(2,1)S(1)}, bf16[2,16,2048]{2,1,0:T(8,128)(2,1)S(1)}, u32[]{:S(2)}, u32[]{:S(2)}) collective-permute-start(bf16[2,16,2048]{2,1,0:T(8,128)(2,1)S(1)} %pad_maximum_fusion.4), channel_id=1, source_target_pairs={{0,2},{1,3},{2,0},{3,1},{4,6},{5,7},{6,4},{7,5},{8,10},{9,11},{10,... | collective-permute-start | bytes 393224 | tf_op jit(solution)/shard_map/ppermute | solution.py:22
  90.9 5.8 %collective-permute-start.20 = (bf16[16,19,256]{2,1,0:T(8,128)(2,1)S(1)}, bf16[16,19,256]{2,1,0:T(8,128)(2,1)S(1)}, u32[]{:S(2)}, u32[]{:S(2)}) collective-permute-start(bf16[16,19,256]{2,1,0:T(8,128)(2,1)S(1)} %add.351), channel_id=1, source_target_pairs={{0,32},{8,40},{16,48},{24,56},{32,0},{40,8},{48,16},{56,24},{64,96... | collective-permute-start | bytes 466952 | tf_op jit(solution)/shard_map/ppermute | solution.py:22
  93.1 24.6 %collective-permute-start.14 = (bf16[2,2,16,2048]{3,2,1,0:T(8,128)(2,1)S(1)}, bf16[2,2,16,2048]{3,2,1,0:T(8,128)(2,1)S(1)}, u32[]{:S(2)}, u32[]{:S(2)}) collective-permute-start(bf16[2,2,16,2048]{3,2,1,0:T(8,128)(2,1)S(1)} %pad_maximum_fusion.1), channel_id=1, source_target_pairs={{0,1},{1,0},{2,3},{3,2},{4,5},{5,4},{6,7},{7,6},{8,9},{9,8},{10,11... | collective-permute-start | bytes 786440 | tf_op jit(solution)/shard_map/ppermute | solution.py:22
  96.7 10.1 %collective-permute-start.21 = (bf16[16,19,256]{2,1,0:T(8,128)(2,1)S(1)}, bf16[16,19,256]{2,1,0:T(8,128)(2,1)S(1)}, u32[]{:S(2)}, u32[]{:S(2)}) collective-permute-start(bf16[16,19,256]{2,1,0:T(8,128)(2,1)S(1)} %add.352), channel_id=1, source_target_pairs={{0,64},{8,72},{16,80},{24,88},{32,96},{40,104},{48,112},{56,120},{... | collective-permute-start | bytes 466952 | tf_op jit(solution)/shard_map/ppermute | solution.py:22
  101.1 16.7 %copy-start.1 = (bf16[2048,512]{1,0:T(8,128)(2,1)S(1)}, bf16[2048,512]{1,0:T(8,128)(2,1)}, u32[]{:S(2)}) copy-start(bf16[2048,512]{1,0:T(8,128)(2,1)} %param.31) | copy-start | bytes 6291460
  107.6 14.0 %collective-permute-start.22 = (bf16[16,19,256]{2,1,0:T(8,128)(2,1)}, bf16[16,19,256]{2,1,0:T(8,128)(2,1)}, u32[]{:S(2)}, u32[]{:S(2)}) collective-permute-start(bf16[16,19,256]{2,1,0:T(8,128)(2,1)} %add.353), channel_id=1, source_target_pairs={{0,128},{8,136},{16,144},{24,152},{32,160},{40,168},{48,176},{56,1... | collective-permute-start | bytes 466952 | tf_op jit(solution)/shard_map/ppermute | solution.py:22
  120.7 2.3 %copy-start.11 = (s32[4]{0:T(128)S(1)}, s32[4]{0:T(128)}, u32[]{:S(2)}) copy-start(s32[4]{0:T(128)} %param.35) | copy-start | bytes 52
  120.8 2.0 %collective-permute-start.15 = (bf16[2,2,16,2048]{3,2,0,1:T(8,128)(2,1)S(1)}, bf16[2,2,16,2048]{3,2,0,1:T(8,128)(2,1)S(1)}, u32[]{:S(2)}, u32[]{:S(2)}) collective-permute-start(bf16[2,2,16,2048]{3,2,0,1:T(8,128)(2,1)S(1)} %bitcast.177), channel_id=1, source_target_pairs={{0,1},{1,0},{2,3},{3,2},{4,5},{5,4},{6,7},{7,6},{8,9},{9,8},{10,11... | collective-permute-start | bytes 786440 | tf_op jit(solution)/shard_map/ppermute | solution.py:22
  122.8 5.3 %collective-permute-start.16 = (bf16[2,16,2048]{2,1,0:T(8,128)(2,1)S(1)}, bf16[2,16,2048]{2,1,0:T(8,128)(2,1)S(1)}, u32[]{:S(2)}, u32[]{:S(2)}) collective-permute-start(bf16[2,16,2048]{2,1,0:T(8,128)(2,1)S(1)} %fusion.16), channel_id=1, source_target_pairs={{0,2},{1,3},{2,0},{3,1},{4,6},{5,7},{6,4},{7,5},{8,10},{9,11},{10,... | collective-permute-start | bytes 393224 | tf_op jit(solution)/shard_map/ppermute | solution.py:22
  128.2 5.9 %collective-permute-start.17 = (bf16[16,2048]{1,0:T(8,128)(2,1)S(1)}, bf16[16,2048]{1,0:T(8,128)(2,1)S(1)}, u32[]{:S(2)}, u32[]{:S(2)}) collective-permute-start(bf16[16,2048]{1,0:T(8,128)(2,1)S(1)} %fusion.31), channel_id=1, source_target_pairs={{0,4},{1,5},{2,6},{3,7},{4,0},{5,1},{6,2},{7,3},{8,12},{9,13},{10,... | collective-permute-start | bytes 196616 | tf_op jit(solution)/shard_map/ppermute | solution.py:22

commit v6 on v5

--- a/solution.py
+++ b/solution.py
@@ -22,51 +22,81 @@
     return lax.ppermute(x, axis, [(i, i ^ bit) for i in range(devices)])
 
 
-def bits_of(devices):
+RINGS = {"seq": (8, 4), "tp": (4, 2)}
+
+
+def ring_vectors(size):
+    return {1: [], 2: [1], 4: [1, 3], 8: [1, 2, 6]}[size]
+
+
+def basis_of(axis):
+    devices = lax.axis_size(axis)
+    rings = RINGS.get(axis, ())
+    prod = 1
+    for r in rings:
+        prod *= r
+    if prod != devices or any(r not in (1, 2, 4, 8) for r in rings):
+        rings = (devices,)
     out = []
-    bit = 1
-    while bit < devices:
-        out.append(bit)
-        bit *= 2
-    assert bit == devices
+    shift = 0
+    for r in reversed(rings):
+        if r > 8:
+            vecs = [1 << i for i in range(r.bit_length() - 1)]
+            assert 1 << len(vecs) == r
+        else:
+            vecs = ring_vectors(r)
+        for v in vecs:
+            out.append((v << shift, (v << shift).bit_length() - 1))
+        shift += len(vecs)
+    assert 1 << shift == devices
     return out
 
 
 def butterfly_sum(x, axis, send_dtype):
-    for bit in bits_of(lax.axis_size(axis)):
-        x = x + swap(x.astype(send_dtype), axis, bit).astype(x.dtype)
+    for mask, _ in basis_of(axis):
+        x = x + swap(x.astype(send_dtype), axis, mask).astype(x.dtype)
     return x
 
 
+def scatter_order(axis):
+    order = sorted(basis_of(axis), key=lambda vh: -vh[1])
+    if order[-1] == (1, 0) and all(mask % 2 == 0 for mask, _ in order[:-1]):
+        order = order[-1:] + order[:-1]
+    return order
+
+
 def scatter_rows(x, axis, first_dtype):
     devices = lax.axis_size(axis)
-    bits = bits_of(devices)
     me = lax.axis_index(axis)
-    depth = len(bits)
+    depth = devices.bit_length() - 1
     rows = x.shape[0] // devices
     buf = x.reshape((2,) * depth + (rows, x.shape[1]))
+    left = list(range(depth - 1, -1, -1))
     send_dtype = first_dtype
-    for level, bit in enumerate(bits):
-        at = depth - 1 - level
-        mine = ((me // bit) % 2).astype(jnp.int32)
+    for mask, top in scatter_order(axis):
+        at = left.index(top)
+        mine = ((me // (1 << top)) % 2).astype(jnp.int32)
         keep = lax.dynamic_index_in_dim(buf, mine, at, False)
         give = lax.dynamic_index_in_dim(buf, 1 - mine, at, False)
-        got = swap(give.astype(send_dtype), axis, bit)
+        got = swap(give.astype(send_dtype), axis, mask)
         buf = keep.astype(jnp.float32) + got.astype(jnp.float32)
+        left.remove(top)
     return buf
 
 
 def gather_rows(x, axis):
     devices = lax.axis_size(axis)
-    bits = bits_of(devices)
     me = lax.axis_index(axis)
     buf = x
-    for level, bit in enumerate(reversed(bits)):
-        got = swap(buf, axis, bit)
-        upper = ((me // bit) % 2) == 1
+    held = []
+    for mask, top in reversed(scatter_order(axis)):
+        got = swap(buf, axis, mask)
+        upper = ((me // (1 << top)) % 2) == 1
         low = jnp.where(upper, got, buf)
         high = jnp.where(upper, buf, got)
-        buf = jnp.stack([low, high], axis=level)
+        at = sum(1 for b in held if b > top)
+        buf = jnp.stack([low, high], axis=at)
+        held.insert(at, top)
     return buf.reshape((devices * x.shape[0], x.shape[1]))
 
 
@@ -154,10 +184,10 @@
     me = lax.axis_index(axis)
     tot_a, tot_s = a_blk, s_blk
     exc_a, exc_s = jnp.ones_like(a_blk), jnp.zeros_like(s_blk)
-    for bit in bits_of(lax.axis_size(axis)):
-        got = swap(jnp.stack([tot_a, tot_s]), axis, bit)
+    for mask, top in basis_of(axis):
+        got = swap(jnp.stack([tot_a, tot_s]), axis, mask)
         got_a, got_s = got[0], got[1]
-        upper = ((me // bit) % 2) == 1
+        upper = ((me // (1 << top)) % 2) == 1
         low_a = jnp.where(upper, got_a, tot_a)
         low_s = jnp.where(upper, got_s, tot_s)
         high_a = jnp.where(upper, tot_a, got_a)

time: 135 us -> 129 us (0.956)
  the two profiles are of different devices: /device:TPU:16 before, /device:TPU:40 now
where the time goes in v6:
time: 129 us; the launch traced here: 128 us
  waiting for transfers between devices  49.9 us (39%)
  starting transfers between devices  39 us (30%)
  other arithmetic  15.4 us (12%)
  matrix products  9.01 us (7%)
  Pallas kernels  8.58 us (7%)
  local copies, waits for them, and re-layouts  5.31 us (4%)
    ppermute x22, waiting for transfers between devices, swap(): return lax.ppermute(x, axis, [(i, i ^ bit) for i in range(devices)])  49.9 us
    ppermute x22, starting transfers between devices, swap(): return lax.ppermute(x, axis, [(i, i ^ bit) for i in range(devices)])  37.3 us
    pallas_call x1, Pallas kernels, block_output(): pl.pallas_call(block_output_kernel, out_shape=(jax.ShapeDtypeStruct((t, e...  5.44 us
    pallas_call x1, Pallas kernels, block_summary(): pl.pallas_call(block_summary_kernel, out_shape=(jax.ShapeDtypeStruct((n,...  3.14 us
  transfers between devices with their start and end apart: 23, of which 19 were waited for; matrix products, arithmetic and copies ran while one was open for 13% of the time, Pallas kernels for 0%

profile of v6, /device:TPU:40, one launch (start us, length us, event | category | flops | bytes accessed | tf_op | source)
XLA Modules:
  0.0 128.4 jit_solution(11468123835353665562)
XLA Ops:
  0.7 0.9 slice.69
  1.6 1.7 %collective-permute-start = (bf16[3,2048]{1,0:T(4,128)(2,1)S(1)}, bf16[3,2048]{1,0:T(4,128)(2,1)S(1)}, u32[]{:S(2)}, u32[]{:S(2)}) collective-permute-start(bf16[3,2048]{1,0:T(4,128)(2,1)S(1)} %slice.69), channel_id=1, source_target_pairs={{0,8},{8,16},{16,24},{24,32},{32,40},{40,48},{48,56},{56,64},{64,7... | collective-permute-start | bytes 36872 | tf_op jit(solution)/shard_map/ppermute | solution.py:248
  3.3 1.2 fusion.2
  4.5 0.8 fusion.68
  6.3 1.2 broadcast_add_fusion
  7.6 1.8 %convolution_convert_fusion.3 = bf16[128,256]{1,0:T(8,128)(2,1)S(1)} fusion(bf16[2048,256]{1,0:T(8,128)(2,1)} %param.20, bf16[128,2048]{1,0:T(8,128)(2,1)} %param.18, f32[2048]{0:T(1024)} %param.19, f32[128]{0:T(128)S(1)} %add_rsqrt_fusion.2), kind=kOutput, calls=%fused_computation.10 | convolution fusion | flops 135299072 | bytes 1647104 | tf_op jit(solution)/shard_map/dot_general | solution.py:255
  10.4 1.2 collective-permute-done.1
  11.6 1.6 %collective-permute-start.2 = (f32[128,160]{0,1:T(8,128)S(1)}, f32[128,160]{0,1:T(8,128)S(1)}, u32[]{:S(2)}, u32[]{:S(2)}) collective-permute-start(f32[128,160]{0,1:T(8,128)S(1)} %add.303), channel_id=1, source_target_pairs={{0,2},{1,3},{2,0},{3,1},{4,6},{5,7},{6,4},{7,5},{8,10},{9,11},{10,... | collective-permute-start | bytes 245768 | tf_op jit(solution)/shard_map/ppermute | solution.py:22
  13.3 2.9 %collective-permute-done.2 = f32[128,160]{0,1:T(8,128)S(1)} collective-permute-done((f32[128,160]{0,1:T(8,128)S(1)}, f32[128,160]{0,1:T(8,128)S(1)}, u32[]{:S(2)}, u32[]{:S(2)}) %collective-permute-start.2) | collective-permute-done | bytes 81952 | tf_op jit(solution)/shard_map/ppermute | solution.py:22
  16.2 2.8 %collective-permute-start.3 = (f32[128,160]{0,1:T(8,128)S(1)}, f32[128,160]{0,1:T(8,128)S(1)}, u32[]{:S(2)}, u32[]{:S(2)}) collective-permute-start(f32[128,160]{0,1:T(8,128)S(1)} %add.304), channel_id=1, source_target_pairs={{0,6},{1,7},{2,4},{3,5},{4,2},{5,3},{6,0},{7,1},{8,14},{9,15},{10,... | collective-permute-start | bytes 245768 | tf_op jit(solution)/shard_map/ppermute | solution.py:22
  19.1 2.9 %collective-permute-done.3 = f32[128,160]{0,1:T(8,128)S(1)} collective-permute-done((f32[128,160]{0,1:T(8,128)S(1)}, f32[128,160]{0,1:T(8,128)S(1)}, u32[]{:S(2)}, u32[]{:S(2)}) %collective-permute-start.3) | collective-permute-done | bytes 81952 | tf_op jit(solution)/shard_map/ppermute | solution.py:22
  22.4 2.4 %exponential_multiply_fusion = (f32[128,16,256]{2,1,0:T(8,128)}, f32[128,16,256]{2,1,0:T(8,128)}) fusion(f32[128]{0:T(128)S(1)} %convert_subtract_fusion, f32[16,256]{1,0:T(8,128)S(1)} %exponential_negate_fusion, f32[128,256]{1,0:T(8,128)S(1)} %get-tuple-element.56, f32[128,16]{1,0:T(8,128)S(1)} %copy.51, f32[128,256]{1,0:T(8,128)S(1)} %get-tuple-element.55), kind=kLoop, calls=%fused_computation.2 | loop fusion | flops 1572864 | bytes 4481536 | tf_op jit(solution)/shard_map/mul | solution.py:279
  24.8 3.1 %shard_map.193 = (f32[16,256]{1,0:T(8,128)}, f32[16,256]{1,0:T(8,128)}) custom-call(f32[128,16,256]{2,1,0:T(8,128)} %get-tuple-element.57.da_ref, f32[128,16,256]{2,1,0:T(8,128)} %get-tuple-element.58.dr_ref), custom_call_target="tpu_custom_call" | custom-call | tf_op jit(solution)/shard_map/pallas_call | solution.py:155
  29.1 3.5 %collective-permute-done.4 = f32[2,16,256]{2,1,0:T(8,128)S(1)} collective-permute-done((f32[2,16,256]{2,1,0:T(8,128)S(1)}, f32[2,16,256]{2,1,0:T(8,128)S(1)}, u32[]{:S(2)}, u32[]{:S(2)}) %collective-permute-start.4) | collective-permute-done | bytes 32800 | tf_op jit(solution)/shard_map/ppermute | solution.py:22
  32.6 0.7 select_multiply_fusion.2
  33.3 1.4 %collective-permute-start.5 = (f32[2,16,256]{2,1,0:T(8,128)S(1)}, f32[2,16,256]{2,1,0:T(8,128)S(1)}, u32[]{:S(2)}, u32[]{:S(2)}) collective-permute-start(f32[2,16,256]{2,1,0:T(8,128)S(1)} %pad_maximum_fusion.6), channel_id=1, source_target_pairs={{0,24},{8,16},{16,8},{24,0},{32,56},{40,48},{48,40},{56,32},{64,88... | collective-permute-start | bytes 98312 | tf_op jit(solution)/shard_map/ppermute | solution.py:22
  34.7 2.6 %collective-permute-done.5 = f32[2,16,256]{2,1,0:T(8,128)S(1)} collective-permute-done((f32[2,16,256]{2,1,0:T(8,128)S(1)}, f32[2,16,256]{2,1,0:T(8,128)S(1)}, u32[]{:S(2)}, u32[]{:S(2)}) %collective-permute-start.5) | collective-permute-done | bytes 32800 | tf_op jit(solution)/shard_map/ppermute | solution.py:22
  37.4 0.9 collective-permute-start.6
  38.2 3.3 %collective-permute-done.6 = f32[2,16,256]{2,1,0:T(8,128)S(1)} collective-permute-done((f32[2,16,256]{2,1,0:T(8,128)S(1)}, f32[2,16,256]{2,1,0:T(8,128)S(1)}, u32[]{:S(2)}, u32[]{:S(2)}) %collective-permute-start.6) | collective-permute-done | bytes 32800 | tf_op jit(solution)/shard_map/ppermute | solution.py:22
  41.6 3.2 %collective-permute-start.7 = (f32[2,16,256]{2,1,0:T(8,128)S(1)}, f32[2,16,256]{2,1,0:T(8,128)S(1)}, u32[]{:S(2)}, u32[]{:S(2)}) collective-permute-start(f32[2,16,256]{2,1,0:T(8,128)S(1)} %pad_maximum_fusion.8), channel_id=1, source_target_pairs={{0,64},{8,72},{16,80},{24,88},{32,96},{40,104},{48,112},{56,120},{... | collective-permute-start | bytes 98312 | tf_op jit(solution)/shard_map/ppermute | solution.py:22
  45.3 1.3 %collective-permute-done.7 = f32[2,16,256]{2,1,0:T(8,128)S(1)} collective-permute-done((f32[2,16,256]{2,1,0:T(8,128)S(1)}, f32[2,16,256]{2,1,0:T(8,128)S(1)}, u32[]{:S(2)}, u32[]{:S(2)}) %collective-permute-start.7) | collective-permute-done | bytes 32800 | tf_op jit(solution)/shard_map/ppermute | solution.py:22
  46.7 5.1 %collective-permute-start.8 = (f32[2,16,256]{2,1,0:T(8,128)S(1)}, f32[2,16,256]{2,1,0:T(8,128)S(1)}, u32[]{:S(2)}, u32[]{:S(2)}) collective-permute-start(f32[2,16,256]{2,1,0:T(8,128)S(1)} %pad_maximum_fusion.9), channel_id=1, source_target_pairs={{0,192},{8,200},{16,208},{24,216},{32,224},{40,232},{48,240},{56,2... | collective-permute-start | bytes 98312 | tf_op jit(solution)/shard_map/ppermute | solution.py:22
  54.3 1.7 %broadcast_in_dim.20.om_ref = f32[128,16,256]{2,1,0:T(8,128)} broadcast(f32[128,16]{1,0:T(8,128)S(1)} %copy.52), dimensions={0,1} | broadcast | bytes 2105344 | tf_op jit(solution)/shard_map/broadcast_in_dim | solution.py:281
  56.0 5.4 %shard_map.194 = (f32[128,256]{1,0:T(8,128)}, f32[16,16,256]{2,1,0:T(8,128)}) custom-call(f32[128,16,256]{2,1,0:T(8,128)} %get-tuple-element.57.da_ref, f32[128,16,256]{2,1,0:T(8,128)} %get-tuple-element.58.dr_ref, f32[128,16,256]{2,1,0:T(8,128)} %broadcast_in_dim.20.om_ref, f32[16,256]{1,0:T(8,128)} %add_select_fusion.sin_ref, ...), custom_call_target="tpu_custom_call" | custom-call | tf_op jit(solution)/shard_map/pallas_call | solution.py:171
  61.5 2.5 %convolution_convert_fusion.1 = bf16[128,2048]{1,0:T(8,128)(2,1)S(1)} fusion(bf16[256,2048]{1,0:T(8,128)(2,1)} %param.29, f32[128,256]{1,0:T(8,128)} %get-tuple-element.9, bf16[128,256]{1,0:T(8,128)(2,1)S(1)} %multiply_convert_fusion.1, bf16[2048,256]{1,0:T(8,128)(2,1)} %param.21, bf16[128,2048]{1,0:T(8,128)(2,1)S(1)} %copy-done.3, f32[2048]{0:T(1024)S(1)} %copy-done.10, ...), kind=kOutput, calls=%fused_computation.1 | convolution fusion | flops 270106624 | bytes 3352064 | tf_op jit(solution)/shard_map/dot_general | solution.py:312
  64.8 1.0 collective-permute-done.9
  65.8 1.0 convert_add_fusion.1
  66.8 2.8 %collective-permute-start.10 = (bf16[2,16,2048]{2,1,0:T(8,128)(2,1)S(1)}, bf16[2,16,2048]{2,1,0:T(8,128)(2,1)S(1)}, u32[]{:S(2)}, u32[]{:S(2)}) collective-permute-start(bf16[2,16,2048]{2,1,0:T(8,128)(2,1)S(1)} %fusion.15), channel_id=1, source_target_pairs={{0,6},{1,7},{2,4},{3,5},{4,2},{5,3},{6,0},{7,1},{8,14},{9,15},{10,... | collective-permute-start | bytes 393224 | tf_op jit(solution)/shard_map/ppermute | solution.py:22
  69.9 1.0 convert_element_type.221
  70.8 2.8 %collective-permute-done.10 = bf16[2,16,2048]{2,1,0:T(8,128)(2,1)S(1)} collective-permute-done((bf16[2,16,2048]{2,1,0:T(8,128)(2,1)S(1)}, bf16[2,16,2048]{2,1,0:T(8,128)(2,1)S(1)}, u32[]{:S(2)}, u32[]{:S(2)}) %collective-permute-start.10) | collective-permute-done | bytes 131104 | tf_op jit(solution)/shard_map/ppermute | solution.py:22
  73.8 1.8 %collective-permute-start.18 = (bf16[16,19,256]{2,1,0:T(8,128)(2,1)S(1)}, bf16[16,19,256]{2,1,0:T(8,128)(2,1)S(1)}, u32[]{:S(2)}, u32[]{:S(2)}) collective-permute-start(bf16[16,19,256]{2,1,0:T(8,128)(2,1)S(1)} %pad_maximum_fusion.2), channel_id=1, source_target_pairs={{0,8},{8,0},{16,24},{24,16},{32,40},{40,32},{48,56},{56,48},{64,72... | collective-permute-start | bytes 466952 | tf_op jit(solution)/shard_map/ppermute | solution.py:22
  75.6 2.4 %collective-permute-done.11 = bf16[16,2048]{1,0:T(8,128)(2,1)S(1)} collective-permute-done((bf16[16,2048]{1,0:T(8,128)(2,1)S(1)}, bf16[16,2048]{1,0:T(8,128)(2,1)S(1)}, u32[]{:S(2)}, u32[]{:S(2)}) %collective-permute-start.11) | collective-permute-done | bytes 65568 | tf_op jit(solution)/shard_map/ppermute | solution.py:22
  78.4 1.6 %collective-permute-done.18 = bf16[16,19,256]{2,1,0:T(8,128)(2,1)S(1)} collective-permute-done((bf16[16,19,256]{2,1,0:T(8,128)(2,1)S(1)}, bf16[16,19,256]{2,1,0:T(8,128)(2,1)S(1)}, u32[]{:S(2)}, u32[]{:S(2)}) %collective-permute-start.18) | collective-permute-done | bytes 155680 | tf_op jit(solution)/shard_map/ppermute | solution.py:22
  80.1 3.1 %collective-permute-start.19 = (bf16[16,19,256]{2,1,0:T(8,128)(2,1)S(1)}, bf16[16,19,256]{2,1,0:T(8,128)(2,1)S(1)}, u32[]{:S(2)}, u32[]{:S(2)}) collective-permute-start(bf16[16,19,256]{2,1,0:T(8,128)(2,1)S(1)} %fusion.64), channel_id=1, source_target_pairs={{0,24},{8,16},{16,8},{24,0},{32,56},{40,48},{48,40},{56,32},{64,88... | collective-permute-start | bytes 466952 | tf_op jit(solution)/shard_map/ppermute | solution.py:22
  83.3 2.8 %collective-permute-start.13 = (bf16[2,16,2048]{2,1,0:T(8,128)(2,1)S(1)}, bf16[2,16,2048]{2,1,0:T(8,128)(2,1)S(1)}, u32[]{:S(2)}, u32[]{:S(2)}) collective-permute-start(bf16[2,16,2048]{2,1,0:T(8,128)(2,1)S(1)} %pad_maximum_fusion.4), channel_id=1, source_target_pairs={{0,6},{1,7},{2,4},{3,5},{4,2},{5,3},{6,0},{7,1},{8,14},{9,15},{10,... | collective-permute-start | bytes 393224 | tf_op jit(solution)/shard_map/ppermute | solution.py:22
  86.2 0.8 collective-permute-done.19
  87.2 2.4 %collective-permute-done.13 = bf16[2,16,2048]{2,1,0:T(8,128)(2,1)S(1)} collective-permute-done((bf16[2,16,2048]{2,1,0:T(8,128)(2,1)S(1)}, bf16[2,16,2048]{2,1,0:T(8,128)(2,1)S(1)}, u32[]{:S(2)}, u32[]{:S(2)}) %collective-permute-start.13) | collective-permute-done | bytes 131104 | tf_op jit(solution)/shard_map/ppermute | solution.py:22
  89.7 3.0 %collective-permute-done.20 = bf16[16,19,256]{2,1,0:T(8,128)(2,1)S(1)} collective-permute-done((bf16[16,19,256]{2,1,0:T(8,128)(2,1)S(1)}, bf16[16,19,256]{2,1,0:T(8,128)(2,1)S(1)}, u32[]{:S(2)}, u32[]{:S(2)}) %collective-permute-start.20) | collective-permute-done | bytes 155680 | tf_op jit(solution)/shard_map/ppermute | solution.py:22
  92.8 2.7 %collective-permute-start.21 = (bf16[16,19,256]{2,1,0:T(8,128)(2,1)S(1)}, bf16[16,19,256]{2,1,0:T(8,128)(2,1)S(1)}, u32[]{:S(2)}, u32[]{:S(2)}) collective-permute-start(bf16[16,19,256]{2,1,0:T(8,128)(2,1)S(1)} %add.352), channel_id=1, source_target_pairs={{0,64},{8,72},{16,80},{24,88},{32,96},{40,104},{48,112},{56,120},{... | collective-permute-start | bytes 466952 | tf_op jit(solution)/shard_map/ppermute | solution.py:22
  95.6 5.5 %collective-permute-done.21 = bf16[16,19,256]{2,1,0:T(8,128)(2,1)S(1)} collective-permute-done((bf16[16,19,256]{2,1,0:T(8,128)(2,1)S(1)}, bf16[16,19,256]{2,1,0:T(8,128)(2,1)S(1)}, u32[]{:S(2)}, u32[]{:S(2)}) %collective-permute-start.21) | collective-permute-done | bytes 155680 | tf_op jit(solution)/shard_map/ppermute | solution.py:22
  101.8 4.8 %collective-permute-start.22 = (bf16[16,19,256]{2,1,0:T(8,128)(2,1)}, bf16[16,19,256]{2,1,0:T(8,128)(2,1)}, u32[]{:S(2)}, u32[]{:S(2)}) collective-permute-start(bf16[16,19,256]{2,1,0:T(8,128)(2,1)} %add.353), channel_id=1, source_target_pairs={{0,192},{8,200},{16,208},{24,216},{32,224},{40,232},{48,240},{56,2... | collective-permute-start | bytes 466952 | tf_op jit(solution)/shard_map/ppermute | solution.py:22
  107.2 2.4 %convolution_convert_fusion = bf16[128,2048]{1,0:T(8,128)(2,1)S(1)} fusion(bf16[512,2048]{1,0:T(8,128)(2,1)S(1)} %copy-done, bf16[128,2048]{1,0:T(8,128)(2,1)S(1)} %bitcast.169, bf16[2048,512]{1,0:T(8,128)(2,1)} %param.32, f32[128,512]{1,0:T(8,128)S(1)} %fusion.70), kind=kOutput, calls=%fused_computation | convolution fusion | flops 537526272 | bytes 5505024 | tf_op jit(solution)/shard_map/dot_general | solution.py:324
  109.9 5.5 %collective-permute-done.22 = bf16[16,19,256]{2,1,0:T(8,128)(2,1)} collective-permute-done((bf16[16,19,256]{2,1,0:T(8,128)(2,1)}, bf16[16,19,256]{2,1,0:T(8,128)(2,1)}, u32[]{:S(2)}, u32[]{:S(2)}) %collective-permute-start.22) | collective-permute-done | bytes 155680 | tf_op jit(solution)/shard_map/ppermute | solution.py:22
  115.3 1.1 add.354
  116.6 2.8 %collective-permute-start.16 = (bf16[2,16,2048]{2,1,0:T(8,128)(2,1)S(1)}, bf16[2,16,2048]{2,1,0:T(8,128)(2,1)S(1)}, u32[]{:S(2)}, u32[]{:S(2)}) collective-permute-start(bf16[2,16,2048]{2,1,0:T(8,128)(2,1)S(1)} %fusion.16), channel_id=1, source_target_pairs={{0,6},{1,7},{2,4},{3,5},{4,2},{5,3},{6,0},{7,1},{8,14},{9,15},{10,... | collective-permute-start | bytes 393224 | tf_op jit(solution)/shard_map/ppermute | solution.py:22
  119.6 3.6 %collective-permute-done.16 = bf16[2,16,2048]{2,1,0:T(8,128)(2,1)S(1)} collective-permute-done((bf16[2,16,2048]{2,1,0:T(8,128)(2,1)S(1)}, bf16[2,16,2048]{2,1,0:T(8,128)(2,1)S(1)}, u32[]{:S(2)}, u32[]{:S(2)}) %collective-permute-start.16) | collective-permute-done | bytes 131104 | tf_op jit(solution)/shard_map/ppermute | solution.py:22
  123.4 0.8 convolution_convert_fusion.5
  124.8 2.8 %collective-permute-done.17 = bf16[16,2048]{1,0:T(8,128)(2,1)S(1)} collective-permute-done((bf16[16,2048]{1,0:T(8,128)(2,1)S(1)}, bf16[16,2048]{1,0:T(8,128)(2,1)S(1)}, u32[]{:S(2)}, u32[]{:S(2)}) %collective-permute-start.17) | collective-permute-done | bytes 65568 | tf_op jit(solution)/shard_map/ppermute | solution.py:22
  (121 shorter events, 12.2 us)
Async XLA Ops:
  0.6 106.5 %copy-start = (bf16[512,2048]{1,0:T(8,128)(2,1)S(1)}, bf16[512,2048]{1,0:T(8,128)(2,1)}, u32[]{:S(2)}) copy-start(bf16[512,2048]{1,0:T(8,128)(2,1)} %param.33) | copy-start | bytes 6291460
  0.6 9.0 %copy-start.10 = (f32[2048]{0:T(1024)S(1)}, f32[2048]{0:T(1024)}, u32[]{:S(2)}) copy-start(f32[2048]{0:T(1024)} %param.19) | copy-start | bytes 24580
  0.7 8.9 %copy-start.2 = (bf16[2048,256]{1,0:T(8,128)(2,1)S(1)}, bf16[2048,256]{1,0:T(8,128)(2,1)}, u32[]{:S(2)}) copy-start(bf16[2048,256]{1,0:T(8,128)(2,1)} %param.20) | copy-start | bytes 3145732
  0.7 9.2 %copy-start.12 = (f32[256]{0:T(256)S(1)}, f32[256]{0:T(256)}, u32[]{:S(2)}) copy-start(f32[256]{0:T(256)} %param.23) | copy-start | bytes 3076
  0.7 9.4 %copy-start.4 = (bf16[256,160]{0,1:T(8,128)(2,1)S(1)}, bf16[256,160]{0,1:T(8,128)(2,1)}, u32[]{:S(2)}) copy-start(bf16[256,160]{0,1:T(8,128)(2,1)} %param.24) | copy-start | bytes 245764
  0.7 9.7 %copy-start.9 = (f32[16,256]{1,0:T(8,128)S(1)}, f32[16,256]{1,0:T(8,128)}, u32[]{:S(2)}) copy-start(f32[16,256]{1,0:T(8,128)} %param.27) | copy-start | bytes 49156
  1.6 7.8 %collective-permute-start = (bf16[3,2048]{1,0:T(4,128)(2,1)S(1)}, bf16[3,2048]{1,0:T(4,128)(2,1)S(1)}, u32[]{:S(2)}, u32[]{:S(2)}) collective-permute-start(bf16[3,2048]{1,0:T(4,128)(2,1)S(1)} %slice.69), channel_id=1, source_target_pairs={{0,8},{8,16},{16,24},{24,32},{32,40},{40,48},{48,56},{56,64},{64,7... | collective-permute-start | bytes 36872 | tf_op jit(solution)/shard_map/ppermute | solution.py:248
  7.4 20.5 %copy-start.11 = (s32[16]{0:T(128)}, s32[16]{0:T(128)S(1)}, u32[]{:S(2)}) copy-start(s32[16]{0:T(128)S(1)} %get-tuple-element.51) | copy-start | bytes 196
  7.5 37.2 %copy-start.16 = (s32[128]{0:T(128)}, s32[128]{0:T(128)S(1)}, u32[]{:S(2)}) copy-start(s32[128]{0:T(128)S(1)} %convert_reduce_fusion) | copy-start | bytes 1540
  7.6 14.5 %copy-start.5 = (bf16[128,256]{1,0:T(8,128)(2,1)S(1)}, bf16[128,256]{1,0:T(8,128)(2,1)}, u32[]{:S(2)}) copy-start(bf16[128,256]{1,0:T(8,128)(2,1)} %param.25) | copy-start | bytes 196612
  7.6 14.5 %copy-start.13 = (f32[256]{0:T(256)S(1)}, f32[256]{0:T(256)}, u32[]{:S(2)}) copy-start(f32[256]{0:T(256)} %param.26) | copy-start | bytes 3076
  9.4 12.6 %copy-start.6 = (bf16[128,256]{1,0:T(8,128)(2,1)}, bf16[128,256]{1,0:T(8,128)(2,1)S(1)}, u32[]{:S(2)}) copy-start(bf16[128,256]{1,0:T(8,128)(2,1)S(1)} %convolution_convert_fusion.3) | copy-start | bytes 196612
  10.2 1.4 %collective-permute-start.1 = (f32[128,160]{0,1:T(8,128)S(1)}, f32[128,160]{0,1:T(8,128)S(1)}, u32[]{:S(2)}, u32[]{:S(2)}) collective-permute-start(f32[128,160]{0,1:T(8,128)S(1)} %fusion.69), channel_id=1, source_target_pairs={{0,1},{1,0},{2,3},{3,2},{4,5},{5,4},{6,7},{7,6},{8,9},{9,8},{10,11... | collective-permute-start | bytes 245768 | tf_op jit(solution)/shard_map/ppermute | solution.py:22
  11.6 4.6 %collective-permute-start.2 = (f32[128,160]{0,1:T(8,128)S(1)}, f32[128,160]{0,1:T(8,128)S(1)}, u32[]{:S(2)}, u32[]{:S(2)}) collective-permute-start(f32[128,160]{0,1:T(8,128)S(1)} %add.303), channel_id=1, source_target_pairs={{0,2},{1,3},{2,0},{3,1},{4,6},{5,7},{6,4},{7,5},{8,10},{9,11},{10,... | collective-permute-start | bytes 245768 | tf_op jit(solution)/shard_map/ppermute | solution.py:22
  16.2 5.7 %collective-permute-start.3 = (f32[128,160]{0,1:T(8,128)S(1)}, f32[128,160]{0,1:T(8,128)S(1)}, u32[]{:S(2)}, u32[]{:S(2)}) collective-permute-start(f32[128,160]{0,1:T(8,128)S(1)} %add.304), channel_id=1, source_target_pairs={{0,6},{1,7},{2,4},{3,5},{4,2},{5,3},{6,0},{7,1},{8,14},{9,15},{10,... | collective-permute-start | bytes 245768 | tf_op jit(solution)/shard_map/ppermute | solution.py:22
  28.7 3.9 %collective-permute-start.4 = (f32[2,16,256]{2,1,0:T(8,128)S(1)}, f32[2,16,256]{2,1,0:T(8,128)S(1)}, u32[]{:S(2)}, u32[]{:S(2)}) collective-permute-start(f32[2,16,256]{2,1,0:T(8,128)S(1)} %pad_maximum_fusion.5), channel_id=1, source_target_pairs={{0,8},{8,0},{16,24},{24,16},{32,40},{40,32},{48,56},{56,48},{64,72... | collective-permute-start | bytes 98312 | tf_op jit(solution)/shard_map/ppermute | solution.py:22
  33.3 4.0 %collective-permute-start.5 = (f32[2,16,256]{2,1,0:T(8,128)S(1)}, f32[2,16,256]{2,1,0:T(8,128)S(1)}, u32[]{:S(2)}, u32[]{:S(2)}) collective-permute-start(f32[2,16,256]{2,1,0:T(8,128)S(1)} %pad_maximum_fusion.6), channel_id=1, source_target_pairs={{0,24},{8,16},{16,8},{24,0},{32,56},{40,48},{48,40},{56,32},{64,88... | collective-permute-start | bytes 98312 | tf_op jit(solution)/shard_map/ppermute | solution.py:22
  37.4 4.2 %collective-permute-start.6 = (f32[2,16,256]{2,1,0:T(8,128)S(1)}, f32[2,16,256]{2,1,0:T(8,128)S(1)}, u32[]{:S(2)}, u32[]{:S(2)}) collective-permute-start(f32[2,16,256]{2,1,0:T(8,128)S(1)} %pad_maximum_fusion.7), channel_id=1, source_target_pairs={{0,32},{8,40},{16,48},{24,56},{32,0},{40,8},{48,16},{56,24},{64,96... | collective-permute-start | bytes 98312 | tf_op jit(solution)/shard_map/ppermute | solution.py:22
  41.6 5.1 %collective-permute-start.7 = (f32[2,16,256]{2,1,0:T(8,128)S(1)}, f32[2,16,256]{2,1,0:T(8,128)S(1)}, u32[]{:S(2)}, u32[]{:S(2)}) collective-permute-start(f32[2,16,256]{2,1,0:T(8,128)S(1)} %pad_maximum_fusion.8), channel_id=1, source_target_pairs={{0,64},{8,72},{16,80},{24,88},{32,96},{40,104},{48,112},{56,120},{... | collective-permute-start | bytes 98312 | tf_op jit(solution)/shard_map/ppermute | solution.py:22
  46.7 7.0 %collective-permute-start.8 = (f32[2,16,256]{2,1,0:T(8,128)S(1)}, f32[2,16,256]{2,1,0:T(8,128)S(1)}, u32[]{:S(2)}, u32[]{:S(2)}) collective-permute-start(f32[2,16,256]{2,1,0:T(8,128)S(1)} %pad_maximum_fusion.9), channel_id=1, source_target_pairs={{0,192},{8,200},{16,208},{24,216},{32,224},{40,232},{48,240},{56,2... | collective-permute-start | bytes 98312 | tf_op jit(solution)/shard_map/ppermute | solution.py:22
  56.0 5.4 %copy-start.3 = (bf16[128,2048]{1,0:T(8,128)(2,1)S(1)}, bf16[128,2048]{1,0:T(8,128)(2,1)}, u32[]{:S(2)}) copy-start(bf16[128,2048]{1,0:T(8,128)(2,1)} %param.18) | copy-start | bytes 1572868
  56.0 5.4 %copy-start.15 = (f32[256]{0:T(256)S(1)}, f32[256]{0:T(256)}, u32[]{:S(2)}) copy-start(f32[256]{0:T(256)} %param.28) | copy-start | bytes 3076
  61.5 8.2 %copy-start.7 = (bf16[128,256]{1,0:T(8,128)(2,1)S(1)}, bf16[128,256]{1,0:T(8,128)(2,1)}, u32[]{:S(2)}) copy-start(bf16[128,256]{1,0:T(8,128)(2,1)} %copy-done.6) | copy-start | bytes 196612
  64.0 14.2 %copy-start.8 = (f32[2048]{0:T(1024)S(1)}, f32[2048]{0:T(1024)}, u32[]{:S(2)}) copy-start(f32[2048]{0:T(1024)} %param.30) | copy-start | bytes 24580
  64.0 1.8 %collective-permute-start.9 = (bf16[2,2,16,2048]{3,2,1,0:T(8,128)(2,1)S(1)}, bf16[2,2,16,2048]{3,2,1,0:T(8,128)(2,1)}, u32[]{:S(2)}, u32[]{:S(2)}) collective-permute-start(bf16[2,2,16,2048]{3,2,1,0:T(8,128)(2,1)S(1)} %dynamic-slice_bitcast_fusion.1), channel_id=1, source_target_pairs={{0,1},{1,0},{2,3},{3,2},{4,5},{5,4},{6,7},{7,6},{8,9},{9,8},{10,11... | collective-permute-start | bytes 786440 | tf_op jit(solution)/shard_map/ppermute | solution.py:22
  66.8 6.8 %collective-permute-start.10 = (bf16[2,16,2048]{2,1,0:T(8,128)(2,1)S(1)}, bf16[2,16,2048]{2,1,0:T(8,128)(2,1)S(1)}, u32[]{:S(2)}, u32[]{:S(2)}) collective-permute-start(bf16[2,16,2048]{2,1,0:T(8,128)(2,1)S(1)} %fusion.15), channel_id=1, source_target_pairs={{0,6},{1,7},{2,4},{3,5},{4,2},{5,3},{6,0},{7,1},{8,14},{9,15},{10,... | collective-permute-start | bytes 393224 | tf_op jit(solution)/shard_map/ppermute | solution.py:22
  73.7 4.4 %collective-permute-start.11 = (bf16[16,2048]{1,0:T(8,128)(2,1)S(1)}, bf16[16,2048]{1,0:T(8,128)(2,1)S(1)}, u32[]{:S(2)}, u32[]{:S(2)}) collective-permute-start(bf16[16,2048]{1,0:T(8,128)(2,1)S(1)} %fusion.30), channel_id=1, source_target_pairs={{0,2},{1,3},{2,0},{3,1},{4,6},{5,7},{6,4},{7,5},{8,10},{9,11},{10,... | collective-permute-start | bytes 196616 | tf_op jit(solution)/shard_map/ppermute | solution.py:22
  73.8 6.2 %collective-permute-start.18 = (bf16[16,19,256]{2,1,0:T(8,128)(2,1)S(1)}, bf16[16,19,256]{2,1,0:T(8,128)(2,1)S(1)}, u32[]{:S(2)}, u32[]{:S(2)}) collective-permute-start(bf16[16,19,256]{2,1,0:T(8,128)(2,1)S(1)} %pad_maximum_fusion.2), channel_id=1, source_target_pairs={{0,8},{8,0},{16,24},{24,16},{32,40},{40,32},{48,56},{56,48},{64,72... | collective-permute-start | bytes 466952 | tf_op jit(solution)/shard_map/ppermute | solution.py:22
  78.3 4.9 %collective-permute-start.12 = (bf16[16,2048]{1,0:T(8,128)(2,1)S(1)}, bf16[16,2048]{1,0:T(8,128)(2,1)S(1)}, u32[]{:S(2)}, u32[]{:S(2)}) collective-permute-start(bf16[16,2048]{1,0:T(8,128)(2,1)S(1)} %multiply_convert_fusion), channel_id=1, source_target_pairs={{0,2},{1,3},{2,0},{3,1},{4,6},{5,7},{6,4},{7,5},{8,10},{9,11},{10,... | collective-permute-start | bytes 196616 | tf_op jit(solution)/shard_map/ppermute | solution.py:22
  80.1 6.9 %collective-permute-start.19 = (bf16[16,19,256]{2,1,0:T(8,128)(2,1)S(1)}, bf16[16,19,256]{2,1,0:T(8,128)(2,1)S(1)}, u32[]{:S(2)}, u32[]{:S(2)}) collective-permute-start(bf16[16,19,256]{2,1,0:T(8,128)(2,1)S(1)} %fusion.64), channel_id=1, source_target_pairs={{0,24},{8,16},{16,8},{24,0},{32,56},{40,48},{48,40},{56,32},{64,88... | collective-permute-start | bytes 466952 | tf_op jit(solution)/shard_map/ppermute | solution.py:22
  83.3 6.3 %collective-permute-start.13 = (bf16[2,16,2048]{2,1,0:T(8,128)(2,1)S(1)}, bf16[2,16,2048]{2,1,0:T(8,128)(2,1)S(1)}, u32[]{:S(2)}, u32[]{:S(2)}) collective-permute-start(bf16[2,16,2048]{2,1,0:T(8,128)(2,1)S(1)} %pad_maximum_fusion.4), channel_id=1, source_target_pairs={{0,6},{1,7},{2,4},{3,5},{4,2},{5,3},{6,0},{7,1},{8,14},{9,15},{10,... | collective-permute-start | bytes 393224 | tf_op jit(solution)/shard_map/ppermute | solution.py:22
  87.0 5.8 %collective-permute-start.20 = (bf16[16,19,256]{2,1,0:T(8,128)(2,1)S(1)}, bf16[16,19,256]{2,1,0:T(8,128)(2,1)S(1)}, u32[]{:S(2)}, u32[]{:S(2)}) collective-permute-start(bf16[16,19,256]{2,1,0:T(8,128)(2,1)S(1)} %add.351), channel_id=1, source_target_pairs={{0,32},{8,40},{16,48},{24,56},{32,0},{40,8},{48,16},{56,24},{64,96... | collective-permute-start | bytes 466952 | tf_op jit(solution)/shard_map/ppermute | solution.py:22
  89.6 17.0 %collective-permute-start.14 = (bf16[2,2,16,2048]{3,2,1,0:T(8,128)(2,1)S(1)}, bf16[2,2,16,2048]{3,2,1,0:T(8,128)(2,1)S(1)}, u32[]{:S(2)}, u32[]{:S(2)}) collective-permute-start(bf16[2,2,16,2048]{3,2,1,0:T(8,128)(2,1)S(1)} %pad_maximum_fusion.1), channel_id=1, source_target_pairs={{0,1},{1,0},{2,3},{3,2},{4,5},{5,4},{6,7},{7,6},{8,9},{9,8},{10,11... | collective-permute-start | bytes 786440 | tf_op jit(solution)/shard_map/ppermute | solution.py:22
  92.8 8.2 %collective-permute-start.21 = (bf16[16,19,256]{2,1,0:T(8,128)(2,1)S(1)}, bf16[16,19,256]{2,1,0:T(8,128)(2,1)S(1)}, u32[]{:S(2)}, u32[]{:S(2)}) collective-permute-start(bf16[16,19,256]{2,1,0:T(8,128)(2,1)S(1)} %add.352), channel_id=1, source_target_pairs={{0,64},{8,72},{16,80},{24,88},{32,96},{40,104},{48,112},{56,120},{... | collective-permute-start | bytes 466952 | tf_op jit(solution)/shard_map/ppermute | solution.py:22
  95.6 11.1 %copy-start.1 = (bf16[2048,512]{1,0:T(8,128)(2,1)S(1)}, bf16[2048,512]{1,0:T(8,128)(2,1)}, u32[]{:S(2)}) copy-start(bf16[2048,512]{1,0:T(8,128)(2,1)} %param.31) | copy-start | bytes 6291460
  101.8 13.6 %collective-permute-start.22 = (bf16[16,19,256]{2,1,0:T(8,128)(2,1)}, bf16[16,19,256]{2,1,0:T(8,128)(2,1)}, u32[]{:S(2)}, u32[]{:S(2)}) collective-permute-start(bf16[16,19,256]{2,1,0:T(8,128)(2,1)} %add.353), channel_id=1, source_target_pairs={{0,192},{8,200},{16,208},{24,216},{32,224},{40,232},{48,240},{56,2... | collective-permute-start | bytes 466952 | tf_op jit(solution)/shard_map/ppermute | solution.py:22
  107.2 2.6 %copy-start.17 = (s32[128]{0:T(128)S(1)}, s32[128]{0:T(128)}, u32[]{:S(2)}) copy-start(s32[128]{0:T(128)} %copy-done.16) | copy-start | bytes 1540
  109.6 9.8 %copy-start.14 = (s32[4]{0:T(128)S(1)}, s32[4]{0:T(128)}, u32[]{:S(2)}) copy-start(s32[4]{0:T(128)} %param.35) | copy-start | bytes 52
  109.7 6.8 %collective-permute-start.15 = (bf16[2,2,16,2048]{3,2,1,0:T(8,128)(2,1)S(1)}, bf16[2,2,16,2048]{3,2,1,0:T(8,128)(2,1)S(1)}, u32[]{:S(2)}, u32[]{:S(2)}) collective-permute-start(bf16[2,2,16,2048]{3,2,1,0:T(8,128)(2,1)S(1)} %dynamic-slice_bitcast_fusion), channel_id=1, source_target_pairs={{0,1},{1,0},{2,3},{3,2},{4,5},{5,4},{6,7},{7,6},{8,9},{9,8},{10,11... | collective-permute-start | bytes 786440 | tf_op jit(solution)/shard_map/ppermute | solution.py:22
  116.6 6.7 %collective-permute-start.16 = (bf16[2,16,2048]{2,1,0:T(8,128)(2,1)S(1)}, bf16[2,16,2048]{2,1,0:T(8,128)(2,1)S(1)}, u32[]{:S(2)}, u32[]{:S(2)}) collective-permute-start(bf16[2,16,2048]{2,1,0:T(8,128)(2,1)S(1)} %fusion.16), channel_id=1, source_target_pairs={{0,6},{1,7},{2,4},{3,5},{4,2},{5,3},{6,0},{7,1},{8,14},{9,15},{10,... | collective-permute-start | bytes 393224 | tf_op jit(solution)/shard_map/ppermute | solution.py:22
  123.3 4.4 %collective-permute-start.17 = (bf16[16,2048]{1,0:T(8,128)(2,1)S(1)}, bf16[16,2048]{1,0:T(8,128)(2,1)S(1)}, u32[]{:S(2)}, u32[]{:S(2)}) collective-permute-start(bf16[16,2048]{1,0:T(8,128)(2,1)S(1)} %fusion.31), channel_id=1, source_target_pairs={{0,2},{1,3},{2,0},{3,1},{4,6},{5,7},{6,4},{7,5},{8,10},{9,11},{10,... | collective-permute-start | bytes 196616 | tf_op jit(solution)/shard_map/ppermute | solution.py:22

commit v7 on v6

--- a/solution.py
+++ b/solution.py
@@ -100,21 +100,36 @@
     return buf.reshape((devices * x.shape[0], x.shape[1]))
 
 
+def fin_round(buf, mask, tie):
+    got = swap(buf, "seq", mask)
+    got, tie = lax.optimization_barrier((got, tie))
+    return buf + got, tie
+
+
 def rms_norm(values, gain):
     scale = lax.rsqrt(jnp.mean(values * values, axis=-1, keepdims=True) + EPSILON)
     return values * scale * gain
 
 
-def block_summary_kernel(da_ref, dr_ref, send_ref, atot_ref):
+def block_summary_kernel(da_ref, dr_ref, endf_ref, pid_ref, send_ref, atot_ref, fs_ref, fd_ref):
     steps = da_ref.shape[0]
+    fs_ref[...] = jnp.zeros(fs_ref.shape, jnp.float32)
+    fd_ref[...] = jnp.zeros(fd_ref.shape, jnp.float32)
 
     def chunk(c, carry):
         state, acum = carry
         base = c * 8
         for i in range(8):
-            da = da_ref[base + i]
-            state = da * state + dr_ref[base + i]
+            t = base + i
+            da = da_ref[t]
+            state = da * state + dr_ref[t]
             acum = da * acum
+
+            @pl.when(endf_ref[t] != 0)
+            def _():
+                fs_ref[pid_ref[t]] = state
+                fd_ref[pid_ref[t]] = acum
+
         return state, acum
 
     zero = jnp.zeros(send_ref.shape, jnp.float32)
@@ -124,10 +139,9 @@
     atot_ref[...] = acum
 
 
-def block_output_kernel(da_ref, dr_ref, om_ref, sin_ref, endf_ref, pid_ref, y_ref, fin_ref):
+def block_output_kernel(da_ref, dr_ref, om_ref, sin_ref, y_ref):
     steps = da_ref.shape[0]
     width = y_ref.shape[1]
-    fin_ref[...] = jnp.zeros(fin_ref.shape, jnp.float32)
     row_ids = lax.broadcasted_iota(jnp.int32, (8, width), 0)
 
     def chunk(c, state):
@@ -138,46 +152,40 @@
             state = da_ref[t] * state + dr_ref[t]
             here = jnp.sum(om_ref[t] * state, axis=0, keepdims=True)
             rows = jnp.where(row_ids == i, here, rows)
-
-            @pl.when(endf_ref[t] != 0)
-            def _():
-                fin_ref[pid_ref[t]] = state
-
         y_ref[pl.ds(base, 8), :] = rows
         return state
 
     lax.fori_loop(0, steps // 8, chunk, sin_ref[...])
 
 
-def block_summary(da, dr):
+def block_summary(da, dr, endf, pid, prompts):
     _, n, e = da.shape
     vmem = pl.BlockSpec(memory_space=pltpu.VMEM)
+    smem = pl.BlockSpec(memory_space=pltpu.SMEM)
     return pl.pallas_call(
         block_summary_kernel,
         out_shape=(
             jax.ShapeDtypeStruct((n, e), jnp.float32),
             jax.ShapeDtypeStruct((n, e), jnp.float32),
+            jax.ShapeDtypeStruct((prompts, n, e), jnp.float32),
+            jax.ShapeDtypeStruct((prompts, n, e), jnp.float32),
         ),
-        in_specs=[vmem, vmem],
-        out_specs=(vmem, vmem),
+        in_specs=[vmem, vmem, smem, smem],
+        out_specs=(vmem, vmem, vmem, vmem),
         interpret=INTERPRET,
-    )(da, dr)
-
-
-def block_output(da, dr, om, sin, endf, pid, prompts):
+    )(da, dr, endf, pid)
+
+
+def block_output(da, dr, om, sin):
     t, n, e = da.shape
     vmem = pl.BlockSpec(memory_space=pltpu.VMEM)
-    smem = pl.BlockSpec(memory_space=pltpu.SMEM)
     return pl.pallas_call(
         block_output_kernel,
-        out_shape=(
-            jax.ShapeDtypeStruct((t, e), jnp.float32),
-            jax.ShapeDtypeStruct((prompts, n, e), jnp.float32),
-        ),
-        in_specs=[vmem, vmem, vmem, vmem, smem, smem],
-        out_specs=(vmem, vmem),
+        out_shape=jax.ShapeDtypeStruct((t, e), jnp.float32),
+        in_specs=[vmem, vmem, vmem, vmem],
+        out_specs=vmem,
         interpret=INTERPRET,
-    )(da, dr, om, sin, endf, pid)
+    )(da, dr, om, sin)
 
 
 def entering_state(a_blk, s_blk, axis):
@@ -279,13 +287,13 @@
     decay = jnp.exp(step_size[:, None, :] * decay_rates[None, :, :]) * carry_on[:, None, None]
     drive = (step_size * conv_float)[:, None, :] * in_map[:, :, None]
     out_wide = jnp.broadcast_to(out_map[:, :, None], decay.shape)
-    s_blk, a_blk = block_summary(decay, drive)
-    state_in = entering_state(a_blk, s_blk, "seq")
     end_flag = ends_here.astype(jnp.int32)
     slot_of = jnp.minimum(prompt_of, prompts - 1).astype(jnp.int32)
-    mixer_y, final_part = block_output(decay, drive, out_wide, state_in, end_flag, slot_of, prompts)
-    mixer_y = mixer_y + d_skip[None, :] * conv_float
-    gated = (mixer_y * jax.nn.silu(z_branch.astype(jnp.float32))).astype(jnp.bfloat16)
+    s_blk, a_blk, end_state, end_decay = block_summary(decay, drive, end_flag, slot_of, prompts)
+    state_in = entering_state(a_blk, s_blk, "seq")
+    final_part = end_state + end_decay * state_in[None]
+    mixer_y = block_output(decay, drive, out_wide, state_in)
+    fin_masks = [mask for mask, _ in basis_of("seq")]
     ends_local = (prompt_end - 1 >= first_row) & (prompt_end - 1 < first_row + block_len)
     lag_ids = jnp.arange(edge_len, dtype=jnp.int32)
     ext_rows = jnp.arange(block_len + edge_len, dtype=jnp.int32)
@@ -300,7 +308,27 @@
     handed = jnp.concatenate(
         [final_part.astype(jnp.bfloat16), edge_part.astype(jnp.bfloat16)], axis=1
     )
-    handed = butterfly_sum(handed, "seq", jnp.bfloat16).astype(jnp.float32)
+    handed, mixer_y = fin_round(handed, fin_masks[0], mixer_y)
+    mixer_y = mixer_y + d_skip[None, :] * conv_float
+    gated = (mixer_y * jax.nn.silu(z_branch.astype(jnp.float32))).astype(jnp.bfloat16)
+    mixed_part = jnp.dot(gated, w_out, preferred_element_type=jnp.float32).astype(jnp.bfloat16)
+    handed, mixed_part = fin_round(handed, fin_masks[1], mixed_part)
+    mixed_rows = scatter_rows(mixed_part, "tp", jnp.bfloat16)
+    handed, mixed_rows = fin_round(handed, fin_masks[2], mixed_rows)
+    token_rows = lax.dynamic_slice_in_dim(tokens, tp_pos * row_count, row_count, 0)
+    residual_rows = token_rows.astype(jnp.float32) + mixed_rows
+    normed_rows = rms_norm(residual_rows, mlp_gain).astype(jnp.bfloat16)
+    normed_two = gather_rows(normed_rows, "tp")
+    handed, normed_two = fin_round(handed, fin_masks[3], normed_two)
+    gate_val = jnp.dot(normed_two, w_gate, preferred_element_type=jnp.float32)
+    up_val = jnp.dot(normed_two, w_up, preferred_element_type=jnp.float32)
+    hidden = (jax.nn.silu(gate_val) * up_val).astype(jnp.bfloat16)
+    mlp_part = jnp.dot(hidden, w_down, preferred_element_type=jnp.float32).astype(jnp.bfloat16)
+    handed, mlp_part = fin_round(handed, fin_masks[4], mlp_part)
+    for mask in fin_masks[5:]:
+        handed = handed + swap(handed, "seq", mask)
+    handed = handed.astype(jnp.float32)
+    mlp_share = scatter_rows(mlp_part, "tp", jnp.bfloat16)
     final_all = handed[:, :state_dim]
     edge_all = handed[:, state_dim:]
     chooser = (request_prompt[:, None] == prompt_ids[None, :]).astype(jnp.float32)
@@ -308,23 +336,6 @@
     req_edges = jnp.einsum(
         "rp,pje->rje", chooser, edge_all, precision=lax.Precision.HIGHEST
     ).astype(jnp.bfloat16)
-    mixed_rows = scatter_rows(
-        jnp.dot(gated, w_out, preferred_element_type=jnp.float32).astype(jnp.bfloat16),
-        "tp",
-        jnp.bfloat16,
-    )
-    token_rows = lax.dynamic_slice_in_dim(tokens, tp_pos * row_count, row_count, 0)
-    residual_rows = token_rows.astype(jnp.float32) + mixed_rows
-    normed_rows = rms_norm(residual_rows, mlp_gain).astype(jnp.bfloat16)
-    normed_two = gather_rows(normed_rows, "tp")
-    gate_val = jnp.dot(normed_two, w_gate, preferred_element_type=jnp.float32)
-    up_val = jnp.dot(normed_two, w_up, preferred_element_type=jnp.float32)
-    hidden = (jax.nn.silu(gate_val) * up_val).astype(jnp.bfloat16)
-    mlp_share = scatter_rows(
-        jnp.dot(hidden, w_down, preferred_element_type=jnp.float32).astype(jnp.bfloat16),
-        "tp",
-        jnp.bfloat16,
-    )
     live_rows = lax.dynamic_slice_in_dim(is_live, tp_pos * row_count, row_count, 0).astype(
         jnp.float32
     )

time: 129 us -> 144 us (1.12)
  waiting for transfers between devices: 49.9 us -> 60.1 us
  other arithmetic: 15.4 us -> 17.4 us
    ppermute x22, waiting for transfers between devices: 49.9 us -> 60.1 us  [swap(): return lax.ppermute(x, axis, [(i, i ^ bit) for i in range(devices)])]
    add x0 -> x5, other arithmetic: none -> 4.06 us  [fin_round(): return (buf + got, tie)]
    add x8 -> x3, other arithmetic: 1.98 us -> 0.03 us  [butterfly_sum(): x = x + swap(x.astype(send_dtype), axis, mask).astype(x.dtype)]
  transfers between devices with their start and end apart: 23 -> 23, of which waited for: 19 -> 20; matrix products, arithmetic and copies ran while one was open for 13% -> 14% of each run, Pallas kernels for 0% -> 3%
where the time goes in v7:
time: 144 us; the launch traced here: 143 us
  waiting for transfers between devices  60.1 us (42%)
  starting transfers between devices  39.8 us (28%)
  other arithmetic  17.4 us (12%)
  matrix products  8.96 us (6%)
  Pallas kernels  8.56 us (6%)
  local copies, waits for them, and re-layouts  6.54 us (5%)
    ppermute x22, waiting for transfers between devices, swap(): return lax.ppermute(x, axis, [(i, i ^ bit) for i in range(devices)])  60.1 us
    ppermute x22, starting transfers between devices, swap(): return lax.ppermute(x, axis, [(i, i ^ bit) for i in range(devices)])  38.2 us
    pallas_call x1, Pallas kernels, block_summary(): pl.pallas_call(block_summary_kernel, out_shape=(jax.ShapeDtypeStruct((n,...  4.33 us
    pallas_call x1, Pallas kernels, block_output(): pl.pallas_call(block_output_kernel, out_shape=jax.ShapeDtypeStruct((t, e)...  4.23 us
    add x5, other arithmetic, fin_round(): return (buf + got, tie)  4.06 us
  transfers between devices with their start and end apart: 23, of which 20 were waited for; matrix products, arithmetic and copies ran while one was open for 14% of the time, Pallas kernels for 3%

profile of v7, /device:TPU:40, one launch (start us, length us, event | category | flops | bytes accessed | tf_op | source)
XLA Modules:
  0.0 142.6 jit_solution(6785760823799508498)
XLA Ops:
  0.7 0.9 slice.69
  1.6 1.7 %collective-permute-start = (bf16[3,2048]{1,0:T(4,128)(2,1)S(1)}, bf16[3,2048]{1,0:T(4,128)(2,1)S(1)}, u32[]{:S(2)}, u32[]{:S(2)}) collective-permute-start(bf16[3,2048]{1,0:T(4,128)(2,1)S(1)} %slice.69), channel_id=1, source_target_pairs={{0,8},{8,16},{16,24},{24,32},{32,40},{40,48},{48,56},{56,64},{64,7... | collective-permute-start | bytes 36872 | tf_op jit(solution)/shard_map/ppermute | solution.py:256
  3.3 1.2 fusion.1
  7.0 0.8 fusion.73
  7.8 1.8 %convolution_convert_fusion.3 = bf16[128,256]{1,0:T(8,128)(2,1)S(1)} fusion(bf16[2048,256]{1,0:T(8,128)(2,1)} %param.20, bf16[128,2048]{1,0:T(8,128)(2,1)} %param.18, f32[2048]{0:T(1024)} %param.19, f32[128]{0:T(128)S(1)} %add_rsqrt_fusion.2), kind=kOutput, calls=%fused_computation.8 | convolution fusion | flops 135299072 | bytes 1647104 | tf_op jit(solution)/shard_map/dot_general | solution.py:263
  11.8 1.6 %collective-permute-start.2 = (f32[128,160]{0,1:T(8,128)S(1)}, f32[128,160]{0,1:T(8,128)S(1)}, u32[]{:S(2)}, u32[]{:S(2)}) collective-permute-start(f32[128,160]{0,1:T(8,128)S(1)} %add.318), channel_id=1, source_target_pairs={{0,2},{1,3},{2,0},{3,1},{4,6},{5,7},{6,4},{7,5},{8,10},{9,11},{10,... | collective-permute-start | bytes 245768 | tf_op jit(solution)/shard_map/ppermute | solution.py:22
  13.5 2.9 %collective-permute-done.2 = f32[128,160]{0,1:T(8,128)S(1)} collective-permute-done((f32[128,160]{0,1:T(8,128)S(1)}, f32[128,160]{0,1:T(8,128)S(1)}, u32[]{:S(2)}, u32[]{:S(2)}) %collective-permute-start.2) | collective-permute-done | bytes 81952 | tf_op jit(solution)/shard_map/ppermute | solution.py:22
  16.4 2.8 %collective-permute-start.3 = (f32[128,160]{0,1:T(8,128)S(1)}, f32[128,160]{0,1:T(8,128)S(1)}, u32[]{:S(2)}, u32[]{:S(2)}) collective-permute-start(f32[128,160]{0,1:T(8,128)S(1)} %add.319), channel_id=1, source_target_pairs={{0,6},{1,7},{2,4},{3,5},{4,2},{5,3},{6,0},{7,1},{8,14},{9,15},{10,... | collective-permute-start | bytes 245768 | tf_op jit(solution)/shard_map/ppermute | solution.py:22
  19.8 2.4 %collective-permute-done.3 = f32[128,160]{0,1:T(8,128)S(1)} collective-permute-done((f32[128,160]{0,1:T(8,128)S(1)}, f32[128,160]{0,1:T(8,128)S(1)}, u32[]{:S(2)}, u32[]{:S(2)}) %collective-permute-start.3) | collective-permute-done | bytes 81952 | tf_op jit(solution)/shard_map/ppermute | solution.py:22
  22.6 2.4 %exponential_multiply_fusion = (f32[128,16,256]{2,1,0:T(8,128)}, f32[128,16,256]{2,1,0:T(8,128)}) fusion(f32[128]{0:T(128)S(1)} %convert_subtract_fusion, f32[16,256]{1,0:T(8,128)S(1)} %exponential_negate_fusion, f32[128,256]{1,0:T(8,128)S(1)} %get-tuple-element.74, f32[128,16]{1,0:T(8,128)S(1)} %copy.51, f32[128,256]{1,0:T(8,128)S(1)} %get-tuple-element.73), kind=kLoop, calls=%fused_computation.2 | loop fusion | flops 1572864 | bytes 4481536 | tf_op jit(solution)/shard_map/mul | solution.py:287
  25.0 4.3 %shard_map.193 = (f32[16,256]{1,0:T(8,128)}, f32[16,256]{1,0:T(8,128)}, f32[16,16,256]{2,1,0:T(8,128)}, f32[16,16,256]{2,1,0:T(8,128)}) custom-call(f32[128,16,256]{2,1,0:T(8,128)} %get-tuple-element.75.da_ref, f32[128,16,256]{2,1,0:T(8,128)} %get-tuple-element.76.dr_ref, s32[128]{0:T(128)} %convert_element_type.193.endf_ref, s32[128]{0:T(128)} %broadcast_minimum_fusion.pid_ref), custom_call_target="tpu_custom_call" | custom-call | tf_op jit(solution)/shard_map/pallas_call | solution.py:165
  30.5 3.5 %collective-permute-done.4 = f32[2,16,256]{2,1,0:T(8,128)S(1)} collective-permute-done((f32[2,16,256]{2,1,0:T(8,128)S(1)}, f32[2,16,256]{2,1,0:T(8,128)S(1)}, u32[]{:S(2)}, u32[]{:S(2)}) %collective-permute-start.4) | collective-permute-done | bytes 32800 | tf_op jit(solution)/shard_map/ppermute | solution.py:22
  34.7 1.4 collective-permute-start.5
  36.1 2.6 %collective-permute-done.5 = f32[2,16,256]{2,1,0:T(8,128)S(1)} collective-permute-done((f32[2,16,256]{2,1,0:T(8,128)S(1)}, f32[2,16,256]{2,1,0:T(8,128)S(1)}, u32[]{:S(2)}, u32[]{:S(2)}) %collective-permute-start.5) | collective-permute-done | bytes 32800 | tf_op jit(solution)/shard_map/ppermute | solution.py:22
  39.4 3.5 %collective-permute-done.6 = f32[2,16,256]{2,1,0:T(8,128)S(1)} collective-permute-done((f32[2,16,256]{2,1,0:T(8,128)S(1)}, f32[2,16,256]{2,1,0:T(8,128)S(1)}, u32[]{:S(2)}, u32[]{:S(2)}) %collective-permute-start.6) | collective-permute-done | bytes 32800 | tf_op jit(solution)/shard_map/ppermute | solution.py:22
  42.9 3.2 %collective-permute-start.7 = (f32[2,16,256]{2,1,0:T(8,128)S(1)}, f32[2,16,256]{2,1,0:T(8,128)S(1)}, u32[]{:S(2)}, u32[]{:S(2)}) collective-permute-start(f32[2,16,256]{2,1,0:T(8,128)S(1)} %pad_maximum_fusion.8), channel_id=1, source_target_pairs={{0,64},{8,72},{16,80},{24,88},{32,96},{40,104},{48,112},{56,120},{... | collective-permute-start | bytes 98312 | tf_op jit(solution)/shard_map/ppermute | solution.py:22
  46.1 1.9 %collective-permute-done.7 = f32[2,16,256]{2,1,0:T(8,128)S(1)} collective-permute-done((f32[2,16,256]{2,1,0:T(8,128)S(1)}, f32[2,16,256]{2,1,0:T(8,128)S(1)}, u32[]{:S(2)}, u32[]{:S(2)}) %collective-permute-start.7) | collective-permute-done | bytes 32800 | tf_op jit(solution)/shard_map/ppermute | solution.py:22
  48.0 5.1 %collective-permute-start.8 = (f32[2,16,256]{2,1,0:T(8,128)S(1)}, f32[2,16,256]{2,1,0:T(8,128)S(1)}, u32[]{:S(2)}, u32[]{:S(2)}) collective-permute-start(f32[2,16,256]{2,1,0:T(8,128)S(1)} %pad_maximum_fusion.9), channel_id=1, source_target_pairs={{0,192},{8,200},{16,208},{24,216},{32,224},{40,232},{48,240},{56,2... | collective-permute-start | bytes 98312 | tf_op jit(solution)/shard_map/ppermute | solution.py:22
  53.5 1.6 %collective-permute-done.8 = f32[2,16,256]{2,1,0:T(8,128)S(1)} collective-permute-done((f32[2,16,256]{2,1,0:T(8,128)S(1)}, f32[2,16,256]{2,1,0:T(8,128)S(1)}, u32[]{:S(2)}, u32[]{:S(2)}) %collective-permute-start.8) | collective-permute-done | bytes 32800 | tf_op jit(solution)/shard_map/ppermute | solution.py:22
  55.1 1.1 add_convert_fusion
  56.2 2.5 %collective-permute-start.9 = (bf16[16,19,256]{2,1,0:T(8,128)(2,1)S(1)}, bf16[16,19,256]{2,1,0:T(8,128)(2,1)S(1)}, u32[]{:S(2)}, u32[]{:S(2)}) collective-permute-start(bf16[16,19,256]{2,1,0:T(8,128)(2,1)S(1)} %pad_maximum_fusion.2), channel_id=1, source_target_pairs={{0,8},{8,0},{16,24},{24,16},{32,40},{40,32},{48,56},{56,48},{64,72... | collective-permute-start | bytes 466952 | tf_op jit(solution)/shard_map/ppermute | solution.py:22
  59.3 1.7 %broadcast_in_dim.26.om_ref = f32[128,16,256]{2,1,0:T(8,128)} broadcast(f32[128,16]{1,0:T(8,128)S(1)} %copy.53), dimensions={0,1} | broadcast | bytes 2105344 | tf_op jit(solution)/shard_map/broadcast_in_dim | solution.py:289
  61.0 4.2 %shard_map.194 = f32[128,256]{1,0:T(8,128)} custom-call(f32[128,16,256]{2,1,0:T(8,128)} %get-tuple-element.75.da_ref, f32[128,16,256]{2,1,0:T(8,128)} %get-tuple-element.76.dr_ref, f32[128,16,256]{2,1,0:T(8,128)} %broadcast_in_dim.26.om_ref, f32[16,256]{1,0:T(8,128)} %add_select_fusion.sin_ref), custom_call_target="tpu_custom_call" | custom-call | tf_op jit(solution)/shard_map/pallas_call | solution.py:182
  65.3 2.3 %collective-permute-start.10 = (bf16[16,19,256]{2,1,0:T(8,128)(2,1)S(1)}, bf16[16,19,256]{2,1,0:T(8,128)(2,1)}, u32[]{:S(2)}, u32[]{:S(2)}) collective-permute-start(bf16[16,19,256]{2,1,0:T(8,128)(2,1)S(1)} %fusion.70), channel_id=1, source_target_pairs={{0,24},{8,16},{16,8},{24,0},{32,56},{40,48},{48,40},{56,32},{64,88... | collective-permute-start | bytes 466952 | tf_op jit(solution)/shard_map/ppermute | solution.py:22
  67.6 2.4 %convolution_convert_fusion.1 = bf16[128,2048]{1,0:T(8,128)(2,1)S(1)} fusion(bf16[256,2048]{1,0:T(8,128)(2,1)} %param.29, f32[128,256]{1,0:T(8,128)} %shard_map.194, bf16[128,256]{1,0:T(8,128)(2,1)S(1)} %multiply_convert_fusion.3, bf16[2048,256]{1,0:T(8,128)(2,1)} %param.21, bf16[128,2048]{1,0:T(8,128)(2,1)S(1)} %copy-done.3, f32[2048]{0:T(1024)S(1)} %copy-done.9, ...), kind=kOutput, calls=%fused_computation.1 | convolution fusion | flops 270106624 | bytes 3352064 | tf_op jit(solution)/shard_map/dot_general | solution.py:314
  70.0 1.3 collective-permute-done.10
  72.1 1.9 %collective-permute-done.12 = bf16[2,2,16,2048]{3,2,1,0:T(8,128)(2,1)} collective-permute-done((bf16[2,2,16,2048]{3,2,1,0:T(8,128)(2,1)}, bf16[2,2,16,2048]{3,2,1,0:T(8,128)(2,1)}, u32[]{:S(2)}, u32[]{:S(2)}) %collective-permute-start.12) | collective-permute-done | bytes 262176 | tf_op jit(solution)/shard_map/ppermute | solution.py:22
  73.9 1.1 convert_add_fusion.1
  75.1 2.8 %collective-permute-start.13 = (bf16[2,16,2048]{2,1,0:T(8,128)(2,1)S(1)}, bf16[2,16,2048]{2,1,0:T(8,128)(2,1)S(1)}, u32[]{:S(2)}, u32[]{:S(2)}) collective-permute-start(bf16[2,16,2048]{2,1,0:T(8,128)(2,1)S(1)} %fusion.9), channel_id=1, source_target_pairs={{0,6},{1,7},{2,4},{3,5},{4,2},{5,3},{6,0},{7,1},{8,14},{9,15},{10,... | collective-permute-start | bytes 393224 | tf_op jit(solution)/shard_map/ppermute | solution.py:22
  77.9 4.0 %collective-permute-done.13 = bf16[2,16,2048]{2,1,0:T(8,128)(2,1)S(1)} collective-permute-done((bf16[2,16,2048]{2,1,0:T(8,128)(2,1)S(1)}, bf16[2,16,2048]{2,1,0:T(8,128)(2,1)S(1)}, u32[]{:S(2)}, u32[]{:S(2)}) %collective-permute-start.13) | collective-permute-done | bytes 131104 | tf_op jit(solution)/shard_map/ppermute | solution.py:22
  82.1 1.1 add.352
  83.6 2.7 %collective-permute-done.14 = bf16[16,2048]{1,0:T(8,128)(2,1)S(1)} collective-permute-done((bf16[16,2048]{1,0:T(8,128)(2,1)S(1)}, bf16[16,2048]{1,0:T(8,128)(2,1)S(1)}, u32[]{:S(2)}, u32[]{:S(2)}) %collective-permute-start.14) | collective-permute-done | bytes 65568 | tf_op jit(solution)/shard_map/ppermute | solution.py:22
  86.3 3.2 %collective-permute-done.11 = bf16[16,19,256]{2,1,0:T(8,128)(2,1)S(1)} collective-permute-done((bf16[16,19,256]{2,1,0:T(8,128)(2,1)S(1)}, bf16[16,19,256]{2,1,0:T(8,128)(2,1)S(1)}, u32[]{:S(2)}, u32[]{:S(2)}) %collective-permute-start.11) | collective-permute-done | bytes 155680 | tf_op jit(solution)/shard_map/ppermute | solution.py:22
  90.3 1.8 %collective-permute-start.16 = (bf16[16,2048]{1,0:T(8,128)(2,1)S(1)}, bf16[16,2048]{1,0:T(8,128)(2,1)S(1)}, u32[]{:S(2)}, u32[]{:S(2)}) collective-permute-start(bf16[16,2048]{1,0:T(8,128)(2,1)S(1)} %multiply_convert_fusion.2), channel_id=1, source_target_pairs={{0,2},{1,3},{2,0},{3,1},{4,6},{5,7},{6,4},{7,5},{8,10},{9,11},{10,... | collective-permute-start | bytes 196616 | tf_op jit(solution)/shard_map/ppermute | solution.py:22
  92.1 2.5 %collective-permute-done.16 = bf16[16,2048]{1,0:T(8,128)(2,1)S(1)} collective-permute-done((bf16[16,2048]{1,0:T(8,128)(2,1)S(1)}, bf16[16,2048]{1,0:T(8,128)(2,1)S(1)}, u32[]{:S(2)}, u32[]{:S(2)}) %collective-permute-start.16) | collective-permute-done | bytes 65568 | tf_op jit(solution)/shard_map/ppermute | solution.py:22
  94.7 2.8 %collective-permute-start.17 = (bf16[2,16,2048]{2,1,0:T(8,128)(2,1)S(1)}, bf16[2,16,2048]{2,1,0:T(8,128)(2,1)S(1)}, u32[]{:S(2)}, u32[]{:S(2)}) collective-permute-start(bf16[2,16,2048]{2,1,0:T(8,128)(2,1)S(1)} %pad_maximum_fusion.4), channel_id=1, source_target_pairs={{0,6},{1,7},{2,4},{3,5},{4,2},{5,3},{6,0},{7,1},{8,14},{9,15},{10,... | collective-permute-start | bytes 393224 | tf_op jit(solution)/shard_map/ppermute | solution.py:22
  97.5 3.4 %collective-permute-done.17 = bf16[2,16,2048]{2,1,0:T(8,128)(2,1)S(1)} collective-permute-done((bf16[2,16,2048]{2,1,0:T(8,128)(2,1)S(1)}, bf16[2,16,2048]{2,1,0:T(8,128)(2,1)S(1)}, u32[]{:S(2)}, u32[]{:S(2)}) %collective-permute-start.17) | collective-permute-done | bytes 131104 | tf_op jit(solution)/shard_map/ppermute | solution.py:22
  101.1 1.1 add.366
  102.3 2.7 %collective-permute-start.15 = (bf16[16,19,256]{2,1,0:T(8,128)(2,1)S(1)}, bf16[16,19,256]{2,1,0:T(8,128)(2,1)S(1)}, u32[]{:S(2)}, u32[]{:S(2)}) collective-permute-start(bf16[16,19,256]{2,1,0:T(8,128)(2,1)S(1)} %add.366), channel_id=1, source_target_pairs={{0,64},{8,72},{16,80},{24,88},{32,96},{40,104},{48,112},{56,120},{... | collective-permute-start | bytes 466952 | tf_op jit(solution)/shard_map/ppermute | solution.py:22
  105.1 8.7 %collective-permute-done.15 = bf16[16,19,256]{2,1,0:T(8,128)(2,1)S(1)} collective-permute-done((bf16[16,19,256]{2,1,0:T(8,128)(2,1)S(1)}, bf16[16,19,256]{2,1,0:T(8,128)(2,1)S(1)}, u32[]{:S(2)}, u32[]{:S(2)}) %collective-permute-start.15) | collective-permute-done | bytes 155680 | tf_op jit(solution)/shard_map/ppermute | solution.py:22
  114.5 4.2 %collective-permute-start.19 = (bf16[16,19,256]{2,1,0:T(8,128)(2,1)}, bf16[16,19,256]{2,1,0:T(8,128)(2,1)}, u32[]{:S(2)}, u32[]{:S(2)}) collective-permute-start(bf16[16,19,256]{2,1,0:T(8,128)(2,1)} %add.368), channel_id=1, source_target_pairs={{0,192},{8,200},{16,208},{24,216},{32,224},{40,232},{48,240},{56,2... | collective-permute-start | bytes 466952 | tf_op jit(solution)/shard_map/ppermute | solution.py:22
  119.1 2.4 %convolution_convert_fusion = bf16[128,2048]{1,0:T(8,128)(2,1)S(1)} fusion(bf16[512,2048]{1,0:T(8,128)(2,1)S(1)} %copy-done, f32[128,512]{1,0:T(8,128)S(1)} %fusion.77, bf16[128,2048]{1,0:T(8,128)(2,1)S(1)} %bitcast.188, bf16[2048,512]{1,0:T(8,128)(2,1)} %param.32), kind=kOutput, calls=%fused_computation | convolution fusion | flops 537526272 | bytes 5505024 | tf_op jit(solution)/shard_map/dot_general | solution.py:326
  121.6 6.4 %collective-permute-done.19 = bf16[16,19,256]{2,1,0:T(8,128)(2,1)} collective-permute-done((bf16[16,19,256]{2,1,0:T(8,128)(2,1)}, bf16[16,19,256]{2,1,0:T(8,128)(2,1)}, u32[]{:S(2)}, u32[]{:S(2)}) %collective-permute-start.19) | collective-permute-done | bytes 155680 | tf_op jit(solution)/shard_map/ppermute | solution.py:22
  128.2 1.1 add.374
  129.7 2.8 %collective-permute-start.21 = (bf16[2,16,2048]{2,1,0:T(8,128)(2,1)S(1)}, bf16[2,16,2048]{2,1,0:T(8,128)(2,1)S(1)}, u32[]{:S(2)}, u32[]{:S(2)}) collective-permute-start(bf16[2,16,2048]{2,1,0:T(8,128)(2,1)S(1)} %fusion.10), channel_id=1, source_target_pairs={{0,6},{1,7},{2,4},{3,5},{4,2},{5,3},{6,0},{7,1},{8,14},{9,15},{10,... | collective-permute-start | bytes 393224 | tf_op jit(solution)/shard_map/ppermute | solution.py:22
  132.8 3.8 %collective-permute-done.21 = bf16[2,16,2048]{2,1,0:T(8,128)(2,1)S(1)} collective-permute-done((bf16[2,16,2048]{2,1,0:T(8,128)(2,1)S(1)}, bf16[2,16,2048]{2,1,0:T(8,128)(2,1)S(1)}, u32[]{:S(2)}, u32[]{:S(2)}) %collective-permute-start.21) | collective-permute-done | bytes 131104 | tf_op jit(solution)/shard_map/ppermute | solution.py:22
  138.2 2.8 %collective-permute-done.22 = bf16[16,2048]{1,0:T(8,128)(2,1)S(1)} collective-permute-done((bf16[16,2048]{1,0:T(8,128)(2,1)S(1)}, bf16[16,2048]{1,0:T(8,128)(2,1)S(1)}, u32[]{:S(2)}, u32[]{:S(2)}) %collective-permute-start.22) | collective-permute-done | bytes 65568 | tf_op jit(solution)/shard_map/ppermute | solution.py:22
  141.0 1.5 %fusion.13 = bf16[16,2048]{1,0:T(8,128)(2,1)} fusion(bf16[16,2048]{1,0:T(8,128)(2,1)S(1)} %collective-permute-done.22, f32[2,16,2048]{2,1,0:T(8,128)S(1)} %bitcast_add_fusion, s32[]{:T(128)S(6)} %select_n.362, f32[16]{0:T(128)S(1)} %dynamic-slice_convert_fusion.4, f32[16,2048]{1,0:T(8,128)S(1)} %bitcast_add_fusion.3, bf16[128,2048]{1,0:T(8,128)(2,1)} %param.18, ...), kind=kLoop, calls=%fused_computation.47 | loop fusion | flops 229376 | bytes 458824 | tf_op jit(solution)/shard_map/convert_element_type | solution.py:342
  (119 shorter events, 15.3 us)
Async XLA Ops:
  0.6 118.5 %copy-start = (bf16[512,2048]{1,0:T(8,128)(2,1)S(1)}, bf16[512,2048]{1,0:T(8,128)(2,1)}, u32[]{:S(2)}) copy-start(bf16[512,2048]{1,0:T(8,128)(2,1)} %param.33) | copy-start | bytes 6291460
  0.6 9.1 %copy-start.2 = (bf16[2048,256]{1,0:T(8,128)(2,1)S(1)}, bf16[2048,256]{1,0:T(8,128)(2,1)}, u32[]{:S(2)}) copy-start(bf16[2048,256]{1,0:T(8,128)(2,1)} %param.20) | copy-start | bytes 3145732
  0.7 9.1 %copy-start.9 = (f32[2048]{0:T(1024)S(1)}, f32[2048]{0:T(1024)}, u32[]{:S(2)}) copy-start(f32[2048]{0:T(1024)} %param.19) | copy-start | bytes 24580
  0.7 9.4 %copy-start.11 = (f32[256]{0:T(256)S(1)}, f32[256]{0:T(256)}, u32[]{:S(2)}) copy-start(f32[256]{0:T(256)} %param.23) | copy-start | bytes 3076
  0.7 9.6 %copy-start.7 = (bf16[256,160]{0,1:T(8,128)(2,1)S(1)}, bf16[256,160]{0,1:T(8,128)(2,1)}, u32[]{:S(2)}) copy-start(bf16[256,160]{0,1:T(8,128)(2,1)} %param.24) | copy-start | bytes 245764
  1.6 8.0 %collective-permute-start = (bf16[3,2048]{1,0:T(4,128)(2,1)S(1)}, bf16[3,2048]{1,0:T(4,128)(2,1)S(1)}, u32[]{:S(2)}, u32[]{:S(2)}) collective-permute-start(bf16[3,2048]{1,0:T(4,128)(2,1)S(1)} %slice.69), channel_id=1, source_target_pairs={{0,8},{8,16},{16,24},{24,32},{32,40},{40,48},{48,56},{56,64},{64,7... | collective-permute-start | bytes 36872 | tf_op jit(solution)/shard_map/ppermute | solution.py:256
  4.5 17.7 %copy-start.15 = (f32[128]{0:T(128)}, f32[128]{0:T(128)S(1)}, u32[]{:S(2)}) copy-start(f32[128]{0:T(128)S(1)} %add_rsqrt_fusion.2) | copy-start | bytes 1540
  7.8 14.5 %copy-start.8 = (bf16[128,256]{1,0:T(8,128)(2,1)S(1)}, bf16[128,256]{1,0:T(8,128)(2,1)}, u32[]{:S(2)}) copy-start(bf16[128,256]{1,0:T(8,128)(2,1)} %param.25) | copy-start | bytes 196612
  7.8 14.5 %copy-start.12 = (f32[256]{0:T(256)S(1)}, f32[256]{0:T(256)}, u32[]{:S(2)}) copy-start(f32[256]{0:T(256)} %param.26) | copy-start | bytes 3076
  10.4 1.4 collective-permute-start.1
  11.8 4.6 %collective-permute-start.2 = (f32[128,160]{0,1:T(8,128)S(1)}, f32[128,160]{0,1:T(8,128)S(1)}, u32[]{:S(2)}, u32[]{:S(2)}) collective-permute-start(f32[128,160]{0,1:T(8,128)S(1)} %add.318), channel_id=1, source_target_pairs={{0,2},{1,3},{2,0},{3,1},{4,6},{5,7},{6,4},{7,5},{8,10},{9,11},{10,... | collective-permute-start | bytes 245768 | tf_op jit(solution)/shard_map/ppermute | solution.py:22
  16.4 5.7 %collective-permute-start.3 = (f32[128,160]{0,1:T(8,128)S(1)}, f32[128,160]{0,1:T(8,128)S(1)}, u32[]{:S(2)}, u32[]{:S(2)}) collective-permute-start(f32[128,160]{0,1:T(8,128)S(1)} %add.319), channel_id=1, source_target_pairs={{0,6},{1,7},{2,4},{3,5},{4,2},{5,3},{6,0},{7,1},{8,14},{9,15},{10,... | collective-permute-start | bytes 245768 | tf_op jit(solution)/shard_map/ppermute | solution.py:22
  30.0 3.9 %collective-permute-start.4 = (f32[2,16,256]{2,1,0:T(8,128)S(1)}, f32[2,16,256]{2,1,0:T(8,128)S(1)}, u32[]{:S(2)}, u32[]{:S(2)}) collective-permute-start(f32[2,16,256]{2,1,0:T(8,128)S(1)} %pad_maximum_fusion.5), channel_id=1, source_target_pairs={{0,8},{8,0},{16,24},{24,16},{32,40},{40,32},{48,56},{56,48},{64,72... | collective-permute-start | bytes 98312 | tf_op jit(solution)/shard_map/ppermute | solution.py:22
  34.7 4.0 %collective-permute-start.5 = (f32[2,16,256]{2,1,0:T(8,128)S(1)}, f32[2,16,256]{2,1,0:T(8,128)S(1)}, u32[]{:S(2)}, u32[]{:S(2)}) collective-permute-start(f32[2,16,256]{2,1,0:T(8,128)S(1)} %pad_maximum_fusion.6), channel_id=1, source_target_pairs={{0,24},{8,16},{16,8},{24,0},{32,56},{40,48},{48,40},{56,32},{64,88... | collective-permute-start | bytes 98312 | tf_op jit(solution)/shard_map/ppermute | solution.py:22
  38.7 4.2 %collective-permute-start.6 = (f32[2,16,256]{2,1,0:T(8,128)S(1)}, f32[2,16,256]{2,1,0:T(8,128)S(1)}, u32[]{:S(2)}, u32[]{:S(2)}) collective-permute-start(f32[2,16,256]{2,1,0:T(8,128)S(1)} %pad_maximum_fusion.7), channel_id=1, source_target_pairs={{0,32},{8,40},{16,48},{24,56},{32,0},{40,8},{48,16},{56,24},{64,96... | collective-permute-start | bytes 98312 | tf_op jit(solution)/shard_map/ppermute | solution.py:22
  42.9 5.1 %collective-permute-start.7 = (f32[2,16,256]{2,1,0:T(8,128)S(1)}, f32[2,16,256]{2,1,0:T(8,128)S(1)}, u32[]{:S(2)}, u32[]{:S(2)}) collective-permute-start(f32[2,16,256]{2,1,0:T(8,128)S(1)} %pad_maximum_fusion.8), channel_id=1, source_target_pairs={{0,64},{8,72},{16,80},{24,88},{32,96},{40,104},{48,112},{56,120},{... | collective-permute-start | bytes 98312 | tf_op jit(solution)/shard_map/ppermute | solution.py:22
  48.0 7.0 %collective-permute-start.8 = (f32[2,16,256]{2,1,0:T(8,128)S(1)}, f32[2,16,256]{2,1,0:T(8,128)S(1)}, u32[]{:S(2)}, u32[]{:S(2)}) collective-permute-start(f32[2,16,256]{2,1,0:T(8,128)S(1)} %pad_maximum_fusion.9), channel_id=1, source_target_pairs={{0,192},{8,200},{16,208},{24,216},{32,224},{40,232},{48,240},{56,2... | collective-permute-start | bytes 98312 | tf_op jit(solution)/shard_map/ppermute | solution.py:22
  56.2 9.1 %collective-permute-start.9 = (bf16[16,19,256]{2,1,0:T(8,128)(2,1)S(1)}, bf16[16,19,256]{2,1,0:T(8,128)(2,1)S(1)}, u32[]{:S(2)}, u32[]{:S(2)}) collective-permute-start(bf16[16,19,256]{2,1,0:T(8,128)(2,1)S(1)} %pad_maximum_fusion.2), channel_id=1, source_target_pairs={{0,8},{8,0},{16,24},{24,16},{32,40},{40,32},{48,56},{56,48},{64,72... | collective-permute-start | bytes 466952 | tf_op jit(solution)/shard_map/ppermute | solution.py:22
  61.0 6.6 %copy-start.3 = (bf16[128,2048]{1,0:T(8,128)(2,1)S(1)}, bf16[128,2048]{1,0:T(8,128)(2,1)}, u32[]{:S(2)}) copy-start(bf16[128,2048]{1,0:T(8,128)(2,1)} %param.18) | copy-start | bytes 1572868
  61.0 6.6 %copy-start.14 = (f32[256]{0:T(256)S(1)}, f32[256]{0:T(256)}, u32[]{:S(2)}) copy-start(f32[256]{0:T(256)} %param.28) | copy-start | bytes 3076
  65.3 6.8 %copy-start.4 = (bf16[16,19,256]{2,1,0:T(8,128)(2,1)}, bf16[16,19,256]{2,1,0:T(8,128)(2,1)S(1)}, u32[]{:S(2)}) copy-start(bf16[16,19,256]{2,1,0:T(8,128)(2,1)S(1)} %fusion.70) | copy-start | bytes 466948
  65.3 6.0 %collective-permute-start.10 = (bf16[16,19,256]{2,1,0:T(8,128)(2,1)S(1)}, bf16[16,19,256]{2,1,0:T(8,128)(2,1)}, u32[]{:S(2)}, u32[]{:S(2)}) collective-permute-start(bf16[16,19,256]{2,1,0:T(8,128)(2,1)S(1)} %fusion.70), channel_id=1, source_target_pairs={{0,24},{8,16},{16,8},{24,0},{32,56},{40,48},{48,40},{56,32},{64,88... | collective-permute-start | bytes 466952 | tf_op jit(solution)/shard_map/ppermute | solution.py:22
  70.0 2.1 %copy-start.5 = (bf16[128,2048]{1,0:T(8,128)(2,1)}, bf16[128,2048]{1,0:T(8,128)(2,1)S(1)}, u32[]{:S(2)}) copy-start(bf16[128,2048]{1,0:T(8,128)(2,1)S(1)} %convolution_convert_fusion.1) | copy-start | bytes 1572868
  70.0 20.2 %copy-start.10 = (f32[2048]{0:T(1024)S(1)}, f32[2048]{0:T(1024)}, u32[]{:S(2)}) copy-start(f32[2048]{0:T(1024)} %param.30) | copy-start | bytes 24580
  72.1 1.9 %collective-permute-start.12 = (bf16[2,2,16,2048]{3,2,1,0:T(8,128)(2,1)}, bf16[2,2,16,2048]{3,2,1,0:T(8,128)(2,1)}, u32[]{:S(2)}, u32[]{:S(2)}) collective-permute-start(bf16[2,2,16,2048]{3,2,1,0:T(8,128)(2,1)} %dynamic-slice_bitcast_fusion.1), channel_id=1, source_target_pairs={{0,1},{1,0},{2,3},{3,2},{4,5},{5,4},{6,7},{7,6},{8,9},{9,8},{10,11... | collective-permute-start | bytes 786440 | tf_op jit(solution)/shard_map/ppermute | solution.py:22
  75.1 6.8 %collective-permute-start.13 = (bf16[2,16,2048]{2,1,0:T(8,128)(2,1)S(1)}, bf16[2,16,2048]{2,1,0:T(8,128)(2,1)S(1)}, u32[]{:S(2)}, u32[]{:S(2)}) collective-permute-start(bf16[2,16,2048]{2,1,0:T(8,128)(2,1)S(1)} %fusion.9), channel_id=1, source_target_pairs={{0,6},{1,7},{2,4},{3,5},{4,2},{5,3},{6,0},{7,1},{8,14},{9,15},{10,... | collective-permute-start | bytes 393224 | tf_op jit(solution)/shard_map/ppermute | solution.py:22
  82.0 4.4 %collective-permute-start.14 = (bf16[16,2048]{1,0:T(8,128)(2,1)S(1)}, bf16[16,2048]{1,0:T(8,128)(2,1)S(1)}, u32[]{:S(2)}, u32[]{:S(2)}) collective-permute-start(bf16[16,2048]{1,0:T(8,128)(2,1)S(1)} %fusion.19), channel_id=1, source_target_pairs={{0,2},{1,3},{2,0},{3,1},{4,6},{5,7},{6,4},{7,5},{8,10},{9,11},{10,... | collective-permute-start | bytes 196616 | tf_op jit(solution)/shard_map/ppermute | solution.py:22
  83.1 6.4 %collective-permute-start.11 = (bf16[16,19,256]{2,1,0:T(8,128)(2,1)S(1)}, bf16[16,19,256]{2,1,0:T(8,128)(2,1)S(1)}, u32[]{:S(2)}, u32[]{:S(2)}) collective-permute-start(bf16[16,19,256]{2,1,0:T(8,128)(2,1)S(1)} %add.352), channel_id=1, source_target_pairs={{0,32},{8,40},{16,48},{24,56},{32,0},{40,8},{48,16},{56,24},{64,96... | collective-permute-start | bytes 466952 | tf_op jit(solution)/shard_map/ppermute | solution.py:22
  89.5 0.7 copy-start.6
  90.3 4.4 %collective-permute-start.16 = (bf16[16,2048]{1,0:T(8,128)(2,1)S(1)}, bf16[16,2048]{1,0:T(8,128)(2,1)S(1)}, u32[]{:S(2)}, u32[]{:S(2)}) collective-permute-start(bf16[16,2048]{1,0:T(8,128)(2,1)S(1)} %multiply_convert_fusion.2), channel_id=1, source_target_pairs={{0,2},{1,3},{2,0},{3,1},{4,6},{5,7},{6,4},{7,5},{8,10},{9,11},{10,... | collective-permute-start | bytes 196616 | tf_op jit(solution)/shard_map/ppermute | solution.py:22
  94.7 6.3 %collective-permute-start.17 = (bf16[2,16,2048]{2,1,0:T(8,128)(2,1)S(1)}, bf16[2,16,2048]{2,1,0:T(8,128)(2,1)S(1)}, u32[]{:S(2)}, u32[]{:S(2)}) collective-permute-start(bf16[2,16,2048]{2,1,0:T(8,128)(2,1)S(1)} %pad_maximum_fusion.4), channel_id=1, source_target_pairs={{0,6},{1,7},{2,4},{3,5},{4,2},{5,3},{6,0},{7,1},{8,14},{9,15},{10,... | collective-permute-start | bytes 393224 | tf_op jit(solution)/shard_map/ppermute | solution.py:22
  101.0 4.0 %collective-permute-start.18 = (bf16[2,2,16,2048]{3,2,1,0:T(8,128)(2,1)S(1)}, bf16[2,2,16,2048]{3,2,1,0:T(8,128)(2,1)S(1)}, u32[]{:S(2)}, u32[]{:S(2)}) collective-permute-start(bf16[2,2,16,2048]{3,2,1,0:T(8,128)(2,1)S(1)} %pad_maximum_fusion.1), channel_id=1, source_target_pairs={{0,1},{1,0},{2,3},{3,2},{4,5},{5,4},{6,7},{7,6},{8,9},{9,8},{10,11... | collective-permute-start | bytes 786440 | tf_op jit(solution)/shard_map/ppermute | solution.py:22
  101.1 17.6 %copy-start.1 = (bf16[2048,512]{1,0:T(8,128)(2,1)S(1)}, bf16[2048,512]{1,0:T(8,128)(2,1)}, u32[]{:S(2)}) copy-start(bf16[2048,512]{1,0:T(8,128)(2,1)} %param.31) | copy-start | bytes 6291460
  102.3 11.5 %collective-permute-start.15 = (bf16[16,19,256]{2,1,0:T(8,128)(2,1)S(1)}, bf16[16,19,256]{2,1,0:T(8,128)(2,1)S(1)}, u32[]{:S(2)}, u32[]{:S(2)}) collective-permute-start(bf16[16,19,256]{2,1,0:T(8,128)(2,1)S(1)} %add.366), channel_id=1, source_target_pairs={{0,64},{8,72},{16,80},{24,88},{32,96},{40,104},{48,112},{56,120},{... | collective-permute-start | bytes 466952 | tf_op jit(solution)/shard_map/ppermute | solution.py:22
  114.5 13.5 %collective-permute-start.19 = (bf16[16,19,256]{2,1,0:T(8,128)(2,1)}, bf16[16,19,256]{2,1,0:T(8,128)(2,1)}, u32[]{:S(2)}, u32[]{:S(2)}) collective-permute-start(bf16[16,19,256]{2,1,0:T(8,128)(2,1)} %add.368), channel_id=1, source_target_pairs={{0,192},{8,200},{16,208},{24,216},{32,224},{40,232},{48,240},{56,2... | collective-permute-start | bytes 466952 | tf_op jit(solution)/shard_map/ppermute | solution.py:22
  121.6 11.0 %copy-start.13 = (s32[4]{0:T(128)S(1)}, s32[4]{0:T(128)}, u32[]{:S(2)}) copy-start(s32[4]{0:T(128)} %param.35) | copy-start | bytes 52
  128.0 1.6 %collective-permute-start.20 = (bf16[2,2,16,2048]{3,2,1,0:T(8,128)(2,1)S(1)}, bf16[2,2,16,2048]{3,2,1,0:T(8,128)(2,1)S(1)}, u32[]{:S(2)}, u32[]{:S(2)}) collective-permute-start(bf16[2,2,16,2048]{3,2,1,0:T(8,128)(2,1)S(1)} %dynamic-slice_bitcast_fusion), channel_id=1, source_target_pairs={{0,1},{1,0},{2,3},{3,2},{4,5},{5,4},{6,7},{7,6},{8,9},{9,8},{10,11... | collective-permute-start | bytes 786440 | tf_op jit(solution)/shard_map/ppermute | solution.py:22
  129.7 6.9 %collective-permute-start.21 = (bf16[2,16,2048]{2,1,0:T(8,128)(2,1)S(1)}, bf16[2,16,2048]{2,1,0:T(8,128)(2,1)S(1)}, u32[]{:S(2)}, u32[]{:S(2)}) collective-permute-start(bf16[2,16,2048]{2,1,0:T(8,128)(2,1)S(1)} %fusion.10), channel_id=1, source_target_pairs={{0,6},{1,7},{2,4},{3,5},{4,2},{5,3},{6,0},{7,1},{8,14},{9,15},{10,... | collective-permute-start | bytes 393224 | tf_op jit(solution)/shard_map/ppermute | solution.py:22
  136.7 4.4 %collective-permute-start.22 = (bf16[16,2048]{1,0:T(8,128)(2,1)S(1)}, bf16[16,2048]{1,0:T(8,128)(2,1)S(1)}, u32[]{:S(2)}, u32[]{:S(2)}) collective-permute-start(bf16[16,2048]{1,0:T(8,128)(2,1)S(1)} %fusion.20), channel_id=1, source_target_pairs={{0,2},{1,3},{2,0},{3,1},{4,6},{5,7},{6,4},{7,5},{8,10},{9,11},{10,... | collective-permute-start | bytes 196616 | tf_op jit(solution)/shard_map/ppermute | solution.py:22

commit v8 on v6

--- a/solution.py
+++ b/solution.py
@@ -107,21 +107,25 @@
 
 def block_summary_kernel(da_ref, dr_ref, send_ref, atot_ref):
     steps = da_ref.shape[0]
+    half = steps // 2
 
     def chunk(c, carry):
-        state, acum = carry
+        s1, a1, s2, a2 = carry
         base = c * 8
         for i in range(8):
-            da = da_ref[base + i]
-            state = da * state + dr_ref[base + i]
-            acum = da * acum
-        return state, acum
+            d1 = da_ref[base + i]
+            d2 = da_ref[half + base + i]
+            s1 = d1 * s1 + dr_ref[base + i]
+            s2 = d2 * s2 + dr_ref[half + base + i]
+            a1 = d1 * a1
+            a2 = d2 * a2
+        return s1, a1, s2, a2
 
     zero = jnp.zeros(send_ref.shape, jnp.float32)
     one = jnp.ones(atot_ref.shape, jnp.float32)
-    state, acum = lax.fori_loop(0, steps // 8, chunk, (zero, one))
-    send_ref[...] = state
-    atot_ref[...] = acum
+    s1, a1, s2, a2 = lax.fori_loop(0, half // 8, chunk, (zero, one, zero, one))
+    send_ref[...] = a2 * s1 + s2
+    atot_ref[...] = a1 * a2
 
 
 def block_output_kernel(da_ref, dr_ref, om_ref, sin_ref, endf_ref, pid_ref, y_ref, fin_ref):
@@ -278,7 +282,7 @@
     carry_on = 1.0 - starts_here.astype(jnp.float32)
     decay = jnp.exp(step_size[:, None, :] * decay_rates[None, :, :]) * carry_on[:, None, None]
     drive = (step_size * conv_float)[:, None, :] * in_map[:, :, None]
-    out_wide = jnp.broadcast_to(out_map[:, :, None], decay.shape)
+    out_wide = out_map[:, :, None]
     s_blk, a_blk = block_summary(decay, drive)
     state_in = entering_state(a_blk, s_blk, "seq")
     end_flag = ends_here.astype(jnp.int32)

time: 129 us -> 135 us (1.047)
  Pallas kernels: 8.58 us -> 16.6 us
  waiting for transfers between devices: 49.9 us -> 48.1 us
    pallas_call x1, Pallas kernels: 5.44 us -> 13.5 us  [block_output(): pl.pallas_call(block_output_kernel, out_shape=(jax.ShapeDtypeStruct((t, e...]
    ppermute x22, waiting for transfers between devices: 49.9 us -> 48.1 us  [swap(): return lax.ppermute(x, axis, [(i, i ^ bit) for i in range(devices)])]
  transfers between devices with their start and end apart: 23 -> 23, of which waited for: 19 -> 19; matrix products, arithmetic and copies ran while one was open for 13% -> 14% of each run, Pallas kernels for 0% -> 0%
where the time goes in v8:
time: 135 us; the launch traced here: 134 us
  waiting for transfers between devices  48.1 us (36%)
  starting transfers between devices  38.9 us (29%)
  Pallas kernels  16.6 us (12%)
  other arithmetic  15.5 us (11%)
  matrix products  9.02 us (7%)
  local copies, waits for them, and re-layouts  4.96 us (4%)
    ppermute x22, waiting for transfers between devices, swap(): return lax.ppermute(x, axis, [(i, i ^ bit) for i in range(devices)])  48.1 us
    ppermute x22, starting transfers between devices, swap(): return lax.ppermute(x, axis, [(i, i ^ bit) for i in range(devices)])  37.2 us
    pallas_call x1, Pallas kernels, block_output(): pl.pallas_call(block_output_kernel, out_shape=(jax.ShapeDtypeStruct((t, e...  13.5 us
    pallas_call x1, Pallas kernels, block_summary(): pl.pallas_call(block_summary_kernel, out_shape=(jax.ShapeDtypeStruct((n,...  3.08 us
  transfers between devices with their start and end apart: 23, of which 19 were waited for; matrix products, arithmetic and copies ran while one was open for 14% of the time, Pallas kernels for 0%

profile of v8, /device:TPU:40, one launch (start us, length us, event | category | flops | bytes accessed | tf_op | source)
XLA Modules:
  0.0 134.2 jit_solution(9938480723924692035)
XLA Ops:
  0.7 0.9 slice.69
  1.6 1.7 %collective-permute-start = (bf16[3,2048]{1,0:T(4,128)(2,1)S(1)}, bf16[3,2048]{1,0:T(4,128)(2,1)S(1)}, u32[]{:S(2)}, u32[]{:S(2)}) collective-permute-start(bf16[3,2048]{1,0:T(4,128)(2,1)S(1)} %slice.69), channel_id=1, source_target_pairs={{0,8},{8,16},{16,24},{24,32},{32,40},{40,48},{48,56},{56,64},{64,7... | collective-permute-start | bytes 36872 | tf_op jit(solution)/shard_map/ppermute | solution.py:252
  3.3 1.2 fusion.2
  4.5 0.8 fusion.67
  6.3 1.2 broadcast_add_fusion
  7.6 1.8 %convolution_convert_fusion.3 = bf16[128,256]{1,0:T(8,128)(2,1)S(1)} fusion(bf16[2048,256]{1,0:T(8,128)(2,1)} %param.20, bf16[128,2048]{1,0:T(8,128)(2,1)} %param.18, f32[2048]{0:T(1024)} %param.19, f32[128]{0:T(128)S(1)} %add_rsqrt_fusion.2), kind=kOutput, calls=%fused_computation.10 | convolution fusion | flops 135299072 | bytes 1647104 | tf_op jit(solution)/shard_map/dot_general | solution.py:259
  10.4 1.2 collective-permute-done.1
  11.6 1.6 %collective-permute-start.2 = (f32[128,160]{0,1:T(8,128)S(1)}, f32[128,160]{0,1:T(8,128)S(1)}, u32[]{:S(2)}, u32[]{:S(2)}) collective-permute-start(f32[128,160]{0,1:T(8,128)S(1)} %add.303), channel_id=1, source_target_pairs={{0,2},{1,3},{2,0},{3,1},{4,6},{5,7},{6,4},{7,5},{8,10},{9,11},{10,... | collective-permute-start | bytes 245768 | tf_op jit(solution)/shard_map/ppermute | solution.py:22
  13.3 2.9 %collective-permute-done.2 = f32[128,160]{0,1:T(8,128)S(1)} collective-permute-done((f32[128,160]{0,1:T(8,128)S(1)}, f32[128,160]{0,1:T(8,128)S(1)}, u32[]{:S(2)}, u32[]{:S(2)}) %collective-permute-start.2) | collective-permute-done | bytes 81952 | tf_op jit(solution)/shard_map/ppermute | solution.py:22
  16.2 2.8 %collective-permute-start.3 = (f32[128,160]{0,1:T(8,128)S(1)}, f32[128,160]{0,1:T(8,128)S(1)}, u32[]{:S(2)}, u32[]{:S(2)}) collective-permute-start(f32[128,160]{0,1:T(8,128)S(1)} %add.304), channel_id=1, source_target_pairs={{0,6},{1,7},{2,4},{3,5},{4,2},{5,3},{6,0},{7,1},{8,14},{9,15},{10,... | collective-permute-start | bytes 245768 | tf_op jit(solution)/shard_map/ppermute | solution.py:22
  19.1 2.9 %collective-permute-done.3 = f32[128,160]{0,1:T(8,128)S(1)} collective-permute-done((f32[128,160]{0,1:T(8,128)S(1)}, f32[128,160]{0,1:T(8,128)S(1)}, u32[]{:S(2)}, u32[]{:S(2)}) %collective-permute-start.3) | collective-permute-done | bytes 81952 | tf_op jit(solution)/shard_map/ppermute | solution.py:22
  22.4 2.4 %exponential_multiply_fusion = (f32[128,16,256]{2,1,0:T(8,128)}, f32[128,16,256]{2,1,0:T(8,128)}) fusion(f32[128]{0:T(128)S(1)} %convert_subtract_fusion, f32[16,256]{1,0:T(8,128)S(1)} %exponential_negate_fusion, f32[128,256]{1,0:T(8,128)S(1)} %get-tuple-element.56, f32[128,16]{1,0:T(8,128)S(1)} %copy.51, f32[128,256]{1,0:T(8,128)S(1)} %get-tuple-element.55), kind=kLoop, calls=%fused_computation.2 | loop fusion | flops 1572864 | bytes 4481536 | tf_op jit(solution)/shard_map/mul | solution.py:283
  24.8 3.1 %shard_map.193 = (f32[16,256]{1,0:T(8,128)}, f32[16,256]{1,0:T(8,128)}) custom-call(f32[128,16,256]{2,1,0:T(8,128)} %get-tuple-element.57.da_ref, f32[128,16,256]{2,1,0:T(8,128)} %get-tuple-element.58.dr_ref), custom_call_target="tpu_custom_call" | custom-call | tf_op jit(solution)/shard_map/pallas_call | solution.py:159
  29.0 3.5 %collective-permute-done.4 = f32[2,16,256]{2,1,0:T(8,128)S(1)} collective-permute-done((f32[2,16,256]{2,1,0:T(8,128)S(1)}, f32[2,16,256]{2,1,0:T(8,128)S(1)}, u32[]{:S(2)}, u32[]{:S(2)}) %collective-permute-start.4) | collective-permute-done | bytes 32800 | tf_op jit(solution)/shard_map/ppermute | solution.py:22
  32.5 0.7 select_multiply_fusion.2
  33.3 1.4 %collective-permute-start.5 = (f32[2,16,256]{2,1,0:T(8,128)S(1)}, f32[2,16,256]{2,1,0:T(8,128)S(1)}, u32[]{:S(2)}, u32[]{:S(2)}) collective-permute-start(f32[2,16,256]{2,1,0:T(8,128)S(1)} %pad_maximum_fusion.6), channel_id=1, source_target_pairs={{0,24},{8,16},{16,8},{24,0},{32,56},{40,48},{48,40},{56,32},{64,88... | collective-permute-start | bytes 98312 | tf_op jit(solution)/shard_map/ppermute | solution.py:22
  34.6 2.6 %collective-permute-done.5 = f32[2,16,256]{2,1,0:T(8,128)S(1)} collective-permute-done((f32[2,16,256]{2,1,0:T(8,128)S(1)}, f32[2,16,256]{2,1,0:T(8,128)S(1)}, u32[]{:S(2)}, u32[]{:S(2)}) %collective-permute-start.5) | collective-permute-done | bytes 32800 | tf_op jit(solution)/shard_map/ppermute | solution.py:22
  37.3 0.9 collective-permute-start.6
  38.2 3.3 %collective-permute-done.6 = f32[2,16,256]{2,1,0:T(8,128)S(1)} collective-permute-done((f32[2,16,256]{2,1,0:T(8,128)S(1)}, f32[2,16,256]{2,1,0:T(8,128)S(1)}, u32[]{:S(2)}, u32[]{:S(2)}) %collective-permute-start.6) | collective-permute-done | bytes 32800 | tf_op jit(solution)/shard_map/ppermute | solution.py:22
  41.5 3.2 %collective-permute-start.7 = (f32[2,16,256]{2,1,0:T(8,128)S(1)}, f32[2,16,256]{2,1,0:T(8,128)S(1)}, u32[]{:S(2)}, u32[]{:S(2)}) collective-permute-start(f32[2,16,256]{2,1,0:T(8,128)S(1)} %pad_maximum_fusion.8), channel_id=1, source_target_pairs={{0,64},{8,72},{16,80},{24,88},{32,96},{40,104},{48,112},{56,120},{... | collective-permute-start | bytes 98312 | tf_op jit(solution)/shard_map/ppermute | solution.py:22
  45.2 1.4 %collective-permute-done.7 = f32[2,16,256]{2,1,0:T(8,128)S(1)} collective-permute-done((f32[2,16,256]{2,1,0:T(8,128)S(1)}, f32[2,16,256]{2,1,0:T(8,128)S(1)}, u32[]{:S(2)}, u32[]{:S(2)}) %collective-permute-start.7) | collective-permute-done | bytes 32800 | tf_op jit(solution)/shard_map/ppermute | solution.py:22
  46.6 5.1 %collective-permute-start.8 = (f32[2,16,256]{2,1,0:T(8,128)S(1)}, f32[2,16,256]{2,1,0:T(8,128)S(1)}, u32[]{:S(2)}, u32[]{:S(2)}) collective-permute-start(f32[2,16,256]{2,1,0:T(8,128)S(1)} %pad_maximum_fusion.9), channel_id=1, source_target_pairs={{0,192},{8,200},{16,208},{24,216},{32,224},{40,232},{48,240},{56,2... | collective-permute-start | bytes 98312 | tf_op jit(solution)/shard_map/ppermute | solution.py:22
  52.9 1.4 %copy.52.om_ref = f32[128,16,1]{2,1,0:T(8,128)} copy(f32[128,16,1]{0,1,2:T(8,128)S(1)} %get-tuple-element.35) | data formatting | bytes 16384 | tf_op jit(solution)/shard_map/broadcast_in_dim | solution.py:285
  55.0 13.5 %shard_map.194 = (f32[128,256]{1,0:T(8,128)}, f32[16,16,256]{2,1,0:T(8,128)}) custom-call(f32[128,16,256]{2,1,0:T(8,128)} %get-tuple-element.57.da_ref, f32[128,16,256]{2,1,0:T(8,128)} %get-tuple-element.58.dr_ref, f32[128,16,1]{2,1,0:T(8,128)} %copy.52.om_ref, f32[16,256]{1,0:T(8,128)} %add_select_fusion.sin_ref, s32[128]{0:T(128)} %convert_element_type.193.endf_ref, ...), custom_call_target="tpu_custom_call" | custom-call | tf_op jit(solution)/shard_map/pallas_call | solution.py:175
  68.5 2.5 %convolution_convert_fusion.1 = bf16[128,2048]{1,0:T(8,128)(2,1)S(1)} fusion(bf16[256,2048]{1,0:T(8,128)(2,1)} %param.29, f32[128,256]{1,0:T(8,128)} %get-tuple-element.9, bf16[128,256]{1,0:T(8,128)(2,1)S(1)} %multiply_convert_fusion.1, bf16[2048,256]{1,0:T(8,128)(2,1)} %param.21, bf16[128,2048]{1,0:T(8,128)(2,1)S(1)} %copy-done.3, f32[2048]{0:T(1024)S(1)} %copy-done.10, ...), kind=kOutput, calls=%fused_computation.1 | convolution fusion | flops 270106624 | bytes 3352064 | tf_op jit(solution)/shard_map/dot_general | solution.py:316
  71.8 1.0 collective-permute-done.9
  72.7 1.0 convert_add_fusion.1
  73.8 2.8 %collective-permute-start.10 = (bf16[2,16,2048]{2,1,0:T(8,128)(2,1)S(1)}, bf16[2,16,2048]{2,1,0:T(8,128)(2,1)S(1)}, u32[]{:S(2)}, u32[]{:S(2)}) collective-permute-start(bf16[2,16,2048]{2,1,0:T(8,128)(2,1)S(1)} %fusion.15), channel_id=1, source_target_pairs={{0,6},{1,7},{2,4},{3,5},{4,2},{5,3},{6,0},{7,1},{8,14},{9,15},{10,... | collective-permute-start | bytes 393224 | tf_op jit(solution)/shard_map/ppermute | solution.py:22
  76.9 1.0 convert_element_type.221
  77.8 2.8 %collective-permute-done.10 = bf16[2,16,2048]{2,1,0:T(8,128)(2,1)S(1)} collective-permute-done((bf16[2,16,2048]{2,1,0:T(8,128)(2,1)S(1)}, bf16[2,16,2048]{2,1,0:T(8,128)(2,1)S(1)}, u32[]{:S(2)}, u32[]{:S(2)}) %collective-permute-start.10) | collective-permute-done | bytes 131104 | tf_op jit(solution)/shard_map/ppermute | solution.py:22
  80.8 1.7 %collective-permute-start.18 = (bf16[16,19,256]{2,1,0:T(8,128)(2,1)S(1)}, bf16[16,19,256]{2,1,0:T(8,128)(2,1)S(1)}, u32[]{:S(2)}, u32[]{:S(2)}) collective-permute-start(bf16[16,19,256]{2,1,0:T(8,128)(2,1)S(1)} %pad_maximum_fusion.2), channel_id=1, source_target_pairs={{0,8},{8,0},{16,24},{24,16},{32,40},{40,32},{48,56},{56,48},{64,72... | collective-permute-start | bytes 466952 | tf_op jit(solution)/shard_map/ppermute | solution.py:22
  82.6 2.5 %collective-permute-done.11 = bf16[16,2048]{1,0:T(8,128)(2,1)S(1)} collective-permute-done((bf16[16,2048]{1,0:T(8,128)(2,1)S(1)}, bf16[16,2048]{1,0:T(8,128)(2,1)S(1)}, u32[]{:S(2)}, u32[]{:S(2)}) %collective-permute-start.11) | collective-permute-done | bytes 65568 | tf_op jit(solution)/shard_map/ppermute | solution.py:22
  85.4 1.6 %collective-permute-done.18 = bf16[16,19,256]{2,1,0:T(8,128)(2,1)S(1)} collective-permute-done((bf16[16,19,256]{2,1,0:T(8,128)(2,1)S(1)}, bf16[16,19,256]{2,1,0:T(8,128)(2,1)S(1)}, u32[]{:S(2)}, u32[]{:S(2)}) %collective-permute-start.18) | collective-permute-done | bytes 155680 | tf_op jit(solution)/shard_map/ppermute | solution.py:22
  87.0 2.4 %collective-permute-start.19 = (bf16[16,19,256]{2,1,0:T(8,128)(2,1)S(1)}, bf16[16,19,256]{2,1,0:T(8,128)(2,1)S(1)}, u32[]{:S(2)}, u32[]{:S(2)}) collective-permute-start(bf16[16,19,256]{2,1,0:T(8,128)(2,1)S(1)} %fusion.64), channel_id=1, source_target_pairs={{0,24},{8,16},{16,8},{24,0},{32,56},{40,48},{48,40},{56,32},{64,88... | collective-permute-start | bytes 466952 | tf_op jit(solution)/shard_map/ppermute | solution.py:22
  89.8 2.8 %collective-permute-start.13 = (bf16[2,16,2048]{2,1,0:T(8,128)(2,1)S(1)}, bf16[2,16,2048]{2,1,0:T(8,128)(2,1)S(1)}, u32[]{:S(2)}, u32[]{:S(2)}) collective-permute-start(bf16[2,16,2048]{2,1,0:T(8,128)(2,1)S(1)} %pad_maximum_fusion.4), channel_id=1, source_target_pairs={{0,6},{1,7},{2,4},{3,5},{4,2},{5,3},{6,0},{7,1},{8,14},{9,15},{10,... | collective-permute-start | bytes 393224 | tf_op jit(solution)/shard_map/ppermute | solution.py:22
  93.3 0.8 collective-permute-start.20
  94.1 1.9 %collective-permute-done.13 = bf16[2,16,2048]{2,1,0:T(8,128)(2,1)S(1)} collective-permute-done((bf16[2,16,2048]{2,1,0:T(8,128)(2,1)S(1)}, bf16[2,16,2048]{2,1,0:T(8,128)(2,1)S(1)}, u32[]{:S(2)}, u32[]{:S(2)}) %collective-permute-start.13) | collective-permute-done | bytes 131104 | tf_op jit(solution)/shard_map/ppermute | solution.py:22
  96.2 2.9 %collective-permute-done.20 = bf16[16,19,256]{2,1,0:T(8,128)(2,1)S(1)} collective-permute-done((bf16[16,19,256]{2,1,0:T(8,128)(2,1)S(1)}, bf16[16,19,256]{2,1,0:T(8,128)(2,1)S(1)}, u32[]{:S(2)}, u32[]{:S(2)}) %collective-permute-start.20) | collective-permute-done | bytes 155680 | tf_op jit(solution)/shard_map/ppermute | solution.py:22
  99.1 2.7 %collective-permute-start.21 = (bf16[16,19,256]{2,1,0:T(8,128)(2,1)S(1)}, bf16[16,19,256]{2,1,0:T(8,128)(2,1)S(1)}, u32[]{:S(2)}, u32[]{:S(2)}) collective-permute-start(bf16[16,19,256]{2,1,0:T(8,128)(2,1)S(1)} %add.352), channel_id=1, source_target_pairs={{0,64},{8,72},{16,80},{24,88},{32,96},{40,104},{48,112},{56,120},{... | collective-permute-start | bytes 466952 | tf_op jit(solution)/shard_map/ppermute | solution.py:22
  101.9 5.5 %collective-permute-done.21 = bf16[16,19,256]{2,1,0:T(8,128)(2,1)S(1)} collective-permute-done((bf16[16,19,256]{2,1,0:T(8,128)(2,1)S(1)}, bf16[16,19,256]{2,1,0:T(8,128)(2,1)S(1)}, u32[]{:S(2)}, u32[]{:S(2)}) %collective-permute-start.21) | collective-permute-done | bytes 155680 | tf_op jit(solution)/shard_map/ppermute | solution.py:22
  108.0 4.8 %collective-permute-start.22 = (bf16[16,19,256]{2,1,0:T(8,128)(2,1)}, bf16[16,19,256]{2,1,0:T(8,128)(2,1)}, u32[]{:S(2)}, u32[]{:S(2)}) collective-permute-start(bf16[16,19,256]{2,1,0:T(8,128)(2,1)} %add.353), channel_id=1, source_target_pairs={{0,192},{8,200},{16,208},{24,216},{32,224},{40,232},{48,240},{56,2... | collective-permute-start | bytes 466952 | tf_op jit(solution)/shard_map/ppermute | solution.py:22
  113.5 2.4 %convolution_convert_fusion = bf16[128,2048]{1,0:T(8,128)(2,1)S(1)} fusion(bf16[512,2048]{1,0:T(8,128)(2,1)S(1)} %copy-done, bf16[128,2048]{1,0:T(8,128)(2,1)S(1)} %bitcast.171, bf16[2048,512]{1,0:T(8,128)(2,1)} %param.32, f32[128,512]{1,0:T(8,128)S(1)} %fusion.69), kind=kOutput, calls=%fused_computation | convolution fusion | flops 537526272 | bytes 5505024 | tf_op jit(solution)/shard_map/dot_general | solution.py:328
  116.1 5.5 %collective-permute-done.22 = bf16[16,19,256]{2,1,0:T(8,128)(2,1)} collective-permute-done((bf16[16,19,256]{2,1,0:T(8,128)(2,1)}, bf16[16,19,256]{2,1,0:T(8,128)(2,1)}, u32[]{:S(2)}, u32[]{:S(2)}) %collective-permute-start.22) | collective-permute-done | bytes 155680 | tf_op jit(solution)/shard_map/ppermute | solution.py:22
  121.6 1.1 add.354
  122.8 2.8 %collective-permute-start.16 = (bf16[2,16,2048]{2,1,0:T(8,128)(2,1)S(1)}, bf16[2,16,2048]{2,1,0:T(8,128)(2,1)S(1)}, u32[]{:S(2)}, u32[]{:S(2)}) collective-permute-start(bf16[2,16,2048]{2,1,0:T(8,128)(2,1)S(1)} %fusion.16), channel_id=1, source_target_pairs={{0,6},{1,7},{2,4},{3,5},{4,2},{5,3},{6,0},{7,1},{8,14},{9,15},{10,... | collective-permute-start | bytes 393224 | tf_op jit(solution)/shard_map/ppermute | solution.py:22
  125.9 3.2 %collective-permute-done.16 = bf16[2,16,2048]{2,1,0:T(8,128)(2,1)S(1)} collective-permute-done((bf16[2,16,2048]{2,1,0:T(8,128)(2,1)S(1)}, bf16[2,16,2048]{2,1,0:T(8,128)(2,1)S(1)}, u32[]{:S(2)}, u32[]{:S(2)}) %collective-permute-start.16) | collective-permute-done | bytes 131104 | tf_op jit(solution)/shard_map/ppermute | solution.py:22
  129.2 0.8 convolution_convert_fusion.5
  130.7 2.8 %collective-permute-done.17 = bf16[16,2048]{1,0:T(8,128)(2,1)S(1)} collective-permute-done((bf16[16,2048]{1,0:T(8,128)(2,1)S(1)}, bf16[16,2048]{1,0:T(8,128)(2,1)S(1)}, u32[]{:S(2)}, u32[]{:S(2)}) %collective-permute-start.17) | collective-permute-done | bytes 65568 | tf_op jit(solution)/shard_map/ppermute | solution.py:22
  (120 shorter events, 12.1 us)
Async XLA Ops:
  0.6 112.8 %copy-start = (bf16[512,2048]{1,0:T(8,128)(2,1)S(1)}, bf16[512,2048]{1,0:T(8,128)(2,1)}, u32[]{:S(2)}) copy-start(bf16[512,2048]{1,0:T(8,128)(2,1)} %param.33) | copy-start | bytes 6291460
  0.6 9.0 %copy-start.10 = (f32[2048]{0:T(1024)S(1)}, f32[2048]{0:T(1024)}, u32[]{:S(2)}) copy-start(f32[2048]{0:T(1024)} %param.19) | copy-start | bytes 24580
  0.7 8.9 %copy-start.2 = (bf16[2048,256]{1,0:T(8,128)(2,1)S(1)}, bf16[2048,256]{1,0:T(8,128)(2,1)}, u32[]{:S(2)}) copy-start(bf16[2048,256]{1,0:T(8,128)(2,1)} %param.20) | copy-start | bytes 3145732
  0.7 9.2 %copy-start.12 = (f32[256]{0:T(256)S(1)}, f32[256]{0:T(256)}, u32[]{:S(2)}) copy-start(f32[256]{0:T(256)} %param.23) | copy-start | bytes 3076
  0.7 9.4 %copy-start.4 = (bf16[256,160]{0,1:T(8,128)(2,1)S(1)}, bf16[256,160]{0,1:T(8,128)(2,1)}, u32[]{:S(2)}) copy-start(bf16[256,160]{0,1:T(8,128)(2,1)} %param.24) | copy-start | bytes 245764
  0.7 9.7 %copy-start.9 = (f32[16,256]{1,0:T(8,128)S(1)}, f32[16,256]{1,0:T(8,128)}, u32[]{:S(2)}) copy-start(f32[16,256]{1,0:T(8,128)} %param.27) | copy-start | bytes 49156
  1.6 7.8 %collective-permute-start = (bf16[3,2048]{1,0:T(4,128)(2,1)S(1)}, bf16[3,2048]{1,0:T(4,128)(2,1)S(1)}, u32[]{:S(2)}, u32[]{:S(2)}) collective-permute-start(bf16[3,2048]{1,0:T(4,128)(2,1)S(1)} %slice.69), channel_id=1, source_target_pairs={{0,8},{8,16},{16,24},{24,32},{32,40},{40,48},{48,56},{56,64},{64,7... | collective-permute-start | bytes 36872 | tf_op jit(solution)/shard_map/ppermute | solution.py:252
  7.4 20.4 %copy-start.11 = (s32[16]{0:T(128)}, s32[16]{0:T(128)S(1)}, u32[]{:S(2)}) copy-start(s32[16]{0:T(128)S(1)} %get-tuple-element.51) | copy-start | bytes 196
  7.5 37.2 %copy-start.16 = (s32[128]{0:T(128)}, s32[128]{0:T(128)S(1)}, u32[]{:S(2)}) copy-start(s32[128]{0:T(128)S(1)} %convert_reduce_fusion) | copy-start | bytes 1540
  7.6 14.5 %copy-start.5 = (bf16[128,256]{1,0:T(8,128)(2,1)S(1)}, bf16[128,256]{1,0:T(8,128)(2,1)}, u32[]{:S(2)}) copy-start(bf16[128,256]{1,0:T(8,128)(2,1)} %param.25) | copy-start | bytes 196612
  7.6 14.5 %copy-start.13 = (f32[256]{0:T(256)S(1)}, f32[256]{0:T(256)}, u32[]{:S(2)}) copy-start(f32[256]{0:T(256)} %param.26) | copy-start | bytes 3076
  9.4 12.6 %copy-start.6 = (bf16[128,256]{1,0:T(8,128)(2,1)}, bf16[128,256]{1,0:T(8,128)(2,1)S(1)}, u32[]{:S(2)}) copy-start(bf16[128,256]{1,0:T(8,128)(2,1)S(1)} %convolution_convert_fusion.3) | copy-start | bytes 196612
  10.2 1.4 %collective-permute-start.1 = (f32[128,160]{0,1:T(8,128)S(1)}, f32[128,160]{0,1:T(8,128)S(1)}, u32[]{:S(2)}, u32[]{:S(2)}) collective-permute-start(f32[128,160]{0,1:T(8,128)S(1)} %fusion.68), channel_id=1, source_target_pairs={{0,1},{1,0},{2,3},{3,2},{4,5},{5,4},{6,7},{7,6},{8,9},{9,8},{10,11... | collective-permute-start | bytes 245768 | tf_op jit(solution)/shard_map/ppermute | solution.py:22
  11.6 4.6 %collective-permute-start.2 = (f32[128,160]{0,1:T(8,128)S(1)}, f32[128,160]{0,1:T(8,128)S(1)}, u32[]{:S(2)}, u32[]{:S(2)}) collective-permute-start(f32[128,160]{0,1:T(8,128)S(1)} %add.303), channel_id=1, source_target_pairs={{0,2},{1,3},{2,0},{3,1},{4,6},{5,7},{6,4},{7,5},{8,10},{9,11},{10,... | collective-permute-start | bytes 245768 | tf_op jit(solution)/shard_map/ppermute | solution.py:22
  16.2 5.7 %collective-permute-start.3 = (f32[128,160]{0,1:T(8,128)S(1)}, f32[128,160]{0,1:T(8,128)S(1)}, u32[]{:S(2)}, u32[]{:S(2)}) collective-permute-start(f32[128,160]{0,1:T(8,128)S(1)} %add.304), channel_id=1, source_target_pairs={{0,6},{1,7},{2,4},{3,5},{4,2},{5,3},{6,0},{7,1},{8,14},{9,15},{10,... | collective-permute-start | bytes 245768 | tf_op jit(solution)/shard_map/ppermute | solution.py:22
  28.6 3.9 %collective-permute-start.4 = (f32[2,16,256]{2,1,0:T(8,128)S(1)}, f32[2,16,256]{2,1,0:T(8,128)S(1)}, u32[]{:S(2)}, u32[]{:S(2)}) collective-permute-start(f32[2,16,256]{2,1,0:T(8,128)S(1)} %pad_maximum_fusion.5), channel_id=1, source_target_pairs={{0,8},{8,0},{16,24},{24,16},{32,40},{40,32},{48,56},{56,48},{64,72... | collective-permute-start | bytes 98312 | tf_op jit(solution)/shard_map/ppermute | solution.py:22
  33.3 4.0 %collective-permute-start.5 = (f32[2,16,256]{2,1,0:T(8,128)S(1)}, f32[2,16,256]{2,1,0:T(8,128)S(1)}, u32[]{:S(2)}, u32[]{:S(2)}) collective-permute-start(f32[2,16,256]{2,1,0:T(8,128)S(1)} %pad_maximum_fusion.6), channel_id=1, source_target_pairs={{0,24},{8,16},{16,8},{24,0},{32,56},{40,48},{48,40},{56,32},{64,88... | collective-permute-start | bytes 98312 | tf_op jit(solution)/shard_map/ppermute | solution.py:22
  37.3 4.2 %collective-permute-start.6 = (f32[2,16,256]{2,1,0:T(8,128)S(1)}, f32[2,16,256]{2,1,0:T(8,128)S(1)}, u32[]{:S(2)}, u32[]{:S(2)}) collective-permute-start(f32[2,16,256]{2,1,0:T(8,128)S(1)} %pad_maximum_fusion.7), channel_id=1, source_target_pairs={{0,32},{8,40},{16,48},{24,56},{32,0},{40,8},{48,16},{56,24},{64,96... | collective-permute-start | bytes 98312 | tf_op jit(solution)/shard_map/ppermute | solution.py:22
  41.5 5.1 %collective-permute-start.7 = (f32[2,16,256]{2,1,0:T(8,128)S(1)}, f32[2,16,256]{2,1,0:T(8,128)S(1)}, u32[]{:S(2)}, u32[]{:S(2)}) collective-permute-start(f32[2,16,256]{2,1,0:T(8,128)S(1)} %pad_maximum_fusion.8), channel_id=1, source_target_pairs={{0,64},{8,72},{16,80},{24,88},{32,96},{40,104},{48,112},{56,120},{... | collective-permute-start | bytes 98312 | tf_op jit(solution)/shard_map/ppermute | solution.py:22
  46.6 7.7 %collective-permute-start.8 = (f32[2,16,256]{2,1,0:T(8,128)S(1)}, f32[2,16,256]{2,1,0:T(8,128)S(1)}, u32[]{:S(2)}, u32[]{:S(2)}) collective-permute-start(f32[2,16,256]{2,1,0:T(8,128)S(1)} %pad_maximum_fusion.9), channel_id=1, source_target_pairs={{0,192},{8,200},{16,208},{24,216},{32,224},{40,232},{48,240},{56,2... | collective-permute-start | bytes 98312 | tf_op jit(solution)/shard_map/ppermute | solution.py:22
  55.0 13.5 %copy-start.3 = (bf16[128,2048]{1,0:T(8,128)(2,1)S(1)}, bf16[128,2048]{1,0:T(8,128)(2,1)}, u32[]{:S(2)}) copy-start(bf16[128,2048]{1,0:T(8,128)(2,1)} %param.18) | copy-start | bytes 1572868
  55.0 13.5 %copy-start.15 = (f32[256]{0:T(256)S(1)}, f32[256]{0:T(256)}, u32[]{:S(2)}) copy-start(f32[256]{0:T(256)} %param.28) | copy-start | bytes 3076
  68.4 8.2 %copy-start.7 = (bf16[128,256]{1,0:T(8,128)(2,1)S(1)}, bf16[128,256]{1,0:T(8,128)(2,1)}, u32[]{:S(2)}) copy-start(bf16[128,256]{1,0:T(8,128)(2,1)} %copy-done.6) | copy-start | bytes 196612
  70.9 14.2 %copy-start.8 = (f32[2048]{0:T(1024)S(1)}, f32[2048]{0:T(1024)}, u32[]{:S(2)}) copy-start(f32[2048]{0:T(1024)} %param.30) | copy-start | bytes 24580
  71.0 1.8 %collective-permute-start.9 = (bf16[2,2,16,2048]{3,2,1,0:T(8,128)(2,1)S(1)}, bf16[2,2,16,2048]{3,2,1,0:T(8,128)(2,1)}, u32[]{:S(2)}, u32[]{:S(2)}) collective-permute-start(bf16[2,2,16,2048]{3,2,1,0:T(8,128)(2,1)S(1)} %dynamic-slice_bitcast_fusion.1), channel_id=1, source_target_pairs={{0,1},{1,0},{2,3},{3,2},{4,5},{5,4},{6,7},{7,6},{8,9},{9,8},{10,11... | collective-permute-start | bytes 786440 | tf_op jit(solution)/shard_map/ppermute | solution.py:22
  73.8 6.8 %collective-permute-start.10 = (bf16[2,16,2048]{2,1,0:T(8,128)(2,1)S(1)}, bf16[2,16,2048]{2,1,0:T(8,128)(2,1)S(1)}, u32[]{:S(2)}, u32[]{:S(2)}) collective-permute-start(bf16[2,16,2048]{2,1,0:T(8,128)(2,1)S(1)} %fusion.15), channel_id=1, source_target_pairs={{0,6},{1,7},{2,4},{3,5},{4,2},{5,3},{6,0},{7,1},{8,14},{9,15},{10,... | collective-permute-start | bytes 393224 | tf_op jit(solution)/shard_map/ppermute | solution.py:22
  80.7 4.4 %collective-permute-start.11 = (bf16[16,2048]{1,0:T(8,128)(2,1)S(1)}, bf16[16,2048]{1,0:T(8,128)(2,1)S(1)}, u32[]{:S(2)}, u32[]{:S(2)}) collective-permute-start(bf16[16,2048]{1,0:T(8,128)(2,1)S(1)} %fusion.30), channel_id=1, source_target_pairs={{0,2},{1,3},{2,0},{3,1},{4,6},{5,7},{6,4},{7,5},{8,10},{9,11},{10,... | collective-permute-start | bytes 196616 | tf_op jit(solution)/shard_map/ppermute | solution.py:22
  80.8 6.2 %collective-permute-start.18 = (bf16[16,19,256]{2,1,0:T(8,128)(2,1)S(1)}, bf16[16,19,256]{2,1,0:T(8,128)(2,1)S(1)}, u32[]{:S(2)}, u32[]{:S(2)}) collective-permute-start(bf16[16,19,256]{2,1,0:T(8,128)(2,1)S(1)} %pad_maximum_fusion.2), channel_id=1, source_target_pairs={{0,8},{8,0},{16,24},{24,16},{32,40},{40,32},{48,56},{56,48},{64,72... | collective-permute-start | bytes 466952 | tf_op jit(solution)/shard_map/ppermute | solution.py:22
  85.3 4.4 %collective-permute-start.12 = (bf16[16,2048]{1,0:T(8,128)(2,1)S(1)}, bf16[16,2048]{1,0:T(8,128)(2,1)S(1)}, u32[]{:S(2)}, u32[]{:S(2)}) collective-permute-start(bf16[16,2048]{1,0:T(8,128)(2,1)S(1)} %multiply_convert_fusion), channel_id=1, source_target_pairs={{0,2},{1,3},{2,0},{3,1},{4,6},{5,7},{6,4},{7,5},{8,10},{9,11},{10,... | collective-permute-start | bytes 196616 | tf_op jit(solution)/shard_map/ppermute | solution.py:22
  87.0 6.2 %collective-permute-start.19 = (bf16[16,19,256]{2,1,0:T(8,128)(2,1)S(1)}, bf16[16,19,256]{2,1,0:T(8,128)(2,1)S(1)}, u32[]{:S(2)}, u32[]{:S(2)}) collective-permute-start(bf16[16,19,256]{2,1,0:T(8,128)(2,1)S(1)} %fusion.64), channel_id=1, source_target_pairs={{0,24},{8,16},{16,8},{24,0},{32,56},{40,48},{48,40},{56,32},{64,88... | collective-permute-start | bytes 466952 | tf_op jit(solution)/shard_map/ppermute | solution.py:22
  89.8 6.3 %collective-permute-start.13 = (bf16[2,16,2048]{2,1,0:T(8,128)(2,1)S(1)}, bf16[2,16,2048]{2,1,0:T(8,128)(2,1)S(1)}, u32[]{:S(2)}, u32[]{:S(2)}) collective-permute-start(bf16[2,16,2048]{2,1,0:T(8,128)(2,1)S(1)} %pad_maximum_fusion.4), channel_id=1, source_target_pairs={{0,6},{1,7},{2,4},{3,5},{4,2},{5,3},{6,0},{7,1},{8,14},{9,15},{10,... | collective-permute-start | bytes 393224 | tf_op jit(solution)/shard_map/ppermute | solution.py:22
  93.3 5.8 %collective-permute-start.20 = (bf16[16,19,256]{2,1,0:T(8,128)(2,1)S(1)}, bf16[16,19,256]{2,1,0:T(8,128)(2,1)S(1)}, u32[]{:S(2)}, u32[]{:S(2)}) collective-permute-start(bf16[16,19,256]{2,1,0:T(8,128)(2,1)S(1)} %add.351), channel_id=1, source_target_pairs={{0,32},{8,40},{16,48},{24,56},{32,0},{40,8},{48,16},{56,24},{64,96... | collective-permute-start | bytes 466952 | tf_op jit(solution)/shard_map/ppermute | solution.py:22
  96.1 16.8 %collective-permute-start.14 = (bf16[2,2,16,2048]{3,2,1,0:T(8,128)(2,1)S(1)}, bf16[2,2,16,2048]{3,2,1,0:T(8,128)(2,1)S(1)}, u32[]{:S(2)}, u32[]{:S(2)}) collective-permute-start(bf16[2,2,16,2048]{3,2,1,0:T(8,128)(2,1)S(1)} %pad_maximum_fusion.1), channel_id=1, source_target_pairs={{0,1},{1,0},{2,3},{3,2},{4,5},{5,4},{6,7},{7,6},{8,9},{9,8},{10,11... | collective-permute-start | bytes 786440 | tf_op jit(solution)/shard_map/ppermute | solution.py:22
  99.1 8.2 %collective-permute-start.21 = (bf16[16,19,256]{2,1,0:T(8,128)(2,1)S(1)}, bf16[16,19,256]{2,1,0:T(8,128)(2,1)S(1)}, u32[]{:S(2)}, u32[]{:S(2)}) collective-permute-start(bf16[16,19,256]{2,1,0:T(8,128)(2,1)S(1)} %add.352), channel_id=1, source_target_pairs={{0,64},{8,72},{16,80},{24,88},{32,96},{40,104},{48,112},{56,120},{... | collective-permute-start | bytes 466952 | tf_op jit(solution)/shard_map/ppermute | solution.py:22
  101.8 11.1 %copy-start.1 = (bf16[2048,512]{1,0:T(8,128)(2,1)S(1)}, bf16[2048,512]{1,0:T(8,128)(2,1)}, u32[]{:S(2)}) copy-start(bf16[2048,512]{1,0:T(8,128)(2,1)} %param.31) | copy-start | bytes 6291460
  108.0 13.6 %collective-permute-start.22 = (bf16[16,19,256]{2,1,0:T(8,128)(2,1)}, bf16[16,19,256]{2,1,0:T(8,128)(2,1)}, u32[]{:S(2)}, u32[]{:S(2)}) collective-permute-start(bf16[16,19,256]{2,1,0:T(8,128)(2,1)} %add.353), channel_id=1, source_target_pairs={{0,192},{8,200},{16,208},{24,216},{32,224},{40,232},{48,240},{56,2... | collective-permute-start | bytes 466952 | tf_op jit(solution)/shard_map/ppermute | solution.py:22
  113.5 2.6 %copy-start.17 = (s32[128]{0:T(128)S(1)}, s32[128]{0:T(128)}, u32[]{:S(2)}) copy-start(s32[128]{0:T(128)} %copy-done.16) | copy-start | bytes 1540
  115.9 9.8 %copy-start.14 = (s32[4]{0:T(128)S(1)}, s32[4]{0:T(128)}, u32[]{:S(2)}) copy-start(s32[4]{0:T(128)} %param.35) | copy-start | bytes 52
  115.9 6.8 %collective-permute-start.15 = (bf16[2,2,16,2048]{3,2,1,0:T(8,128)(2,1)S(1)}, bf16[2,2,16,2048]{3,2,1,0:T(8,128)(2,1)S(1)}, u32[]{:S(2)}, u32[]{:S(2)}) collective-permute-start(bf16[2,2,16,2048]{3,2,1,0:T(8,128)(2,1)S(1)} %dynamic-slice_bitcast_fusion), channel_id=1, source_target_pairs={{0,1},{1,0},{2,3},{3,2},{4,5},{5,4},{6,7},{7,6},{8,9},{9,8},{10,11... | collective-permute-start | bytes 786440 | tf_op jit(solution)/shard_map/ppermute | solution.py:22
  122.8 6.3 %collective-permute-start.16 = (bf16[2,16,2048]{2,1,0:T(8,128)(2,1)S(1)}, bf16[2,16,2048]{2,1,0:T(8,128)(2,1)S(1)}, u32[]{:S(2)}, u32[]{:S(2)}) collective-permute-start(bf16[2,16,2048]{2,1,0:T(8,128)(2,1)S(1)} %fusion.16), channel_id=1, source_target_pairs={{0,6},{1,7},{2,4},{3,5},{4,2},{5,3},{6,0},{7,1},{8,14},{9,15},{10,... | collective-permute-start | bytes 393224 | tf_op jit(solution)/shard_map/ppermute | solution.py:22
  129.1 4.4 %collective-permute-start.17 = (bf16[16,2048]{1,0:T(8,128)(2,1)S(1)}, bf16[16,2048]{1,0:T(8,128)(2,1)S(1)}, u32[]{:S(2)}, u32[]{:S(2)}) collective-permute-start(bf16[16,2048]{1,0:T(8,128)(2,1)S(1)} %fusion.31), channel_id=1, source_target_pairs={{0,2},{1,3},{2,0},{3,1},{4,6},{5,7},{6,4},{7,5},{8,10},{9,11},{10,... | collective-permute-start | bytes 196616 | tf_op jit(solution)/shard_map/ppermute | solution.py:22

commit v9 on v6

--- a/solution.py
+++ b/solution.py
@@ -180,12 +180,15 @@
     )(da, dr, om, sin, endf, pid)
 
 
-def entering_state(a_blk, s_blk, axis):
+def entering_state(a_blk, s_blk, axis, rider):
     me = lax.axis_index(axis)
     tot_a, tot_s = a_blk, s_blk
     exc_a, exc_s = jnp.ones_like(a_blk), jnp.zeros_like(s_blk)
     for mask, top in basis_of(axis):
         got = swap(jnp.stack([tot_a, tot_s]), axis, mask)
+        if rider is not None:
+            got, rider = lax.optimization_barrier((got, rider))
+            rider_out, rider = rider, None
         got_a, got_s = got[0], got[1]
         upper = ((me // (1 << top)) % 2) == 1
         low_a = jnp.where(upper, got_a, tot_a)
@@ -197,7 +200,7 @@
             jnp.where(upper, exc_a * got_s + exc_s, exc_s),
         )
         tot_a, tot_s = low_a * high_a, high_a * low_s + high_s
-    return exc_s
+    return exc_s, rider_out
 
 
 def local(
@@ -266,7 +269,7 @@
     conv_out = jax.nn.silu(conv_sum).astype(jnp.bfloat16)
     conv_float = conv_out.astype(jnp.float32)
     projected = butterfly_sum(
-        jnp.dot(conv_out, w_xproj, preferred_element_type=jnp.float32), "tp", jnp.float32
+        jnp.dot(conv_out, w_xproj, preferred_element_type=jnp.float32), "tp", jnp.bfloat16
     )
     low_rank = projected[:, :low_dim].astype(jnp.bfloat16)
     in_map = projected[:, low_dim : low_dim + state_dim]
@@ -280,7 +283,7 @@
     drive = (step_size * conv_float)[:, None, :] * in_map[:, :, None]
     out_wide = jnp.broadcast_to(out_map[:, :, None], decay.shape)
     s_blk, a_blk = block_summary(decay, drive)
-    state_in = entering_state(a_blk, s_blk, "seq")
+    state_in, out_wide = entering_state(a_blk, s_blk, "seq", out_wide)
     end_flag = ends_here.astype(jnp.int32)
     slot_of = jnp.minimum(prompt_of, prompts - 1).astype(jnp.int32)
     mixer_y, final_part = block_output(decay, drive, out_wide, state_in, end_flag, slot_of, prompts)

time: 129 us -> 127 us (0.984)
  no operation moved by 1% of the time
where the time goes in v9:
time: 127 us
  waiting for transfers between devices  49.1 us (39%)
  starting transfers between devices  38.8 us (31%)
  other arithmetic  14.7 us (12%)
  matrix products  9.03 us (7%)
  Pallas kernels  8.56 us (7%)
  local copies, waits for them, and re-layouts  5.32 us (4%)
    ppermute x22, waiting for transfers between devices, swap(): return lax.ppermute(x, axis, [(i, i ^ bit) for i in range(devices)])  49.1 us
    ppermute x22, starting transfers between devices, swap(): return lax.ppermute(x, axis, [(i, i ^ bit) for i in range(devices)])  37.1 us
    pallas_call x1, Pallas kernels, block_output(): pl.pallas_call(block_output_kernel, out_shape=(jax.ShapeDtypeStruct((t, e...  5.42 us
    pallas_call x1, Pallas kernels, block_summary(): pl.pallas_call(block_summary_kernel, out_shape=(jax.ShapeDtypeStruct((n,...  3.14 us
  transfers between devices with their start and end apart: 23, of which 19 were waited for; matrix products, arithmetic and copies ran while one was open for 13% of the time, Pallas kernels for 0%

profile of v9, /device:TPU:40, one launch (start us, length us, event | category | flops | bytes accessed | tf_op | source)
XLA Modules:
  0.0 126.7 jit_solution(7995535676187317717)
XLA Ops:
  0.7 0.9 slice.69
  1.6 1.7 %collective-permute-start = (bf16[3,2048]{1,0:T(4,128)(2,1)S(1)}, bf16[3,2048]{1,0:T(4,128)(2,1)S(1)}, u32[]{:S(2)}, u32[]{:S(2)}) collective-permute-start(bf16[3,2048]{1,0:T(4,128)(2,1)S(1)} %slice.69), channel_id=1, source_target_pairs={{0,8},{8,16},{16,24},{24,32},{32,40},{40,48},{48,56},{56,64},{64,7... | collective-permute-start | bytes 36872 | tf_op jit(solution)/shard_map/ppermute | solution.py:251
  3.3 1.2 fusion.2
  4.5 0.8 fusion.73
  6.3 1.2 broadcast_add_fusion
  7.6 1.8 %convolution_convert_fusion.3 = bf16[128,256]{1,0:T(8,128)(2,1)S(1)} fusion(bf16[2048,256]{1,0:T(8,128)(2,1)} %param.20, bf16[128,2048]{1,0:T(8,128)(2,1)} %param.18, f32[2048]{0:T(1024)} %param.19, f32[128]{0:T(128)S(1)} %add_rsqrt_fusion.2), kind=kOutput, calls=%fused_computation.10 | convolution fusion | flops 135299072 | bytes 1647104 | tf_op jit(solution)/shard_map/dot_general | solution.py:258
  10.4 1.2 collective-permute-done.1
  11.6 1.6 %collective-permute-start.2 = (bf16[128,160]{0,1:T(8,128)(2,1)S(1)}, bf16[128,160]{0,1:T(8,128)(2,1)S(1)}, u32[]{:S(2)}, u32[]{:S(2)}) collective-permute-start(bf16[128,160]{0,1:T(8,128)(2,1)S(1)} %fusion.39), channel_id=1, source_target_pairs={{0,2},{1,3},{2,0},{3,1},{4,6},{5,7},{6,4},{7,5},{8,10},{9,11},{10,... | collective-permute-start | bytes 122888 | tf_op jit(solution)/shard_map/ppermute | solution.py:22
  13.2 2.4 %collective-permute-done.2 = bf16[128,160]{0,1:T(8,128)(2,1)S(1)} collective-permute-done((bf16[128,160]{0,1:T(8,128)(2,1)S(1)}, bf16[128,160]{0,1:T(8,128)(2,1)S(1)}, u32[]{:S(2)}, u32[]{:S(2)}) %collective-permute-start.2) | collective-permute-done | bytes 40992 | tf_op jit(solution)/shard_map/ppermute | solution.py:22
  15.7 2.8 %collective-permute-start.3 = (bf16[128,160]{0,1:T(8,128)(2,1)S(1)}, bf16[128,160]{0,1:T(8,128)(2,1)S(1)}, u32[]{:S(2)}, u32[]{:S(2)}) collective-permute-start(bf16[128,160]{0,1:T(8,128)(2,1)S(1)} %fusion.45), channel_id=1, source_target_pairs={{0,6},{1,7},{2,4},{3,5},{4,2},{5,3},{6,0},{7,1},{8,14},{9,15},{10,... | collective-permute-start | bytes 122888 | tf_op jit(solution)/shard_map/ppermute | solution.py:22
  18.5 2.4 %collective-permute-done.3 = bf16[128,160]{0,1:T(8,128)(2,1)S(1)} collective-permute-done((bf16[128,160]{0,1:T(8,128)(2,1)S(1)}, bf16[128,160]{0,1:T(8,128)(2,1)S(1)}, u32[]{:S(2)}, u32[]{:S(2)}) %collective-permute-start.3) | collective-permute-done | bytes 40992 | tf_op jit(solution)/shard_map/ppermute | solution.py:22
  21.4 2.4 %exponential_multiply_fusion = (f32[128,16,256]{2,1,0:T(8,128)}, f32[128,16,256]{2,1,0:T(8,128)}) fusion(f32[128]{0:T(128)S(1)} %convert_subtract_fusion, f32[16,256]{1,0:T(8,128)S(1)} %exponential_negate_fusion, f32[128,256]{1,0:T(8,128)S(1)} %get-tuple-element.62, f32[128,16]{1,0:T(8,128)S(1)} %copy.51, f32[128,256]{1,0:T(8,128)S(1)} %get-tuple-element.61), kind=kLoop, calls=%fused_computation.2 | loop fusion | flops 1572864 | bytes 4481536 | tf_op jit(solution)/shard_map/mul | solution.py:282
  23.8 3.1 %shard_map.193 = (f32[16,256]{1,0:T(8,128)}, f32[16,256]{1,0:T(8,128)}) custom-call(f32[128,16,256]{2,1,0:T(8,128)} %get-tuple-element.63.da_ref, f32[128,16,256]{2,1,0:T(8,128)} %get-tuple-element.64.dr_ref), custom_call_target="tpu_custom_call" | custom-call | tf_op jit(solution)/shard_map/pallas_call | solution.py:155
  27.0 0.8 pad_maximum_fusion.5
  28.3 3.4 %collective-permute-done.4 = f32[2,16,256]{2,1,0:T(8,128)S(1)} collective-permute-done((f32[2,16,256]{2,1,0:T(8,128)S(1)}, f32[2,16,256]{2,1,0:T(8,128)S(1)}, u32[]{:S(2)}, u32[]{:S(2)}) %collective-permute-start.4) | collective-permute-done | bytes 32800 | tf_op jit(solution)/shard_map/ppermute | solution.py:22
  31.7 1.7 %broadcast_in_dim.20.om_ref = f32[128,16,256]{2,1,0:T(8,128)} broadcast(f32[128,16]{1,0:T(8,128)S(1)} %copy.52), dimensions={0,1} | broadcast | bytes 2105344 | tf_op jit(solution)/shard_map/broadcast_in_dim | solution.py:284
  33.4 1.4 %collective-permute-start.5 = (f32[2,16,256]{2,1,0:T(8,128)S(1)}, f32[2,16,256]{2,1,0:T(8,128)S(1)}, u32[]{:S(2)}, u32[]{:S(2)}) collective-permute-start(f32[2,16,256]{2,1,0:T(8,128)S(1)} %pad_maximum_fusion.6), channel_id=1, source_target_pairs={{0,24},{8,16},{16,8},{24,0},{32,56},{40,48},{48,40},{56,32},{64,88... | collective-permute-start | bytes 98312 | tf_op jit(solution)/shard_map/ppermute | solution.py:22
  34.8 2.6 %collective-permute-done.5 = f32[2,16,256]{2,1,0:T(8,128)S(1)} collective-permute-done((f32[2,16,256]{2,1,0:T(8,128)S(1)}, f32[2,16,256]{2,1,0:T(8,128)S(1)}, u32[]{:S(2)}, u32[]{:S(2)}) %collective-permute-start.5) | collective-permute-done | bytes 32800 | tf_op jit(solution)/shard_map/ppermute | solution.py:22
  37.4 0.9 collective-permute-start.6
  38.3 3.1 %collective-permute-done.6 = f32[2,16,256]{2,1,0:T(8,128)S(1)} collective-permute-done((f32[2,16,256]{2,1,0:T(8,128)S(1)}, f32[2,16,256]{2,1,0:T(8,128)S(1)}, u32[]{:S(2)}, u32[]{:S(2)}) %collective-permute-start.6) | collective-permute-done | bytes 32800 | tf_op jit(solution)/shard_map/ppermute | solution.py:22
  41.5 3.4 %collective-permute-start.7 = (f32[2,16,256]{2,1,0:T(8,128)S(1)}, f32[2,16,256]{2,1,0:T(8,128)S(1)}, u32[]{:S(2)}, u32[]{:S(2)}) collective-permute-start(f32[2,16,256]{2,1,0:T(8,128)S(1)} %pad_maximum_fusion.8), channel_id=1, source_target_pairs={{0,64},{8,72},{16,80},{24,88},{32,96},{40,104},{48,112},{56,120},{... | collective-permute-start | bytes 98312 | tf_op jit(solution)/shard_map/ppermute | solution.py:22
  45.3 1.8 %collective-permute-done.7 = f32[2,16,256]{2,1,0:T(8,128)S(1)} collective-permute-done((f32[2,16,256]{2,1,0:T(8,128)S(1)}, f32[2,16,256]{2,1,0:T(8,128)S(1)}, u32[]{:S(2)}, u32[]{:S(2)}) %collective-permute-start.7) | collective-permute-done | bytes 32800 | tf_op jit(solution)/shard_map/ppermute | solution.py:22
  47.1 4.8 %collective-permute-start.8 = (f32[2,16,256]{2,1,0:T(8,128)S(1)}, f32[2,16,256]{2,1,0:T(8,128)S(1)}, u32[]{:S(2)}, u32[]{:S(2)}) collective-permute-start(f32[2,16,256]{2,1,0:T(8,128)S(1)} %pad_maximum_fusion.9), channel_id=1, source_target_pairs={{0,192},{8,200},{16,208},{24,216},{32,224},{40,232},{48,240},{56,2... | collective-permute-start | bytes 98312 | tf_op jit(solution)/shard_map/ppermute | solution.py:22
  54.4 5.4 %shard_map.194 = (f32[128,256]{1,0:T(8,128)}, f32[16,16,256]{2,1,0:T(8,128)}) custom-call(f32[128,16,256]{2,1,0:T(8,128)} %get-tuple-element.63.da_ref, f32[128,16,256]{2,1,0:T(8,128)} %get-tuple-element.64.dr_ref, f32[128,16,256]{2,1,0:T(8,128)} %broadcast_in_dim.20.om_ref, f32[16,256]{1,0:T(8,128)} %add_select_fusion.sin_ref, ...), custom_call_target="tpu_custom_call" | custom-call | tf_op jit(solution)/shard_map/pallas_call | solution.py:171
  59.8 2.5 %convolution_convert_fusion.1 = bf16[128,2048]{1,0:T(8,128)(2,1)S(1)} fusion(bf16[256,2048]{1,0:T(8,128)(2,1)} %param.29, f32[128,256]{1,0:T(8,128)} %get-tuple-element.13, bf16[128,256]{1,0:T(8,128)(2,1)S(1)} %multiply_convert_fusion.1, bf16[2048,256]{1,0:T(8,128)(2,1)} %param.21, bf16[128,2048]{1,0:T(8,128)(2,1)S(1)} %copy-done.3, ...), kind=kOutput, calls=%fused_computation.1 | convolution fusion | flops 270106624 | bytes 3352064 | tf_op jit(solution)/shard_map/dot_general | solution.py:315
  63.2 0.9 collective-permute-done.9
  64.1 1.0 convert_add_fusion.1
  65.2 2.8 %collective-permute-start.10 = (bf16[2,16,2048]{2,1,0:T(8,128)(2,1)S(1)}, bf16[2,16,2048]{2,1,0:T(8,128)(2,1)S(1)}, u32[]{:S(2)}, u32[]{:S(2)}) collective-permute-start(bf16[2,16,2048]{2,1,0:T(8,128)(2,1)S(1)} %fusion.15), channel_id=1, source_target_pairs={{0,6},{1,7},{2,4},{3,5},{4,2},{5,3},{6,0},{7,1},{8,14},{9,15},{10,... | collective-permute-start | bytes 393224 | tf_op jit(solution)/shard_map/ppermute | solution.py:22
  68.2 1.0 convert_element_type.245
  69.2 2.8 %collective-permute-done.10 = bf16[2,16,2048]{2,1,0:T(8,128)(2,1)S(1)} collective-permute-done((bf16[2,16,2048]{2,1,0:T(8,128)(2,1)S(1)}, bf16[2,16,2048]{2,1,0:T(8,128)(2,1)S(1)}, u32[]{:S(2)}, u32[]{:S(2)}) %collective-permute-start.10) | collective-permute-done | bytes 131104 | tf_op jit(solution)/shard_map/ppermute | solution.py:22
  72.2 1.8 %collective-permute-start.18 = (bf16[16,19,256]{2,1,0:T(8,128)(2,1)S(1)}, bf16[16,19,256]{2,1,0:T(8,128)(2,1)S(1)}, u32[]{:S(2)}, u32[]{:S(2)}) collective-permute-start(bf16[16,19,256]{2,1,0:T(8,128)(2,1)S(1)} %pad_maximum_fusion.2), channel_id=1, source_target_pairs={{0,8},{8,0},{16,24},{24,16},{32,40},{40,32},{48,56},{56,48},{64,72... | collective-permute-start | bytes 466952 | tf_op jit(solution)/shard_map/ppermute | solution.py:22
  74.0 2.4 %collective-permute-done.11 = bf16[16,2048]{1,0:T(8,128)(2,1)S(1)} collective-permute-done((bf16[16,2048]{1,0:T(8,128)(2,1)S(1)}, bf16[16,2048]{1,0:T(8,128)(2,1)S(1)}, u32[]{:S(2)}, u32[]{:S(2)}) %collective-permute-start.11) | collective-permute-done | bytes 65568 | tf_op jit(solution)/shard_map/ppermute | solution.py:22
  76.8 1.6 %collective-permute-done.18 = bf16[16,19,256]{2,1,0:T(8,128)(2,1)S(1)} collective-permute-done((bf16[16,19,256]{2,1,0:T(8,128)(2,1)S(1)}, bf16[16,19,256]{2,1,0:T(8,128)(2,1)S(1)}, u32[]{:S(2)}, u32[]{:S(2)}) %collective-permute-start.18) | collective-permute-done | bytes 155680 | tf_op jit(solution)/shard_map/ppermute | solution.py:22
  78.4 3.2 %collective-permute-start.19 = (bf16[16,19,256]{2,1,0:T(8,128)(2,1)S(1)}, bf16[16,19,256]{2,1,0:T(8,128)(2,1)S(1)}, u32[]{:S(2)}, u32[]{:S(2)}) collective-permute-start(bf16[16,19,256]{2,1,0:T(8,128)(2,1)S(1)} %fusion.69), channel_id=1, source_target_pairs={{0,24},{8,16},{16,8},{24,0},{32,56},{40,48},{48,40},{56,32},{64,88... | collective-permute-start | bytes 466952 | tf_op jit(solution)/shard_map/ppermute | solution.py:22
  81.8 2.8 %collective-permute-start.13 = (bf16[2,16,2048]{2,1,0:T(8,128)(2,1)S(1)}, bf16[2,16,2048]{2,1,0:T(8,128)(2,1)S(1)}, u32[]{:S(2)}, u32[]{:S(2)}) collective-permute-start(bf16[2,16,2048]{2,1,0:T(8,128)(2,1)S(1)} %pad_maximum_fusion.4), channel_id=1, source_target_pairs={{0,6},{1,7},{2,4},{3,5},{4,2},{5,3},{6,0},{7,1},{8,14},{9,15},{10,... | collective-permute-start | bytes 393224 | tf_op jit(solution)/shard_map/ppermute | solution.py:22
  84.6 0.8 collective-permute-done.19
  85.6 2.5 %collective-permute-done.13 = bf16[2,16,2048]{2,1,0:T(8,128)(2,1)S(1)} collective-permute-done((bf16[2,16,2048]{2,1,0:T(8,128)(2,1)S(1)}, bf16[2,16,2048]{2,1,0:T(8,128)(2,1)S(1)}, u32[]{:S(2)}, u32[]{:S(2)}) %collective-permute-start.13) | collective-permute-done | bytes 131104 | tf_op jit(solution)/shard_map/ppermute | solution.py:22
  88.2 3.0 %collective-permute-done.20 = bf16[16,19,256]{2,1,0:T(8,128)(2,1)S(1)} collective-permute-done((bf16[16,19,256]{2,1,0:T(8,128)(2,1)S(1)}, bf16[16,19,256]{2,1,0:T(8,128)(2,1)S(1)}, u32[]{:S(2)}, u32[]{:S(2)}) %collective-permute-start.20) | collective-permute-done | bytes 155680 | tf_op jit(solution)/shard_map/ppermute | solution.py:22
  91.3 2.7 %collective-permute-start.21 = (bf16[16,19,256]{2,1,0:T(8,128)(2,1)S(1)}, bf16[16,19,256]{2,1,0:T(8,128)(2,1)S(1)}, u32[]{:S(2)}, u32[]{:S(2)}) collective-permute-start(bf16[16,19,256]{2,1,0:T(8,128)(2,1)S(1)} %add.352), channel_id=1, source_target_pairs={{0,64},{8,72},{16,80},{24,88},{32,96},{40,104},{48,112},{56,120},{... | collective-permute-start | bytes 466952 | tf_op jit(solution)/shard_map/ppermute | solution.py:22
  93.9 5.5 %collective-permute-done.21 = bf16[16,19,256]{2,1,0:T(8,128)(2,1)S(1)} collective-permute-done((bf16[16,19,256]{2,1,0:T(8,128)(2,1)S(1)}, bf16[16,19,256]{2,1,0:T(8,128)(2,1)S(1)}, u32[]{:S(2)}, u32[]{:S(2)}) %collective-permute-start.21) | collective-permute-done | bytes 155680 | tf_op jit(solution)/shard_map/ppermute | solution.py:22
  100.1 4.8 %collective-permute-start.22 = (bf16[16,19,256]{2,1,0:T(8,128)(2,1)}, bf16[16,19,256]{2,1,0:T(8,128)(2,1)}, u32[]{:S(2)}, u32[]{:S(2)}) collective-permute-start(bf16[16,19,256]{2,1,0:T(8,128)(2,1)} %add.353), channel_id=1, source_target_pairs={{0,192},{8,200},{16,208},{24,216},{32,224},{40,232},{48,240},{56,2... | collective-permute-start | bytes 466952 | tf_op jit(solution)/shard_map/ppermute | solution.py:22
  105.5 2.4 %convolution_convert_fusion = bf16[128,2048]{1,0:T(8,128)(2,1)S(1)} fusion(bf16[512,2048]{1,0:T(8,128)(2,1)S(1)} %copy-done, bf16[128,2048]{1,0:T(8,128)(2,1)S(1)} %bitcast.175, bf16[2048,512]{1,0:T(8,128)(2,1)} %param.32, f32[128,512]{1,0:T(8,128)S(1)} %fusion.75), kind=kOutput, calls=%fused_computation | convolution fusion | flops 537526272 | bytes 5505024 | tf_op jit(solution)/shard_map/dot_general | solution.py:327
  108.2 5.4 %collective-permute-done.22 = bf16[16,19,256]{2,1,0:T(8,128)(2,1)} collective-permute-done((bf16[16,19,256]{2,1,0:T(8,128)(2,1)}, bf16[16,19,256]{2,1,0:T(8,128)(2,1)}, u32[]{:S(2)}, u32[]{:S(2)}) %collective-permute-start.22) | collective-permute-done | bytes 155680 | tf_op jit(solution)/shard_map/ppermute | solution.py:22
  113.6 1.1 add.354
  114.9 2.8 %collective-permute-start.16 = (bf16[2,16,2048]{2,1,0:T(8,128)(2,1)S(1)}, bf16[2,16,2048]{2,1,0:T(8,128)(2,1)S(1)}, u32[]{:S(2)}, u32[]{:S(2)}) collective-permute-start(bf16[2,16,2048]{2,1,0:T(8,128)(2,1)S(1)} %fusion.16), channel_id=1, source_target_pairs={{0,6},{1,7},{2,4},{3,5},{4,2},{5,3},{6,0},{7,1},{8,14},{9,15},{10,... | collective-permute-start | bytes 393224 | tf_op jit(solution)/shard_map/ppermute | solution.py:22
  117.9 3.7 %collective-permute-done.16 = bf16[2,16,2048]{2,1,0:T(8,128)(2,1)S(1)} collective-permute-done((bf16[2,16,2048]{2,1,0:T(8,128)(2,1)S(1)}, bf16[2,16,2048]{2,1,0:T(8,128)(2,1)S(1)}, u32[]{:S(2)}, u32[]{:S(2)}) %collective-permute-start.16) | collective-permute-done | bytes 131104 | tf_op jit(solution)/shard_map/ppermute | solution.py:22
  121.7 0.8 convolution_convert_fusion.5
  123.1 2.8 %collective-permute-done.17 = bf16[16,2048]{1,0:T(8,128)(2,1)S(1)} collective-permute-done((bf16[16,2048]{1,0:T(8,128)(2,1)S(1)}, bf16[16,2048]{1,0:T(8,128)(2,1)S(1)}, u32[]{:S(2)}, u32[]{:S(2)}) %collective-permute-start.17) | collective-permute-done | bytes 65568 | tf_op jit(solution)/shard_map/ppermute | solution.py:22
  (125 shorter events, 11.5 us)
Async XLA Ops:
  0.6 104.9 %copy-start = (bf16[512,2048]{1,0:T(8,128)(2,1)S(1)}, bf16[512,2048]{1,0:T(8,128)(2,1)}, u32[]{:S(2)}) copy-start(bf16[512,2048]{1,0:T(8,128)(2,1)} %param.33) | copy-start | bytes 6291460
  0.6 9.0 %copy-start.12 = (f32[2048]{0:T(1024)S(1)}, f32[2048]{0:T(1024)}, u32[]{:S(2)}) copy-start(f32[2048]{0:T(1024)} %param.19) | copy-start | bytes 24580
  0.7 8.9 %copy-start.2 = (bf16[2048,256]{1,0:T(8,128)(2,1)S(1)}, bf16[2048,256]{1,0:T(8,128)(2,1)}, u32[]{:S(2)}) copy-start(bf16[2048,256]{1,0:T(8,128)(2,1)} %param.20) | copy-start | bytes 3145732
  0.7 9.2 %copy-start.14 = (f32[256]{0:T(256)S(1)}, f32[256]{0:T(256)}, u32[]{:S(2)}) copy-start(f32[256]{0:T(256)} %param.23) | copy-start | bytes 3076
  0.7 9.4 %copy-start.4 = (bf16[256,160]{0,1:T(8,128)(2,1)S(1)}, bf16[256,160]{0,1:T(8,128)(2,1)}, u32[]{:S(2)}) copy-start(bf16[256,160]{0,1:T(8,128)(2,1)} %param.24) | copy-start | bytes 245764
  0.7 9.7 %copy-start.11 = (f32[16,256]{1,0:T(8,128)S(1)}, f32[16,256]{1,0:T(8,128)}, u32[]{:S(2)}) copy-start(f32[16,256]{1,0:T(8,128)} %param.27) | copy-start | bytes 49156
  1.6 7.8 %collective-permute-start = (bf16[3,2048]{1,0:T(4,128)(2,1)S(1)}, bf16[3,2048]{1,0:T(4,128)(2,1)S(1)}, u32[]{:S(2)}, u32[]{:S(2)}) collective-permute-start(bf16[3,2048]{1,0:T(4,128)(2,1)S(1)} %slice.69), channel_id=1, source_target_pairs={{0,8},{8,16},{16,24},{24,32},{32,40},{40,48},{48,56},{56,64},{64,7... | collective-permute-start | bytes 36872 | tf_op jit(solution)/shard_map/ppermute | solution.py:251
  7.4 19.5 %copy-start.13 = (s32[16]{0:T(128)}, s32[16]{0:T(128)S(1)}, u32[]{:S(2)}) copy-start(s32[16]{0:T(128)S(1)} %get-tuple-element.55) | copy-start | bytes 196
  7.5 37.3 %copy-start.18 = (s32[128]{0:T(128)}, s32[128]{0:T(128)S(1)}, u32[]{:S(2)}) copy-start(s32[128]{0:T(128)S(1)} %convert_reduce_fusion) | copy-start | bytes 1540
  7.6 13.5 %copy-start.5 = (bf16[128,256]{1,0:T(8,128)(2,1)S(1)}, bf16[128,256]{1,0:T(8,128)(2,1)}, u32[]{:S(2)}) copy-start(bf16[128,256]{1,0:T(8,128)(2,1)} %param.25) | copy-start | bytes 196612
  7.6 13.5 %copy-start.15 = (f32[256]{0:T(256)S(1)}, f32[256]{0:T(256)}, u32[]{:S(2)}) copy-start(f32[256]{0:T(256)} %param.26) | copy-start | bytes 3076
  9.4 11.6 %copy-start.6 = (bf16[128,256]{1,0:T(8,128)(2,1)}, bf16[128,256]{1,0:T(8,128)(2,1)S(1)}, u32[]{:S(2)}) copy-start(bf16[128,256]{1,0:T(8,128)(2,1)S(1)} %convolution_convert_fusion.3) | copy-start | bytes 196612
  10.3 1.3 %collective-permute-start.1 = (bf16[128,160]{0,1:T(8,128)(2,1)S(1)}, bf16[128,160]{0,1:T(8,128)(2,1)S(1)}, u32[]{:S(2)}, u32[]{:S(2)}) collective-permute-start(bf16[128,160]{0,1:T(8,128)(2,1)S(1)} %get-tuple-element.59), channel_id=1, source_target_pairs={{0,1},{1,0},{2,3},{3,2},{4,5},{5,4},{6,7},{7,6},{8,9},{9,8},{10,11... | collective-permute-start | bytes 122888 | tf_op jit(solution)/shard_map/ppermute | solution.py:22
  11.6 4.1 %collective-permute-start.2 = (bf16[128,160]{0,1:T(8,128)(2,1)S(1)}, bf16[128,160]{0,1:T(8,128)(2,1)S(1)}, u32[]{:S(2)}, u32[]{:S(2)}) collective-permute-start(bf16[128,160]{0,1:T(8,128)(2,1)S(1)} %fusion.39), channel_id=1, source_target_pairs={{0,2},{1,3},{2,0},{3,1},{4,6},{5,7},{6,4},{7,5},{8,10},{9,11},{10,... | collective-permute-start | bytes 122888 | tf_op jit(solution)/shard_map/ppermute | solution.py:22
  15.7 5.3 %collective-permute-start.3 = (bf16[128,160]{0,1:T(8,128)(2,1)S(1)}, bf16[128,160]{0,1:T(8,128)(2,1)S(1)}, u32[]{:S(2)}, u32[]{:S(2)}) collective-permute-start(bf16[128,160]{0,1:T(8,128)(2,1)S(1)} %fusion.45), channel_id=1, source_target_pairs={{0,6},{1,7},{2,4},{3,5},{4,2},{5,3},{6,0},{7,1},{8,14},{9,15},{10,... | collective-permute-start | bytes 122888 | tf_op jit(solution)/shard_map/ppermute | solution.py:22
  27.0 6.4 %copy-start.8 = (f32[16,256]{1,0:T(8,128)S(1)}, f32[16,256]{1,0:T(8,128)}, u32[]{:S(2)}) copy-start(f32[16,256]{1,0:T(8,128)} %get-tuple-element.10) | copy-start | bytes 49156
  27.0 6.4 %copy-start.9 = (f32[16,256]{1,0:T(8,128)S(1)}, f32[16,256]{1,0:T(8,128)}, u32[]{:S(2)}) copy-start(f32[16,256]{1,0:T(8,128)} %get-tuple-element.9) | copy-start | bytes 49156
  27.8 3.9 %collective-permute-start.4 = (f32[2,16,256]{2,1,0:T(8,128)S(1)}, f32[2,16,256]{2,1,0:T(8,128)S(1)}, u32[]{:S(2)}, u32[]{:S(2)}) collective-permute-start(f32[2,16,256]{2,1,0:T(8,128)S(1)} %pad_maximum_fusion.5), channel_id=1, source_target_pairs={{0,8},{8,0},{16,24},{24,16},{32,40},{40,32},{48,56},{56,48},{64,72... | collective-permute-start | bytes 98312 | tf_op jit(solution)/shard_map/ppermute | solution.py:22
  33.4 4.0 %collective-permute-start.5 = (f32[2,16,256]{2,1,0:T(8,128)S(1)}, f32[2,16,256]{2,1,0:T(8,128)S(1)}, u32[]{:S(2)}, u32[]{:S(2)}) collective-permute-start(f32[2,16,256]{2,1,0:T(8,128)S(1)} %pad_maximum_fusion.6), channel_id=1, source_target_pairs={{0,24},{8,16},{16,8},{24,0},{32,56},{40,48},{48,40},{56,32},{64,88... | collective-permute-start | bytes 98312 | tf_op jit(solution)/shard_map/ppermute | solution.py:22
  37.4 4.0 %collective-permute-start.6 = (f32[2,16,256]{2,1,0:T(8,128)S(1)}, f32[2,16,256]{2,1,0:T(8,128)S(1)}, u32[]{:S(2)}, u32[]{:S(2)}) collective-permute-start(f32[2,16,256]{2,1,0:T(8,128)S(1)} %pad_maximum_fusion.7), channel_id=1, source_target_pairs={{0,32},{8,40},{16,48},{24,56},{32,0},{40,8},{48,16},{56,24},{64,96... | collective-permute-start | bytes 98312 | tf_op jit(solution)/shard_map/ppermute | solution.py:22
  41.5 5.6 %collective-permute-start.7 = (f32[2,16,256]{2,1,0:T(8,128)S(1)}, f32[2,16,256]{2,1,0:T(8,128)S(1)}, u32[]{:S(2)}, u32[]{:S(2)}) collective-permute-start(f32[2,16,256]{2,1,0:T(8,128)S(1)} %pad_maximum_fusion.8), channel_id=1, source_target_pairs={{0,64},{8,72},{16,80},{24,88},{32,96},{40,104},{48,112},{56,120},{... | collective-permute-start | bytes 98312 | tf_op jit(solution)/shard_map/ppermute | solution.py:22
  47.1 6.7 %collective-permute-start.8 = (f32[2,16,256]{2,1,0:T(8,128)S(1)}, f32[2,16,256]{2,1,0:T(8,128)S(1)}, u32[]{:S(2)}, u32[]{:S(2)}) collective-permute-start(f32[2,16,256]{2,1,0:T(8,128)S(1)} %pad_maximum_fusion.9), channel_id=1, source_target_pairs={{0,192},{8,200},{16,208},{24,216},{32,224},{40,232},{48,240},{56,2... | collective-permute-start | bytes 98312 | tf_op jit(solution)/shard_map/ppermute | solution.py:22
  54.4 5.4 %copy-start.3 = (bf16[128,2048]{1,0:T(8,128)(2,1)S(1)}, bf16[128,2048]{1,0:T(8,128)(2,1)}, u32[]{:S(2)}) copy-start(bf16[128,2048]{1,0:T(8,128)(2,1)} %param.18) | copy-start | bytes 1572868
  54.4 5.4 %copy-start.17 = (f32[256]{0:T(256)S(1)}, f32[256]{0:T(256)}, u32[]{:S(2)}) copy-start(f32[256]{0:T(256)} %param.28) | copy-start | bytes 3076
  59.8 8.2 %copy-start.7 = (bf16[128,256]{1,0:T(8,128)(2,1)S(1)}, bf16[128,256]{1,0:T(8,128)(2,1)}, u32[]{:S(2)}) copy-start(bf16[128,256]{1,0:T(8,128)(2,1)} %copy-done.6) | copy-start | bytes 196612
  62.3 14.2 %copy-start.10 = (f32[2048]{0:T(1024)S(1)}, f32[2048]{0:T(1024)}, u32[]{:S(2)}) copy-start(f32[2048]{0:T(1024)} %param.30) | copy-start | bytes 24580
  62.4 1.8 %collective-permute-start.9 = (bf16[2,2,16,2048]{3,2,1,0:T(8,128)(2,1)S(1)}, bf16[2,2,16,2048]{3,2,1,0:T(8,128)(2,1)}, u32[]{:S(2)}, u32[]{:S(2)}) collective-permute-start(bf16[2,2,16,2048]{3,2,1,0:T(8,128)(2,1)S(1)} %dynamic-slice_bitcast_fusion.1), channel_id=1, source_target_pairs={{0,1},{1,0},{2,3},{3,2},{4,5},{5,4},{6,7},{7,6},{8,9},{9,8},{10,11... | collective-permute-start | bytes 786440 | tf_op jit(solution)/shard_map/ppermute | solution.py:22
  65.2 6.8 %collective-permute-start.10 = (bf16[2,16,2048]{2,1,0:T(8,128)(2,1)S(1)}, bf16[2,16,2048]{2,1,0:T(8,128)(2,1)S(1)}, u32[]{:S(2)}, u32[]{:S(2)}) collective-permute-start(bf16[2,16,2048]{2,1,0:T(8,128)(2,1)S(1)} %fusion.15), channel_id=1, source_target_pairs={{0,6},{1,7},{2,4},{3,5},{4,2},{5,3},{6,0},{7,1},{8,14},{9,15},{10,... | collective-permute-start | bytes 393224 | tf_op jit(solution)/shard_map/ppermute | solution.py:22
  72.0 4.4 %collective-permute-start.11 = (bf16[16,2048]{1,0:T(8,128)(2,1)S(1)}, bf16[16,2048]{1,0:T(8,128)(2,1)S(1)}, u32[]{:S(2)}, u32[]{:S(2)}) collective-permute-start(bf16[16,2048]{1,0:T(8,128)(2,1)S(1)} %fusion.26), channel_id=1, source_target_pairs={{0,2},{1,3},{2,0},{3,1},{4,6},{5,7},{6,4},{7,5},{8,10},{9,11},{10,... | collective-permute-start | bytes 196616 | tf_op jit(solution)/shard_map/ppermute | solution.py:22
  72.2 6.2 %collective-permute-start.18 = (bf16[16,19,256]{2,1,0:T(8,128)(2,1)S(1)}, bf16[16,19,256]{2,1,0:T(8,128)(2,1)S(1)}, u32[]{:S(2)}, u32[]{:S(2)}) collective-permute-start(bf16[16,19,256]{2,1,0:T(8,128)(2,1)S(1)} %pad_maximum_fusion.2), channel_id=1, source_target_pairs={{0,8},{8,0},{16,24},{24,16},{32,40},{40,32},{48,56},{56,48},{64,72... | collective-permute-start | bytes 466952 | tf_op jit(solution)/shard_map/ppermute | solution.py:22
  76.7 5.0 %collective-permute-start.12 = (bf16[16,2048]{1,0:T(8,128)(2,1)S(1)}, bf16[16,2048]{1,0:T(8,128)(2,1)S(1)}, u32[]{:S(2)}, u32[]{:S(2)}) collective-permute-start(bf16[16,2048]{1,0:T(8,128)(2,1)S(1)} %multiply_convert_fusion), channel_id=1, source_target_pairs={{0,2},{1,3},{2,0},{3,1},{4,6},{5,7},{6,4},{7,5},{8,10},{9,11},{10,... | collective-permute-start | bytes 196616 | tf_op jit(solution)/shard_map/ppermute | solution.py:22
  78.4 7.0 %collective-permute-start.19 = (bf16[16,19,256]{2,1,0:T(8,128)(2,1)S(1)}, bf16[16,19,256]{2,1,0:T(8,128)(2,1)S(1)}, u32[]{:S(2)}, u32[]{:S(2)}) collective-permute-start(bf16[16,19,256]{2,1,0:T(8,128)(2,1)S(1)} %fusion.69), channel_id=1, source_target_pairs={{0,24},{8,16},{16,8},{24,0},{32,56},{40,48},{48,40},{56,32},{64,88... | collective-permute-start | bytes 466952 | tf_op jit(solution)/shard_map/ppermute | solution.py:22
  81.8 6.3 %collective-permute-start.13 = (bf16[2,16,2048]{2,1,0:T(8,128)(2,1)S(1)}, bf16[2,16,2048]{2,1,0:T(8,128)(2,1)S(1)}, u32[]{:S(2)}, u32[]{:S(2)}) collective-permute-start(bf16[2,16,2048]{2,1,0:T(8,128)(2,1)S(1)} %pad_maximum_fusion.4), channel_id=1, source_target_pairs={{0,6},{1,7},{2,4},{3,5},{4,2},{5,3},{6,0},{7,1},{8,14},{9,15},{10,... | collective-permute-start | bytes 393224 | tf_op jit(solution)/shard_map/ppermute | solution.py:22
  85.5 5.8 %collective-permute-start.20 = (bf16[16,19,256]{2,1,0:T(8,128)(2,1)S(1)}, bf16[16,19,256]{2,1,0:T(8,128)(2,1)S(1)}, u32[]{:S(2)}, u32[]{:S(2)}) collective-permute-start(bf16[16,19,256]{2,1,0:T(8,128)(2,1)S(1)} %add.351), channel_id=1, source_target_pairs={{0,32},{8,40},{16,48},{24,56},{32,0},{40,8},{48,16},{56,24},{64,96... | collective-permute-start | bytes 466952 | tf_op jit(solution)/shard_map/ppermute | solution.py:22
  88.1 16.9 %collective-permute-start.14 = (bf16[2,2,16,2048]{3,2,1,0:T(8,128)(2,1)S(1)}, bf16[2,2,16,2048]{3,2,1,0:T(8,128)(2,1)S(1)}, u32[]{:S(2)}, u32[]{:S(2)}) collective-permute-start(bf16[2,2,16,2048]{3,2,1,0:T(8,128)(2,1)S(1)} %pad_maximum_fusion.1), channel_id=1, source_target_pairs={{0,1},{1,0},{2,3},{3,2},{4,5},{5,4},{6,7},{7,6},{8,9},{9,8},{10,11... | collective-permute-start | bytes 786440 | tf_op jit(solution)/shard_map/ppermute | solution.py:22
  91.3 8.1 %collective-permute-start.21 = (bf16[16,19,256]{2,1,0:T(8,128)(2,1)S(1)}, bf16[16,19,256]{2,1,0:T(8,128)(2,1)S(1)}, u32[]{:S(2)}, u32[]{:S(2)}) collective-permute-start(bf16[16,19,256]{2,1,0:T(8,128)(2,1)S(1)} %add.352), channel_id=1, source_target_pairs={{0,64},{8,72},{16,80},{24,88},{32,96},{40,104},{48,112},{56,120},{... | collective-permute-start | bytes 466952 | tf_op jit(solution)/shard_map/ppermute | solution.py:22
  93.9 11.1 %copy-start.1 = (bf16[2048,512]{1,0:T(8,128)(2,1)S(1)}, bf16[2048,512]{1,0:T(8,128)(2,1)}, u32[]{:S(2)}) copy-start(bf16[2048,512]{1,0:T(8,128)(2,1)} %param.31) | copy-start | bytes 6291460
  100.1 13.5 %collective-permute-start.22 = (bf16[16,19,256]{2,1,0:T(8,128)(2,1)}, bf16[16,19,256]{2,1,0:T(8,128)(2,1)}, u32[]{:S(2)}, u32[]{:S(2)}) collective-permute-start(bf16[16,19,256]{2,1,0:T(8,128)(2,1)} %add.353), channel_id=1, source_target_pairs={{0,192},{8,200},{16,208},{24,216},{32,224},{40,232},{48,240},{56,2... | collective-permute-start | bytes 466952 | tf_op jit(solution)/shard_map/ppermute | solution.py:22
  105.5 2.6 %copy-start.19 = (s32[128]{0:T(128)S(1)}, s32[128]{0:T(128)}, u32[]{:S(2)}) copy-start(s32[128]{0:T(128)} %copy-done.18) | copy-start | bytes 1540
  108.0 9.7 %copy-start.16 = (s32[4]{0:T(128)S(1)}, s32[4]{0:T(128)}, u32[]{:S(2)}) copy-start(s32[4]{0:T(128)} %param.35) | copy-start | bytes 52
  108.0 6.7 %collective-permute-start.15 = (bf16[2,2,16,2048]{3,2,1,0:T(8,128)(2,1)S(1)}, bf16[2,2,16,2048]{3,2,1,0:T(8,128)(2,1)S(1)}, u32[]{:S(2)}, u32[]{:S(2)}) collective-permute-start(bf16[2,2,16,2048]{3,2,1,0:T(8,128)(2,1)S(1)} %dynamic-slice_bitcast_fusion), channel_id=1, source_target_pairs={{0,1},{1,0},{2,3},{3,2},{4,5},{5,4},{6,7},{7,6},{8,9},{9,8},{10,11... | collective-permute-start | bytes 786440 | tf_op jit(solution)/shard_map/ppermute | solution.py:22
  114.9 6.7 %collective-permute-start.16 = (bf16[2,16,2048]{2,1,0:T(8,128)(2,1)S(1)}, bf16[2,16,2048]{2,1,0:T(8,128)(2,1)S(1)}, u32[]{:S(2)}, u32[]{:S(2)}) collective-permute-start(bf16[2,16,2048]{2,1,0:T(8,128)(2,1)S(1)} %fusion.16), channel_id=1, source_target_pairs={{0,6},{1,7},{2,4},{3,5},{4,2},{5,3},{6,0},{7,1},{8,14},{9,15},{10,... | collective-permute-start | bytes 393224 | tf_op jit(solution)/shard_map/ppermute | solution.py:22
  121.6 4.4 %collective-permute-start.17 = (bf16[16,2048]{1,0:T(8,128)(2,1)S(1)}, bf16[16,2048]{1,0:T(8,128)(2,1)S(1)}, u32[]{:S(2)}, u32[]{:S(2)}) collective-permute-start(bf16[16,2048]{1,0:T(8,128)(2,1)S(1)} %fusion.27), channel_id=1, source_target_pairs={{0,2},{1,3},{2,0},{3,1},{4,6},{5,7},{6,4},{7,5},{8,10},{9,11},{10,... | collective-permute-start | bytes 196616 | tf_op jit(solution)/shard_map/ppermute | solution.py:22

commit v10 on v9

--- a/solution.py
+++ b/solution.py
@@ -124,26 +124,21 @@
     atot_ref[...] = acum
 
 
-def block_output_kernel(da_ref, dr_ref, om_ref, sin_ref, endf_ref, pid_ref, y_ref, fin_ref):
+def block_output_kernel(da_ref, dr_ref, sin_ref, endf_ref, pid_ref, st_ref, fin_ref):
     steps = da_ref.shape[0]
-    width = y_ref.shape[1]
     fin_ref[...] = jnp.zeros(fin_ref.shape, jnp.float32)
-    row_ids = lax.broadcasted_iota(jnp.int32, (8, width), 0)
 
     def chunk(c, state):
-        base = pl.multiple_of(c * 8, 8)
-        rows = jnp.zeros((8, width), jnp.float32)
+        base = c * 8
         for i in range(8):
             t = base + i
             state = da_ref[t] * state + dr_ref[t]
-            here = jnp.sum(om_ref[t] * state, axis=0, keepdims=True)
-            rows = jnp.where(row_ids == i, here, rows)
+            st_ref[t] = state
 
             @pl.when(endf_ref[t] != 0)
             def _():
                 fin_ref[pid_ref[t]] = state
 
-        y_ref[pl.ds(base, 8), :] = rows
         return state
 
     lax.fori_loop(0, steps // 8, chunk, sin_ref[...])
@@ -164,26 +159,27 @@
     )(da, dr)
 
 
-def block_output(da, dr, om, sin, endf, pid, prompts):
+def block_output(da, dr, sin, endf, pid, prompts):
     t, n, e = da.shape
     vmem = pl.BlockSpec(memory_space=pltpu.VMEM)
     smem = pl.BlockSpec(memory_space=pltpu.SMEM)
     return pl.pallas_call(
         block_output_kernel,
         out_shape=(
-            jax.ShapeDtypeStruct((t, e), jnp.float32),
+            jax.ShapeDtypeStruct((t, n, e), jnp.float32),
             jax.ShapeDtypeStruct((prompts, n, e), jnp.float32),
         ),
-        in_specs=[vmem, vmem, vmem, vmem, smem, smem],
+        in_specs=[vmem, vmem, vmem, smem, smem],
         out_specs=(vmem, vmem),
         interpret=INTERPRET,
-    )(da, dr, om, sin, endf, pid)
+    )(da, dr, sin, endf, pid)
 
 
 def entering_state(a_blk, s_blk, axis, rider):
     me = lax.axis_index(axis)
     tot_a, tot_s = a_blk, s_blk
     exc_a, exc_s = jnp.ones_like(a_blk), jnp.zeros_like(s_blk)
+    rider_out = None
     for mask, top in basis_of(axis):
         got = swap(jnp.stack([tot_a, tot_s]), axis, mask)
         if rider is not None:
@@ -281,12 +277,12 @@
     carry_on = 1.0 - starts_here.astype(jnp.float32)
     decay = jnp.exp(step_size[:, None, :] * decay_rates[None, :, :]) * carry_on[:, None, None]
     drive = (step_size * conv_float)[:, None, :] * in_map[:, :, None]
-    out_wide = jnp.broadcast_to(out_map[:, :, None], decay.shape)
     s_blk, a_blk = block_summary(decay, drive)
-    state_in, out_wide = entering_state(a_blk, s_blk, "seq", out_wide)
+    state_in, _ = entering_state(a_blk, s_blk, "seq", None)
     end_flag = ends_here.astype(jnp.int32)
     slot_of = jnp.minimum(prompt_of, prompts - 1).astype(jnp.int32)
-    mixer_y, final_part = block_output(decay, drive, out_wide, state_in, end_flag, slot_of, prompts)
+    states, final_part = block_output(decay, drive, state_in, end_flag, slot_of, prompts)
+    mixer_y = jnp.sum(out_map[:, :, None] * states, axis=1)
     mixer_y = mixer_y + d_skip[None, :] * conv_float
     gated = (mixer_y * jax.nn.silu(z_branch.astype(jnp.float32))).astype(jnp.bfloat16)
     ends_local = (prompt_end - 1 >= first_row) & (prompt_end - 1 < first_row + block_len)

time: 127 us -> 128 us (level)
  other arithmetic: 14.7 us -> 17.6 us
  local copies, waits for them, and re-layouts: 5.32 us -> 3.61 us
    reduce_sum x0 -> x1, other arithmetic: none -> 2.21 us  [local(): mixer_y = jnp.sum(out_map[:, :, None] * states, axis=1)]
    broadcast_in_dim x1 -> x0, local copies, waits for them, and re-layouts: 1.71 us -> none  [local(): out_wide = jnp.broadcast_to(out_map[:, :, None], decay.shape)]
where the time goes in v10:
time: 128 us; the launch traced here: 127 us
  waiting for transfers between devices  49 us (38%)
  starting transfers between devices  38.8 us (30%)
  other arithmetic  17.6 us (14%)
  matrix products  8.96 us (7%)
  Pallas kernels  8.09 us (6%)
  local copies, waits for them, and re-layouts  3.61 us (3%)
    ppermute x22, waiting for transfers between devices, swap(): return lax.ppermute(x, axis, [(i, i ^ bit) for i in range(devices)])  49 us
    ppermute x22, starting transfers between devices, swap(): return lax.ppermute(x, axis, [(i, i ^ bit) for i in range(devices)])  37.1 us
    pallas_call x1, Pallas kernels, block_output(): pl.pallas_call(block_output_kernel, out_shape=(jax.ShapeDtypeStruct((t, n...  4.95 us
    pallas_call x1, Pallas kernels, block_summary(): pl.pallas_call(block_summary_kernel, out_shape=(jax.ShapeDtypeStruct((n,...  3.14 us
  transfers between devices with their start and end apart: 23, of which 19 were waited for; matrix products, arithmetic and copies ran while one was open for 13% of the time, Pallas kernels for 0%

profile of v10, /device:TPU:40, one launch (start us, length us, event | category | flops | bytes accessed | tf_op | source)
XLA Modules:
  0.0 127.3 jit_solution(11979948649883148621)
XLA Ops:
  0.7 0.9 slice.69
  1.6 1.7 %collective-permute-start = (bf16[3,2048]{1,0:T(4,128)(2,1)S(1)}, bf16[3,2048]{1,0:T(4,128)(2,1)S(1)}, u32[]{:S(2)}, u32[]{:S(2)}) collective-permute-start(bf16[3,2048]{1,0:T(4,128)(2,1)S(1)} %slice.69), channel_id=1, source_target_pairs={{0,8},{8,16},{16,24},{24,32},{32,40},{40,48},{48,56},{56,64},{64,7... | collective-permute-start | bytes 36872 | tf_op jit(solution)/shard_map/ppermute | solution.py:247
  3.3 1.2 fusion.2
  5.4 1.2 broadcast_add_fusion
  6.8 0.8 fusion.70
  7.6 1.8 %convolution_convert_fusion.3 = bf16[128,256]{1,0:T(8,128)(2,1)S(1)} fusion(bf16[2048,256]{1,0:T(8,128)(2,1)} %param.20, bf16[128,2048]{1,0:T(8,128)(2,1)} %param.18, f32[2048]{0:T(1024)} %param.19, f32[128]{0:T(128)S(1)} %add_rsqrt_fusion.2), kind=kOutput, calls=%fused_computation.11 | convolution fusion | flops 135299072 | bytes 1647104 | tf_op jit(solution)/shard_map/dot_general | solution.py:254
  10.4 1.2 collective-permute-done.1
  11.6 1.6 %collective-permute-start.2 = (bf16[128,160]{0,1:T(8,128)(2,1)S(1)}, bf16[128,160]{0,1:T(8,128)(2,1)S(1)}, u32[]{:S(2)}, u32[]{:S(2)}) collective-permute-start(bf16[128,160]{0,1:T(8,128)(2,1)S(1)} %fusion.38), channel_id=1, source_target_pairs={{0,2},{1,3},{2,0},{3,1},{4,6},{5,7},{6,4},{7,5},{8,10},{9,11},{10,... | collective-permute-start | bytes 122888 | tf_op jit(solution)/shard_map/ppermute | solution.py:22
  13.2 2.4 %collective-permute-done.2 = bf16[128,160]{0,1:T(8,128)(2,1)S(1)} collective-permute-done((bf16[128,160]{0,1:T(8,128)(2,1)S(1)}, bf16[128,160]{0,1:T(8,128)(2,1)S(1)}, u32[]{:S(2)}, u32[]{:S(2)}) %collective-permute-start.2) | collective-permute-done | bytes 40992 | tf_op jit(solution)/shard_map/ppermute | solution.py:22
  15.7 2.8 %collective-permute-start.3 = (bf16[128,160]{0,1:T(8,128)(2,1)S(1)}, bf16[128,160]{0,1:T(8,128)(2,1)S(1)}, u32[]{:S(2)}, u32[]{:S(2)}) collective-permute-start(bf16[128,160]{0,1:T(8,128)(2,1)S(1)} %fusion.44), channel_id=1, source_target_pairs={{0,6},{1,7},{2,4},{3,5},{4,2},{5,3},{6,0},{7,1},{8,14},{9,15},{10,... | collective-permute-start | bytes 122888 | tf_op jit(solution)/shard_map/ppermute | solution.py:22
  18.5 2.4 %collective-permute-done.3 = bf16[128,160]{0,1:T(8,128)(2,1)S(1)} collective-permute-done((bf16[128,160]{0,1:T(8,128)(2,1)S(1)}, bf16[128,160]{0,1:T(8,128)(2,1)S(1)}, u32[]{:S(2)}, u32[]{:S(2)}) %collective-permute-start.3) | collective-permute-done | bytes 40992 | tf_op jit(solution)/shard_map/ppermute | solution.py:22
  21.4 2.4 %exponential_multiply_fusion = (f32[128,16,256]{2,1,0:T(8,128)}, f32[128,16,256]{2,1,0:T(8,128)}) fusion(f32[128]{0:T(128)S(1)} %convert_subtract_fusion, f32[16,256]{1,0:T(8,128)S(1)} %exponential_negate_fusion, f32[128,256]{1,0:T(8,128)S(1)} %get-tuple-element.58, f32[128,16]{1,0:T(8,128)S(1)} %copy.52, f32[128,256]{1,0:T(8,128)S(1)} %get-tuple-element.57), kind=kLoop, calls=%fused_computation.3 | loop fusion | flops 1572864 | bytes 4481536 | tf_op jit(solution)/shard_map/mul | solution.py:278
  23.8 3.1 %shard_map.193 = (f32[16,256]{1,0:T(8,128)}, f32[16,256]{1,0:T(8,128)}) custom-call(f32[128,16,256]{2,1,0:T(8,128)} %get-tuple-element.59.da_ref, f32[128,16,256]{2,1,0:T(8,128)} %get-tuple-element.60.dr_ref), custom_call_target="tpu_custom_call" | custom-call | tf_op jit(solution)/shard_map/pallas_call | solution.py:150
  28.1 3.5 %collective-permute-done.4 = f32[2,16,256]{2,1,0:T(8,128)S(1)} collective-permute-done((f32[2,16,256]{2,1,0:T(8,128)S(1)}, f32[2,16,256]{2,1,0:T(8,128)S(1)}, u32[]{:S(2)}, u32[]{:S(2)}) %collective-permute-start.4) | collective-permute-done | bytes 32800 | tf_op jit(solution)/shard_map/ppermute | solution.py:22
  31.6 0.7 select_multiply_fusion.2
  32.4 1.4 %collective-permute-start.5 = (f32[2,16,256]{2,1,0:T(8,128)S(1)}, f32[2,16,256]{2,1,0:T(8,128)S(1)}, u32[]{:S(2)}, u32[]{:S(2)}) collective-permute-start(f32[2,16,256]{2,1,0:T(8,128)S(1)} %pad_maximum_fusion.6), channel_id=1, source_target_pairs={{0,24},{8,16},{16,8},{24,0},{32,56},{40,48},{48,40},{56,32},{64,88... | collective-permute-start | bytes 98312 | tf_op jit(solution)/shard_map/ppermute | solution.py:22
  33.7 2.6 %collective-permute-done.5 = f32[2,16,256]{2,1,0:T(8,128)S(1)} collective-permute-done((f32[2,16,256]{2,1,0:T(8,128)S(1)}, f32[2,16,256]{2,1,0:T(8,128)S(1)}, u32[]{:S(2)}, u32[]{:S(2)}) %collective-permute-start.5) | collective-permute-done | bytes 32800 | tf_op jit(solution)/shard_map/ppermute | solution.py:22
  36.4 0.9 collective-permute-start.6
  37.3 3.1 %collective-permute-done.6 = f32[2,16,256]{2,1,0:T(8,128)S(1)} collective-permute-done((f32[2,16,256]{2,1,0:T(8,128)S(1)}, f32[2,16,256]{2,1,0:T(8,128)S(1)}, u32[]{:S(2)}, u32[]{:S(2)}) %collective-permute-start.6) | collective-permute-done | bytes 32800 | tf_op jit(solution)/shard_map/ppermute | solution.py:22
  40.4 3.4 %collective-permute-start.7 = (f32[2,16,256]{2,1,0:T(8,128)S(1)}, f32[2,16,256]{2,1,0:T(8,128)S(1)}, u32[]{:S(2)}, u32[]{:S(2)}) collective-permute-start(f32[2,16,256]{2,1,0:T(8,128)S(1)} %pad_maximum_fusion.8), channel_id=1, source_target_pairs={{0,64},{8,72},{16,80},{24,88},{32,96},{40,104},{48,112},{56,120},{... | collective-permute-start | bytes 98312 | tf_op jit(solution)/shard_map/ppermute | solution.py:22
  44.3 1.7 %collective-permute-done.7 = f32[2,16,256]{2,1,0:T(8,128)S(1)} collective-permute-done((f32[2,16,256]{2,1,0:T(8,128)S(1)}, f32[2,16,256]{2,1,0:T(8,128)S(1)}, u32[]{:S(2)}, u32[]{:S(2)}) %collective-permute-start.7) | collective-permute-done | bytes 32800 | tf_op jit(solution)/shard_map/ppermute | solution.py:22
  46.1 4.8 %collective-permute-start.8 = (f32[2,16,256]{2,1,0:T(8,128)S(1)}, f32[2,16,256]{2,1,0:T(8,128)S(1)}, u32[]{:S(2)}, u32[]{:S(2)}) collective-permute-start(f32[2,16,256]{2,1,0:T(8,128)S(1)} %pad_maximum_fusion.9), channel_id=1, source_target_pairs={{0,192},{8,200},{16,208},{24,216},{32,224},{40,232},{48,240},{56,2... | collective-permute-start | bytes 98312 | tf_op jit(solution)/shard_map/ppermute | solution.py:22
  53.3 4.9 %shard_map.194 = (f32[128,16,256]{2,1,0:T(8,128)}, f32[16,16,256]{2,1,0:T(8,128)}) custom-call(f32[128,16,256]{2,1,0:T(8,128)} %get-tuple-element.59.da_ref, f32[128,16,256]{2,1,0:T(8,128)} %get-tuple-element.60.dr_ref, f32[16,256]{1,0:T(8,128)} %add_select_fusion.sin_ref, s32[128]{0:T(128)} %convert_element_type.217.endf_ref, s32[128]{0:T(128)} %broadcast_minimum_fusion.pid_ref), custom_call_target="tpu_custom_call" | custom-call | tf_op jit(solution)/shard_map/pallas_call | solution.py:166
  58.3 2.2 %multiply_reduce_fusion = f32[128,256]{1,0:T(8,128)S(1)} fusion(f32[128,16,256]{2,1,0:T(8,128)} %get-tuple-element.9, f32[128,16]{1,0:T(8,128)S(1)} %copy.51), kind=kLoop, calls=%fused_computation.2 | loop fusion | flops 1015808 | bytes 2236416 | tf_op jit(solution)/shard_map/reduce_sum | solution.py:285
  60.5 2.4 %convolution_convert_fusion.1 = bf16[128,2048]{1,0:T(8,128)(2,1)S(1)} fusion(bf16[256,2048]{1,0:T(8,128)(2,1)} %param.29, f32[128,256]{1,0:T(8,128)S(1)} %multiply_reduce_fusion, bf16[128,256]{1,0:T(8,128)(2,1)S(1)} %multiply_convert_fusion.1, bf16[2048,256]{1,0:T(8,128)(2,1)} %param.21, bf16[128,2048]{1,0:T(8,128)(2,1)S(1)} %copy-done.3, ...), kind=kOutput, calls=%fused_computation.1 | convolution fusion | flops 270106624 | bytes 3352064 | tf_op jit(solution)/shard_map/dot_general | solution.py:311
  63.8 1.0 collective-permute-done.9
  64.8 1.0 convert_add_fusion.1
  65.8 2.8 %collective-permute-start.10 = (bf16[2,16,2048]{2,1,0:T(8,128)(2,1)S(1)}, bf16[2,16,2048]{2,1,0:T(8,128)(2,1)S(1)}, u32[]{:S(2)}, u32[]{:S(2)}) collective-permute-start(bf16[2,16,2048]{2,1,0:T(8,128)(2,1)S(1)} %fusion.15), channel_id=1, source_target_pairs={{0,6},{1,7},{2,4},{3,5},{4,2},{5,3},{6,0},{7,1},{8,14},{9,15},{10,... | collective-permute-start | bytes 393224 | tf_op jit(solution)/shard_map/ppermute | solution.py:22
  68.9 1.0 convert_element_type.245
  69.8 2.8 %collective-permute-done.10 = bf16[2,16,2048]{2,1,0:T(8,128)(2,1)S(1)} collective-permute-done((bf16[2,16,2048]{2,1,0:T(8,128)(2,1)S(1)}, bf16[2,16,2048]{2,1,0:T(8,128)(2,1)S(1)}, u32[]{:S(2)}, u32[]{:S(2)}) %collective-permute-start.10) | collective-permute-done | bytes 131104 | tf_op jit(solution)/shard_map/ppermute | solution.py:22
  72.8 1.8 %collective-permute-start.18 = (bf16[16,19,256]{2,1,0:T(8,128)(2,1)S(1)}, bf16[16,19,256]{2,1,0:T(8,128)(2,1)S(1)}, u32[]{:S(2)}, u32[]{:S(2)}) collective-permute-start(bf16[16,19,256]{2,1,0:T(8,128)(2,1)S(1)} %pad_maximum_fusion.2), channel_id=1, source_target_pairs={{0,8},{8,0},{16,24},{24,16},{32,40},{40,32},{48,56},{56,48},{64,72... | collective-permute-start | bytes 466952 | tf_op jit(solution)/shard_map/ppermute | solution.py:22
  74.6 2.4 %collective-permute-done.11 = bf16[16,2048]{1,0:T(8,128)(2,1)S(1)} collective-permute-done((bf16[16,2048]{1,0:T(8,128)(2,1)S(1)}, bf16[16,2048]{1,0:T(8,128)(2,1)S(1)}, u32[]{:S(2)}, u32[]{:S(2)}) %collective-permute-start.11) | collective-permute-done | bytes 65568 | tf_op jit(solution)/shard_map/ppermute | solution.py:22
  77.4 1.6 %collective-permute-done.18 = bf16[16,19,256]{2,1,0:T(8,128)(2,1)S(1)} collective-permute-done((bf16[16,19,256]{2,1,0:T(8,128)(2,1)S(1)}, bf16[16,19,256]{2,1,0:T(8,128)(2,1)S(1)}, u32[]{:S(2)}, u32[]{:S(2)}) %collective-permute-start.18) | collective-permute-done | bytes 155680 | tf_op jit(solution)/shard_map/ppermute | solution.py:22
  79.1 3.2 %collective-permute-start.19 = (bf16[16,19,256]{2,1,0:T(8,128)(2,1)S(1)}, bf16[16,19,256]{2,1,0:T(8,128)(2,1)S(1)}, u32[]{:S(2)}, u32[]{:S(2)}) collective-permute-start(bf16[16,19,256]{2,1,0:T(8,128)(2,1)S(1)} %fusion.66), channel_id=1, source_target_pairs={{0,24},{8,16},{16,8},{24,0},{32,56},{40,48},{48,40},{56,32},{64,88... | collective-permute-start | bytes 466952 | tf_op jit(solution)/shard_map/ppermute | solution.py:22
  82.4 2.8 %collective-permute-start.13 = (bf16[2,16,2048]{2,1,0:T(8,128)(2,1)S(1)}, bf16[2,16,2048]{2,1,0:T(8,128)(2,1)S(1)}, u32[]{:S(2)}, u32[]{:S(2)}) collective-permute-start(bf16[2,16,2048]{2,1,0:T(8,128)(2,1)S(1)} %pad_maximum_fusion.4), channel_id=1, source_target_pairs={{0,6},{1,7},{2,4},{3,5},{4,2},{5,3},{6,0},{7,1},{8,14},{9,15},{10,... | collective-permute-start | bytes 393224 | tf_op jit(solution)/shard_map/ppermute | solution.py:22
  85.3 0.8 collective-permute-done.19
  86.2 2.5 %collective-permute-done.13 = bf16[2,16,2048]{2,1,0:T(8,128)(2,1)S(1)} collective-permute-done((bf16[2,16,2048]{2,1,0:T(8,128)(2,1)S(1)}, bf16[2,16,2048]{2,1,0:T(8,128)(2,1)S(1)}, u32[]{:S(2)}, u32[]{:S(2)}) %collective-permute-start.13) | collective-permute-done | bytes 131104 | tf_op jit(solution)/shard_map/ppermute | solution.py:22
  88.8 3.0 %collective-permute-done.20 = bf16[16,19,256]{2,1,0:T(8,128)(2,1)S(1)} collective-permute-done((bf16[16,19,256]{2,1,0:T(8,128)(2,1)S(1)}, bf16[16,19,256]{2,1,0:T(8,128)(2,1)S(1)}, u32[]{:S(2)}, u32[]{:S(2)}) %collective-permute-start.20) | collective-permute-done | bytes 155680 | tf_op jit(solution)/shard_map/ppermute | solution.py:22
  91.9 2.7 %collective-permute-start.21 = (bf16[16,19,256]{2,1,0:T(8,128)(2,1)S(1)}, bf16[16,19,256]{2,1,0:T(8,128)(2,1)S(1)}, u32[]{:S(2)}, u32[]{:S(2)}) collective-permute-start(bf16[16,19,256]{2,1,0:T(8,128)(2,1)S(1)} %add.352), channel_id=1, source_target_pairs={{0,64},{8,72},{16,80},{24,88},{32,96},{40,104},{48,112},{56,120},{... | collective-permute-start | bytes 466952 | tf_op jit(solution)/shard_map/ppermute | solution.py:22
  94.6 5.5 %collective-permute-done.21 = bf16[16,19,256]{2,1,0:T(8,128)(2,1)S(1)} collective-permute-done((bf16[16,19,256]{2,1,0:T(8,128)(2,1)S(1)}, bf16[16,19,256]{2,1,0:T(8,128)(2,1)S(1)}, u32[]{:S(2)}, u32[]{:S(2)}) %collective-permute-start.21) | collective-permute-done | bytes 155680 | tf_op jit(solution)/shard_map/ppermute | solution.py:22
  100.8 4.8 %collective-permute-start.22 = (bf16[16,19,256]{2,1,0:T(8,128)(2,1)}, bf16[16,19,256]{2,1,0:T(8,128)(2,1)}, u32[]{:S(2)}, u32[]{:S(2)}) collective-permute-start(bf16[16,19,256]{2,1,0:T(8,128)(2,1)} %add.353), channel_id=1, source_target_pairs={{0,192},{8,200},{16,208},{24,216},{32,224},{40,232},{48,240},{56,2... | collective-permute-start | bytes 466952 | tf_op jit(solution)/shard_map/ppermute | solution.py:22
  106.2 2.4 %convolution_convert_fusion = bf16[128,2048]{1,0:T(8,128)(2,1)S(1)} fusion(bf16[512,2048]{1,0:T(8,128)(2,1)S(1)} %copy-done, bf16[128,2048]{1,0:T(8,128)(2,1)S(1)} %bitcast.169, bf16[2048,512]{1,0:T(8,128)(2,1)} %param.32, f32[128,512]{1,0:T(8,128)S(1)} %fusion.72), kind=kOutput, calls=%fused_computation | convolution fusion | flops 537526272 | bytes 5505024 | tf_op jit(solution)/shard_map/dot_general | solution.py:323
  108.9 5.4 %collective-permute-done.22 = bf16[16,19,256]{2,1,0:T(8,128)(2,1)} collective-permute-done((bf16[16,19,256]{2,1,0:T(8,128)(2,1)}, bf16[16,19,256]{2,1,0:T(8,128)(2,1)}, u32[]{:S(2)}, u32[]{:S(2)}) %collective-permute-start.22) | collective-permute-done | bytes 155680 | tf_op jit(solution)/shard_map/ppermute | solution.py:22
  114.3 1.1 add.354
  115.5 2.8 %collective-permute-start.16 = (bf16[2,16,2048]{2,1,0:T(8,128)(2,1)S(1)}, bf16[2,16,2048]{2,1,0:T(8,128)(2,1)S(1)}, u32[]{:S(2)}, u32[]{:S(2)}) collective-permute-start(bf16[2,16,2048]{2,1,0:T(8,128)(2,1)S(1)} %fusion.16), channel_id=1, source_target_pairs={{0,6},{1,7},{2,4},{3,5},{4,2},{5,3},{6,0},{7,1},{8,14},{9,15},{10,... | collective-permute-start | bytes 393224 | tf_op jit(solution)/shard_map/ppermute | solution.py:22
  118.6 3.7 %collective-permute-done.16 = bf16[2,16,2048]{2,1,0:T(8,128)(2,1)S(1)} collective-permute-done((bf16[2,16,2048]{2,1,0:T(8,128)(2,1)S(1)}, bf16[2,16,2048]{2,1,0:T(8,128)(2,1)S(1)}, u32[]{:S(2)}, u32[]{:S(2)}) %collective-permute-start.16) | collective-permute-done | bytes 131104 | tf_op jit(solution)/shard_map/ppermute | solution.py:22
  122.4 0.8 convolution_convert_fusion.5
  123.8 2.8 %collective-permute-done.17 = bf16[16,2048]{1,0:T(8,128)(2,1)S(1)} collective-permute-done((bf16[16,2048]{1,0:T(8,128)(2,1)S(1)}, bf16[16,2048]{1,0:T(8,128)(2,1)S(1)}, u32[]{:S(2)}, u32[]{:S(2)}) %collective-permute-start.17) | collective-permute-done | bytes 65568 | tf_op jit(solution)/shard_map/ppermute | solution.py:22
  (121 shorter events, 12.1 us)
Async XLA Ops:
  0.6 105.6 %copy-start = (bf16[512,2048]{1,0:T(8,128)(2,1)S(1)}, bf16[512,2048]{1,0:T(8,128)(2,1)}, u32[]{:S(2)}) copy-start(bf16[512,2048]{1,0:T(8,128)(2,1)} %param.33) | copy-start | bytes 6291460
  0.6 9.0 %copy-start.10 = (f32[2048]{0:T(1024)S(1)}, f32[2048]{0:T(1024)}, u32[]{:S(2)}) copy-start(f32[2048]{0:T(1024)} %param.19) | copy-start | bytes 24580
  0.7 8.9 %copy-start.2 = (bf16[2048,256]{1,0:T(8,128)(2,1)S(1)}, bf16[2048,256]{1,0:T(8,128)(2,1)}, u32[]{:S(2)}) copy-start(bf16[2048,256]{1,0:T(8,128)(2,1)} %param.20) | copy-start | bytes 3145732
  0.7 9.2 %copy-start.12 = (f32[256]{0:T(256)S(1)}, f32[256]{0:T(256)}, u32[]{:S(2)}) copy-start(f32[256]{0:T(256)} %param.23) | copy-start | bytes 3076
  0.7 9.4 %copy-start.4 = (bf16[256,160]{0,1:T(8,128)(2,1)S(1)}, bf16[256,160]{0,1:T(8,128)(2,1)}, u32[]{:S(2)}) copy-start(bf16[256,160]{0,1:T(8,128)(2,1)} %param.24) | copy-start | bytes 245764
  0.7 9.7 %copy-start.9 = (f32[16,256]{1,0:T(8,128)S(1)}, f32[16,256]{1,0:T(8,128)}, u32[]{:S(2)}) copy-start(f32[16,256]{1,0:T(8,128)} %param.27) | copy-start | bytes 49156
  1.6 7.8 %collective-permute-start = (bf16[3,2048]{1,0:T(4,128)(2,1)S(1)}, bf16[3,2048]{1,0:T(4,128)(2,1)S(1)}, u32[]{:S(2)}, u32[]{:S(2)}) collective-permute-start(bf16[3,2048]{1,0:T(4,128)(2,1)S(1)} %slice.69), channel_id=1, source_target_pairs={{0,8},{8,16},{16,24},{24,32},{32,40},{40,48},{48,56},{56,64},{64,7... | collective-permute-start | bytes 36872 | tf_op jit(solution)/shard_map/ppermute | solution.py:247
  6.6 14.6 %copy-start.11 = (s32[16]{0:T(128)}, s32[16]{0:T(128)S(1)}, u32[]{:S(2)}) copy-start(s32[16]{0:T(128)S(1)} %get-tuple-element.51) | copy-start | bytes 196
  6.7 37.1 %copy-start.16 = (s32[128]{0:T(128)}, s32[128]{0:T(128)S(1)}, u32[]{:S(2)}) copy-start(s32[128]{0:T(128)S(1)} %convert_reduce_fusion) | copy-start | bytes 1540
  7.6 13.5 %copy-start.5 = (bf16[128,256]{1,0:T(8,128)(2,1)S(1)}, bf16[128,256]{1,0:T(8,128)(2,1)}, u32[]{:S(2)}) copy-start(bf16[128,256]{1,0:T(8,128)(2,1)} %param.25) | copy-start | bytes 196612
  7.6 13.5 %copy-start.13 = (f32[256]{0:T(256)S(1)}, f32[256]{0:T(256)}, u32[]{:S(2)}) copy-start(f32[256]{0:T(256)} %param.26) | copy-start | bytes 3076
  9.4 11.6 %copy-start.6 = (bf16[128,256]{1,0:T(8,128)(2,1)}, bf16[128,256]{1,0:T(8,128)(2,1)S(1)}, u32[]{:S(2)}) copy-start(bf16[128,256]{1,0:T(8,128)(2,1)S(1)} %convolution_convert_fusion.3) | copy-start | bytes 196612
  10.3 1.3 %collective-permute-start.1 = (bf16[128,160]{0,1:T(8,128)(2,1)S(1)}, bf16[128,160]{0,1:T(8,128)(2,1)S(1)}, u32[]{:S(2)}, u32[]{:S(2)}) collective-permute-start(bf16[128,160]{0,1:T(8,128)(2,1)S(1)} %get-tuple-element.55), channel_id=1, source_target_pairs={{0,1},{1,0},{2,3},{3,2},{4,5},{5,4},{6,7},{7,6},{8,9},{9,8},{10,11... | collective-permute-start | bytes 122888 | tf_op jit(solution)/shard_map/ppermute | solution.py:22
  11.6 4.1 %collective-permute-start.2 = (bf16[128,160]{0,1:T(8,128)(2,1)S(1)}, bf16[128,160]{0,1:T(8,128)(2,1)S(1)}, u32[]{:S(2)}, u32[]{:S(2)}) collective-permute-start(bf16[128,160]{0,1:T(8,128)(2,1)S(1)} %fusion.38), channel_id=1, source_target_pairs={{0,2},{1,3},{2,0},{3,1},{4,6},{5,7},{6,4},{7,5},{8,10},{9,11},{10,... | collective-permute-start | bytes 122888 | tf_op jit(solution)/shard_map/ppermute | solution.py:22
  15.7 5.3 %collective-permute-start.3 = (bf16[128,160]{0,1:T(8,128)(2,1)S(1)}, bf16[128,160]{0,1:T(8,128)(2,1)S(1)}, u32[]{:S(2)}, u32[]{:S(2)}) collective-permute-start(bf16[128,160]{0,1:T(8,128)(2,1)S(1)} %fusion.44), channel_id=1, source_target_pairs={{0,6},{1,7},{2,4},{3,5},{4,2},{5,3},{6,0},{7,1},{8,14},{9,15},{10,... | collective-permute-start | bytes 122888 | tf_op jit(solution)/shard_map/ppermute | solution.py:22
  27.7 3.9 %collective-permute-start.4 = (f32[2,16,256]{2,1,0:T(8,128)S(1)}, f32[2,16,256]{2,1,0:T(8,128)S(1)}, u32[]{:S(2)}, u32[]{:S(2)}) collective-permute-start(f32[2,16,256]{2,1,0:T(8,128)S(1)} %pad_maximum_fusion.5), channel_id=1, source_target_pairs={{0,8},{8,0},{16,24},{24,16},{32,40},{40,32},{48,56},{56,48},{64,72... | collective-permute-start | bytes 98312 | tf_op jit(solution)/shard_map/ppermute | solution.py:22
  32.4 4.0 %collective-permute-start.5 = (f32[2,16,256]{2,1,0:T(8,128)S(1)}, f32[2,16,256]{2,1,0:T(8,128)S(1)}, u32[]{:S(2)}, u32[]{:S(2)}) collective-permute-start(f32[2,16,256]{2,1,0:T(8,128)S(1)} %pad_maximum_fusion.6), channel_id=1, source_target_pairs={{0,24},{8,16},{16,8},{24,0},{32,56},{40,48},{48,40},{56,32},{64,88... | collective-permute-start | bytes 98312 | tf_op jit(solution)/shard_map/ppermute | solution.py:22
  36.4 4.0 %collective-permute-start.6 = (f32[2,16,256]{2,1,0:T(8,128)S(1)}, f32[2,16,256]{2,1,0:T(8,128)S(1)}, u32[]{:S(2)}, u32[]{:S(2)}) collective-permute-start(f32[2,16,256]{2,1,0:T(8,128)S(1)} %pad_maximum_fusion.7), channel_id=1, source_target_pairs={{0,32},{8,40},{16,48},{24,56},{32,0},{40,8},{48,16},{56,24},{64,96... | collective-permute-start | bytes 98312 | tf_op jit(solution)/shard_map/ppermute | solution.py:22
  40.4 5.6 %collective-permute-start.7 = (f32[2,16,256]{2,1,0:T(8,128)S(1)}, f32[2,16,256]{2,1,0:T(8,128)S(1)}, u32[]{:S(2)}, u32[]{:S(2)}) collective-permute-start(f32[2,16,256]{2,1,0:T(8,128)S(1)} %pad_maximum_fusion.8), channel_id=1, source_target_pairs={{0,64},{8,72},{16,80},{24,88},{32,96},{40,104},{48,112},{56,120},{... | collective-permute-start | bytes 98312 | tf_op jit(solution)/shard_map/ppermute | solution.py:22
  46.1 6.6 %collective-permute-start.8 = (f32[2,16,256]{2,1,0:T(8,128)S(1)}, f32[2,16,256]{2,1,0:T(8,128)S(1)}, u32[]{:S(2)}, u32[]{:S(2)}) collective-permute-start(f32[2,16,256]{2,1,0:T(8,128)S(1)} %pad_maximum_fusion.9), channel_id=1, source_target_pairs={{0,192},{8,200},{16,208},{24,216},{32,224},{40,232},{48,240},{56,2... | collective-permute-start | bytes 98312 | tf_op jit(solution)/shard_map/ppermute | solution.py:22
  58.3 2.2 %copy-start.3 = (bf16[128,2048]{1,0:T(8,128)(2,1)S(1)}, bf16[128,2048]{1,0:T(8,128)(2,1)}, u32[]{:S(2)}) copy-start(bf16[128,2048]{1,0:T(8,128)(2,1)} %param.18) | copy-start | bytes 1572868
  58.3 2.2 %copy-start.15 = (f32[256]{0:T(256)S(1)}, f32[256]{0:T(256)}, u32[]{:S(2)}) copy-start(f32[256]{0:T(256)} %param.28) | copy-start | bytes 3076
  60.5 8.1 %copy-start.7 = (bf16[128,256]{1,0:T(8,128)(2,1)S(1)}, bf16[128,256]{1,0:T(8,128)(2,1)}, u32[]{:S(2)}) copy-start(bf16[128,256]{1,0:T(8,128)(2,1)} %copy-done.6) | copy-start | bytes 196612
  63.0 14.2 %copy-start.8 = (f32[2048]{0:T(1024)S(1)}, f32[2048]{0:T(1024)}, u32[]{:S(2)}) copy-start(f32[2048]{0:T(1024)} %param.30) | copy-start | bytes 24580
  63.0 1.8 %collective-permute-start.9 = (bf16[2,2,16,2048]{3,2,1,0:T(8,128)(2,1)S(1)}, bf16[2,2,16,2048]{3,2,1,0:T(8,128)(2,1)}, u32[]{:S(2)}, u32[]{:S(2)}) collective-permute-start(bf16[2,2,16,2048]{3,2,1,0:T(8,128)(2,1)S(1)} %dynamic-slice_bitcast_fusion.1), channel_id=1, source_target_pairs={{0,1},{1,0},{2,3},{3,2},{4,5},{5,4},{6,7},{7,6},{8,9},{9,8},{10,11... | collective-permute-start | bytes 786440 | tf_op jit(solution)/shard_map/ppermute | solution.py:22
  65.8 6.8 %collective-permute-start.10 = (bf16[2,16,2048]{2,1,0:T(8,128)(2,1)S(1)}, bf16[2,16,2048]{2,1,0:T(8,128)(2,1)S(1)}, u32[]{:S(2)}, u32[]{:S(2)}) collective-permute-start(bf16[2,16,2048]{2,1,0:T(8,128)(2,1)S(1)} %fusion.15), channel_id=1, source_target_pairs={{0,6},{1,7},{2,4},{3,5},{4,2},{5,3},{6,0},{7,1},{8,14},{9,15},{10,... | collective-permute-start | bytes 393224 | tf_op jit(solution)/shard_map/ppermute | solution.py:22
  72.7 4.4 %collective-permute-start.11 = (bf16[16,2048]{1,0:T(8,128)(2,1)S(1)}, bf16[16,2048]{1,0:T(8,128)(2,1)S(1)}, u32[]{:S(2)}, u32[]{:S(2)}) collective-permute-start(bf16[16,2048]{1,0:T(8,128)(2,1)S(1)} %fusion.30), channel_id=1, source_target_pairs={{0,2},{1,3},{2,0},{3,1},{4,6},{5,7},{6,4},{7,5},{8,10},{9,11},{10,... | collective-permute-start | bytes 196616 | tf_op jit(solution)/shard_map/ppermute | solution.py:22
  72.8 6.2 %collective-permute-start.18 = (bf16[16,19,256]{2,1,0:T(8,128)(2,1)S(1)}, bf16[16,19,256]{2,1,0:T(8,128)(2,1)S(1)}, u32[]{:S(2)}, u32[]{:S(2)}) collective-permute-start(bf16[16,19,256]{2,1,0:T(8,128)(2,1)S(1)} %pad_maximum_fusion.2), channel_id=1, source_target_pairs={{0,8},{8,0},{16,24},{24,16},{32,40},{40,32},{48,56},{56,48},{64,72... | collective-permute-start | bytes 466952 | tf_op jit(solution)/shard_map/ppermute | solution.py:22
  77.3 5.0 %collective-permute-start.12 = (bf16[16,2048]{1,0:T(8,128)(2,1)S(1)}, bf16[16,2048]{1,0:T(8,128)(2,1)S(1)}, u32[]{:S(2)}, u32[]{:S(2)}) collective-permute-start(bf16[16,2048]{1,0:T(8,128)(2,1)S(1)} %multiply_convert_fusion), channel_id=1, source_target_pairs={{0,2},{1,3},{2,0},{3,1},{4,6},{5,7},{6,4},{7,5},{8,10},{9,11},{10,... | collective-permute-start | bytes 196616 | tf_op jit(solution)/shard_map/ppermute | solution.py:22
  79.1 7.0 %collective-permute-start.19 = (bf16[16,19,256]{2,1,0:T(8,128)(2,1)S(1)}, bf16[16,19,256]{2,1,0:T(8,128)(2,1)S(1)}, u32[]{:S(2)}, u32[]{:S(2)}) collective-permute-start(bf16[16,19,256]{2,1,0:T(8,128)(2,1)S(1)} %fusion.66), channel_id=1, source_target_pairs={{0,24},{8,16},{16,8},{24,0},{32,56},{40,48},{48,40},{56,32},{64,88... | collective-permute-start | bytes 466952 | tf_op jit(solution)/shard_map/ppermute | solution.py:22
  82.4 6.3 %collective-permute-start.13 = (bf16[2,16,2048]{2,1,0:T(8,128)(2,1)S(1)}, bf16[2,16,2048]{2,1,0:T(8,128)(2,1)S(1)}, u32[]{:S(2)}, u32[]{:S(2)}) collective-permute-start(bf16[2,16,2048]{2,1,0:T(8,128)(2,1)S(1)} %pad_maximum_fusion.4), channel_id=1, source_target_pairs={{0,6},{1,7},{2,4},{3,5},{4,2},{5,3},{6,0},{7,1},{8,14},{9,15},{10,... | collective-permute-start | bytes 393224 | tf_op jit(solution)/shard_map/ppermute | solution.py:22
  86.1 5.8 %collective-permute-start.20 = (bf16[16,19,256]{2,1,0:T(8,128)(2,1)S(1)}, bf16[16,19,256]{2,1,0:T(8,128)(2,1)S(1)}, u32[]{:S(2)}, u32[]{:S(2)}) collective-permute-start(bf16[16,19,256]{2,1,0:T(8,128)(2,1)S(1)} %add.351), channel_id=1, source_target_pairs={{0,32},{8,40},{16,48},{24,56},{32,0},{40,8},{48,16},{56,24},{64,96... | collective-permute-start | bytes 466952 | tf_op jit(solution)/shard_map/ppermute | solution.py:22
  88.7 16.9 %collective-permute-start.14 = (bf16[2,2,16,2048]{3,2,1,0:T(8,128)(2,1)S(1)}, bf16[2,2,16,2048]{3,2,1,0:T(8,128)(2,1)S(1)}, u32[]{:S(2)}, u32[]{:S(2)}) collective-permute-start(bf16[2,2,16,2048]{3,2,1,0:T(8,128)(2,1)S(1)} %pad_maximum_fusion.1), channel_id=1, source_target_pairs={{0,1},{1,0},{2,3},{3,2},{4,5},{5,4},{6,7},{7,6},{8,9},{9,8},{10,11... | collective-permute-start | bytes 786440 | tf_op jit(solution)/shard_map/ppermute | solution.py:22
  91.9 8.1 %collective-permute-start.21 = (bf16[16,19,256]{2,1,0:T(8,128)(2,1)S(1)}, bf16[16,19,256]{2,1,0:T(8,128)(2,1)S(1)}, u32[]{:S(2)}, u32[]{:S(2)}) collective-permute-start(bf16[16,19,256]{2,1,0:T(8,128)(2,1)S(1)} %add.352), channel_id=1, source_target_pairs={{0,64},{8,72},{16,80},{24,88},{32,96},{40,104},{48,112},{56,120},{... | collective-permute-start | bytes 466952 | tf_op jit(solution)/shard_map/ppermute | solution.py:22
  94.6 11.1 %copy-start.1 = (bf16[2048,512]{1,0:T(8,128)(2,1)S(1)}, bf16[2048,512]{1,0:T(8,128)(2,1)}, u32[]{:S(2)}) copy-start(bf16[2048,512]{1,0:T(8,128)(2,1)} %param.31) | copy-start | bytes 6291460
  100.8 13.5 %collective-permute-start.22 = (bf16[16,19,256]{2,1,0:T(8,128)(2,1)}, bf16[16,19,256]{2,1,0:T(8,128)(2,1)}, u32[]{:S(2)}, u32[]{:S(2)}) collective-permute-start(bf16[16,19,256]{2,1,0:T(8,128)(2,1)} %add.353), channel_id=1, source_target_pairs={{0,192},{8,200},{16,208},{24,216},{32,224},{40,232},{48,240},{56,2... | collective-permute-start | bytes 466952 | tf_op jit(solution)/shard_map/ppermute | solution.py:22
  106.2 2.6 %copy-start.17 = (s32[128]{0:T(128)S(1)}, s32[128]{0:T(128)}, u32[]{:S(2)}) copy-start(s32[128]{0:T(128)} %copy-done.16) | copy-start | bytes 1540
  108.6 9.7 %copy-start.14 = (s32[4]{0:T(128)S(1)}, s32[4]{0:T(128)}, u32[]{:S(2)}) copy-start(s32[4]{0:T(128)} %param.35) | copy-start | bytes 52
  108.7 6.7 %collective-permute-start.15 = (bf16[2,2,16,2048]{3,2,1,0:T(8,128)(2,1)S(1)}, bf16[2,2,16,2048]{3,2,1,0:T(8,128)(2,1)S(1)}, u32[]{:S(2)}, u32[]{:S(2)}) collective-permute-start(bf16[2,2,16,2048]{3,2,1,0:T(8,128)(2,1)S(1)} %dynamic-slice_bitcast_fusion), channel_id=1, source_target_pairs={{0,1},{1,0},{2,3},{3,2},{4,5},{5,4},{6,7},{7,6},{8,9},{9,8},{10,11... | collective-permute-start | bytes 786440 | tf_op jit(solution)/shard_map/ppermute | solution.py:22
  115.5 6.7 %collective-permute-start.16 = (bf16[2,16,2048]{2,1,0:T(8,128)(2,1)S(1)}, bf16[2,16,2048]{2,1,0:T(8,128)(2,1)S(1)}, u32[]{:S(2)}, u32[]{:S(2)}) collective-permute-start(bf16[2,16,2048]{2,1,0:T(8,128)(2,1)S(1)} %fusion.16), channel_id=1, source_target_pairs={{0,6},{1,7},{2,4},{3,5},{4,2},{5,3},{6,0},{7,1},{8,14},{9,15},{10,... | collective-permute-start | bytes 393224 | tf_op jit(solution)/shard_map/ppermute | solution.py:22
  122.3 4.4 %collective-permute-start.17 = (bf16[16,2048]{1,0:T(8,128)(2,1)S(1)}, bf16[16,2048]{1,0:T(8,128)(2,1)S(1)}, u32[]{:S(2)}, u32[]{:S(2)}) collective-permute-start(bf16[16,2048]{1,0:T(8,128)(2,1)S(1)} %fusion.31), channel_id=1, source_target_pairs={{0,2},{1,3},{2,0},{3,1},{4,6},{5,7},{6,4},{7,5},{8,10},{9,11},{10,... | collective-permute-start | bytes 196616 | tf_op jit(solution)/shard_map/ppermute | solution.py:22

commit v11 on v9

--- a/solution.py
+++ b/solution.py
@@ -184,6 +184,7 @@
     me = lax.axis_index(axis)
     tot_a, tot_s = a_blk, s_blk
     exc_a, exc_s = jnp.ones_like(a_blk), jnp.zeros_like(s_blk)
+    rider_out = None
     for mask, top in basis_of(axis):
         got = swap(jnp.stack([tot_a, tot_s]), axis, mask)
         if rider is not None:
@@ -281,9 +282,9 @@
     carry_on = 1.0 - starts_here.astype(jnp.float32)
     decay = jnp.exp(step_size[:, None, :] * decay_rates[None, :, :]) * carry_on[:, None, None]
     drive = (step_size * conv_float)[:, None, :] * in_map[:, :, None]
-    out_wide = jnp.broadcast_to(out_map[:, :, None], decay.shape)
+    out_wide = out_map[:, :, None] + 0.0 * decay
     s_blk, a_blk = block_summary(decay, drive)
-    state_in, out_wide = entering_state(a_blk, s_blk, "seq", out_wide)
+    state_in, _ = entering_state(a_blk, s_blk, "seq", None)
     end_flag = ends_here.astype(jnp.int32)
     slot_of = jnp.minimum(prompt_of, prompts - 1).astype(jnp.int32)
     mixer_y, final_part = block_output(decay, drive, out_wide, state_in, end_flag, slot_of, prompts)

time: 127 us -> 128 us (level)
  other arithmetic: 14.7 us -> 17.3 us
  local copies, waits for them, and re-layouts: 5.32 us -> 3.61 us
    add x0 -> x1, other arithmetic: none -> 2.51 us  [local(): out_wide = out_map[:, :, None] + 0.0 * decay]
    broadcast_in_dim x1 -> x0, local copies, waits for them, and re-layouts: 1.71 us -> none  [local(): out_wide = jnp.broadcast_to(out_map[:, :, None], decay.shape)]
where the time goes in v11:
time: 128 us
  waiting for transfers between devices  49.1 us (38%)
  starting transfers between devices  38.8 us (30%)
  other arithmetic  17.3 us (14%)
  matrix products  9.04 us (7%)
  Pallas kernels  8.58 us (7%)
  local copies, waits for them, and re-layouts  3.61 us (3%)
    ppermute x22, waiting for transfers between devices, swap(): return lax.ppermute(x, axis, [(i, i ^ bit) for i in range(devices)])  49.1 us
    ppermute x22, starting transfers between devices, swap(): return lax.ppermute(x, axis, [(i, i ^ bit) for i in range(devices)])  37.1 us
    pallas_call x1, Pallas kernels, block_output(): pl.pallas_call(block_output_kernel, out_shape=(jax.ShapeDtypeStruct((t, e...  5.44 us
    pallas_call x1, Pallas kernels, block_summary(): pl.pallas_call(block_summary_kernel, out_shape=(jax.ShapeDtypeStruct((n,...  3.14 us
  transfers between devices with their start and end apart: 23, of which 19 were waited for; matrix products, arithmetic and copies ran while one was open for 13% of the time, Pallas kernels for 0%

profile of v11, /device:TPU:40, one launch (start us, length us, event | category | flops | bytes accessed | tf_op | source)
XLA Modules:
  0.0 127.6 jit_solution(8938330182112447440)
XLA Ops:
  0.7 0.9 slice.69
  1.6 1.7 %collective-permute-start = (bf16[3,2048]{1,0:T(4,128)(2,1)S(1)}, bf16[3,2048]{1,0:T(4,128)(2,1)S(1)}, u32[]{:S(2)}, u32[]{:S(2)}) collective-permute-start(bf16[3,2048]{1,0:T(4,128)(2,1)S(1)} %slice.69), channel_id=1, source_target_pairs={{0,8},{8,16},{16,24},{24,32},{32,40},{40,48},{48,56},{56,64},{64,7... | collective-permute-start | bytes 36872 | tf_op jit(solution)/shard_map/ppermute | solution.py:252
  3.3 1.2 fusion.2
  4.5 0.8 fusion.70
  6.3 1.2 broadcast_add_fusion
  7.6 1.8 %convolution_convert_fusion.3 = bf16[128,256]{1,0:T(8,128)(2,1)S(1)} fusion(bf16[2048,256]{1,0:T(8,128)(2,1)} %param.20, bf16[128,2048]{1,0:T(8,128)(2,1)} %param.18, f32[2048]{0:T(1024)} %param.19, f32[128]{0:T(128)S(1)} %add_rsqrt_fusion.2), kind=kOutput, calls=%fused_computation.11 | convolution fusion | flops 135299072 | bytes 1647104 | tf_op jit(solution)/shard_map/dot_general | solution.py:259
  10.4 1.2 collective-permute-done.1
  11.6 1.6 %collective-permute-start.2 = (bf16[128,160]{0,1:T(8,128)(2,1)S(1)}, bf16[128,160]{0,1:T(8,128)(2,1)S(1)}, u32[]{:S(2)}, u32[]{:S(2)}) collective-permute-start(bf16[128,160]{0,1:T(8,128)(2,1)S(1)} %fusion.38), channel_id=1, source_target_pairs={{0,2},{1,3},{2,0},{3,1},{4,6},{5,7},{6,4},{7,5},{8,10},{9,11},{10,... | collective-permute-start | bytes 122888 | tf_op jit(solution)/shard_map/ppermute | solution.py:22
  13.2 2.4 %collective-permute-done.2 = bf16[128,160]{0,1:T(8,128)(2,1)S(1)} collective-permute-done((bf16[128,160]{0,1:T(8,128)(2,1)S(1)}, bf16[128,160]{0,1:T(8,128)(2,1)S(1)}, u32[]{:S(2)}, u32[]{:S(2)}) %collective-permute-start.2) | collective-permute-done | bytes 40992 | tf_op jit(solution)/shard_map/ppermute | solution.py:22
  15.7 2.8 %collective-permute-start.3 = (bf16[128,160]{0,1:T(8,128)(2,1)S(1)}, bf16[128,160]{0,1:T(8,128)(2,1)S(1)}, u32[]{:S(2)}, u32[]{:S(2)}) collective-permute-start(bf16[128,160]{0,1:T(8,128)(2,1)S(1)} %fusion.44), channel_id=1, source_target_pairs={{0,6},{1,7},{2,4},{3,5},{4,2},{5,3},{6,0},{7,1},{8,14},{9,15},{10,... | collective-permute-start | bytes 122888 | tf_op jit(solution)/shard_map/ppermute | solution.py:22
  18.5 2.4 %collective-permute-done.3 = bf16[128,160]{0,1:T(8,128)(2,1)S(1)} collective-permute-done((bf16[128,160]{0,1:T(8,128)(2,1)S(1)}, bf16[128,160]{0,1:T(8,128)(2,1)S(1)}, u32[]{:S(2)}, u32[]{:S(2)}) %collective-permute-start.3) | collective-permute-done | bytes 40992 | tf_op jit(solution)/shard_map/ppermute | solution.py:22
  21.5 1.7 %broadcast_multiply_fusion.dr_ref = f32[128,16,256]{2,1,0:T(8,128)} fusion(f32[128,16]{1,0:T(8,128)S(1)} %copy.51, f32[128,256]{1,0:T(8,128)S(1)} %get-tuple-element.59), kind=kLoop, calls=%fused_computation.18 | loop fusion | flops 524288 | bytes 2236416 | tf_op jit(solution)/shard_map/mul | solution.py:284
  23.3 2.5 %multiply_add_fusion = (f32[128,16,256]{2,1,0:T(8,128)}, f32[128,16,256]{2,1,0:T(8,128)}) fusion(f32[128,16]{1,0:T(8,128)S(1)} %copy.52, f32[128]{0:T(128)S(1)} %convert_subtract_fusion, f32[16,256]{1,0:T(8,128)S(1)} %exponential_negate_fusion, f32[128,256]{1,0:T(8,128)S(1)} %get-tuple-element.60), kind=kLoop, calls=%fused_computation.2 | loop fusion | flops 2097152 | bytes 4350464 | tf_op jit(solution)/shard_map/add | solution.py:285
  25.8 3.1 %shard_map.193 = (f32[16,256]{1,0:T(8,128)}, f32[16,256]{1,0:T(8,128)}) custom-call(f32[128,16,256]{2,1,0:T(8,128)} %get-tuple-element.34.da_ref, f32[128,16,256]{2,1,0:T(8,128)} %broadcast_multiply_fusion.dr_ref), custom_call_target="tpu_custom_call" | custom-call | tf_op jit(solution)/shard_map/pallas_call | solution.py:155
  30.1 3.5 %collective-permute-done.4 = f32[2,16,256]{2,1,0:T(8,128)S(1)} collective-permute-done((f32[2,16,256]{2,1,0:T(8,128)S(1)}, f32[2,16,256]{2,1,0:T(8,128)S(1)}, u32[]{:S(2)}, u32[]{:S(2)}) %collective-permute-start.4) | collective-permute-done | bytes 32800 | tf_op jit(solution)/shard_map/ppermute | solution.py:22
  34.3 1.4 %collective-permute-start.5 = (f32[2,16,256]{2,1,0:T(8,128)S(1)}, f32[2,16,256]{2,1,0:T(8,128)S(1)}, u32[]{:S(2)}, u32[]{:S(2)}) collective-permute-start(f32[2,16,256]{2,1,0:T(8,128)S(1)} %pad_maximum_fusion.6), channel_id=1, source_target_pairs={{0,24},{8,16},{16,8},{24,0},{32,56},{40,48},{48,40},{56,32},{64,88... | collective-permute-start | bytes 98312 | tf_op jit(solution)/shard_map/ppermute | solution.py:22
  35.7 2.6 %collective-permute-done.5 = f32[2,16,256]{2,1,0:T(8,128)S(1)} collective-permute-done((f32[2,16,256]{2,1,0:T(8,128)S(1)}, f32[2,16,256]{2,1,0:T(8,128)S(1)}, u32[]{:S(2)}, u32[]{:S(2)}) %collective-permute-start.5) | collective-permute-done | bytes 32800 | tf_op jit(solution)/shard_map/ppermute | solution.py:22
  38.3 0.9 collective-permute-start.6
  39.2 3.1 %collective-permute-done.6 = f32[2,16,256]{2,1,0:T(8,128)S(1)} collective-permute-done((f32[2,16,256]{2,1,0:T(8,128)S(1)}, f32[2,16,256]{2,1,0:T(8,128)S(1)}, u32[]{:S(2)}, u32[]{:S(2)}) %collective-permute-start.6) | collective-permute-done | bytes 32800 | tf_op jit(solution)/shard_map/ppermute | solution.py:22
  42.4 3.4 %collective-permute-start.7 = (f32[2,16,256]{2,1,0:T(8,128)S(1)}, f32[2,16,256]{2,1,0:T(8,128)S(1)}, u32[]{:S(2)}, u32[]{:S(2)}) collective-permute-start(f32[2,16,256]{2,1,0:T(8,128)S(1)} %pad_maximum_fusion.8), channel_id=1, source_target_pairs={{0,64},{8,72},{16,80},{24,88},{32,96},{40,104},{48,112},{56,120},{... | collective-permute-start | bytes 98312 | tf_op jit(solution)/shard_map/ppermute | solution.py:22
  46.3 1.7 %collective-permute-done.7 = f32[2,16,256]{2,1,0:T(8,128)S(1)} collective-permute-done((f32[2,16,256]{2,1,0:T(8,128)S(1)}, f32[2,16,256]{2,1,0:T(8,128)S(1)}, u32[]{:S(2)}, u32[]{:S(2)}) %collective-permute-start.7) | collective-permute-done | bytes 32800 | tf_op jit(solution)/shard_map/ppermute | solution.py:22
  48.0 4.8 %collective-permute-start.8 = (f32[2,16,256]{2,1,0:T(8,128)S(1)}, f32[2,16,256]{2,1,0:T(8,128)S(1)}, u32[]{:S(2)}, u32[]{:S(2)}) collective-permute-start(f32[2,16,256]{2,1,0:T(8,128)S(1)} %pad_maximum_fusion.9), channel_id=1, source_target_pairs={{0,192},{8,200},{16,208},{24,216},{32,224},{40,232},{48,240},{56,2... | collective-permute-start | bytes 98312 | tf_op jit(solution)/shard_map/ppermute | solution.py:22
  53.9 0.8 collective-permute-done.8
  55.3 5.4 %shard_map.194 = (f32[128,256]{1,0:T(8,128)}, f32[16,16,256]{2,1,0:T(8,128)}) custom-call(f32[128,16,256]{2,1,0:T(8,128)} %get-tuple-element.34.da_ref, f32[128,16,256]{2,1,0:T(8,128)} %broadcast_multiply_fusion.dr_ref, f32[128,16,256]{2,1,0:T(8,128)} %get-tuple-element.33.om_ref, f32[16,256]{1,0:T(8,128)} %add_select_fusion.sin_ref, ...), custom_call_target="tpu_custom_call" | custom-call | tf_op jit(solution)/shard_map/pallas_call | solution.py:171
  60.8 2.5 %convolution_convert_fusion.1 = bf16[128,2048]{1,0:T(8,128)(2,1)S(1)} fusion(bf16[256,2048]{1,0:T(8,128)(2,1)} %param.29, f32[128,256]{1,0:T(8,128)} %get-tuple-element.9, bf16[128,256]{1,0:T(8,128)(2,1)S(1)} %multiply_convert_fusion.1, bf16[2048,256]{1,0:T(8,128)(2,1)} %param.21, bf16[128,2048]{1,0:T(8,128)(2,1)S(1)} %copy-done.3, f32[2048]{0:T(1024)S(1)} %copy-done.10, ...), kind=kOutput, calls=%fused_computation.1 | convolution fusion | flops 270106624 | bytes 3352064 | tf_op jit(solution)/shard_map/dot_general | solution.py:316
  64.1 1.0 collective-permute-done.9
  65.0 1.0 convert_add_fusion.1
  66.1 2.8 %collective-permute-start.10 = (bf16[2,16,2048]{2,1,0:T(8,128)(2,1)S(1)}, bf16[2,16,2048]{2,1,0:T(8,128)(2,1)S(1)}, u32[]{:S(2)}, u32[]{:S(2)}) collective-permute-start(bf16[2,16,2048]{2,1,0:T(8,128)(2,1)S(1)} %fusion.15), channel_id=1, source_target_pairs={{0,6},{1,7},{2,4},{3,5},{4,2},{5,3},{6,0},{7,1},{8,14},{9,15},{10,... | collective-permute-start | bytes 393224 | tf_op jit(solution)/shard_map/ppermute | solution.py:22
  69.2 1.0 convert_element_type.245
  70.1 2.8 %collective-permute-done.10 = bf16[2,16,2048]{2,1,0:T(8,128)(2,1)S(1)} collective-permute-done((bf16[2,16,2048]{2,1,0:T(8,128)(2,1)S(1)}, bf16[2,16,2048]{2,1,0:T(8,128)(2,1)S(1)}, u32[]{:S(2)}, u32[]{:S(2)}) %collective-permute-start.10) | collective-permute-done | bytes 131104 | tf_op jit(solution)/shard_map/ppermute | solution.py:22
  73.1 1.8 %collective-permute-start.18 = (bf16[16,19,256]{2,1,0:T(8,128)(2,1)S(1)}, bf16[16,19,256]{2,1,0:T(8,128)(2,1)S(1)}, u32[]{:S(2)}, u32[]{:S(2)}) collective-permute-start(bf16[16,19,256]{2,1,0:T(8,128)(2,1)S(1)} %pad_maximum_fusion.2), channel_id=1, source_target_pairs={{0,8},{8,0},{16,24},{24,16},{32,40},{40,32},{48,56},{56,48},{64,72... | collective-permute-start | bytes 466952 | tf_op jit(solution)/shard_map/ppermute | solution.py:22
  74.9 2.4 %collective-permute-done.11 = bf16[16,2048]{1,0:T(8,128)(2,1)S(1)} collective-permute-done((bf16[16,2048]{1,0:T(8,128)(2,1)S(1)}, bf16[16,2048]{1,0:T(8,128)(2,1)S(1)}, u32[]{:S(2)}, u32[]{:S(2)}) %collective-permute-start.11) | collective-permute-done | bytes 65568 | tf_op jit(solution)/shard_map/ppermute | solution.py:22
  77.7 1.6 %collective-permute-done.18 = bf16[16,19,256]{2,1,0:T(8,128)(2,1)S(1)} collective-permute-done((bf16[16,19,256]{2,1,0:T(8,128)(2,1)S(1)}, bf16[16,19,256]{2,1,0:T(8,128)(2,1)S(1)}, u32[]{:S(2)}, u32[]{:S(2)}) %collective-permute-start.18) | collective-permute-done | bytes 155680 | tf_op jit(solution)/shard_map/ppermute | solution.py:22
  79.3 3.2 %collective-permute-start.19 = (bf16[16,19,256]{2,1,0:T(8,128)(2,1)S(1)}, bf16[16,19,256]{2,1,0:T(8,128)(2,1)S(1)}, u32[]{:S(2)}, u32[]{:S(2)}) collective-permute-start(bf16[16,19,256]{2,1,0:T(8,128)(2,1)S(1)} %fusion.66), channel_id=1, source_target_pairs={{0,24},{8,16},{16,8},{24,0},{32,56},{40,48},{48,40},{56,32},{64,88... | collective-permute-start | bytes 466952 | tf_op jit(solution)/shard_map/ppermute | solution.py:22
  82.7 2.8 %collective-permute-start.13 = (bf16[2,16,2048]{2,1,0:T(8,128)(2,1)S(1)}, bf16[2,16,2048]{2,1,0:T(8,128)(2,1)S(1)}, u32[]{:S(2)}, u32[]{:S(2)}) collective-permute-start(bf16[2,16,2048]{2,1,0:T(8,128)(2,1)S(1)} %pad_maximum_fusion.4), channel_id=1, source_target_pairs={{0,6},{1,7},{2,4},{3,5},{4,2},{5,3},{6,0},{7,1},{8,14},{9,15},{10,... | collective-permute-start | bytes 393224 | tf_op jit(solution)/shard_map/ppermute | solution.py:22
  85.5 0.8 collective-permute-done.19
  86.5 2.5 %collective-permute-done.13 = bf16[2,16,2048]{2,1,0:T(8,128)(2,1)S(1)} collective-permute-done((bf16[2,16,2048]{2,1,0:T(8,128)(2,1)S(1)}, bf16[2,16,2048]{2,1,0:T(8,128)(2,1)S(1)}, u32[]{:S(2)}, u32[]{:S(2)}) %collective-permute-start.13) | collective-permute-done | bytes 131104 | tf_op jit(solution)/shard_map/ppermute | solution.py:22
  89.1 3.0 %collective-permute-done.20 = bf16[16,19,256]{2,1,0:T(8,128)(2,1)S(1)} collective-permute-done((bf16[16,19,256]{2,1,0:T(8,128)(2,1)S(1)}, bf16[16,19,256]{2,1,0:T(8,128)(2,1)S(1)}, u32[]{:S(2)}, u32[]{:S(2)}) %collective-permute-start.20) | collective-permute-done | bytes 155680 | tf_op jit(solution)/shard_map/ppermute | solution.py:22
  92.2 2.7 %collective-permute-start.21 = (bf16[16,19,256]{2,1,0:T(8,128)(2,1)S(1)}, bf16[16,19,256]{2,1,0:T(8,128)(2,1)S(1)}, u32[]{:S(2)}, u32[]{:S(2)}) collective-permute-start(bf16[16,19,256]{2,1,0:T(8,128)(2,1)S(1)} %add.362), channel_id=1, source_target_pairs={{0,64},{8,72},{16,80},{24,88},{32,96},{40,104},{48,112},{56,120},{... | collective-permute-start | bytes 466952 | tf_op jit(solution)/shard_map/ppermute | solution.py:22
  94.9 5.5 %collective-permute-done.21 = bf16[16,19,256]{2,1,0:T(8,128)(2,1)S(1)} collective-permute-done((bf16[16,19,256]{2,1,0:T(8,128)(2,1)S(1)}, bf16[16,19,256]{2,1,0:T(8,128)(2,1)S(1)}, u32[]{:S(2)}, u32[]{:S(2)}) %collective-permute-start.21) | collective-permute-done | bytes 155680 | tf_op jit(solution)/shard_map/ppermute | solution.py:22
  101.0 4.8 %collective-permute-start.22 = (bf16[16,19,256]{2,1,0:T(8,128)(2,1)}, bf16[16,19,256]{2,1,0:T(8,128)(2,1)}, u32[]{:S(2)}, u32[]{:S(2)}) collective-permute-start(bf16[16,19,256]{2,1,0:T(8,128)(2,1)} %add.363), channel_id=1, source_target_pairs={{0,192},{8,200},{16,208},{24,216},{32,224},{40,232},{48,240},{56,2... | collective-permute-start | bytes 466952 | tf_op jit(solution)/shard_map/ppermute | solution.py:22
  106.5 2.4 %convolution_convert_fusion = bf16[128,2048]{1,0:T(8,128)(2,1)S(1)} fusion(bf16[512,2048]{1,0:T(8,128)(2,1)S(1)} %copy-done, bf16[128,2048]{1,0:T(8,128)(2,1)S(1)} %bitcast.169, bf16[2048,512]{1,0:T(8,128)(2,1)} %param.32, f32[128,512]{1,0:T(8,128)S(1)} %fusion.72), kind=kOutput, calls=%fused_computation | convolution fusion | flops 537526272 | bytes 5505024 | tf_op jit(solution)/shard_map/dot_general | solution.py:328
  109.2 5.4 %collective-permute-done.22 = bf16[16,19,256]{2,1,0:T(8,128)(2,1)} collective-permute-done((bf16[16,19,256]{2,1,0:T(8,128)(2,1)}, bf16[16,19,256]{2,1,0:T(8,128)(2,1)}, u32[]{:S(2)}, u32[]{:S(2)}) %collective-permute-start.22) | collective-permute-done | bytes 155680 | tf_op jit(solution)/shard_map/ppermute | solution.py:22
  114.6 1.1 add.364
  115.8 2.8 %collective-permute-start.16 = (bf16[2,16,2048]{2,1,0:T(8,128)(2,1)S(1)}, bf16[2,16,2048]{2,1,0:T(8,128)(2,1)S(1)}, u32[]{:S(2)}, u32[]{:S(2)}) collective-permute-start(bf16[2,16,2048]{2,1,0:T(8,128)(2,1)S(1)} %fusion.16), channel_id=1, source_target_pairs={{0,6},{1,7},{2,4},{3,5},{4,2},{5,3},{6,0},{7,1},{8,14},{9,15},{10,... | collective-permute-start | bytes 393224 | tf_op jit(solution)/shard_map/ppermute | solution.py:22
  118.8 3.7 %collective-permute-done.16 = bf16[2,16,2048]{2,1,0:T(8,128)(2,1)S(1)} collective-permute-done((bf16[2,16,2048]{2,1,0:T(8,128)(2,1)S(1)}, bf16[2,16,2048]{2,1,0:T(8,128)(2,1)S(1)}, u32[]{:S(2)}, u32[]{:S(2)}) %collective-permute-start.16) | collective-permute-done | bytes 131104 | tf_op jit(solution)/shard_map/ppermute | solution.py:22
  122.6 0.8 convolution_convert_fusion.5
  124.1 2.8 %collective-permute-done.17 = bf16[16,2048]{1,0:T(8,128)(2,1)S(1)} collective-permute-done((bf16[16,2048]{1,0:T(8,128)(2,1)S(1)}, bf16[16,2048]{1,0:T(8,128)(2,1)S(1)}, u32[]{:S(2)}, u32[]{:S(2)}) %collective-permute-start.17) | collective-permute-done | bytes 65568 | tf_op jit(solution)/shard_map/ppermute | solution.py:22
  (121 shorter events, 12.3 us)
Async XLA Ops:
  0.6 105.8 %copy-start = (bf16[512,2048]{1,0:T(8,128)(2,1)S(1)}, bf16[512,2048]{1,0:T(8,128)(2,1)}, u32[]{:S(2)}) copy-start(bf16[512,2048]{1,0:T(8,128)(2,1)} %param.33) | copy-start | bytes 6291460
  0.6 9.0 %copy-start.10 = (f32[2048]{0:T(1024)S(1)}, f32[2048]{0:T(1024)}, u32[]{:S(2)}) copy-start(f32[2048]{0:T(1024)} %param.19) | copy-start | bytes 24580
  0.7 8.9 %copy-start.2 = (bf16[2048,256]{1,0:T(8,128)(2,1)S(1)}, bf16[2048,256]{1,0:T(8,128)(2,1)}, u32[]{:S(2)}) copy-start(bf16[2048,256]{1,0:T(8,128)(2,1)} %param.20) | copy-start | bytes 3145732
  0.7 9.2 %copy-start.12 = (f32[256]{0:T(256)S(1)}, f32[256]{0:T(256)}, u32[]{:S(2)}) copy-start(f32[256]{0:T(256)} %param.23) | copy-start | bytes 3076
  0.7 9.4 %copy-start.4 = (bf16[256,160]{0,1:T(8,128)(2,1)S(1)}, bf16[256,160]{0,1:T(8,128)(2,1)}, u32[]{:S(2)}) copy-start(bf16[256,160]{0,1:T(8,128)(2,1)} %param.24) | copy-start | bytes 245764
  0.7 9.7 %copy-start.9 = (f32[16,256]{1,0:T(8,128)S(1)}, f32[16,256]{1,0:T(8,128)}, u32[]{:S(2)}) copy-start(f32[16,256]{1,0:T(8,128)} %param.27) | copy-start | bytes 49156
  1.6 7.8 %collective-permute-start = (bf16[3,2048]{1,0:T(4,128)(2,1)S(1)}, bf16[3,2048]{1,0:T(4,128)(2,1)S(1)}, u32[]{:S(2)}, u32[]{:S(2)}) collective-permute-start(bf16[3,2048]{1,0:T(4,128)(2,1)S(1)} %slice.69), channel_id=1, source_target_pairs={{0,8},{8,16},{16,24},{24,32},{32,40},{40,48},{48,56},{56,64},{64,7... | collective-permute-start | bytes 36872 | tf_op jit(solution)/shard_map/ppermute | solution.py:252
  7.4 21.5 %copy-start.11 = (s32[16]{0:T(128)}, s32[16]{0:T(128)S(1)}, u32[]{:S(2)}) copy-start(s32[16]{0:T(128)S(1)} %get-tuple-element.53) | copy-start | bytes 196
  7.5 38.2 %copy-start.16 = (s32[128]{0:T(128)}, s32[128]{0:T(128)S(1)}, u32[]{:S(2)}) copy-start(s32[128]{0:T(128)S(1)} %convert_reduce_fusion) | copy-start | bytes 1540
  7.6 13.6 %copy-start.5 = (bf16[128,256]{1,0:T(8,128)(2,1)S(1)}, bf16[128,256]{1,0:T(8,128)(2,1)}, u32[]{:S(2)}) copy-start(bf16[128,256]{1,0:T(8,128)(2,1)} %param.25) | copy-start | bytes 196612
  7.6 13.6 %copy-start.13 = (f32[256]{0:T(256)S(1)}, f32[256]{0:T(256)}, u32[]{:S(2)}) copy-start(f32[256]{0:T(256)} %param.26) | copy-start | bytes 3076
  9.4 11.6 %copy-start.6 = (bf16[128,256]{1,0:T(8,128)(2,1)}, bf16[128,256]{1,0:T(8,128)(2,1)S(1)}, u32[]{:S(2)}) copy-start(bf16[128,256]{1,0:T(8,128)(2,1)S(1)} %convolution_convert_fusion.3) | copy-start | bytes 196612
  10.3 1.3 %collective-permute-start.1 = (bf16[128,160]{0,1:T(8,128)(2,1)S(1)}, bf16[128,160]{0,1:T(8,128)(2,1)S(1)}, u32[]{:S(2)}, u32[]{:S(2)}) collective-permute-start(bf16[128,160]{0,1:T(8,128)(2,1)S(1)} %get-tuple-element.57), channel_id=1, source_target_pairs={{0,1},{1,0},{2,3},{3,2},{4,5},{5,4},{6,7},{7,6},{8,9},{9,8},{10,11... | collective-permute-start | bytes 122888 | tf_op jit(solution)/shard_map/ppermute | solution.py:22
  11.6 4.1 %collective-permute-start.2 = (bf16[128,160]{0,1:T(8,128)(2,1)S(1)}, bf16[128,160]{0,1:T(8,128)(2,1)S(1)}, u32[]{:S(2)}, u32[]{:S(2)}) collective-permute-start(bf16[128,160]{0,1:T(8,128)(2,1)S(1)} %fusion.38), channel_id=1, source_target_pairs={{0,2},{1,3},{2,0},{3,1},{4,6},{5,7},{6,4},{7,5},{8,10},{9,11},{10,... | collective-permute-start | bytes 122888 | tf_op jit(solution)/shard_map/ppermute | solution.py:22
  15.7 5.3 %collective-permute-start.3 = (bf16[128,160]{0,1:T(8,128)(2,1)S(1)}, bf16[128,160]{0,1:T(8,128)(2,1)S(1)}, u32[]{:S(2)}, u32[]{:S(2)}) collective-permute-start(bf16[128,160]{0,1:T(8,128)(2,1)S(1)} %fusion.44), channel_id=1, source_target_pairs={{0,6},{1,7},{2,4},{3,5},{4,2},{5,3},{6,0},{7,1},{8,14},{9,15},{10,... | collective-permute-start | bytes 122888 | tf_op jit(solution)/shard_map/ppermute | solution.py:22
  29.7 3.9 %collective-permute-start.4 = (f32[2,16,256]{2,1,0:T(8,128)S(1)}, f32[2,16,256]{2,1,0:T(8,128)S(1)}, u32[]{:S(2)}, u32[]{:S(2)}) collective-permute-start(f32[2,16,256]{2,1,0:T(8,128)S(1)} %pad_maximum_fusion.5), channel_id=1, source_target_pairs={{0,8},{8,0},{16,24},{24,16},{32,40},{40,32},{48,56},{56,48},{64,72... | collective-permute-start | bytes 98312 | tf_op jit(solution)/shard_map/ppermute | solution.py:22
  34.3 4.0 %collective-permute-start.5 = (f32[2,16,256]{2,1,0:T(8,128)S(1)}, f32[2,16,256]{2,1,0:T(8,128)S(1)}, u32[]{:S(2)}, u32[]{:S(2)}) collective-permute-start(f32[2,16,256]{2,1,0:T(8,128)S(1)} %pad_maximum_fusion.6), channel_id=1, source_target_pairs={{0,24},{8,16},{16,8},{24,0},{32,56},{40,48},{48,40},{56,32},{64,88... | collective-permute-start | bytes 98312 | tf_op jit(solution)/shard_map/ppermute | solution.py:22
  38.3 4.0 %collective-permute-start.6 = (f32[2,16,256]{2,1,0:T(8,128)S(1)}, f32[2,16,256]{2,1,0:T(8,128)S(1)}, u32[]{:S(2)}, u32[]{:S(2)}) collective-permute-start(f32[2,16,256]{2,1,0:T(8,128)S(1)} %pad_maximum_fusion.7), channel_id=1, source_target_pairs={{0,32},{8,40},{16,48},{24,56},{32,0},{40,8},{48,16},{56,24},{64,96... | collective-permute-start | bytes 98312 | tf_op jit(solution)/shard_map/ppermute | solution.py:22
  42.4 5.6 %collective-permute-start.7 = (f32[2,16,256]{2,1,0:T(8,128)S(1)}, f32[2,16,256]{2,1,0:T(8,128)S(1)}, u32[]{:S(2)}, u32[]{:S(2)}) collective-permute-start(f32[2,16,256]{2,1,0:T(8,128)S(1)} %pad_maximum_fusion.8), channel_id=1, source_target_pairs={{0,64},{8,72},{16,80},{24,88},{32,96},{40,104},{48,112},{56,120},{... | collective-permute-start | bytes 98312 | tf_op jit(solution)/shard_map/ppermute | solution.py:22
  48.0 6.7 %collective-permute-start.8 = (f32[2,16,256]{2,1,0:T(8,128)S(1)}, f32[2,16,256]{2,1,0:T(8,128)S(1)}, u32[]{:S(2)}, u32[]{:S(2)}) collective-permute-start(f32[2,16,256]{2,1,0:T(8,128)S(1)} %pad_maximum_fusion.9), channel_id=1, source_target_pairs={{0,192},{8,200},{16,208},{24,216},{32,224},{40,232},{48,240},{56,2... | collective-permute-start | bytes 98312 | tf_op jit(solution)/shard_map/ppermute | solution.py:22
  55.3 5.4 %copy-start.3 = (bf16[128,2048]{1,0:T(8,128)(2,1)S(1)}, bf16[128,2048]{1,0:T(8,128)(2,1)}, u32[]{:S(2)}) copy-start(bf16[128,2048]{1,0:T(8,128)(2,1)} %param.18) | copy-start | bytes 1572868
  55.3 5.4 %copy-start.15 = (f32[256]{0:T(256)S(1)}, f32[256]{0:T(256)}, u32[]{:S(2)}) copy-start(f32[256]{0:T(256)} %param.28) | copy-start | bytes 3076
  60.7 8.2 %copy-start.7 = (bf16[128,256]{1,0:T(8,128)(2,1)S(1)}, bf16[128,256]{1,0:T(8,128)(2,1)}, u32[]{:S(2)}) copy-start(bf16[128,256]{1,0:T(8,128)(2,1)} %copy-done.6) | copy-start | bytes 196612
  63.2 14.2 %copy-start.8 = (f32[2048]{0:T(1024)S(1)}, f32[2048]{0:T(1024)}, u32[]{:S(2)}) copy-start(f32[2048]{0:T(1024)} %param.30) | copy-start | bytes 24580
  63.3 1.8 %collective-permute-start.9 = (bf16[2,2,16,2048]{3,2,1,0:T(8,128)(2,1)S(1)}, bf16[2,2,16,2048]{3,2,1,0:T(8,128)(2,1)}, u32[]{:S(2)}, u32[]{:S(2)}) collective-permute-start(bf16[2,2,16,2048]{3,2,1,0:T(8,128)(2,1)S(1)} %dynamic-slice_bitcast_fusion.1), channel_id=1, source_target_pairs={{0,1},{1,0},{2,3},{3,2},{4,5},{5,4},{6,7},{7,6},{8,9},{9,8},{10,11... | collective-permute-start | bytes 786440 | tf_op jit(solution)/shard_map/ppermute | solution.py:22
  66.1 6.8 %collective-permute-start.10 = (bf16[2,16,2048]{2,1,0:T(8,128)(2,1)S(1)}, bf16[2,16,2048]{2,1,0:T(8,128)(2,1)S(1)}, u32[]{:S(2)}, u32[]{:S(2)}) collective-permute-start(bf16[2,16,2048]{2,1,0:T(8,128)(2,1)S(1)} %fusion.15), channel_id=1, source_target_pairs={{0,6},{1,7},{2,4},{3,5},{4,2},{5,3},{6,0},{7,1},{8,14},{9,15},{10,... | collective-permute-start | bytes 393224 | tf_op jit(solution)/shard_map/ppermute | solution.py:22
  73.0 4.4 %collective-permute-start.11 = (bf16[16,2048]{1,0:T(8,128)(2,1)S(1)}, bf16[16,2048]{1,0:T(8,128)(2,1)S(1)}, u32[]{:S(2)}, u32[]{:S(2)}) collective-permute-start(bf16[16,2048]{1,0:T(8,128)(2,1)S(1)} %fusion.30), channel_id=1, source_target_pairs={{0,2},{1,3},{2,0},{3,1},{4,6},{5,7},{6,4},{7,5},{8,10},{9,11},{10,... | collective-permute-start | bytes 196616 | tf_op jit(solution)/shard_map/ppermute | solution.py:22
  73.1 6.2 %collective-permute-start.18 = (bf16[16,19,256]{2,1,0:T(8,128)(2,1)S(1)}, bf16[16,19,256]{2,1,0:T(8,128)(2,1)S(1)}, u32[]{:S(2)}, u32[]{:S(2)}) collective-permute-start(bf16[16,19,256]{2,1,0:T(8,128)(2,1)S(1)} %pad_maximum_fusion.2), channel_id=1, source_target_pairs={{0,8},{8,0},{16,24},{24,16},{32,40},{40,32},{48,56},{56,48},{64,72... | collective-permute-start | bytes 466952 | tf_op jit(solution)/shard_map/ppermute | solution.py:22
  77.6 5.0 %collective-permute-start.12 = (bf16[16,2048]{1,0:T(8,128)(2,1)S(1)}, bf16[16,2048]{1,0:T(8,128)(2,1)S(1)}, u32[]{:S(2)}, u32[]{:S(2)}) collective-permute-start(bf16[16,2048]{1,0:T(8,128)(2,1)S(1)} %multiply_convert_fusion), channel_id=1, source_target_pairs={{0,2},{1,3},{2,0},{3,1},{4,6},{5,7},{6,4},{7,5},{8,10},{9,11},{10,... | collective-permute-start | bytes 196616 | tf_op jit(solution)/shard_map/ppermute | solution.py:22
  79.3 7.0 %collective-permute-start.19 = (bf16[16,19,256]{2,1,0:T(8,128)(2,1)S(1)}, bf16[16,19,256]{2,1,0:T(8,128)(2,1)S(1)}, u32[]{:S(2)}, u32[]{:S(2)}) collective-permute-start(bf16[16,19,256]{2,1,0:T(8,128)(2,1)S(1)} %fusion.66), channel_id=1, source_target_pairs={{0,24},{8,16},{16,8},{24,0},{32,56},{40,48},{48,40},{56,32},{64,88... | collective-permute-start | bytes 466952 | tf_op jit(solution)/shard_map/ppermute | solution.py:22
  82.7 6.3 %collective-permute-start.13 = (bf16[2,16,2048]{2,1,0:T(8,128)(2,1)S(1)}, bf16[2,16,2048]{2,1,0:T(8,128)(2,1)S(1)}, u32[]{:S(2)}, u32[]{:S(2)}) collective-permute-start(bf16[2,16,2048]{2,1,0:T(8,128)(2,1)S(1)} %pad_maximum_fusion.4), channel_id=1, source_target_pairs={{0,6},{1,7},{2,4},{3,5},{4,2},{5,3},{6,0},{7,1},{8,14},{9,15},{10,... | collective-permute-start | bytes 393224 | tf_op jit(solution)/shard_map/ppermute | solution.py:22
  86.4 5.8 %collective-permute-start.20 = (bf16[16,19,256]{2,1,0:T(8,128)(2,1)S(1)}, bf16[16,19,256]{2,1,0:T(8,128)(2,1)S(1)}, u32[]{:S(2)}, u32[]{:S(2)}) collective-permute-start(bf16[16,19,256]{2,1,0:T(8,128)(2,1)S(1)} %add.361), channel_id=1, source_target_pairs={{0,32},{8,40},{16,48},{24,56},{32,0},{40,8},{48,16},{56,24},{64,96... | collective-permute-start | bytes 466952 | tf_op jit(solution)/shard_map/ppermute | solution.py:22
  89.0 16.9 %collective-permute-start.14 = (bf16[2,2,16,2048]{3,2,1,0:T(8,128)(2,1)S(1)}, bf16[2,2,16,2048]{3,2,1,0:T(8,128)(2,1)S(1)}, u32[]{:S(2)}, u32[]{:S(2)}) collective-permute-start(bf16[2,2,16,2048]{3,2,1,0:T(8,128)(2,1)S(1)} %pad_maximum_fusion.1), channel_id=1, source_target_pairs={{0,1},{1,0},{2,3},{3,2},{4,5},{5,4},{6,7},{7,6},{8,9},{9,8},{10,11... | collective-permute-start | bytes 786440 | tf_op jit(solution)/shard_map/ppermute | solution.py:22
  92.2 8.1 %collective-permute-start.21 = (bf16[16,19,256]{2,1,0:T(8,128)(2,1)S(1)}, bf16[16,19,256]{2,1,0:T(8,128)(2,1)S(1)}, u32[]{:S(2)}, u32[]{:S(2)}) collective-permute-start(bf16[16,19,256]{2,1,0:T(8,128)(2,1)S(1)} %add.362), channel_id=1, source_target_pairs={{0,64},{8,72},{16,80},{24,88},{32,96},{40,104},{48,112},{56,120},{... | collective-permute-start | bytes 466952 | tf_op jit(solution)/shard_map/ppermute | solution.py:22
  94.9 11.1 %copy-start.1 = (bf16[2048,512]{1,0:T(8,128)(2,1)S(1)}, bf16[2048,512]{1,0:T(8,128)(2,1)}, u32[]{:S(2)}) copy-start(bf16[2048,512]{1,0:T(8,128)(2,1)} %param.31) | copy-start | bytes 6291460
  101.0 13.5 %collective-permute-start.22 = (bf16[16,19,256]{2,1,0:T(8,128)(2,1)}, bf16[16,19,256]{2,1,0:T(8,128)(2,1)}, u32[]{:S(2)}, u32[]{:S(2)}) collective-permute-start(bf16[16,19,256]{2,1,0:T(8,128)(2,1)} %add.363), channel_id=1, source_target_pairs={{0,192},{8,200},{16,208},{24,216},{32,224},{40,232},{48,240},{56,2... | collective-permute-start | bytes 466952 | tf_op jit(solution)/shard_map/ppermute | solution.py:22
  106.5 2.6 %copy-start.17 = (s32[128]{0:T(128)S(1)}, s32[128]{0:T(128)}, u32[]{:S(2)}) copy-start(s32[128]{0:T(128)} %copy-done.16) | copy-start | bytes 1540
  108.9 9.7 %copy-start.14 = (s32[4]{0:T(128)S(1)}, s32[4]{0:T(128)}, u32[]{:S(2)}) copy-start(s32[4]{0:T(128)} %param.35) | copy-start | bytes 52
  108.9 6.7 %collective-permute-start.15 = (bf16[2,2,16,2048]{3,2,1,0:T(8,128)(2,1)S(1)}, bf16[2,2,16,2048]{3,2,1,0:T(8,128)(2,1)S(1)}, u32[]{:S(2)}, u32[]{:S(2)}) collective-permute-start(bf16[2,2,16,2048]{3,2,1,0:T(8,128)(2,1)S(1)} %dynamic-slice_bitcast_fusion), channel_id=1, source_target_pairs={{0,1},{1,0},{2,3},{3,2},{4,5},{5,4},{6,7},{7,6},{8,9},{9,8},{10,11... | collective-permute-start | bytes 786440 | tf_op jit(solution)/shard_map/ppermute | solution.py:22
  115.8 6.7 %collective-permute-start.16 = (bf16[2,16,2048]{2,1,0:T(8,128)(2,1)S(1)}, bf16[2,16,2048]{2,1,0:T(8,128)(2,1)S(1)}, u32[]{:S(2)}, u32[]{:S(2)}) collective-permute-start(bf16[2,16,2048]{2,1,0:T(8,128)(2,1)S(1)} %fusion.16), channel_id=1, source_target_pairs={{0,6},{1,7},{2,4},{3,5},{4,2},{5,3},{6,0},{7,1},{8,14},{9,15},{10,... | collective-permute-start | bytes 393224 | tf_op jit(solution)/shard_map/ppermute | solution.py:22
  122.5 4.4 %collective-permute-start.17 = (bf16[16,2048]{1,0:T(8,128)(2,1)S(1)}, bf16[16,2048]{1,0:T(8,128)(2,1)S(1)}, u32[]{:S(2)}, u32[]{:S(2)}) collective-permute-start(bf16[16,2048]{1,0:T(8,128)(2,1)S(1)} %fusion.31), channel_id=1, source_target_pairs={{0,2},{1,3},{2,0},{3,1},{4,6},{5,7},{6,4},{7,5},{8,10},{9,11},{10,... | collective-permute-start | bytes 196616 | tf_op jit(solution)/shard_map/ppermute | solution.py:22
